TPU v7x, 32 devices: a whole 2x2x4 slice. The times are simulated.
32 devices in a mesh: groups: 1, rows: 32 (over z, y, x, core).
Axes of the slice: x: 2, y: 2, z: 4, core: 2. Of those that a mesh axis runs over, the one named last changes fastest.
Arguments:
- acts: bfloat16 [4096, 2, 4096], P(('groups', 'rows')), may hold values from -6 to 6
- grads_out: bfloat16 [4096, 2, 4096], P(('groups', 'rows')), may hold values from -6 to 6
- lengths: int32 [32], P('groups'), may hold values from 1 to 512, 4096 in all
- valid: int32 [4096], P(('groups', 'rows')), may hold values 0 or 1
- proj_in: bfloat16 [4096, 128], replicated, may hold values from -0.09375 to 0.09375
- proj_out: bfloat16 [4096, 128], replicated, may hold values from -0.09375 to 0.09375
- fisher_inv: float32 [2, 4096, 4096], P(None, 'rows'), may hold values from -1 to 2, as said below
- database: float32 [4096, 2, 4096], P(('groups', 'rows')), may hold values from -250 to 250
Outputs:
- zscores: float32 [32, 4096], P(None, ('groups', 'rows'))
Inputs may be any that keep to these rules, and one draw needn't show every extreme that they name: The lengths sum to 4096; the largest is exactly 512. `fisher_inv`: each of the 2 blocks is symmetric.
All inputs are finite; a program needn't handle non-finite values. No bound on the sum of `valid` on one device may be relied on, other than what follows from the above.
Results may differ from a plain program's by a relative error of at most 0.0042.
Values sent between devices are 32-bit elements; how exact they have to be, the bound alone decides.
No kernel may reach another device: no remote copies, remote signals or barrier semaphores. Data moves between devices by JAX's collectives and lax.ppermute only.
A program may use at most 64 MiB of HBM per device.

v0:
```python
import jax
import jax.numpy as jnp
from jax import lax
from jax.sharding import PartitionSpec as P


def shards(acts, grads_out, lengths, valid, proj_in, proj_out, fisher_inv, database):
    tok_rows = acts.shape[0]
    modules = acts.shape[1]
    proj_rank = proj_in.shape[1] // modules
    queries = lengths.shape[0]
    flat_width = proj_rank * proj_rank
    first_pos = lax.axis_index("rows") * tok_rows
    positions = first_pos + jnp.arange(tok_rows, dtype=jnp.int32)
    seg_ends = jnp.cumsum(lengths)
    segment = jnp.sum((seg_ends[None, :] <= positions[:, None]).astype(jnp.int32), axis=1)
    selector = (
        (segment[:, None] == jnp.arange(queries, dtype=jnp.int32)[None, :]) & (valid[:, None] == 1)
    ).astype(jnp.bfloat16)
    module_sums = []
    for m in range(modules):
        act_proj = jnp.dot(
            acts[:, m, :],
            proj_in[:, m * proj_rank : (m + 1) * proj_rank],
            preferred_element_type=jnp.float32,
        ).astype(jnp.bfloat16)
        grad_proj = jnp.dot(
            grads_out[:, m, :],
            proj_out[:, m * proj_rank : (m + 1) * proj_rank],
            preferred_element_type=jnp.float32,
        ).astype(jnp.bfloat16)
        spread = (selector[:, :, None] * grad_proj[:, None, :]).reshape(
            tok_rows, queries * proj_rank
        )
        module_sum = lax.dot_general(
            spread, act_proj, (((0,), (0,)), ((), ())), preferred_element_type=jnp.float32
        )
        module_sums.append(module_sum.reshape(queries, flat_width))
    partial_value = jnp.stack(module_sums, axis=1)
    summed = lax.psum(partial_value, "rows")
    precond_cols = jnp.einsum("qmk,mck->qmc", summed, fisher_inv, precision=lax.Precision.HIGHEST)
    scores = jnp.einsum(
        "qmk,nmk->qn",
        lax.all_gather(precond_cols, "rows", axis=2, tiled=True),
        database,
        precision=lax.Precision.HIGHEST,
    )
    db_count = database.shape[0] * lax.axis_size("rows")
    first_moment, second_moment = lax.psum(
        (jnp.sum(scores, axis=1), jnp.sum(scores * scores, axis=1)), "rows"
    )
    avg_score = first_moment / db_count
    variance = second_moment / db_count - avg_score * avg_score
    centred = scores - avg_score[:, None]
    return centred * lax.rsqrt(variance + 1e-06)[:, None]


def solution(mesh):
    placed = (
        P(("groups", "rows"), None, None),
        P(("groups", "rows"), None, None),
        P("groups"),
        P(("groups", "rows")),
        P(),
        P(),
        P(None, "rows", None),
        P(("groups", "rows"), None, None),
    )
    return jax.shard_map(
        shards, mesh=mesh, in_specs=placed, out_specs=P(None, ("groups", "rows")), check_vma=False
    )
```

profile of v0, /device:TPU:0, one launch (start us, length us, event | category | flops | bytes accessed | tf_op | source)
XLA Modules:
  0.0 286.0 jit_solution(3558763104719825832)
XLA Ops:
  6.5 6.1 %fusion.17 = (bf16[128,1,4096]{2,1,0:T(2,128)(2,1)S(1)}, bf16[128,1,4096]{2,1,0:T(2,128)(2,1)S(1)}) fusion(bf16[128,2,4096]{2,1,0:T(2,128)(2,1)} %param.9), kind=kLoop, calls=%fused_computation.33 | loop fusion | bytes 4194304 | tf_op jit(solution)/shard_map/slice | solution.py:28
  12.7 0.0 copy-start.3
  12.7 1.6 convolution_convert_fusion.1
  14.4 1.3 convolution_convert_fusion.3
  15.7 0.1 copy.21
  15.8 0.1 reduce-window.8
  15.8 0.1 reduce
  16.0 5.8 %fusion.16 = (bf16[128,1,4096]{2,1,0:T(2,128)(2,1)}, bf16[128,1,4096]{2,1,0:T(2,128)(2,1)}) fusion(bf16[128,2,4096]{2,1,0:T(2,128)(2,1)S(1)} %copy-done), kind=kLoop, calls=%fused_computation.32 | loop fusion | bytes 4194304 | tf_op jit(solution)/shard_map/slice | solution.py:23
  21.9 0.1 convert_reduce_fusion
  22.0 1.1 broadcast_multiply_fusion.1
  23.0 4.6 %fusion.2 = f32[2048,64]{1,0:T(8,128)} fusion(bf16[128,2048]{0,1:T(8,128)(2,1)} %bitcast.27, bf16[128,1,4096]{2,1,0:T(2,128)(2,1)} %get-tuple-element.9, bf16[4096,128]{1,0:T(8,128)(2,1)S(1)} %copy-done.2), kind=kOutput, calls=%fused_computation.7 | convolution fusion | flops 100671488 | bytes 3145728 | tf_op jit(solution)/shard_map/dot_general | solution.py:35
  27.6 2.4 stack_reshape.6
  30.0 4.0 %fusion.3 = f32[2048,64]{1,0:T(8,128)} fusion(bf16[128,2048]{0,1:T(8,128)(2,1)} %bitcast.26, bf16[128,1,4096]{2,1,0:T(2,128)(2,1)S(1)} %copy-done.1, bf16[4096,128]{1,0:T(8,128)(2,1)S(1)} %copy-done.2), kind=kOutput, calls=%fused_computation.8 | convolution fusion | flops 100671488 | bytes 3145728 | tf_op jit(solution)/shard_map/dot_general | solution.py:35
  34.0 1.6 stack_reshape.7
  35.6 2.1 pad_maximum_fusion
  37.7 0.0 all-reduce.3.cloned.1.call-update
  37.8 0.2 all-gather.2.cloned.1.call-start
  38.0 133.4 %all-reduce.3.cloned.1.call-done = f32[32,2,4096]{2,0,1:T(8,128)} async-done(((f32[32,2,4096]{2,0,1:T(8,128)}), f32[32,2,4096]{2,0,1:T(8,128)}) %all-reduce.3.cloned.1.call-update) | async-done | bytes 1048592 | tf_op jit(solution)/shard_map/psum | solution.py:40
  171.4 7.3 %convolution_bitcast_fusion = f32[32,2,128]{2,0,1:T(8,128)} fusion(f32[32,2,4096]{2,0,1:T(8,128)} %all-reduce.3.cloned.1.call-done, f32[2,128,4096]{2,1,0:T(8,128)} %param.14), kind=kOutput, calls=%fused_computation.2 | convolution fusion | flops 402653184 | bytes 5275648 | tf_op jit(solution)/shard_map/qmk,mck->qmc/dot_general | solution.py:41
  178.7 0.0 all-gather.2.cloned.1.call-update
  178.8 51.4 %all-gather.2.cloned.1.call-done = f32[32,2,4096]{2,0,1:T(8,128)} async-done(((f32[32,2,128]{2,0,1:T(8,128)}), f32[32,2,4096]{2,0,1:T(8,128)}) %all-gather.2.cloned.1.call-update) | async-done | bytes 1048592 | tf_op jit(solution)/shard_map/all_gather | solution.py:44
  230.2 8.2 %fusion.15 = (f32[32]{0:T(128)S(1)}, f32[32]{0:T(128)S(1)}, f32[32,128]{1,0:T(8,128)S(1)}) fusion(f32[32,2,4096]{2,0,1:T(8,128)} %all-gather.2.cloned.1.call-done, f32[128,2,4096]{2,1,0:T(2,128)} %param.15), kind=kOutput, calls=%fused_computation.31 | convolution fusion | flops 402665408 | bytes 5259520 | tf_op jit(solution)/shard_map/qmk,nmk->qn/dot_general | solution.py:42
  238.3 40.1 %all-reduce = (f32[32]{0:T(128)S(1)}, f32[32]{0:T(128)S(1)}) all-reduce(f32[32]{0:T(128)S(1)} %get-tuple-element.6, f32[32]{0:T(128)S(1)} %get-tuple-element.5), channel_id=1, replica_groups=mesh['groups'=1,'rows'=32] {'rows'}, use_global_device_ids=true, to_apply=%region_6.7 | all-reduce | flops 64 | bytes 512 | tf_op jit(solution)/shard_map/psum | solution.py:49
  278.5 0.7 subtract_multiply_fusion
  (16 shorter events, 0.1 us)
Async XLA Ops:
  6.5 164.9 %all-reduce.3.cloned.1.call-start = ((), (), s32[]{:S(2)}) async-start(), calls=%async_computation | async-start | bytes 2097152 | tf_op jit(solution)/shard_map/psum | solution.py:40
  6.5 6.1 %copy-start.4 = (bf16[4096,128]{1,0:T(8,128)(2,1)S(1)}, bf16[4096,128]{1,0:T(8,128)(2,1)}, u32[]{:S(2)}) copy-start(bf16[4096,128]{1,0:T(8,128)(2,1)} %param.13) | copy-start | bytes 3145732
  12.7 3.0 %copy-start.3 = (s32[32]{0:T(128)S(1)}, s32[32]{0:T(128)}, u32[]{:S(2)}) copy-start(s32[32]{0:T(128)} %param.10) | copy-start | bytes 388
  12.7 3.3 %copy-start.5 = (s32[128]{0:T(128)S(1)}, s32[128]{0:T(128)}, u32[]{:S(2)}) copy-start(s32[128]{0:T(128)} %param.11) | copy-start | bytes 1540
  12.7 3.3 %copy-start = (bf16[128,2,4096]{2,1,0:T(2,128)(2,1)S(1)}, bf16[128,2,4096]{2,1,0:T(2,128)(2,1)}, u32[]{:S(2)}) copy-start(bf16[128,2,4096]{2,1,0:T(2,128)(2,1)} %param.8) | copy-start | bytes 6291460
  16.0 7.0 %copy-start.2 = (bf16[4096,128]{1,0:T(8,128)(2,1)S(1)}, bf16[4096,128]{1,0:T(8,128)(2,1)}, u32[]{:S(2)}) copy-start(bf16[4096,128]{1,0:T(8,128)(2,1)} %param.12) | copy-start | bytes 3145732
  23.0 7.0 %copy-start.1 = (bf16[128,1,4096]{2,1,0:T(2,128)(2,1)S(1)}, bf16[128,1,4096]{2,1,0:T(2,128)(2,1)}, u32[]{:S(2)}) copy-start(bf16[128,1,4096]{2,1,0:T(2,128)(2,1)} %get-tuple-element.10) | copy-start | bytes 3145732
  37.8 192.4 %all-gather.2.cloned.1.call-start = ((), (), s32[]{:S(2)}) async-start(), calls=%async_computation.1 | async-start | bytes 1081344 | tf_op jit(solution)/shard_map/all_gather | solution.py:44
Sparse Core Ops, SparseCore 0:
  37.9 133.4 all-reduce.2
  178.9 51.2 all-gather.1
where the time goes:
time: 286 us
  waiting for transfers between devices  185 us (65%)
  blocking collectives  40.1 us (14%)
  matrix products  27.1 us (9%)
  local copies, waits for them, and re-layouts  16 us (6%)
  between operations  13.5 us (5%)
  other arithmetic  4.19 us (1%)
    psum x1, waiting for transfers between devices, shards(): summed = lax.psum(partial_value, 'rows')  133 us
    all_gather x1, waiting for transfers between devices, shards(): lax.all_gather(precond_cols, 'rows', axis=2, tiled=True)  51.4 us
    psum x1, blocking collectives, shards(): lax.psum((jnp.sum(scores, axis=1), jnp.sum(scores * scores, axis=1)), 'ro...  40.1 us
    dot_general x2, matrix products, shards(): lax.dot_general(spread, act_proj, (((0,), (0,)), ((), ())), preferred_ele...  8.6 us
    dot_general x1, matrix products, shards(): jnp.einsum('qmk,nmk->qn', lax.all_gather(precond_cols, 'rows', axis=2, ti...  8.16 us
    dot_general x1, matrix products, shards(): jnp.einsum('qmk,mck->qmc', summed, fisher_inv, precision=lax.Precision.HI...  7.35 us
    slice x1, local copies, waits for them, and re-layouts, shards(): grads_out[:, m, :]  6.11 us
    slice x1, local copies, waits for them, and re-layouts, shards(): acts[:, m, :]  5.84 us
  transfers between devices with their start and end apart: 2, of which 2 were waited for; matrix products, arithmetic and copies ran while one was open for 0% of the time, Pallas kernels for 0%

commit v1 on v0

--- a/solution.py
+++ b/solution.py
@@ -4,7 +4,56 @@
 from jax.sharding import PartitionSpec as P
 
 
-def shards(acts, grads_out, lengths, valid, proj_in, proj_out, fisher_inv, database):
+def _xor_pairs(size, bit):
+    return [(i, i ^ (1 << bit)) for i in range(size)]
+
+
+def _steps(size):
+    steps = size.bit_length() - 1
+    assert (1 << steps) == size
+    return steps
+
+
+def _join(mine, other, low, axis):
+    return jnp.where(
+        low, jnp.concatenate([mine, other], axis), jnp.concatenate([other, mine], axis)
+    )
+
+
+def _allreduce(x, size, axis):
+    me = lax.axis_index("rows")
+    steps = _steps(size)
+    cur = x
+    for s in range(steps):
+        half = cur.shape[axis] // 2
+        lo = lax.slice_in_dim(cur, 0, half, axis=axis)
+        hi = lax.slice_in_dim(cur, half, 2 * half, axis=axis)
+        low = ((me >> s) & 1) == 0
+        keep = jnp.where(low, lo, hi)
+        send = jnp.where(low, hi, lo)
+        cur = keep + lax.ppermute(send, "rows", _xor_pairs(size, s))
+    for s in reversed(range(steps)):
+        low = ((me >> s) & 1) == 0
+        cur = _join(cur, lax.ppermute(cur, "rows", _xor_pairs(size, s)), low, axis)
+    return cur
+
+
+def _allgather(x, size, axis):
+    me = lax.axis_index("rows")
+    cur = x
+    for s in range(_steps(size)):
+        low = ((me >> s) & 1) == 0
+        cur = _join(cur, lax.ppermute(cur, "rows", _xor_pairs(size, s)), low, axis)
+    return cur
+
+
+def _butterfly_sum(x, size):
+    for s in range(_steps(size)):
+        x = x + lax.ppermute(x, "rows", _xor_pairs(size, s))
+    return x
+
+
+def shards(size, acts, grads_out, lengths, valid, proj_in, proj_out, fisher_inv, database):
     tok_rows = acts.shape[0]
     modules = acts.shape[1]
     proj_rank = proj_in.shape[1] // modules
@@ -37,25 +86,26 @@
         )
         module_sums.append(module_sum.reshape(queries, flat_width))
     partial_value = jnp.stack(module_sums, axis=1)
-    summed = lax.psum(partial_value, "rows")
+    summed = _allreduce(partial_value, size, 2)
     precond_cols = jnp.einsum("qmk,mck->qmc", summed, fisher_inv, precision=lax.Precision.HIGHEST)
     scores = jnp.einsum(
         "qmk,nmk->qn",
-        lax.all_gather(precond_cols, "rows", axis=2, tiled=True),
+        _allgather(precond_cols, size, 2),
         database,
         precision=lax.Precision.HIGHEST,
     )
-    db_count = database.shape[0] * lax.axis_size("rows")
-    first_moment, second_moment = lax.psum(
-        (jnp.sum(scores, axis=1), jnp.sum(scores * scores, axis=1)), "rows"
+    db_count = database.shape[0] * size
+    moments = _butterfly_sum(
+        jnp.stack([jnp.sum(scores, axis=1), jnp.sum(scores * scores, axis=1)]), size
     )
-    avg_score = first_moment / db_count
-    variance = second_moment / db_count - avg_score * avg_score
+    avg_score = moments[0] / db_count
+    variance = moments[1] / db_count - avg_score * avg_score
     centred = scores - avg_score[:, None]
     return centred * lax.rsqrt(variance + 1e-06)[:, None]
 
 
 def solution(mesh):
+    size = mesh.shape["rows"]
     placed = (
         P(("groups", "rows"), None, None),
         P(("groups", "rows"), None, None),
@@ -67,5 +117,9 @@
         P(("groups", "rows"), None, None),
     )
     return jax.shard_map(
-        shards, mesh=mesh, in_specs=placed, out_specs=P(None, ("groups", "rows")), check_vma=False
+        lambda *a: shards(size, *a),
+        mesh=mesh,
+        in_specs=placed,
+        out_specs=P(None, ("groups", "rows")),
+        check_vma=False,
     )

time: 286 us -> 151 us (0.53)
  waiting for transfers between devices: 185 us -> 72.5 us
  blocking collectives: 40.1 us -> 0 us
  starting transfers between devices: 0.22 us -> 33.1 us
  between operations: 13.5 us -> 0.23 us
  matrix products: 27.1 us -> 23.8 us
    psum x1 -> x0, waiting for transfers between devices: 133 us -> none  [shards(): summed = lax.psum(partial_value, 'rows')]
    ppermute x0 -> x20, waiting for transfers between devices: none -> 72.5 us  [the longest x5 31.6 us: _allgather(): cur = _join(cur, lax.ppermute(cur, 'rows', _xor_pairs(size, s)), low, axis)]
    all_gather x1 -> x0, waiting for transfers between devices: 51.4 us -> none  [shards(): lax.all_gather(precond_cols, 'rows', axis=2, tiled=True)]
    psum x1 -> x0, blocking collectives: 40.1 us -> none  [shards(): lax.psum((jnp.sum(scores, axis=1), jnp.sum(scores * scores, axis=1)), 'ro...]
    ppermute x0 -> x20, starting transfers between devices: none -> 33.1 us  [the longest x5 10.5 us: _allreduce(): cur = keep + lax.ppermute(send, 'rows', _xor_pairs(size, s))]
  transfers between devices with their start and end apart: 2 -> 20, of which waited for: 2 -> 20; matrix products, arithmetic and copies ran while one was open for 0% -> 0% of each run, Pallas kernels for 0% -> 0%
where the time goes in v1:
time: 151 us; the launch traced here: 150 us
  waiting for transfers between devices  72.5 us (48%)
  starting transfers between devices  33.1 us (22%)
  matrix products  23.8 us (16%)
  local copies, waits for them, and re-layouts  17.6 us (12%)
  other arithmetic  3.21 us (2%)
    ppermute x5, waiting for transfers between devices, _allgather(): cur = _join(cur, lax.ppermute(cur, 'rows', _xor_pairs(size, s)), low, axis)  31.6 us
    ppermute x5, waiting for transfers between devices, _allreduce(): cur = keep + lax.ppermute(send, 'rows', _xor_pairs(size, s))  15.8 us
    ppermute x5, waiting for transfers between devices, _allreduce(): cur = _join(cur, lax.ppermute(cur, 'rows', _xor_pairs(size, s)), low, axis)  14.6 us
    ppermute x5, waiting for transfers between devices, _butterfly_sum(): x = x + lax.ppermute(x, 'rows', _xor_pairs(size, s))  10.5 us
    ppermute x5, starting transfers between devices, _allreduce(): cur = keep + lax.ppermute(send, 'rows', _xor_pairs(size, s))  10.5 us
    dot_general x2, matrix products, shards(): lax.dot_general(spread, act_proj, (((0,), (0,)), ((), ())), preferred_ele...  8.8 us
    ppermute x5, starting transfers between devices, _allgather(): cur = _join(cur, lax.ppermute(cur, 'rows', _xor_pairs(size, s)), low, axis)  8.59 us
    ppermute x5, starting transfers between devices, _allreduce(): cur = _join(cur, lax.ppermute(cur, 'rows', _xor_pairs(size, s)), low, axis)  8.05 us
  transfers between devices with their start and end apart: 20, of which 20 were waited for; matrix products, arithmetic and copies ran while one was open for 0% of the time, Pallas kernels for 0%

profile of v1, /device:TPU:0, one launch (start us, length us, event | category | flops | bytes accessed | tf_op | source)
XLA Modules:
  0.0 150.4 jit_solution(2324543316897395417)
XLA Ops:
  1.6 6.3 %fusion.34 = (bf16[128,1,4096]{2,1,0:T(2,128)(2,1)S(1)}, bf16[128,1,4096]{2,1,0:T(2,128)(2,1)S(1)}) fusion(bf16[128,2,4096]{2,1,0:T(2,128)(2,1)} %param.9), kind=kLoop, calls=%fused_computation.72 | loop fusion | bytes 4194304 | tf_op jit(solution)/shard_map/slice | solution.py:77
  10.9 5.5 %fusion.33 = (bf16[128,1,4096]{2,1,0:T(2,128)(2,1)S(1)}, bf16[128,1,4096]{2,1,0:T(2,128)(2,1)}) fusion(bf16[128,2,4096]{2,1,0:T(2,128)(2,1)S(1)} %copy-done), kind=kLoop, calls=%fused_computation.71 | loop fusion | bytes 4194304 | tf_op jit(solution)/shard_map/slice | solution.py:72
  17.6 4.5 %fusion.2 = f32[2048,64]{1,0:T(8,128)} fusion(bf16[128,2048]{0,1:T(8,128)(2,1)} %bitcast.37, bf16[128,1,4096]{2,1,0:T(2,128)(2,1)} %get-tuple-element.8, bf16[4096,128]{1,0:T(8,128)(2,1)S(1)} %copy-done.1), kind=kOutput, calls=%fused_computation.7 | convolution fusion | flops 100671488 | bytes 3145728 | tf_op jit(solution)/shard_map/dot_general | solution.py:84
  22.1 2.4 %stack_reshape.6 = f32[32,1,4096]{2,0,1:T(8,128)} reshape(f32[2048,64]{1,0:T(8,128)} %fusion.2) | data formatting | bytes 1048576 | tf_op jit(solution)/shard_map/stack;reshape | solution.py:88
  25.5 4.3 %fusion.3 = f32[2048,64]{1,0:T(8,128)} fusion(bf16[128,2048]{0,1:T(8,128)(2,1)} %bitcast.36, bf16[128,1,4096]{2,1,0:T(2,128)(2,1)S(1)} %get-tuple-element.7, bf16[4096,128]{1,0:T(8,128)(2,1)} %param.12), kind=kOutput, calls=%fused_computation.8 | convolution fusion | flops 100671488 | bytes 3145728 | tf_op jit(solution)/shard_map/dot_general | solution.py:84
  33.8 2.9 %collective-permute-start.1 = (f32[32,2,1024]{2,0,1:T(8,128)S(1)}, f32[32,2,1024]{2,0,1:T(8,128)S(1)}, u32[]{:S(2)}, u32[]{:S(2)}) collective-permute-start(f32[32,2,1024]{2,0,1:T(8,128)S(1)} %slice_select_fusion.1), channel_id=1, source_target_pairs={{0,2},{1,3},{2,0},{3,1},{4,6},{5,7},{6,4},{7,5},{8,10},{9,11},{10,... | collective-permute-start | bytes 786440 | tf_op jit(solution)/shard_map/ppermute | solution.py:34
  36.7 6.6 %collective-permute-done.1 = f32[32,2,1024]{2,0,1:T(8,128)S(1)} collective-permute-done((f32[32,2,1024]{2,0,1:T(8,128)S(1)}, f32[32,2,1024]{2,0,1:T(8,128)S(1)}, u32[]{:S(2)}, u32[]{:S(2)}) %collective-permute-start.1) | collective-permute-done | bytes 262176 | tf_op jit(solution)/shard_map/ppermute | solution.py:34
  45.2 3.2 %collective-permute-done.2 = f32[32,2,512]{2,0,1:T(8,128)S(1)} collective-permute-done((f32[32,2,512]{2,0,1:T(8,128)S(1)}, f32[32,2,512]{2,0,1:T(8,128)S(1)}, u32[]{:S(2)}, u32[]{:S(2)}) %collective-permute-start.2) | collective-permute-done | bytes 131104 | tf_op jit(solution)/shard_map/ppermute | solution.py:34
  50.3 2.4 %collective-permute-done.3 = f32[32,2,256]{2,0,1:T(8,128)S(1)} collective-permute-done((f32[32,2,256]{2,0,1:T(8,128)S(1)}, f32[32,2,256]{2,0,1:T(8,128)S(1)}, u32[]{:S(2)}, u32[]{:S(2)}) %collective-permute-start.3) | collective-permute-done | bytes 65568 | tf_op jit(solution)/shard_map/ppermute | solution.py:34
  52.8 3.3 %collective-permute-start.4 = (f32[32,2,128]{2,0,1:T(8,128)S(1)}, f32[32,2,128]{2,0,1:T(8,128)S(1)}, u32[]{:S(2)}, u32[]{:S(2)}) collective-permute-start(f32[32,2,128]{2,0,1:T(8,128)S(1)} %slice_select_fusion.4), channel_id=1, source_target_pairs={{0,16},{1,17},{2,18},{3,19},{4,20},{5,21},{6,22},{7,23},{8,24},{9,... | collective-permute-start | bytes 98312 | tf_op jit(solution)/shard_map/ppermute | solution.py:34
  58.1 2.9 %collective-permute-start.5 = (f32[32,2,128]{2,0,1:T(8,128)S(1)}, f32[32,2,128]{2,0,1:T(8,128)S(1)}, u32[]{:S(2)}, u32[]{:S(2)}) collective-permute-start(f32[32,2,128]{2,0,1:T(8,128)S(1)} %select_add_fusion.4), channel_id=1, source_target_pairs={{0,16},{1,17},{2,18},{3,19},{4,20},{5,21},{6,22},{7,23},{8,24},{9,... | collective-permute-start | bytes 98312 | tf_op jit(solution)/shard_map/ppermute | solution.py:37
  65.0 2.3 %collective-permute-done.6 = f32[32,2,256]{2,0,1:T(8,128)S(1)} collective-permute-done((f32[32,2,256]{2,0,1:T(8,128)S(1)}, f32[32,2,256]{2,0,1:T(8,128)S(1)}, u32[]{:S(2)}, u32[]{:S(2)}) %collective-permute-start.6) | collective-permute-done | bytes 65568 | tf_op jit(solution)/shard_map/ppermute | solution.py:37
  68.9 3.5 %collective-permute-done.7 = f32[32,2,512]{2,0,1:T(8,128)S(1)} collective-permute-done((f32[32,2,512]{2,0,1:T(8,128)S(1)}, f32[32,2,512]{2,0,1:T(8,128)S(1)}, u32[]{:S(2)}, u32[]{:S(2)}) %collective-permute-start.7) | collective-permute-done | bytes 131104 | tf_op jit(solution)/shard_map/ppermute | solution.py:37
  73.9 4.9 %collective-permute-done.8 = f32[32,2,1024]{2,0,1:T(8,128)S(1)} collective-permute-done((f32[32,2,1024]{2,0,1:T(8,128)S(1)}, f32[32,2,1024]{2,0,1:T(8,128)S(1)}, u32[]{:S(2)}, u32[]{:S(2)}) %collective-permute-start.8) | collective-permute-done | bytes 262176 | tf_op jit(solution)/shard_map/ppermute | solution.py:37
  80.8 6.2 %convolution_bitcast_fusion = f32[32,2,128]{2,0,1:T(8,128)S(1)} fusion(f32[2,128,4096]{2,1,0:T(8,128)} %param.14, f32[32,2,2048]{2,0,1:T(8,128)S(1)} %collective-permute-done.9, f32[32,2,2048]{2,0,1:T(8,128)S(1)} %maximum_select_fusion.4, pred[]{:T(512)S(6)} %eq.53), kind=kOutput, calls=%fused_computation.2 | convolution fusion | flops 403439616 | bytes 5275649 | tf_op jit(solution)/shard_map/qmk,mck->qmc/dot_general | solution.py:90
  89.9 2.8 %collective-permute-done.11 = f32[32,2,256]{2,0,1:T(8,128)S(1)} collective-permute-done((f32[32,2,256]{2,0,1:T(8,128)S(1)}, f32[32,2,256]{2,0,1:T(8,128)S(1)}, u32[]{:S(2)}, u32[]{:S(2)}) %collective-permute-start.11) | collective-permute-done | bytes 65568 | tf_op jit(solution)/shard_map/ppermute | solution.py:46
  94.3 3.5 %collective-permute-done.12 = f32[32,2,512]{2,0,1:T(8,128)S(1)} collective-permute-done((f32[32,2,512]{2,0,1:T(8,128)S(1)}, f32[32,2,512]{2,0,1:T(8,128)S(1)}, u32[]{:S(2)}, u32[]{:S(2)}) %collective-permute-start.12) | collective-permute-done | bytes 131104 | tf_op jit(solution)/shard_map/ppermute | solution.py:46
  99.8 4.4 %collective-permute-done.13 = f32[32,2,1024]{2,0,1:T(8,128)S(1)} collective-permute-done((f32[32,2,1024]{2,0,1:T(8,128)S(1)}, f32[32,2,1024]{2,0,1:T(8,128)S(1)}, u32[]{:S(2)}, u32[]{:S(2)}) %collective-permute-start.13) | collective-permute-done | bytes 262176 | tf_op jit(solution)/shard_map/ppermute | solution.py:46
  104.3 3.3 %collective-permute-start.14 = (f32[32,2,2048]{2,0,1:T(8,128)S(1)}, f32[32,2,2048]{2,0,1:T(8,128)S(1)}, u32[]{:S(2)}, u32[]{:S(2)}) collective-permute-start(f32[32,2,2048]{2,0,1:T(8,128)S(1)} %maximum_select_fusion.5), channel_id=1, source_target_pairs={{0,16},{1,17},{2,18},{3,19},{4,20},{5,21},{6,22},{7,23},{8,24},{9,... | collective-permute-start | bytes 1572872 | tf_op jit(solution)/shard_map/ppermute | solution.py:46
  107.5 19.8 %collective-permute-done.14 = f32[32,2,2048]{2,0,1:T(8,128)S(1)} collective-permute-done((f32[32,2,2048]{2,0,1:T(8,128)S(1)}, f32[32,2,2048]{2,0,1:T(8,128)S(1)}, u32[]{:S(2)}, u32[]{:S(2)}) %collective-permute-start.14) | collective-permute-done | bytes 524320 | tf_op jit(solution)/shard_map/ppermute | solution.py:46
  127.4 5.8 %fusion.32 = (f32[32]{0:T(128)S(1)}, f32[32]{0:T(128)S(1)}, f32[32,128]{1,0:T(8,128)S(1)}) fusion(f32[128,2,4096]{2,1,0:T(2,128)S(1)} %copy-done.2, f32[32,2,2048]{2,0,1:T(8,128)S(1)} %collective-permute-done.14, f32[32,2,2048]{2,0,1:T(8,128)S(1)} %maximum_select_fusion.5, pred[]{:T(512)S(6)} %eq.49), kind=kOutput, calls=%fused_computation.70 | convolution fusion | flops 403451840 | bytes 5259521 | tf_op jit(solution)/shard_map/qmk,nmk->qn/dot_general | solution.py:91
  135.9 2.1 %collective-permute-done.16 = f32[2,32]{1,0:T(2,128)S(1)} collective-permute-done((f32[2,32]{1,0:T(2,128)S(1)}, f32[2,32]{1,0:T(2,128)S(1)}, u32[]{:S(2)}, u32[]{:S(2)}) %collective-permute-start.16) | collective-permute-done | bytes 288 | tf_op jit(solution)/shard_map/ppermute | solution.py:52
  142.4 2.9 %collective-permute-done.18 = f32[2,32]{1,0:T(2,128)S(1)} collective-permute-done((f32[2,32]{1,0:T(2,128)S(1)}, f32[2,32]{1,0:T(2,128)S(1)}, u32[]{:S(2)}, u32[]{:S(2)}) %collective-permute-start.18) | collective-permute-done | bytes 288 | tf_op jit(solution)/shard_map/ppermute | solution.py:52
  147.3 2.4 %collective-permute-done.19 = f32[2,32]{1,0:T(2,128)S(1)} collective-permute-done((f32[2,32]{1,0:T(2,128)S(1)}, f32[2,32]{1,0:T(2,128)S(1)}, u32[]{:S(2)}, u32[]{:S(2)}) %collective-permute-start.19) | collective-permute-done | bytes 288 | tf_op jit(solution)/shard_map/ppermute | solution.py:52
  (71 shorter events, 42.1 us)
Async XLA Ops:
  1.6 6.3 %copy-start.3 = (bf16[4096,128]{1,0:T(8,128)(2,1)S(1)}, bf16[4096,128]{1,0:T(8,128)(2,1)}, u32[]{:S(2)}) copy-start(bf16[4096,128]{1,0:T(8,128)(2,1)} %param.13) | copy-start | bytes 3145732
  7.9 3.0 %copy-start = (bf16[128,2,4096]{2,1,0:T(2,128)(2,1)S(1)}, bf16[128,2,4096]{2,1,0:T(2,128)(2,1)}, u32[]{:S(2)}) copy-start(bf16[128,2,4096]{2,1,0:T(2,128)(2,1)} %param.8) | copy-start | bytes 6291460
  10.9 6.7 %copy-start.1 = (bf16[4096,128]{1,0:T(8,128)(2,1)S(1)}, bf16[4096,128]{1,0:T(8,128)(2,1)}, u32[]{:S(2)}) copy-start(bf16[4096,128]{1,0:T(8,128)(2,1)} %param.12) | copy-start | bytes 3145732
  31.6 2.1 %collective-permute-start = (f32[32,2,2048]{2,0,1:T(8,128)S(1)}, f32[32,2,2048]{2,0,1:T(8,128)S(1)}, u32[]{:S(2)}, u32[]{:S(2)}) collective-permute-start(f32[32,2,2048]{2,0,1:T(8,128)S(1)} %slice_select_fusion), channel_id=1, source_target_pairs={{0,1},{1,0},{2,3},{3,2},{4,5},{5,4},{6,7},{7,6},{8,9},{9,8},{10,11... | collective-permute-start | bytes 1572872 | tf_op jit(solution)/shard_map/ppermute | solution.py:34
  33.8 9.5 %collective-permute-start.1 = (f32[32,2,1024]{2,0,1:T(8,128)S(1)}, f32[32,2,1024]{2,0,1:T(8,128)S(1)}, u32[]{:S(2)}, u32[]{:S(2)}) collective-permute-start(f32[32,2,1024]{2,0,1:T(8,128)S(1)} %slice_select_fusion.1), channel_id=1, source_target_pairs={{0,2},{1,3},{2,0},{3,1},{4,6},{5,7},{6,4},{7,5},{8,10},{9,11},{10,... | collective-permute-start | bytes 786440 | tf_op jit(solution)/shard_map/ppermute | solution.py:34
  43.4 5.0 %collective-permute-start.2 = (f32[32,2,512]{2,0,1:T(8,128)S(1)}, f32[32,2,512]{2,0,1:T(8,128)S(1)}, u32[]{:S(2)}, u32[]{:S(2)}) collective-permute-start(f32[32,2,512]{2,0,1:T(8,128)S(1)} %slice_select_fusion.2), channel_id=1, source_target_pairs={{0,4},{1,5},{2,6},{3,7},{4,0},{5,1},{6,2},{7,3},{8,12},{9,13},{10,... | collective-permute-start | bytes 393224 | tf_op jit(solution)/shard_map/ppermute | solution.py:34
  48.5 4.3 %collective-permute-start.3 = (f32[32,2,256]{2,0,1:T(8,128)S(1)}, f32[32,2,256]{2,0,1:T(8,128)S(1)}, u32[]{:S(2)}, u32[]{:S(2)}) collective-permute-start(f32[32,2,256]{2,0,1:T(8,128)S(1)} %slice_select_fusion.3), channel_id=1, source_target_pairs={{0,8},{1,9},{2,10},{3,11},{4,12},{5,13},{6,14},{7,15},{8,0},{9,1},... | collective-permute-start | bytes 196616 | tf_op jit(solution)/shard_map/ppermute | solution.py:34
  52.8 5.3 %collective-permute-start.4 = (f32[32,2,128]{2,0,1:T(8,128)S(1)}, f32[32,2,128]{2,0,1:T(8,128)S(1)}, u32[]{:S(2)}, u32[]{:S(2)}) collective-permute-start(f32[32,2,128]{2,0,1:T(8,128)S(1)} %slice_select_fusion.4), channel_id=1, source_target_pairs={{0,16},{1,17},{2,18},{3,19},{4,20},{5,21},{6,22},{7,23},{8,24},{9,... | collective-permute-start | bytes 98312 | tf_op jit(solution)/shard_map/ppermute | solution.py:34
  58.1 4.9 %collective-permute-start.5 = (f32[32,2,128]{2,0,1:T(8,128)S(1)}, f32[32,2,128]{2,0,1:T(8,128)S(1)}, u32[]{:S(2)}, u32[]{:S(2)}) collective-permute-start(f32[32,2,128]{2,0,1:T(8,128)S(1)} %select_add_fusion.4), channel_id=1, source_target_pairs={{0,16},{1,17},{2,18},{3,19},{4,20},{5,21},{6,22},{7,23},{8,24},{9,... | collective-permute-start | bytes 98312 | tf_op jit(solution)/shard_map/ppermute | solution.py:37
  63.0 4.3 %collective-permute-start.6 = (f32[32,2,256]{2,0,1:T(8,128)S(1)}, f32[32,2,256]{2,0,1:T(8,128)S(1)}, u32[]{:S(2)}, u32[]{:S(2)}) collective-permute-start(f32[32,2,256]{2,0,1:T(8,128)S(1)} %maximum_select_fusion.10), channel_id=1, source_target_pairs={{0,8},{1,9},{2,10},{3,11},{4,12},{5,13},{6,14},{7,15},{8,0},{9,1},... | collective-permute-start | bytes 196616 | tf_op jit(solution)/shard_map/ppermute | solution.py:37
  67.3 5.0 %collective-permute-start.7 = (f32[32,2,512]{2,0,1:T(8,128)S(1)}, f32[32,2,512]{2,0,1:T(8,128)S(1)}, u32[]{:S(2)}, u32[]{:S(2)}) collective-permute-start(f32[32,2,512]{2,0,1:T(8,128)S(1)} %maximum_select_fusion.8), channel_id=1, source_target_pairs={{0,4},{1,5},{2,6},{3,7},{4,0},{5,1},{6,2},{7,3},{8,12},{9,13},{10,... | collective-permute-start | bytes 393224 | tf_op jit(solution)/shard_map/ppermute | solution.py:37
  72.4 6.4 %collective-permute-start.8 = (f32[32,2,1024]{2,0,1:T(8,128)S(1)}, f32[32,2,1024]{2,0,1:T(8,128)S(1)}, u32[]{:S(2)}, u32[]{:S(2)}) collective-permute-start(f32[32,2,1024]{2,0,1:T(8,128)S(1)} %maximum_select_fusion.6), channel_id=1, source_target_pairs={{0,2},{1,3},{2,0},{3,1},{4,6},{5,7},{6,4},{7,5},{8,10},{9,11},{10,... | collective-permute-start | bytes 786440 | tf_op jit(solution)/shard_map/ppermute | solution.py:37
  78.9 2.0 %collective-permute-start.9 = (f32[32,2,2048]{2,0,1:T(8,128)S(1)}, f32[32,2,2048]{2,0,1:T(8,128)S(1)}, u32[]{:S(2)}, u32[]{:S(2)}) collective-permute-start(f32[32,2,2048]{2,0,1:T(8,128)S(1)} %maximum_select_fusion.4), channel_id=1, source_target_pairs={{0,1},{1,0},{2,3},{3,2},{4,5},{5,4},{6,7},{7,6},{8,9},{9,8},{10,11... | collective-permute-start | bytes 1572872 | tf_op jit(solution)/shard_map/ppermute | solution.py:37
  80.8 46.5 %copy-start.2 = (f32[128,2,4096]{2,1,0:T(2,128)S(1)}, f32[128,2,4096]{2,1,0:T(2,128)}, u32[]{:S(2)}) copy-start(f32[128,2,4096]{2,1,0:T(2,128)} %param.15) | copy-start | bytes 12582916
  87.1 1.3 collective-permute-start.10
  88.4 4.3 %collective-permute-start.11 = (f32[32,2,256]{2,0,1:T(8,128)S(1)}, f32[32,2,256]{2,0,1:T(8,128)S(1)}, u32[]{:S(2)}, u32[]{:S(2)}) collective-permute-start(f32[32,2,256]{2,0,1:T(8,128)S(1)} %maximum_select_fusion.11), channel_id=1, source_target_pairs={{0,2},{1,3},{2,0},{3,1},{4,6},{5,7},{6,4},{7,5},{8,10},{9,11},{10,... | collective-permute-start | bytes 196616 | tf_op jit(solution)/shard_map/ppermute | solution.py:46
  92.7 5.0 %collective-permute-start.12 = (f32[32,2,512]{2,0,1:T(8,128)S(1)}, f32[32,2,512]{2,0,1:T(8,128)S(1)}, u32[]{:S(2)}, u32[]{:S(2)}) collective-permute-start(f32[32,2,512]{2,0,1:T(8,128)S(1)} %maximum_select_fusion.9), channel_id=1, source_target_pairs={{0,4},{1,5},{2,6},{3,7},{4,0},{5,1},{6,2},{7,3},{8,12},{9,13},{10,... | collective-permute-start | bytes 393224 | tf_op jit(solution)/shard_map/ppermute | solution.py:46
  97.8 6.4 %collective-permute-start.13 = (f32[32,2,1024]{2,0,1:T(8,128)S(1)}, f32[32,2,1024]{2,0,1:T(8,128)S(1)}, u32[]{:S(2)}, u32[]{:S(2)}) collective-permute-start(f32[32,2,1024]{2,0,1:T(8,128)S(1)} %maximum_select_fusion.7), channel_id=1, source_target_pairs={{0,8},{1,9},{2,10},{3,11},{4,12},{5,13},{6,14},{7,15},{8,0},{9,1},... | collective-permute-start | bytes 786440 | tf_op jit(solution)/shard_map/ppermute | solution.py:46
  104.3 23.1 %collective-permute-start.14 = (f32[32,2,2048]{2,0,1:T(8,128)S(1)}, f32[32,2,2048]{2,0,1:T(8,128)S(1)}, u32[]{:S(2)}, u32[]{:S(2)}) collective-permute-start(f32[32,2,2048]{2,0,1:T(8,128)S(1)} %maximum_select_fusion.5), channel_id=1, source_target_pairs={{0,16},{1,17},{2,18},{3,19},{4,20},{5,21},{6,22},{7,23},{8,24},{9,... | collective-permute-start | bytes 1572872 | tf_op jit(solution)/shard_map/ppermute | solution.py:46
  133.1 1.2 collective-permute-start.15
  134.4 3.6 %collective-permute-start.16 = (f32[2,32]{1,0:T(2,128)S(1)}, f32[2,32]{1,0:T(2,128)S(1)}, u32[]{:S(2)}, u32[]{:S(2)}) collective-permute-start(f32[2,32]{1,0:T(2,128)S(1)} %fusion.31), channel_id=1, source_target_pairs={{0,2},{1,3},{2,0},{3,1},{4,6},{5,7},{6,4},{7,5},{8,10},{9,11},{10,... | collective-permute-start | bytes 776 | tf_op jit(solution)/shard_map/ppermute | solution.py:52
  138.0 3.6 %collective-permute-start.17 = (f32[2,32]{1,0:T(2,128)S(1)}, f32[2,32]{1,0:T(2,128)S(1)}, u32[]{:S(2)}, u32[]{:S(2)}) collective-permute-start(f32[2,32]{1,0:T(2,128)S(1)} %fusion.38), channel_id=1, source_target_pairs={{0,4},{1,5},{2,6},{3,7},{4,0},{5,1},{6,2},{7,3},{8,12},{9,13},{10,... | collective-permute-start | bytes 776 | tf_op jit(solution)/shard_map/ppermute | solution.py:52
  141.7 3.6 %collective-permute-start.18 = (f32[2,32]{1,0:T(2,128)S(1)}, f32[2,32]{1,0:T(2,128)S(1)}, u32[]{:S(2)}, u32[]{:S(2)}) collective-permute-start(f32[2,32]{1,0:T(2,128)S(1)} %add.59), channel_id=1, source_target_pairs={{0,8},{1,9},{2,10},{3,11},{4,12},{5,13},{6,14},{7,15},{8,0},{9,1},... | collective-permute-start | bytes 776 | tf_op jit(solution)/shard_map/ppermute | solution.py:52
  145.2 4.5 %collective-permute-start.19 = (f32[2,32]{1,0:T(2,128)S(1)}, f32[2,32]{1,0:T(2,128)S(1)}, u32[]{:S(2)}, u32[]{:S(2)}) collective-permute-start(f32[2,32]{1,0:T(2,128)S(1)} %add.60), channel_id=1, source_target_pairs={{0,16},{1,17},{2,18},{3,19},{4,20},{5,21},{6,22},{7,23},{8,24},{9,... | collective-permute-start | bytes 776 | tf_op jit(solution)/shard_map/ppermute | solution.py:52

commit v2 on v1

--- a/solution.py
+++ b/solution.py
@@ -38,13 +38,18 @@
     return cur
 
 
-def _allgather(x, size, axis):
+def _allgather(x, size):
     me = lax.axis_index("rows")
     cur = x
-    for s in range(_steps(size)):
+    for s in reversed(range(_steps(size))):
         low = ((me >> s) & 1) == 0
-        cur = _join(cur, lax.ppermute(cur, "rows", _xor_pairs(size, s)), low, axis)
-    return cur
+        other = lax.ppermute(cur, "rows", _xor_pairs(size, s))
+        cur = jnp.where(low, jnp.stack([cur, other], -2), jnp.stack([other, cur], -2))
+    return cur.reshape(*x.shape[:-1], size * x.shape[-1])
+
+
+def _bf16_round(x):
+    return lax.reduce_precision(x, exponent_bits=8, mantissa_bits=7)
 
 
 def _butterfly_sum(x, size):
@@ -66,33 +71,29 @@
     selector = (
         (segment[:, None] == jnp.arange(queries, dtype=jnp.int32)[None, :]) & (valid[:, None] == 1)
     ).astype(jnp.bfloat16)
-    module_sums = []
-    for m in range(modules):
-        act_proj = jnp.dot(
-            acts[:, m, :],
-            proj_in[:, m * proj_rank : (m + 1) * proj_rank],
-            preferred_element_type=jnp.float32,
-        ).astype(jnp.bfloat16)
-        grad_proj = jnp.dot(
-            grads_out[:, m, :],
-            proj_out[:, m * proj_rank : (m + 1) * proj_rank],
-            preferred_element_type=jnp.float32,
-        ).astype(jnp.bfloat16)
-        spread = (selector[:, :, None] * grad_proj[:, None, :]).reshape(
-            tok_rows, queries * proj_rank
-        )
-        module_sum = lax.dot_general(
-            spread, act_proj, (((0,), (0,)), ((), ())), preferred_element_type=jnp.float32
-        )
-        module_sums.append(module_sum.reshape(queries, flat_width))
-    partial_value = jnp.stack(module_sums, axis=1)
+    owner = (jnp.arange(modules * proj_rank) // proj_rank)[None, :] == jnp.arange(modules)[:, None]
+    w_in = jnp.where(owner[:, None, :], proj_in[None, :, :], jnp.zeros((), proj_in.dtype))
+    w_out = jnp.where(owner[:, None, :], proj_out[None, :, :], jnp.zeros((), proj_out.dtype))
+    dims = (((1, 2), (0, 1)), ((), ()))
+    act_proj = lax.dot_general(acts, w_in, dims, preferred_element_type=jnp.float32)
+    grad_proj = lax.dot_general(grads_out, w_out, dims, preferred_element_type=jnp.float32)
+    act_proj = _bf16_round(act_proj).reshape(tok_rows, modules, proj_rank)
+    grad_proj = _bf16_round(grad_proj).reshape(tok_rows, modules, proj_rank)
+    outer = (grad_proj[:, :, :, None] * act_proj[:, :, None, :]).reshape(tok_rows, modules * flat_width)
+    high = _bf16_round(outer)
+    low = outer - high
+    tdims = (((0,), (0,)), ((), ()))
+    partial_value = lax.dot_general(
+        selector, high.astype(jnp.bfloat16), tdims, preferred_element_type=jnp.float32
+    ) + lax.dot_general(selector, low.astype(jnp.bfloat16), tdims, preferred_element_type=jnp.float32)
+    partial_value = partial_value.reshape(queries, modules, flat_width)
     summed = _allreduce(partial_value, size, 2)
-    precond_cols = jnp.einsum("qmk,mck->qmc", summed, fisher_inv, precision=lax.Precision.HIGHEST)
+    precond_cols = jnp.einsum("qmk,mck->qmc", summed, fisher_inv, precision=lax.Precision.HIGH)
     scores = jnp.einsum(
         "qmk,nmk->qn",
-        _allgather(precond_cols, size, 2),
+        _allgather(precond_cols, size),
         database,
-        precision=lax.Precision.HIGHEST,
+        precision=lax.Precision.HIGH,
     )
     db_count = database.shape[0] * size
     moments = _butterfly_sum(

time: 151 us -> 125 us (0.83)
  waiting for transfers between devices: 72.5 us -> 53.7 us
  local copies, waits for them, and re-layouts: 17.6 us -> 9.89 us
  matrix products: 23.8 us -> 18.8 us
  other arithmetic: 3.21 us -> 7.96 us
    ppermute x5, waiting for transfers between devices: 31.6 us -> 14.4 us  [_allgather(): other = lax.ppermute(cur, 'rows', _xor_pairs(size, s))]
    slice x2 -> x1, local copies, waits for them, and re-layouts: 11.8 us -> 1.27 us  [_allreduce(): lo = lax.slice_in_dim(cur, 0, half, axis=axis)]
    dot_general x6, matrix products: 23.8 us -> 18.8 us  [the longest x1 6.62 us: shards(): jnp.einsum('qmk,nmk->qn', _allgather(precond_cols, size), database, preci...]
    another operation x4 -> x1, local copies, waits for them, and re-layouts: 4.73 us -> 0.09 us  [the longest x3 3.99 us: shards(): partial_value = jnp.stack(module_sums, axis=1)]
    select_n x0 -> x2, local copies, waits for them, and re-layouts: none -> 2.81 us  [_allgather(): jnp.where(low, jnp.stack([cur, other], -2), jnp.stack([other, cur], -2))]
    unnamed x9 -> x18, local copies, waits for them, and re-layouts: 1.1 us -> 3.85 us
    convert_element_type x1, other arithmetic: 0.01 us -> 2.61 us  [shards(): low.astype(jnp.bfloat16)]
    ppermute x5, starting transfers between devices: 6.02 us -> 8.05 us  [_butterfly_sum(): x = x + lax.ppermute(x, 'rows', _xor_pairs(size, s))]
where the time goes in v2:
time: 125 us
  waiting for transfers between devices  53.7 us (43%)
  starting transfers between devices  34.5 us (28%)
  matrix products  18.8 us (15%)
  local copies, waits for them, and re-layouts  9.89 us (8%)
  other arithmetic  7.96 us (6%)
    ppermute x5, waiting for transfers between devices, _allreduce(): cur = keep + lax.ppermute(send, 'rows', _xor_pairs(size, s))  16.1 us
    ppermute x5, waiting for transfers between devices, _allreduce(): cur = _join(cur, lax.ppermute(cur, 'rows', _xor_pairs(size, s)), low, axis)  14.6 us
    ppermute x5, waiting for transfers between devices, _allgather(): other = lax.ppermute(cur, 'rows', _xor_pairs(size, s))  14.4 us
    ppermute x5, starting transfers between devices, _allreduce(): cur = keep + lax.ppermute(send, 'rows', _xor_pairs(size, s))  10.4 us
    ppermute x5, waiting for transfers between devices, _butterfly_sum(): x = x + lax.ppermute(x, 'rows', _xor_pairs(size, s))  8.5 us
    ppermute x5, starting transfers between devices, _butterfly_sum(): x = x + lax.ppermute(x, 'rows', _xor_pairs(size, s))  8.05 us
    ppermute x5, starting transfers between devices, _allreduce(): cur = _join(cur, lax.ppermute(cur, 'rows', _xor_pairs(size, s)), low, axis)  8.05 us
    ppermute x5, starting transfers between devices, _allgather(): other = lax.ppermute(cur, 'rows', _xor_pairs(size, s))  8.01 us
  transfers between devices with their start and end apart: 20, of which 20 were waited for; matrix products, arithmetic and copies ran while one was open for 0% of the time, Pallas kernels for 0%

profile of v2, /device:TPU:0, one launch (start us, length us, event | category | flops | bytes accessed | tf_op | source)
XLA Modules:
  0.0 125.1 jit_solution(17415058238536878811)
XLA Ops:
  0.0 2.4 %copy.31 = bf16[4096,128]{0,1:T(8,128)(2,1)} copy(bf16[4096,128]{1,0:T(8,128)(2,1)} %param.12) | data formatting | bytes 2097152 | tf_op args[4]
  3.8 2.8 %fusion.21 = f32[128,128]{1,0:T(8,128)S(1)} fusion(bf16[128,2,4096]{2,1,0:T(2,128)(2,1)S(1)} %copy-done, pred[2,128]{1,0:T(4,128)(4,1)S(1)} %iota_compare_fusion.1, bf16[4096,128]{0,1:T(8,128)(2,1)} %copy.31), kind=kOutput, calls=%fused_computation.17 | convolution fusion | flops 269500416 | bytes 3211520 | tf_op jit(solution)/shard_map/dot_general | solution.py:78
  8.8 2.6 %fusion = (bf16[128,8192]{0,1:T(8,128)(2,1)}, bf16[128,8192]{0,1:T(8,128)(2,1)}) fusion(f32[128,2,64,64]{0,3,2,1:T(8,128)S(1)} %broadcast_multiply_fusion), kind=kLoop, calls=%fused_computation.3 | loop fusion | flops 4194304 | bytes 8388608 | tf_op jit(solution)/shard_map/convert_element_type | solution.py:88
  11.8 2.6 %fusion.48 = f32[32,8192]{1,0:T(8,128)S(1)} fusion(bf16[128,8192]{0,1:T(8,128)(2,1)} %get-tuple-element.8, s32[128]{0:T(128)S(1)} %convert_reduce_fusion, pred[128]{0:T(512)(128)(4,1)S(1)} %broadcast_compare_fusion), kind=kOutput, calls=%fused_computation.56 | convolution fusion | flops 67121152 | bytes 3146368 | tf_op jit(solution)/shard_map/dot_general | solution.py:86
  24.2 2.9 %collective-permute-start.1 = (f32[32,2,1024]{2,0,1:T(8,128)S(1)}, f32[32,2,1024]{2,0,1:T(8,128)S(1)}, u32[]{:S(2)}, u32[]{:S(2)}) collective-permute-start(f32[32,2,1024]{2,0,1:T(8,128)S(1)} %slice_select_fusion), channel_id=1, source_target_pairs={{0,2},{1,3},{2,0},{3,1},{4,6},{5,7},{6,4},{7,5},{8,10},{9,11},{10,... | collective-permute-start | bytes 786440 | tf_op jit(solution)/shard_map/ppermute | solution.py:34
  27.1 6.6 %collective-permute-done.1 = f32[32,2,1024]{2,0,1:T(8,128)S(1)} collective-permute-done((f32[32,2,1024]{2,0,1:T(8,128)S(1)}, f32[32,2,1024]{2,0,1:T(8,128)S(1)}, u32[]{:S(2)}, u32[]{:S(2)}) %collective-permute-start.1) | collective-permute-done | bytes 262176 | tf_op jit(solution)/shard_map/ppermute | solution.py:34
  35.6 3.2 %collective-permute-done.2 = f32[32,2,512]{2,0,1:T(8,128)S(1)} collective-permute-done((f32[32,2,512]{2,0,1:T(8,128)S(1)}, f32[32,2,512]{2,0,1:T(8,128)S(1)}, u32[]{:S(2)}, u32[]{:S(2)}) %collective-permute-start.2) | collective-permute-done | bytes 131104 | tf_op jit(solution)/shard_map/ppermute | solution.py:34
  40.7 2.4 %collective-permute-done.3 = f32[32,2,256]{2,0,1:T(8,128)S(1)} collective-permute-done((f32[32,2,256]{2,0,1:T(8,128)S(1)}, f32[32,2,256]{2,0,1:T(8,128)S(1)}, u32[]{:S(2)}, u32[]{:S(2)}) %collective-permute-start.3) | collective-permute-done | bytes 65568 | tf_op jit(solution)/shard_map/ppermute | solution.py:34
  43.2 3.3 %collective-permute-start.4 = (f32[32,2,128]{2,0,1:T(8,128)S(1)}, f32[32,2,128]{2,0,1:T(8,128)S(1)}, u32[]{:S(2)}, u32[]{:S(2)}) collective-permute-start(f32[32,2,128]{2,0,1:T(8,128)S(1)} %slice_select_fusion.3), channel_id=1, source_target_pairs={{0,16},{1,17},{2,18},{3,19},{4,20},{5,21},{6,22},{7,23},{8,24},{9,... | collective-permute-start | bytes 98312 | tf_op jit(solution)/shard_map/ppermute | solution.py:34
  48.5 2.9 %collective-permute-start.5 = (f32[32,2,128]{2,0,1:T(8,128)S(1)}, f32[32,2,128]{2,0,1:T(8,128)S(1)}, u32[]{:S(2)}, u32[]{:S(2)}) collective-permute-start(f32[32,2,128]{2,0,1:T(8,128)S(1)} %select_add_fusion.4), channel_id=1, source_target_pairs={{0,16},{1,17},{2,18},{3,19},{4,20},{5,21},{6,22},{7,23},{8,24},{9,... | collective-permute-start | bytes 98312 | tf_op jit(solution)/shard_map/ppermute | solution.py:37
  53.3 2.0 %collective-permute-start.6 = (f32[32,2,256]{2,0,1:T(8,128)S(1)}, f32[32,2,256]{2,0,1:T(8,128)S(1)}, u32[]{:S(2)}, u32[]{:S(2)}) collective-permute-start(f32[32,2,256]{2,0,1:T(8,128)S(1)} %maximum_select_fusion.12), channel_id=1, source_target_pairs={{0,8},{1,9},{2,10},{3,11},{4,12},{5,13},{6,14},{7,15},{8,0},{9,1},... | collective-permute-start | bytes 196616 | tf_op jit(solution)/shard_map/ppermute | solution.py:37
  55.4 2.3 %collective-permute-done.6 = f32[32,2,256]{2,0,1:T(8,128)S(1)} collective-permute-done((f32[32,2,256]{2,0,1:T(8,128)S(1)}, f32[32,2,256]{2,0,1:T(8,128)S(1)}, u32[]{:S(2)}, u32[]{:S(2)}) %collective-permute-start.6) | collective-permute-done | bytes 65568 | tf_op jit(solution)/shard_map/ppermute | solution.py:37
  59.2 3.5 %collective-permute-done.7 = f32[32,2,512]{2,0,1:T(8,128)S(1)} collective-permute-done((f32[32,2,512]{2,0,1:T(8,128)S(1)}, f32[32,2,512]{2,0,1:T(8,128)S(1)}, u32[]{:S(2)}, u32[]{:S(2)}) %collective-permute-start.7) | collective-permute-done | bytes 131104 | tf_op jit(solution)/shard_map/ppermute | solution.py:37
  64.3 4.9 %collective-permute-done.8 = f32[32,2,1024]{2,0,1:T(8,128)S(1)} collective-permute-done((f32[32,2,1024]{2,0,1:T(8,128)S(1)}, f32[32,2,1024]{2,0,1:T(8,128)S(1)}, u32[]{:S(2)}, u32[]{:S(2)}) %collective-permute-start.8) | collective-permute-done | bytes 262176 | tf_op jit(solution)/shard_map/ppermute | solution.py:37
  71.2 4.3 %fusion.34 = f32[2,32,128]{2,1,0:T(8,128)S(1)} fusion(f32[2,128,4096]{2,1,0:T(8,128)} %param.14, f32[32,2,2048]{2,0,1:T(8,128)S(1)} %collective-permute-done.9, f32[32,2,2048]{2,0,1:T(8,128)S(1)} %maximum_select_fusion.3, pred[]{:T(512)S(6)} %eq.68), kind=kOutput, calls=%fused_computation.21 | convolution fusion | flops 202113024 | bytes 5275649 | tf_op jit(solution)/shard_map/qmk,mck->qmc/dot_general | solution.py:91
  75.5 2.8 %collective-permute-start.10 = (f32[32,2,128]{2,0,1:T(8,128)S(1)}, f32[32,2,128]{2,0,1:T(8,128)S(1)}, u32[]{:S(2)}, u32[]{:S(2)}) collective-permute-start(f32[32,2,128]{2,0,1:T(8,128)S(1)} %bitcast.66), channel_id=1, source_target_pairs={{0,16},{1,17},{2,18},{3,19},{4,20},{5,21},{6,22},{7,23},{8,24},{9,... | collective-permute-start | bytes 98312 | tf_op jit(solution)/shard_map/ppermute | solution.py:46
  80.4 2.0 %collective-permute-start.11 = (f32[32,2,2,128]{3,0,1,2:T(8,128)S(1)}, f32[32,2,2,128]{3,0,1,2:T(8,128)S(1)}, u32[]{:S(2)}, u32[]{:S(2)}) collective-permute-start(f32[32,2,2,128]{3,0,1,2:T(8,128)S(1)} %maximum_select_fusion.14), channel_id=1, source_target_pairs={{0,8},{1,9},{2,10},{3,11},{4,12},{5,13},{6,14},{7,15},{8,0},{9,1},... | collective-permute-start | bytes 196616 | tf_op jit(solution)/shard_map/ppermute | solution.py:46
  82.4 2.3 %collective-permute-done.11 = f32[32,2,2,128]{3,0,1,2:T(8,128)S(1)} collective-permute-done((f32[32,2,2,128]{3,0,1,2:T(8,128)S(1)}, f32[32,2,2,128]{3,0,1,2:T(8,128)S(1)}, u32[]{:S(2)}, u32[]{:S(2)}) %collective-permute-start.11) | collective-permute-done | bytes 65568 | tf_op jit(solution)/shard_map/ppermute | solution.py:46
  86.3 3.5 %collective-permute-done.12 = f32[32,2,2,2,128]{4,0,1,2,3:T(8,128)S(1)} collective-permute-done((f32[32,2,2,2,128]{4,0,1,2,3:T(8,128)S(1)}, f32[32,2,2,2,128]{4,0,1,2,3:T(8,128)S(1)}, u32[]{:S(2)}, u32[]{:S(2)}) %collective-permute-start.12) | collective-permute-done | bytes 131104 | tf_op jit(solution)/shard_map/ppermute | solution.py:46
  91.3 4.9 %collective-permute-done.13 = f32[32,2,2,2,2,128]{5,0,1,2,3,4:T(8,128)S(1)} collective-permute-done((f32[32,2,2,2,2,128]{5,0,1,2,3,4:T(8,128)S(1)}, f32[32,2,2,2,2,128]{5,0,1,2,3,4:T(8,128)S(1)}, u32[]{:S(2)}, u32[]{:S(2)}) %collective-permute-start.13) | collective-permute-done | bytes 262176 | tf_op jit(solution)/shard_map/ppermute | solution.py:46
  101.2 6.6 %fusion.60 = (f32[32]{0:T(128)S(1)}, f32[32]{0:T(128)S(1)}, f32[32,128]{1,0:T(8,128)S(1)}) fusion(f32[32,2,4096]{2,0,1:T(8,128)} %select_n.271, f32[128,2,4096]{2,1,0:T(2,128)} %param.15), kind=kOutput, calls=%fused_computation.82 | convolution fusion | flops 201338816 | bytes 5259520 | tf_op jit(solution)/shard_map/qmk,nmk->qn/dot_general | solution.py:92
  110.6 2.1 %collective-permute-done.16 = f32[2,32]{1,0:T(2,128)S(1)} collective-permute-done((f32[2,32]{1,0:T(2,128)S(1)}, f32[2,32]{1,0:T(2,128)S(1)}, u32[]{:S(2)}, u32[]{:S(2)}) %collective-permute-start.16) | collective-permute-done | bytes 288 | tf_op jit(solution)/shard_map/ppermute | solution.py:57
  114.2 2.1 %collective-permute-done.17 = f32[2,32]{1,0:T(2,128)S(1)} collective-permute-done((f32[2,32]{1,0:T(2,128)S(1)}, f32[2,32]{1,0:T(2,128)S(1)}, u32[]{:S(2)}, u32[]{:S(2)}) %collective-permute-start.17) | collective-permute-done | bytes 288 | tf_op jit(solution)/shard_map/ppermute | solution.py:57
  119.9 2.8 %collective-permute-start.19 = (f32[2,32]{1,0:T(2,128)S(1)}, f32[2,32]{1,0:T(2,128)S(1)}, u32[]{:S(2)}, u32[]{:S(2)}) collective-permute-start(f32[2,32]{1,0:T(2,128)S(1)} %add.69), channel_id=1, source_target_pairs={{0,16},{1,17},{2,18},{3,19},{4,20},{5,21},{6,22},{7,23},{8,24},{9,... | collective-permute-start | bytes 776 | tf_op jit(solution)/shard_map/ppermute | solution.py:57
  (89 shorter events, 46.8 us)
Async XLA Ops:
  0.0 3.8 %copy-start = (bf16[128,2,4096]{2,1,0:T(2,128)(2,1)S(1)}, bf16[128,2,4096]{2,1,0:T(2,128)(2,1)}, u32[]{:S(2)}) copy-start(bf16[128,2,4096]{2,1,0:T(2,128)(2,1)} %param.8) | copy-start | bytes 6291460
  3.8 2.8 %copy-start.4 = (bf16[4096,128]{0,1:T(8,128)(2,1)S(1)}, bf16[4096,128]{0,1:T(8,128)(2,1)}, u32[]{:S(2)}) copy-start(bf16[4096,128]{0,1:T(8,128)(2,1)} %copy.29) | copy-start | bytes 3145732
  3.8 2.9 %copy-start.6 = (bf16[128,2,4096]{2,1,0:T(2,128)(2,1)S(1)}, bf16[128,2,4096]{2,1,0:T(2,128)(2,1)}, u32[]{:S(2)}) copy-start(bf16[128,2,4096]{2,1,0:T(2,128)(2,1)} %param.9) | copy-start | bytes 6291460
  8.8 2.9 %copy-start.7 = (s32[128]{0:T(128)S(1)}, s32[128]{0:T(128)}, u32[]{:S(2)}) copy-start(s32[128]{0:T(128)} %param.11) | copy-start | bytes 1540
  19.9 2.4 %collective-permute-start = (f32[32,2,2048]{2,0,1:T(8,128)}, f32[32,2,2048]{2,0,1:T(8,128)}, u32[]{:S(2)}, u32[]{:S(2)}) collective-permute-start(f32[32,2,2048]{2,0,1:T(8,128)} %copy_select_fusion), channel_id=1, source_target_pairs={{0,1},{1,0},{2,3},{3,2},{4,5},{5,4},{6,7},{7,6},{8,9},{9,8},{10,11... | collective-permute-start | bytes 1572872 | tf_op jit(solution)/shard_map/ppermute | solution.py:34
  24.2 9.5 %collective-permute-start.1 = (f32[32,2,1024]{2,0,1:T(8,128)S(1)}, f32[32,2,1024]{2,0,1:T(8,128)S(1)}, u32[]{:S(2)}, u32[]{:S(2)}) collective-permute-start(f32[32,2,1024]{2,0,1:T(8,128)S(1)} %slice_select_fusion), channel_id=1, source_target_pairs={{0,2},{1,3},{2,0},{3,1},{4,6},{5,7},{6,4},{7,5},{8,10},{9,11},{10,... | collective-permute-start | bytes 786440 | tf_op jit(solution)/shard_map/ppermute | solution.py:34
  33.7 5.0 %collective-permute-start.2 = (f32[32,2,512]{2,0,1:T(8,128)S(1)}, f32[32,2,512]{2,0,1:T(8,128)S(1)}, u32[]{:S(2)}, u32[]{:S(2)}) collective-permute-start(f32[32,2,512]{2,0,1:T(8,128)S(1)} %slice_select_fusion.1), channel_id=1, source_target_pairs={{0,4},{1,5},{2,6},{3,7},{4,0},{5,1},{6,2},{7,3},{8,12},{9,13},{10,... | collective-permute-start | bytes 393224 | tf_op jit(solution)/shard_map/ppermute | solution.py:34
  38.8 4.3 %collective-permute-start.3 = (f32[32,2,256]{2,0,1:T(8,128)S(1)}, f32[32,2,256]{2,0,1:T(8,128)S(1)}, u32[]{:S(2)}, u32[]{:S(2)}) collective-permute-start(f32[32,2,256]{2,0,1:T(8,128)S(1)} %slice_select_fusion.2), channel_id=1, source_target_pairs={{0,8},{1,9},{2,10},{3,11},{4,12},{5,13},{6,14},{7,15},{8,0},{9,1},... | collective-permute-start | bytes 196616 | tf_op jit(solution)/shard_map/ppermute | solution.py:34
  43.2 5.3 %collective-permute-start.4 = (f32[32,2,128]{2,0,1:T(8,128)S(1)}, f32[32,2,128]{2,0,1:T(8,128)S(1)}, u32[]{:S(2)}, u32[]{:S(2)}) collective-permute-start(f32[32,2,128]{2,0,1:T(8,128)S(1)} %slice_select_fusion.3), channel_id=1, source_target_pairs={{0,16},{1,17},{2,18},{3,19},{4,20},{5,21},{6,22},{7,23},{8,24},{9,... | collective-permute-start | bytes 98312 | tf_op jit(solution)/shard_map/ppermute | solution.py:34
  48.5 4.9 %collective-permute-start.5 = (f32[32,2,128]{2,0,1:T(8,128)S(1)}, f32[32,2,128]{2,0,1:T(8,128)S(1)}, u32[]{:S(2)}, u32[]{:S(2)}) collective-permute-start(f32[32,2,128]{2,0,1:T(8,128)S(1)} %select_add_fusion.4), channel_id=1, source_target_pairs={{0,16},{1,17},{2,18},{3,19},{4,20},{5,21},{6,22},{7,23},{8,24},{9,... | collective-permute-start | bytes 98312 | tf_op jit(solution)/shard_map/ppermute | solution.py:37
  53.3 4.3 %collective-permute-start.6 = (f32[32,2,256]{2,0,1:T(8,128)S(1)}, f32[32,2,256]{2,0,1:T(8,128)S(1)}, u32[]{:S(2)}, u32[]{:S(2)}) collective-permute-start(f32[32,2,256]{2,0,1:T(8,128)S(1)} %maximum_select_fusion.12), channel_id=1, source_target_pairs={{0,8},{1,9},{2,10},{3,11},{4,12},{5,13},{6,14},{7,15},{8,0},{9,1},... | collective-permute-start | bytes 196616 | tf_op jit(solution)/shard_map/ppermute | solution.py:37
  57.7 5.0 %collective-permute-start.7 = (f32[32,2,512]{2,0,1:T(8,128)S(1)}, f32[32,2,512]{2,0,1:T(8,128)S(1)}, u32[]{:S(2)}, u32[]{:S(2)}) collective-permute-start(f32[32,2,512]{2,0,1:T(8,128)S(1)} %maximum_select_fusion.9), channel_id=1, source_target_pairs={{0,4},{1,5},{2,6},{3,7},{4,0},{5,1},{6,2},{7,3},{8,12},{9,13},{10,... | collective-permute-start | bytes 393224 | tf_op jit(solution)/shard_map/ppermute | solution.py:37
  62.7 6.4 %collective-permute-start.8 = (f32[32,2,1024]{2,0,1:T(8,128)S(1)}, f32[32,2,1024]{2,0,1:T(8,128)S(1)}, u32[]{:S(2)}, u32[]{:S(2)}) collective-permute-start(f32[32,2,1024]{2,0,1:T(8,128)S(1)} %maximum_select_fusion.6), channel_id=1, source_target_pairs={{0,2},{1,3},{2,0},{3,1},{4,6},{5,7},{6,4},{7,5},{8,10},{9,11},{10,... | collective-permute-start | bytes 786440 | tf_op jit(solution)/shard_map/ppermute | solution.py:37
  69.2 2.0 %collective-permute-start.9 = (f32[32,2,2048]{2,0,1:T(8,128)S(1)}, f32[32,2,2048]{2,0,1:T(8,128)S(1)}, u32[]{:S(2)}, u32[]{:S(2)}) collective-permute-start(f32[32,2,2048]{2,0,1:T(8,128)S(1)} %maximum_select_fusion.3), channel_id=1, source_target_pairs={{0,1},{1,0},{2,3},{3,2},{4,5},{5,4},{6,7},{7,6},{8,9},{9,8},{10,11... | collective-permute-start | bytes 1572872 | tf_op jit(solution)/shard_map/ppermute | solution.py:37
  75.5 4.8 %collective-permute-start.10 = (f32[32,2,128]{2,0,1:T(8,128)S(1)}, f32[32,2,128]{2,0,1:T(8,128)S(1)}, u32[]{:S(2)}, u32[]{:S(2)}) collective-permute-start(f32[32,2,128]{2,0,1:T(8,128)S(1)} %bitcast.66), channel_id=1, source_target_pairs={{0,16},{1,17},{2,18},{3,19},{4,20},{5,21},{6,22},{7,23},{8,24},{9,... | collective-permute-start | bytes 98312 | tf_op jit(solution)/shard_map/ppermute | solution.py:46
  80.4 4.3 %collective-permute-start.11 = (f32[32,2,2,128]{3,0,1,2:T(8,128)S(1)}, f32[32,2,2,128]{3,0,1,2:T(8,128)S(1)}, u32[]{:S(2)}, u32[]{:S(2)}) collective-permute-start(f32[32,2,2,128]{3,0,1,2:T(8,128)S(1)} %maximum_select_fusion.14), channel_id=1, source_target_pairs={{0,8},{1,9},{2,10},{3,11},{4,12},{5,13},{6,14},{7,15},{8,0},{9,1},... | collective-permute-start | bytes 196616 | tf_op jit(solution)/shard_map/ppermute | solution.py:46
  84.7 5.0 %collective-permute-start.12 = (f32[32,2,2,2,128]{4,0,1,2,3:T(8,128)S(1)}, f32[32,2,2,2,128]{4,0,1,2,3:T(8,128)S(1)}, u32[]{:S(2)}, u32[]{:S(2)}) collective-permute-start(f32[32,2,2,2,128]{4,0,1,2,3:T(8,128)S(1)} %maximum_select_fusion.11), channel_id=1, source_target_pairs={{0,4},{1,5},{2,6},{3,7},{4,0},{5,1},{6,2},{7,3},{8,12},{9,13},{10,... | collective-permute-start | bytes 393224 | tf_op jit(solution)/shard_map/ppermute | solution.py:46
  89.8 6.4 %collective-permute-start.13 = (f32[32,2,2,2,2,128]{5,0,1,2,3,4:T(8,128)S(1)}, f32[32,2,2,2,2,128]{5,0,1,2,3,4:T(8,128)S(1)}, u32[]{:S(2)}, u32[]{:S(2)}) collective-permute-start(f32[32,2,2,2,2,128]{5,0,1,2,3,4:T(8,128)S(1)} %maximum_select_fusion.8), channel_id=1, source_target_pairs={{0,2},{1,3},{2,0},{3,1},{4,6},{5,7},{6,4},{7,5},{8,10},{9,11},{10,... | collective-permute-start | bytes 786440 | tf_op jit(solution)/shard_map/ppermute | solution.py:46
  96.3 2.0 %collective-permute-start.14 = (f32[32,2,2,2,2,2,128]{6,0,1,2,3,4,5:T(8,128)S(1)}, f32[32,2,2,2,2,2,128]{6,0,1,2,3,4,5:T(8,128)S(1)}, u32[]{:S(2)}, u32[]{:S(2)}) collective-permute-start(f32[32,2,2,2,2,2,128]{6,0,1,2,3,4,5:T(8,128)S(1)} %maximum_select_fusion.5), channel_id=1, source_target_pairs={{0,1},{1,0},{2,3},{3,2},{4,5},{5,4},{6,7},{7,6},{8,9},{9,8},{10,11... | collective-permute-start | bytes 1572872 | tf_op jit(solution)/shard_map/ppermute | solution.py:46
  107.8 1.2 collective-permute-start.15
  109.0 3.6 %collective-permute-start.16 = (f32[2,32]{1,0:T(2,128)S(1)}, f32[2,32]{1,0:T(2,128)S(1)}, u32[]{:S(2)}, u32[]{:S(2)}) collective-permute-start(f32[2,32]{1,0:T(2,128)S(1)} %fusion.59), channel_id=1, source_target_pairs={{0,2},{1,3},{2,0},{3,1},{4,6},{5,7},{6,4},{7,5},{8,10},{9,11},{10,... | collective-permute-start | bytes 776 | tf_op jit(solution)/shard_map/ppermute | solution.py:57
  112.7 3.6 %collective-permute-start.17 = (f32[2,32]{1,0:T(2,128)S(1)}, f32[2,32]{1,0:T(2,128)S(1)}, u32[]{:S(2)}, u32[]{:S(2)}) collective-permute-start(f32[2,32]{1,0:T(2,128)S(1)} %fusion.66), channel_id=1, source_target_pairs={{0,4},{1,5},{2,6},{3,7},{4,0},{5,1},{6,2},{7,3},{8,12},{9,13},{10,... | collective-permute-start | bytes 776 | tf_op jit(solution)/shard_map/ppermute | solution.py:57
  116.3 3.6 %collective-permute-start.18 = (f32[2,32]{1,0:T(2,128)S(1)}, f32[2,32]{1,0:T(2,128)S(1)}, u32[]{:S(2)}, u32[]{:S(2)}) collective-permute-start(f32[2,32]{1,0:T(2,128)S(1)} %add.68), channel_id=1, source_target_pairs={{0,8},{1,9},{2,10},{3,11},{4,12},{5,13},{6,14},{7,15},{8,0},{9,1},... | collective-permute-start | bytes 776 | tf_op jit(solution)/shard_map/ppermute | solution.py:57
  119.9 4.5 %collective-permute-start.19 = (f32[2,32]{1,0:T(2,128)S(1)}, f32[2,32]{1,0:T(2,128)S(1)}, u32[]{:S(2)}, u32[]{:S(2)}) collective-permute-start(f32[2,32]{1,0:T(2,128)S(1)} %add.69), channel_id=1, source_target_pairs={{0,16},{1,17},{2,18},{3,19},{4,20},{5,21},{6,22},{7,23},{8,24},{9,... | collective-permute-start | bytes 776 | tf_op jit(solution)/shard_map/ppermute | solution.py:57
  (4 other events, 9.8 us)

commit v3 on v2

--- a/solution.py
+++ b/solution.py
@@ -1,6 +1,7 @@
 import jax
 import jax.numpy as jnp
 from jax import lax
+from jax.experimental import pallas as pl
 from jax.sharding import PartitionSpec as P
 
 
@@ -58,6 +59,39 @@
     return x
 
 
+def _sums_kernel(acts_ref, gout_ref, pin_ref, pout_ref, sel_ref, out_ref):
+    modules = acts_ref.shape[1]
+    rank = pin_ref.shape[1] // modules
+    width = rank * rank
+    col = lax.broadcasted_iota(jnp.int32, (rank, width), 1)
+    row = lax.broadcasted_iota(jnp.int32, (rank, width), 0)
+    repeat = (col // rank == row).astype(jnp.bfloat16)
+    tile = (col % rank == row).astype(jnp.bfloat16)
+    sel = sel_ref[...]
+    for m in range(modules):
+        cols = slice(m * rank, (m + 1) * rank)
+        act_proj = jnp.dot(acts_ref[:, m, :], pin_ref[:, cols], preferred_element_type=jnp.float32)
+        grad_proj = jnp.dot(gout_ref[:, m, :], pout_ref[:, cols], preferred_element_type=jnp.float32)
+        act_wide = jnp.dot(act_proj.astype(jnp.bfloat16), tile, preferred_element_type=jnp.float32)
+        grad_wide = jnp.dot(grad_proj.astype(jnp.bfloat16), repeat, preferred_element_type=jnp.float32)
+        outer = grad_wide * act_wide
+        high = outer.astype(jnp.bfloat16)
+        low = (outer - high.astype(jnp.float32)).astype(jnp.bfloat16)
+        out_ref[:, m, :] = jnp.dot(sel, high, preferred_element_type=jnp.float32) + jnp.dot(
+            sel, low, preferred_element_type=jnp.float32
+        )
+
+
+def _module_sums(acts, grads_out, proj_in, proj_out, selector_t):
+    queries = selector_t.shape[0]
+    modules = acts.shape[1]
+    rank = proj_in.shape[1] // modules
+    return pl.pallas_call(
+        _sums_kernel,
+        out_shape=jax.ShapeDtypeStruct((queries, modules, rank * rank), jnp.float32),
+    )(acts, grads_out, proj_in, proj_out, selector_t)
+
+
 def shards(size, acts, grads_out, lengths, valid, proj_in, proj_out, fisher_inv, database):
     tok_rows = acts.shape[0]
     modules = acts.shape[1]
@@ -71,22 +105,10 @@
     selector = (
         (segment[:, None] == jnp.arange(queries, dtype=jnp.int32)[None, :]) & (valid[:, None] == 1)
     ).astype(jnp.bfloat16)
-    owner = (jnp.arange(modules * proj_rank) // proj_rank)[None, :] == jnp.arange(modules)[:, None]
-    w_in = jnp.where(owner[:, None, :], proj_in[None, :, :], jnp.zeros((), proj_in.dtype))
-    w_out = jnp.where(owner[:, None, :], proj_out[None, :, :], jnp.zeros((), proj_out.dtype))
-    dims = (((1, 2), (0, 1)), ((), ()))
-    act_proj = lax.dot_general(acts, w_in, dims, preferred_element_type=jnp.float32)
-    grad_proj = lax.dot_general(grads_out, w_out, dims, preferred_element_type=jnp.float32)
-    act_proj = _bf16_round(act_proj).reshape(tok_rows, modules, proj_rank)
-    grad_proj = _bf16_round(grad_proj).reshape(tok_rows, modules, proj_rank)
-    outer = (grad_proj[:, :, :, None] * act_proj[:, :, None, :]).reshape(tok_rows, modules * flat_width)
-    high = _bf16_round(outer)
-    low = outer - high
-    tdims = (((0,), (0,)), ((), ()))
-    partial_value = lax.dot_general(
-        selector, high.astype(jnp.bfloat16), tdims, preferred_element_type=jnp.float32
-    ) + lax.dot_general(selector, low.astype(jnp.bfloat16), tdims, preferred_element_type=jnp.float32)
-    partial_value = partial_value.reshape(queries, modules, flat_width)
+    selector_t = (
+        (jnp.arange(queries, dtype=jnp.int32)[:, None] == segment[None, :]) & (valid[None, :] == 1)
+    ).astype(jnp.bfloat16)
+    partial_value = _module_sums(acts, grads_out, proj_in, proj_out, selector_t)
     summed = _allreduce(partial_value, size, 2)
     precond_cols = jnp.einsum("qmk,mck->qmc", summed, fisher_inv, precision=lax.Precision.HIGH)
     scores = jnp.einsum(

time: 125 us -> 124 us (level)
  Pallas kernels: 0 us -> 16 us
  matrix products: 18.8 us -> 8.77 us
  local copies, waits for them, and re-layouts: 9.89 us -> 2.39 us
    pallas_call x0 -> x1, Pallas kernels: none -> 16 us  [_module_sums(): pl.pallas_call(_sums_kernel, out_shape=jax.ShapeDtypeStruct((queries, mod...]
    dot_general x4 -> x0, matrix products: 7.86 us -> none  [the longest x1 2.83 us: shards(): lax.dot_general(acts, w_in, dims, preferred_element_type=jnp.float32)]
    unnamed x18 -> x2, local copies, waits for them, and re-layouts: 3.85 us -> 0.01 us
    convert_element_type x1, other arithmetic: 2.61 us -> 0.61 us  [shards(): selector_t = ((jnp.arange(queries, dtype=jnp.int32)[:, None] == segment[N...]
    reshape x1 -> x0, local copies, waits for them, and re-layouts: 1.88 us -> none  [shards(): partial_value = partial_value.reshape(queries, modules, flat_width)]
    dot_general x1, matrix products: 4.3 us -> 2.47 us  [shards(): jnp.einsum('qmk,mck->qmc', summed, fisher_inv, precision=lax.Precision.HIGH)]
    select_n x4 -> x5, other arithmetic: 0.09 us -> 1.65 us  [_join(): jnp.where(low, jnp.concatenate([mine, other], axis), jnp.concatenate([oth...]
    slice x1 -> x0, local copies, waits for them, and re-layouts: 1.27 us -> none  [_allreduce(): lo = lax.slice_in_dim(cur, 0, half, axis=axis)]
where the time goes in v3:
time: 124 us; the launch traced here: 123 us
  waiting for transfers between devices  53.3 us (43%)
  starting transfers between devices  34.6 us (28%)
  Pallas kernels  16 us (13%)
  matrix products  8.77 us (7%)
  other arithmetic  8.05 us (6%)
  local copies, waits for them, and re-layouts  2.39 us (2%)
    pallas_call x1, Pallas kernels, _module_sums(): pl.pallas_call(_sums_kernel, out_shape=jax.ShapeDtypeStruct((queries, mod...  16 us
    ppermute x5, waiting for transfers between devices, _allreduce(): cur = keep + lax.ppermute(send, 'rows', _xor_pairs(size, s))  15.8 us
    ppermute x5, waiting for transfers between devices, _allreduce(): cur = _join(cur, lax.ppermute(cur, 'rows', _xor_pairs(size, s)), low, axis)  14.6 us
    ppermute x5, waiting for transfers between devices, _allgather(): other = lax.ppermute(cur, 'rows', _xor_pairs(size, s))  14.4 us
    ppermute x5, starting transfers between devices, _allreduce(): cur = keep + lax.ppermute(send, 'rows', _xor_pairs(size, s))  10.5 us
    ppermute x5, waiting for transfers between devices, _butterfly_sum(): x = x + lax.ppermute(x, 'rows', _xor_pairs(size, s))  8.51 us
    ppermute x5, starting transfers between devices, _allgather(): other = lax.ppermute(cur, 'rows', _xor_pairs(size, s))  8.06 us
    ppermute x5, starting transfers between devices, _allreduce(): cur = _join(cur, lax.ppermute(cur, 'rows', _xor_pairs(size, s)), low, axis)  8.05 us
  transfers between devices with their start and end apart: 20, of which 20 were waited for; matrix products, arithmetic and copies ran while one was open for 0% of the time, Pallas kernels for 0%

profile of v3, /device:TPU:0, one launch (start us, length us, event | category | flops | bytes accessed | tf_op | source)
XLA Modules:
  0.0 123.3 jit_solution(17433742529607824246)
XLA Ops:
  2.3 16.0 %shard_map.82 = f32[32,2,4096]{2,1,0:T(2,128)} custom-call(bf16[128,2,4096]{2,1,0:T(2,128)(2,1)} %acts_ref.1, bf16[128,2,4096]{2,1,0:T(2,128)(2,1)} %gout_ref.1, bf16[4096,128]{1,0:T(8,128)(2,1)} %pin_ref.1, bf16[4096,128]{1,0:T(8,128)(2,1)} %pout_ref.1, bf16[32,128]{1,0:T(8,128)(2,1)} %fusion.8.sel_ref), custom_call_target="tpu_custom_call" | custom-call | tf_op jit(solution)/shard_map/pallas_call | solution.py:89
  23.7 2.9 %collective-permute-start.1 = (f32[32,2,1024]{2,1,0:T(2,128)S(1)}, f32[32,2,1024]{2,1,0:T(2,128)S(1)}, u32[]{:S(2)}, u32[]{:S(2)}) collective-permute-start(f32[32,2,1024]{2,1,0:T(2,128)S(1)} %broadcast_select_fusion.1), channel_id=1, source_target_pairs={{0,2},{1,3},{2,0},{3,1},{4,6},{5,7},{6,4},{7,5},{8,10},{9,11},{10,... | collective-permute-start | bytes 786440 | tf_op jit(solution)/shard_map/ppermute | solution.py:35
  26.6 6.6 %collective-permute-done.1 = f32[32,2,1024]{2,1,0:T(2,128)S(1)} collective-permute-done((f32[32,2,1024]{2,1,0:T(2,128)S(1)}, f32[32,2,1024]{2,1,0:T(2,128)S(1)}, u32[]{:S(2)}, u32[]{:S(2)}) %collective-permute-start.1) | collective-permute-done | bytes 262176 | tf_op jit(solution)/shard_map/ppermute | solution.py:35
  35.3 3.2 %collective-permute-done.2 = f32[32,2,512]{2,1,0:T(2,128)S(1)} collective-permute-done((f32[32,2,512]{2,1,0:T(2,128)S(1)}, f32[32,2,512]{2,1,0:T(2,128)S(1)}, u32[]{:S(2)}, u32[]{:S(2)}) %collective-permute-start.2) | collective-permute-done | bytes 131104 | tf_op jit(solution)/shard_map/ppermute | solution.py:35
  40.5 2.4 %collective-permute-done.3 = f32[32,2,256]{2,1,0:T(2,128)S(1)} collective-permute-done((f32[32,2,256]{2,1,0:T(2,128)S(1)}, f32[32,2,256]{2,1,0:T(2,128)S(1)}, u32[]{:S(2)}, u32[]{:S(2)}) %collective-permute-start.3) | collective-permute-done | bytes 65568 | tf_op jit(solution)/shard_map/ppermute | solution.py:35
  43.1 3.3 %collective-permute-start.4 = (f32[32,2,128]{2,1,0:T(2,128)S(1)}, f32[32,2,128]{2,1,0:T(2,128)S(1)}, u32[]{:S(2)}, u32[]{:S(2)}) collective-permute-start(f32[32,2,128]{2,1,0:T(2,128)S(1)} %broadcast_select_fusion.4), channel_id=1, source_target_pairs={{0,16},{1,17},{2,18},{3,19},{4,20},{5,21},{6,22},{7,23},{8,24},{9,... | collective-permute-start | bytes 98312 | tf_op jit(solution)/shard_map/ppermute | solution.py:35
  46.3 2.0 %collective-permute-done.4 = f32[32,2,128]{2,1,0:T(2,128)S(1)} collective-permute-done((f32[32,2,128]{2,1,0:T(2,128)S(1)}, f32[32,2,128]{2,1,0:T(2,128)S(1)}, u32[]{:S(2)}, u32[]{:S(2)}) %collective-permute-start.4) | collective-permute-done | bytes 32800 | tf_op jit(solution)/shard_map/ppermute | solution.py:35
  48.4 2.9 %collective-permute-start.5 = (f32[32,2,128]{2,1,0:T(2,128)S(1)}, f32[32,2,128]{2,1,0:T(2,128)S(1)}, u32[]{:S(2)}, u32[]{:S(2)}) collective-permute-start(f32[32,2,128]{2,1,0:T(2,128)S(1)} %select_add_fusion.4), channel_id=1, source_target_pairs={{0,16},{1,17},{2,18},{3,19},{4,20},{5,21},{6,22},{7,23},{8,24},{9,... | collective-permute-start | bytes 98312 | tf_op jit(solution)/shard_map/ppermute | solution.py:38
  51.2 2.0 %collective-permute-done.5 = f32[32,2,128]{2,1,0:T(2,128)S(1)} collective-permute-done((f32[32,2,128]{2,1,0:T(2,128)S(1)}, f32[32,2,128]{2,1,0:T(2,128)S(1)}, u32[]{:S(2)}, u32[]{:S(2)}) %collective-permute-start.5) | collective-permute-done | bytes 32800 | tf_op jit(solution)/shard_map/ppermute | solution.py:38
  53.3 2.0 %collective-permute-start.6 = (f32[32,2,256]{2,1,0:T(2,128)S(1)}, f32[32,2,256]{2,1,0:T(2,128)S(1)}, u32[]{:S(2)}, u32[]{:S(2)}) collective-permute-start(f32[32,2,256]{2,1,0:T(2,128)S(1)} %maximum_select_fusion.11), channel_id=1, source_target_pairs={{0,8},{1,9},{2,10},{3,11},{4,12},{5,13},{6,14},{7,15},{8,0},{9,1},... | collective-permute-start | bytes 196616 | tf_op jit(solution)/shard_map/ppermute | solution.py:38
  55.3 2.3 %collective-permute-done.6 = f32[32,2,256]{2,1,0:T(2,128)S(1)} collective-permute-done((f32[32,2,256]{2,1,0:T(2,128)S(1)}, f32[32,2,256]{2,1,0:T(2,128)S(1)}, u32[]{:S(2)}, u32[]{:S(2)}) %collective-permute-start.6) | collective-permute-done | bytes 65568 | tf_op jit(solution)/shard_map/ppermute | solution.py:38
  59.2 3.5 %collective-permute-done.7 = f32[32,2,512]{2,1,0:T(2,128)S(1)} collective-permute-done((f32[32,2,512]{2,1,0:T(2,128)S(1)}, f32[32,2,512]{2,1,0:T(2,128)S(1)}, u32[]{:S(2)}, u32[]{:S(2)}) %collective-permute-start.7) | collective-permute-done | bytes 131104 | tf_op jit(solution)/shard_map/ppermute | solution.py:38
  64.5 4.9 %collective-permute-done.8 = f32[32,2,1024]{2,1,0:T(2,128)S(1)} collective-permute-done((f32[32,2,1024]{2,1,0:T(2,128)S(1)}, f32[32,2,1024]{2,1,0:T(2,128)S(1)}, u32[]{:S(2)}, u32[]{:S(2)}) %collective-permute-start.8) | collective-permute-done | bytes 262176 | tf_op jit(solution)/shard_map/ppermute | solution.py:38
  72.7 2.5 %fusion.5 = f32[2,32,128]{2,1,0:T(8,128)S(1)} fusion(f32[2,128,4096]{2,1,0:T(8,128)S(1)} %copy-done, f32[32,2,4096]{2,1,0:T(2,128)S(1)} %maximum_select_fusion), kind=kOutput, calls=%fused_computation.5 | convolution fusion | flops 201326592 | bytes 5275648 | tf_op jit(solution)/shard_map/qmk,mck->qmc/dot_general | solution.py:113
  75.2 2.9 %collective-permute-start.10 = (f32[32,2,128]{2,0,1:T(8,128)S(1)}, f32[32,2,128]{2,0,1:T(8,128)S(1)}, u32[]{:S(2)}, u32[]{:S(2)}) collective-permute-start(f32[32,2,128]{2,0,1:T(8,128)S(1)} %bitcast.47), channel_id=1, source_target_pairs={{0,16},{1,17},{2,18},{3,19},{4,20},{5,21},{6,22},{7,23},{8,24},{9,... | collective-permute-start | bytes 98312 | tf_op jit(solution)/shard_map/ppermute | solution.py:47
  78.1 2.0 %collective-permute-done.10 = f32[32,2,128]{2,0,1:T(8,128)S(1)} collective-permute-done((f32[32,2,128]{2,0,1:T(8,128)S(1)}, f32[32,2,128]{2,0,1:T(8,128)S(1)}, u32[]{:S(2)}, u32[]{:S(2)}) %collective-permute-start.10) | collective-permute-done | bytes 32800 | tf_op jit(solution)/shard_map/ppermute | solution.py:47
  80.1 2.0 %collective-permute-start.11 = (f32[32,2,2,128]{3,0,1,2:T(8,128)S(1)}, f32[32,2,2,128]{3,0,1,2:T(8,128)S(1)}, u32[]{:S(2)}, u32[]{:S(2)}) collective-permute-start(f32[32,2,2,128]{3,0,1,2:T(8,128)S(1)} %maximum_select_fusion.13), channel_id=1, source_target_pairs={{0,8},{1,9},{2,10},{3,11},{4,12},{5,13},{6,14},{7,15},{8,0},{9,1},... | collective-permute-start | bytes 196616 | tf_op jit(solution)/shard_map/ppermute | solution.py:47
  82.1 2.3 %collective-permute-done.11 = f32[32,2,2,128]{3,0,1,2:T(8,128)S(1)} collective-permute-done((f32[32,2,2,128]{3,0,1,2:T(8,128)S(1)}, f32[32,2,2,128]{3,0,1,2:T(8,128)S(1)}, u32[]{:S(2)}, u32[]{:S(2)}) %collective-permute-start.11) | collective-permute-done | bytes 65568 | tf_op jit(solution)/shard_map/ppermute | solution.py:47
  86.0 3.5 %collective-permute-done.12 = f32[32,2,2,2,128]{4,0,1,2,3:T(8,128)S(1)} collective-permute-done((f32[32,2,2,2,128]{4,0,1,2,3:T(8,128)S(1)}, f32[32,2,2,2,128]{4,0,1,2,3:T(8,128)S(1)}, u32[]{:S(2)}, u32[]{:S(2)}) %collective-permute-start.12) | collective-permute-done | bytes 131104 | tf_op jit(solution)/shard_map/ppermute | solution.py:47
  91.1 4.9 %collective-permute-done.13 = f32[32,2,2,2,2,128]{5,0,1,2,3,4:T(8,128)S(1)} collective-permute-done((f32[32,2,2,2,2,128]{5,0,1,2,3,4:T(8,128)S(1)}, f32[32,2,2,2,2,128]{5,0,1,2,3,4:T(8,128)S(1)}, u32[]{:S(2)}, u32[]{:S(2)}) %collective-permute-start.13) | collective-permute-done | bytes 262176 | tf_op jit(solution)/shard_map/ppermute | solution.py:47
  99.7 6.3 %fusion.12 = (f32[32]{0:T(128)S(1)}, f32[32]{0:T(128)S(1)}, f32[32,128]{1,0:T(8,128)S(1)}) fusion(f32[32,2,4096]{2,0,1:T(8,128)S(1)} %select_n.250, f32[128,2,4096]{2,1,0:T(2,128)} %param.15), kind=kOutput, calls=%fused_computation.43 | convolution fusion | flops 201338816 | bytes 5259520 | tf_op jit(solution)/shard_map/qmk,nmk->qn/dot_general | solution.py:114
  108.8 2.1 %collective-permute-done.16 = f32[2,32]{1,0:T(2,128)S(1)} collective-permute-done((f32[2,32]{1,0:T(2,128)S(1)}, f32[2,32]{1,0:T(2,128)S(1)}, u32[]{:S(2)}, u32[]{:S(2)}) %collective-permute-start.16) | collective-permute-done | bytes 288 | tf_op jit(solution)/shard_map/ppermute | solution.py:58
  112.5 2.1 %collective-permute-done.17 = f32[2,32]{1,0:T(2,128)S(1)} collective-permute-done((f32[2,32]{1,0:T(2,128)S(1)}, f32[2,32]{1,0:T(2,128)S(1)}, u32[]{:S(2)}, u32[]{:S(2)}) %collective-permute-start.17) | collective-permute-done | bytes 288 | tf_op jit(solution)/shard_map/ppermute | solution.py:58
  118.1 2.8 %collective-permute-start.19 = (f32[2,32]{1,0:T(2,128)S(1)}, f32[2,32]{1,0:T(2,128)S(1)}, u32[]{:S(2)}, u32[]{:S(2)}) collective-permute-start(f32[2,32]{1,0:T(2,128)S(1)} %add.60), channel_id=1, source_target_pairs={{0,16},{1,17},{2,18},{3,19},{4,20},{5,21},{6,22},{7,23},{8,24},{9,... | collective-permute-start | bytes 776 | tf_op jit(solution)/shard_map/ppermute | solution.py:58
  (66 shorter events, 35.8 us)
Async XLA Ops:
  19.7 2.1 %collective-permute-start = (f32[32,2,2048]{2,1,0:T(2,128)S(1)}, f32[32,2,2048]{2,1,0:T(2,128)S(1)}, u32[]{:S(2)}, u32[]{:S(2)}) collective-permute-start(f32[32,2,2048]{2,1,0:T(2,128)S(1)} %broadcast_select_fusion), channel_id=1, source_target_pairs={{0,1},{1,0},{2,3},{3,2},{4,5},{5,4},{6,7},{7,6},{8,9},{9,8},{10,11... | collective-permute-start | bytes 1572872 | tf_op jit(solution)/shard_map/ppermute | solution.py:35
  23.7 9.5 %collective-permute-start.1 = (f32[32,2,1024]{2,1,0:T(2,128)S(1)}, f32[32,2,1024]{2,1,0:T(2,128)S(1)}, u32[]{:S(2)}, u32[]{:S(2)}) collective-permute-start(f32[32,2,1024]{2,1,0:T(2,128)S(1)} %broadcast_select_fusion.1), channel_id=1, source_target_pairs={{0,2},{1,3},{2,0},{3,1},{4,6},{5,7},{6,4},{7,5},{8,10},{9,11},{10,... | collective-permute-start | bytes 786440 | tf_op jit(solution)/shard_map/ppermute | solution.py:35
  33.5 5.0 %collective-permute-start.2 = (f32[32,2,512]{2,1,0:T(2,128)S(1)}, f32[32,2,512]{2,1,0:T(2,128)S(1)}, u32[]{:S(2)}, u32[]{:S(2)}) collective-permute-start(f32[32,2,512]{2,1,0:T(2,128)S(1)} %broadcast_select_fusion.2), channel_id=1, source_target_pairs={{0,4},{1,5},{2,6},{3,7},{4,0},{5,1},{6,2},{7,3},{8,12},{9,13},{10,... | collective-permute-start | bytes 393224 | tf_op jit(solution)/shard_map/ppermute | solution.py:35
  38.6 4.3 %collective-permute-start.3 = (f32[32,2,256]{2,1,0:T(2,128)S(1)}, f32[32,2,256]{2,1,0:T(2,128)S(1)}, u32[]{:S(2)}, u32[]{:S(2)}) collective-permute-start(f32[32,2,256]{2,1,0:T(2,128)S(1)} %broadcast_select_fusion.3), channel_id=1, source_target_pairs={{0,8},{1,9},{2,10},{3,11},{4,12},{5,13},{6,14},{7,15},{8,0},{9,1},... | collective-permute-start | bytes 196616 | tf_op jit(solution)/shard_map/ppermute | solution.py:35
  40.5 32.2 %copy-start = (f32[2,128,4096]{2,1,0:T(8,128)S(1)}, f32[2,128,4096]{2,1,0:T(8,128)}, u32[]{:S(2)}) copy-start(f32[2,128,4096]{2,1,0:T(8,128)} %param.14) | copy-start | bytes 12582916
  43.1 5.3 %collective-permute-start.4 = (f32[32,2,128]{2,1,0:T(2,128)S(1)}, f32[32,2,128]{2,1,0:T(2,128)S(1)}, u32[]{:S(2)}, u32[]{:S(2)}) collective-permute-start(f32[32,2,128]{2,1,0:T(2,128)S(1)} %broadcast_select_fusion.4), channel_id=1, source_target_pairs={{0,16},{1,17},{2,18},{3,19},{4,20},{5,21},{6,22},{7,23},{8,24},{9,... | collective-permute-start | bytes 98312 | tf_op jit(solution)/shard_map/ppermute | solution.py:35
  48.4 4.9 %collective-permute-start.5 = (f32[32,2,128]{2,1,0:T(2,128)S(1)}, f32[32,2,128]{2,1,0:T(2,128)S(1)}, u32[]{:S(2)}, u32[]{:S(2)}) collective-permute-start(f32[32,2,128]{2,1,0:T(2,128)S(1)} %select_add_fusion.4), channel_id=1, source_target_pairs={{0,16},{1,17},{2,18},{3,19},{4,20},{5,21},{6,22},{7,23},{8,24},{9,... | collective-permute-start | bytes 98312 | tf_op jit(solution)/shard_map/ppermute | solution.py:38
  53.3 4.3 %collective-permute-start.6 = (f32[32,2,256]{2,1,0:T(2,128)S(1)}, f32[32,2,256]{2,1,0:T(2,128)S(1)}, u32[]{:S(2)}, u32[]{:S(2)}) collective-permute-start(f32[32,2,256]{2,1,0:T(2,128)S(1)} %maximum_select_fusion.11), channel_id=1, source_target_pairs={{0,8},{1,9},{2,10},{3,11},{4,12},{5,13},{6,14},{7,15},{8,0},{9,1},... | collective-permute-start | bytes 196616 | tf_op jit(solution)/shard_map/ppermute | solution.py:38
  57.7 5.0 %collective-permute-start.7 = (f32[32,2,512]{2,1,0:T(2,128)S(1)}, f32[32,2,512]{2,1,0:T(2,128)S(1)}, u32[]{:S(2)}, u32[]{:S(2)}) collective-permute-start(f32[32,2,512]{2,1,0:T(2,128)S(1)} %maximum_select_fusion.8), channel_id=1, source_target_pairs={{0,4},{1,5},{2,6},{3,7},{4,0},{5,1},{6,2},{7,3},{8,12},{9,13},{10,... | collective-permute-start | bytes 393224 | tf_op jit(solution)/shard_map/ppermute | solution.py:38
  62.9 6.4 %collective-permute-start.8 = (f32[32,2,1024]{2,1,0:T(2,128)S(1)}, f32[32,2,1024]{2,1,0:T(2,128)S(1)}, u32[]{:S(2)}, u32[]{:S(2)}) collective-permute-start(f32[32,2,1024]{2,1,0:T(2,128)S(1)} %maximum_select_fusion.5), channel_id=1, source_target_pairs={{0,2},{1,3},{2,0},{3,1},{4,6},{5,7},{6,4},{7,5},{8,10},{9,11},{10,... | collective-permute-start | bytes 786440 | tf_op jit(solution)/shard_map/ppermute | solution.py:38
  69.8 2.0 %collective-permute-start.9 = (f32[32,2,2048]{2,1,0:T(2,128)S(1)}, f32[32,2,2048]{2,1,0:T(2,128)S(1)}, u32[]{:S(2)}, u32[]{:S(2)}) collective-permute-start(f32[32,2,2048]{2,1,0:T(2,128)S(1)} %maximum_select_fusion.2), channel_id=1, source_target_pairs={{0,1},{1,0},{2,3},{3,2},{4,5},{5,4},{6,7},{7,6},{8,9},{9,8},{10,11... | collective-permute-start | bytes 1572872 | tf_op jit(solution)/shard_map/ppermute | solution.py:38
  75.2 4.9 %collective-permute-start.10 = (f32[32,2,128]{2,0,1:T(8,128)S(1)}, f32[32,2,128]{2,0,1:T(8,128)S(1)}, u32[]{:S(2)}, u32[]{:S(2)}) collective-permute-start(f32[32,2,128]{2,0,1:T(8,128)S(1)} %bitcast.47), channel_id=1, source_target_pairs={{0,16},{1,17},{2,18},{3,19},{4,20},{5,21},{6,22},{7,23},{8,24},{9,... | collective-permute-start | bytes 98312 | tf_op jit(solution)/shard_map/ppermute | solution.py:47
  80.1 4.3 %collective-permute-start.11 = (f32[32,2,2,128]{3,0,1,2:T(8,128)S(1)}, f32[32,2,2,128]{3,0,1,2:T(8,128)S(1)}, u32[]{:S(2)}, u32[]{:S(2)}) collective-permute-start(f32[32,2,2,128]{3,0,1,2:T(8,128)S(1)} %maximum_select_fusion.13), channel_id=1, source_target_pairs={{0,8},{1,9},{2,10},{3,11},{4,12},{5,13},{6,14},{7,15},{8,0},{9,1},... | collective-permute-start | bytes 196616 | tf_op jit(solution)/shard_map/ppermute | solution.py:47
  84.4 5.0 %collective-permute-start.12 = (f32[32,2,2,2,128]{4,0,1,2,3:T(8,128)S(1)}, f32[32,2,2,2,128]{4,0,1,2,3:T(8,128)S(1)}, u32[]{:S(2)}, u32[]{:S(2)}) collective-permute-start(f32[32,2,2,2,128]{4,0,1,2,3:T(8,128)S(1)} %maximum_select_fusion.10), channel_id=1, source_target_pairs={{0,4},{1,5},{2,6},{3,7},{4,0},{5,1},{6,2},{7,3},{8,12},{9,13},{10,... | collective-permute-start | bytes 393224 | tf_op jit(solution)/shard_map/ppermute | solution.py:47
  89.5 6.4 %collective-permute-start.13 = (f32[32,2,2,2,2,128]{5,0,1,2,3,4:T(8,128)S(1)}, f32[32,2,2,2,2,128]{5,0,1,2,3,4:T(8,128)S(1)}, u32[]{:S(2)}, u32[]{:S(2)}) collective-permute-start(f32[32,2,2,2,2,128]{5,0,1,2,3,4:T(8,128)S(1)} %maximum_select_fusion.7), channel_id=1, source_target_pairs={{0,2},{1,3},{2,0},{3,1},{4,6},{5,7},{6,4},{7,5},{8,10},{9,11},{10,... | collective-permute-start | bytes 786440 | tf_op jit(solution)/shard_map/ppermute | solution.py:47
  96.0 2.0 %collective-permute-start.14 = (f32[32,2,2,2,2,2,128]{6,0,1,2,3,4,5:T(8,128)S(1)}, f32[32,2,2,2,2,2,128]{6,0,1,2,3,4,5:T(8,128)S(1)}, u32[]{:S(2)}, u32[]{:S(2)}) collective-permute-start(f32[32,2,2,2,2,2,128]{6,0,1,2,3,4,5:T(8,128)S(1)} %maximum_select_fusion.4), channel_id=1, source_target_pairs={{0,1},{1,0},{2,3},{3,2},{4,5},{5,4},{6,7},{7,6},{8,9},{9,8},{10,11... | collective-permute-start | bytes 1572872 | tf_op jit(solution)/shard_map/ppermute | solution.py:47
  106.0 1.2 collective-permute-start.15
  107.3 3.6 %collective-permute-start.16 = (f32[2,32]{1,0:T(2,128)S(1)}, f32[2,32]{1,0:T(2,128)S(1)}, u32[]{:S(2)}, u32[]{:S(2)}) collective-permute-start(f32[2,32]{1,0:T(2,128)S(1)} %fusion.11), channel_id=1, source_target_pairs={{0,2},{1,3},{2,0},{3,1},{4,6},{5,7},{6,4},{7,5},{8,10},{9,11},{10,... | collective-permute-start | bytes 776 | tf_op jit(solution)/shard_map/ppermute | solution.py:58
  110.9 3.6 %collective-permute-start.17 = (f32[2,32]{1,0:T(2,128)S(1)}, f32[2,32]{1,0:T(2,128)S(1)}, u32[]{:S(2)}, u32[]{:S(2)}) collective-permute-start(f32[2,32]{1,0:T(2,128)S(1)} %fusion.15), channel_id=1, source_target_pairs={{0,4},{1,5},{2,6},{3,7},{4,0},{5,1},{6,2},{7,3},{8,12},{9,13},{10,... | collective-permute-start | bytes 776 | tf_op jit(solution)/shard_map/ppermute | solution.py:58
  114.6 3.6 %collective-permute-start.18 = (f32[2,32]{1,0:T(2,128)S(1)}, f32[2,32]{1,0:T(2,128)S(1)}, u32[]{:S(2)}, u32[]{:S(2)}) collective-permute-start(f32[2,32]{1,0:T(2,128)S(1)} %add.59), channel_id=1, source_target_pairs={{0,8},{1,9},{2,10},{3,11},{4,12},{5,13},{6,14},{7,15},{8,0},{9,1},... | collective-permute-start | bytes 776 | tf_op jit(solution)/shard_map/ppermute | solution.py:58
  118.1 4.5 %collective-permute-start.19 = (f32[2,32]{1,0:T(2,128)S(1)}, f32[2,32]{1,0:T(2,128)S(1)}, u32[]{:S(2)}, u32[]{:S(2)}) collective-permute-start(f32[2,32]{1,0:T(2,128)S(1)} %add.60), channel_id=1, source_target_pairs={{0,16},{1,17},{2,18},{3,19},{4,20},{5,21},{6,22},{7,23},{8,24},{9,... | collective-permute-start | bytes 776 | tf_op jit(solution)/shard_map/ppermute | solution.py:58

commit v4 on v3

--- a/solution.py
+++ b/solution.py
@@ -2,6 +2,7 @@
 import jax.numpy as jnp
 from jax import lax
 from jax.experimental import pallas as pl
+from jax.experimental.pallas import tpu as pltpu
 from jax.sharding import PartitionSpec as P
 
 
@@ -59,21 +60,29 @@
     return x
 
 
-def _sums_kernel(acts_ref, gout_ref, pin_ref, pout_ref, sel_ref, out_ref):
-    modules = acts_ref.shape[1]
+def _sums_kernel(acts_ref, gout_ref, pin_ref, pout_ref, sel_ref, out_ref, act_scr, grad_scr):
+    tokens, modules, width_in = acts_ref.shape
     rank = pin_ref.shape[1] // modules
     width = rank * rank
-    col = lax.broadcasted_iota(jnp.int32, (rank, width), 1)
-    row = lax.broadcasted_iota(jnp.int32, (rank, width), 0)
-    repeat = (col // rank == row).astype(jnp.bfloat16)
-    tile = (col % rank == row).astype(jnp.bfloat16)
+    act_scr[...] = jnp.dot(
+        acts_ref[...].reshape(tokens * modules, width_in), pin_ref[...],
+        preferred_element_type=jnp.float32,
+    )
+    grad_scr[...] = jnp.dot(
+        gout_ref[...].reshape(tokens * modules, width_in), pout_ref[...],
+        preferred_element_type=jnp.float32,
+    )
+    col = lax.broadcasted_iota(jnp.int32, (modules * rank, width), 1)
+    row = lax.broadcasted_iota(jnp.int32, (modules * rank, width), 0)
     sel = sel_ref[...]
     for m in range(modules):
-        cols = slice(m * rank, (m + 1) * rank)
-        act_proj = jnp.dot(acts_ref[:, m, :], pin_ref[:, cols], preferred_element_type=jnp.float32)
-        grad_proj = jnp.dot(gout_ref[:, m, :], pout_ref[:, cols], preferred_element_type=jnp.float32)
-        act_wide = jnp.dot(act_proj.astype(jnp.bfloat16), tile, preferred_element_type=jnp.float32)
-        grad_wide = jnp.dot(grad_proj.astype(jnp.bfloat16), repeat, preferred_element_type=jnp.float32)
+        repeat = (m * rank + col // rank == row).astype(jnp.bfloat16)
+        tile = (m * rank + col % rank == row).astype(jnp.bfloat16)
+        rows = pl.ds(m, tokens, stride=modules)
+        act_proj = act_scr[rows, :].astype(jnp.bfloat16)
+        grad_proj = grad_scr[rows, :].astype(jnp.bfloat16)
+        act_wide = jnp.dot(act_proj, tile, preferred_element_type=jnp.float32)
+        grad_wide = jnp.dot(grad_proj, repeat, preferred_element_type=jnp.float32)
         outer = grad_wide * act_wide
         high = outer.astype(jnp.bfloat16)
         low = (outer - high.astype(jnp.float32)).astype(jnp.bfloat16)
@@ -84,11 +93,13 @@
 
 def _module_sums(acts, grads_out, proj_in, proj_out, selector_t):
     queries = selector_t.shape[0]
-    modules = acts.shape[1]
+    tokens, modules, _ = acts.shape
     rank = proj_in.shape[1] // modules
+    scratch = pltpu.VMEM((tokens * modules, modules * rank), jnp.float32)
     return pl.pallas_call(
         _sums_kernel,
         out_shape=jax.ShapeDtypeStruct((queries, modules, rank * rank), jnp.float32),
+        scratch_shapes=[scratch, scratch],
     )(acts, grads_out, proj_in, proj_out, selector_t)
 
 

time: 124 us -> 115 us (0.927)
  Pallas kernels: 16 us -> 6.9 us
    pallas_call x1, Pallas kernels: 16 us -> 6.9 us  [_module_sums(): pl.pallas_call(_sums_kernel, out_shape=jax.ShapeDtypeStruct((queries, mod...]
where the time goes in v4:
time: 115 us; the launch traced here: 114 us
  waiting for transfers between devices  53.4 us (46%)
  starting transfers between devices  34.6 us (30%)
  matrix products  8.94 us (8%)
  other arithmetic  8.05 us (7%)
  Pallas kernels  6.9 us (6%)
  local copies, waits for them, and re-layouts  2.39 us (2%)
    ppermute x5, waiting for transfers between devices, _allreduce(): cur = keep + lax.ppermute(send, 'rows', _xor_pairs(size, s))  15.8 us
    ppermute x5, waiting for transfers between devices, _allreduce(): cur = _join(cur, lax.ppermute(cur, 'rows', _xor_pairs(size, s)), low, axis)  14.6 us
    ppermute x5, waiting for transfers between devices, _allgather(): other = lax.ppermute(cur, 'rows', _xor_pairs(size, s))  14.5 us
    ppermute x5, starting transfers between devices, _allreduce(): cur = keep + lax.ppermute(send, 'rows', _xor_pairs(size, s))  10.5 us
    ppermute x5, waiting for transfers between devices, _butterfly_sum(): x = x + lax.ppermute(x, 'rows', _xor_pairs(size, s))  8.52 us
    ppermute x5, starting transfers between devices, _allgather(): other = lax.ppermute(cur, 'rows', _xor_pairs(size, s))  8.04 us
    ppermute x5, starting transfers between devices, _allreduce(): cur = _join(cur, lax.ppermute(cur, 'rows', _xor_pairs(size, s)), low, axis)  8.03 us
    ppermute x5, starting transfers between devices, _butterfly_sum(): x = x + lax.ppermute(x, 'rows', _xor_pairs(size, s))  8.03 us
  transfers between devices with their start and end apart: 20, of which 20 were waited for; matrix products, arithmetic and copies ran while one was open for 0% of the time, Pallas kernels for 0%

profile of v4, /device:TPU:0, one launch (start us, length us, event | category | flops | bytes accessed | tf_op | source)
XLA Modules:
  0.0 114.5 jit_solution(11302657466538272839)
XLA Ops:
  2.3 6.9 %shard_map.82 = f32[32,2,4096]{2,1,0:T(2,128)} custom-call(bf16[128,2,4096]{2,1,0:T(2,128)(2,1)} %acts_ref.1, bf16[128,2,4096]{2,1,0:T(2,128)(2,1)} %gout_ref.1, bf16[4096,128]{1,0:T(8,128)(2,1)} %pin_ref.1, bf16[4096,128]{1,0:T(8,128)(2,1)} %pout_ref.1, bf16[32,128]{1,0:T(8,128)(2,1)} %fusion.8.sel_ref), custom_call_target="tpu_custom_call" | custom-call | tf_op jit(solution)/shard_map/pallas_call | solution.py:99
  14.6 2.9 %collective-permute-start.1 = (f32[32,2,1024]{2,1,0:T(2,128)S(1)}, f32[32,2,1024]{2,1,0:T(2,128)S(1)}, u32[]{:S(2)}, u32[]{:S(2)}) collective-permute-start(f32[32,2,1024]{2,1,0:T(2,128)S(1)} %broadcast_select_fusion.1), channel_id=1, source_target_pairs={{0,2},{1,3},{2,0},{3,1},{4,6},{5,7},{6,4},{7,5},{8,10},{9,11},{10,... | collective-permute-start | bytes 786440 | tf_op jit(solution)/shard_map/ppermute | solution.py:36
  17.5 6.6 %collective-permute-done.1 = f32[32,2,1024]{2,1,0:T(2,128)S(1)} collective-permute-done((f32[32,2,1024]{2,1,0:T(2,128)S(1)}, f32[32,2,1024]{2,1,0:T(2,128)S(1)}, u32[]{:S(2)}, u32[]{:S(2)}) %collective-permute-start.1) | collective-permute-done | bytes 262176 | tf_op jit(solution)/shard_map/ppermute | solution.py:36
  26.3 3.2 %collective-permute-done.2 = f32[32,2,512]{2,1,0:T(2,128)S(1)} collective-permute-done((f32[32,2,512]{2,1,0:T(2,128)S(1)}, f32[32,2,512]{2,1,0:T(2,128)S(1)}, u32[]{:S(2)}, u32[]{:S(2)}) %collective-permute-start.2) | collective-permute-done | bytes 131104 | tf_op jit(solution)/shard_map/ppermute | solution.py:36
  31.5 2.4 %collective-permute-done.3 = f32[32,2,256]{2,1,0:T(2,128)S(1)} collective-permute-done((f32[32,2,256]{2,1,0:T(2,128)S(1)}, f32[32,2,256]{2,1,0:T(2,128)S(1)}, u32[]{:S(2)}, u32[]{:S(2)}) %collective-permute-start.3) | collective-permute-done | bytes 65568 | tf_op jit(solution)/shard_map/ppermute | solution.py:36
  34.0 3.3 %collective-permute-start.4 = (f32[32,2,128]{2,1,0:T(2,128)S(1)}, f32[32,2,128]{2,1,0:T(2,128)S(1)}, u32[]{:S(2)}, u32[]{:S(2)}) collective-permute-start(f32[32,2,128]{2,1,0:T(2,128)S(1)} %broadcast_select_fusion.4), channel_id=1, source_target_pairs={{0,16},{1,17},{2,18},{3,19},{4,20},{5,21},{6,22},{7,23},{8,24},{9,... | collective-permute-start | bytes 98312 | tf_op jit(solution)/shard_map/ppermute | solution.py:36
  37.3 2.0 %collective-permute-done.4 = f32[32,2,128]{2,1,0:T(2,128)S(1)} collective-permute-done((f32[32,2,128]{2,1,0:T(2,128)S(1)}, f32[32,2,128]{2,1,0:T(2,128)S(1)}, u32[]{:S(2)}, u32[]{:S(2)}) %collective-permute-start.4) | collective-permute-done | bytes 32800 | tf_op jit(solution)/shard_map/ppermute | solution.py:36
  39.3 2.9 %collective-permute-start.5 = (f32[32,2,128]{2,1,0:T(2,128)S(1)}, f32[32,2,128]{2,1,0:T(2,128)S(1)}, u32[]{:S(2)}, u32[]{:S(2)}) collective-permute-start(f32[32,2,128]{2,1,0:T(2,128)S(1)} %select_add_fusion.4), channel_id=1, source_target_pairs={{0,16},{1,17},{2,18},{3,19},{4,20},{5,21},{6,22},{7,23},{8,24},{9,... | collective-permute-start | bytes 98312 | tf_op jit(solution)/shard_map/ppermute | solution.py:39
  42.2 2.0 %collective-permute-done.5 = f32[32,2,128]{2,1,0:T(2,128)S(1)} collective-permute-done((f32[32,2,128]{2,1,0:T(2,128)S(1)}, f32[32,2,128]{2,1,0:T(2,128)S(1)}, u32[]{:S(2)}, u32[]{:S(2)}) %collective-permute-start.5) | collective-permute-done | bytes 32800 | tf_op jit(solution)/shard_map/ppermute | solution.py:39
  44.2 2.0 %collective-permute-start.6 = (f32[32,2,256]{2,1,0:T(2,128)S(1)}, f32[32,2,256]{2,1,0:T(2,128)S(1)}, u32[]{:S(2)}, u32[]{:S(2)}) collective-permute-start(f32[32,2,256]{2,1,0:T(2,128)S(1)} %maximum_select_fusion.11), channel_id=1, source_target_pairs={{0,8},{1,9},{2,10},{3,11},{4,12},{5,13},{6,14},{7,15},{8,0},{9,1},... | collective-permute-start | bytes 196616 | tf_op jit(solution)/shard_map/ppermute | solution.py:39
  46.3 2.3 %collective-permute-done.6 = f32[32,2,256]{2,1,0:T(2,128)S(1)} collective-permute-done((f32[32,2,256]{2,1,0:T(2,128)S(1)}, f32[32,2,256]{2,1,0:T(2,128)S(1)}, u32[]{:S(2)}, u32[]{:S(2)}) %collective-permute-start.6) | collective-permute-done | bytes 65568 | tf_op jit(solution)/shard_map/ppermute | solution.py:39
  50.2 3.5 %collective-permute-done.7 = f32[32,2,512]{2,1,0:T(2,128)S(1)} collective-permute-done((f32[32,2,512]{2,1,0:T(2,128)S(1)}, f32[32,2,512]{2,1,0:T(2,128)S(1)}, u32[]{:S(2)}, u32[]{:S(2)}) %collective-permute-start.7) | collective-permute-done | bytes 131104 | tf_op jit(solution)/shard_map/ppermute | solution.py:39
  55.4 4.9 %collective-permute-done.8 = f32[32,2,1024]{2,1,0:T(2,128)S(1)} collective-permute-done((f32[32,2,1024]{2,1,0:T(2,128)S(1)}, f32[32,2,1024]{2,1,0:T(2,128)S(1)}, u32[]{:S(2)}, u32[]{:S(2)}) %collective-permute-start.8) | collective-permute-done | bytes 262176 | tf_op jit(solution)/shard_map/ppermute | solution.py:39
  63.7 2.5 %fusion.5 = f32[2,32,128]{2,1,0:T(8,128)S(1)} fusion(f32[2,128,4096]{2,1,0:T(8,128)S(1)} %copy-done, f32[32,2,4096]{2,1,0:T(2,128)S(1)} %maximum_select_fusion), kind=kOutput, calls=%fused_computation.5 | convolution fusion | flops 201326592 | bytes 5275648 | tf_op jit(solution)/shard_map/qmk,mck->qmc/dot_general | solution.py:124
  66.1 2.9 %collective-permute-start.10 = (f32[32,2,128]{2,0,1:T(8,128)S(1)}, f32[32,2,128]{2,0,1:T(8,128)S(1)}, u32[]{:S(2)}, u32[]{:S(2)}) collective-permute-start(f32[32,2,128]{2,0,1:T(8,128)S(1)} %bitcast.47), channel_id=1, source_target_pairs={{0,16},{1,17},{2,18},{3,19},{4,20},{5,21},{6,22},{7,23},{8,24},{9,... | collective-permute-start | bytes 98312 | tf_op jit(solution)/shard_map/ppermute | solution.py:48
  69.0 2.0 %collective-permute-done.10 = f32[32,2,128]{2,0,1:T(8,128)S(1)} collective-permute-done((f32[32,2,128]{2,0,1:T(8,128)S(1)}, f32[32,2,128]{2,0,1:T(8,128)S(1)}, u32[]{:S(2)}, u32[]{:S(2)}) %collective-permute-start.10) | collective-permute-done | bytes 32800 | tf_op jit(solution)/shard_map/ppermute | solution.py:48
  71.0 2.0 %collective-permute-start.11 = (f32[32,2,2,128]{3,0,1,2:T(8,128)S(1)}, f32[32,2,2,128]{3,0,1,2:T(8,128)S(1)}, u32[]{:S(2)}, u32[]{:S(2)}) collective-permute-start(f32[32,2,2,128]{3,0,1,2:T(8,128)S(1)} %maximum_select_fusion.13), channel_id=1, source_target_pairs={{0,8},{1,9},{2,10},{3,11},{4,12},{5,13},{6,14},{7,15},{8,0},{9,1},... | collective-permute-start | bytes 196616 | tf_op jit(solution)/shard_map/ppermute | solution.py:48
  73.1 2.3 %collective-permute-done.11 = f32[32,2,2,128]{3,0,1,2:T(8,128)S(1)} collective-permute-done((f32[32,2,2,128]{3,0,1,2:T(8,128)S(1)}, f32[32,2,2,128]{3,0,1,2:T(8,128)S(1)}, u32[]{:S(2)}, u32[]{:S(2)}) %collective-permute-start.11) | collective-permute-done | bytes 65568 | tf_op jit(solution)/shard_map/ppermute | solution.py:48
  77.0 3.4 %collective-permute-done.12 = f32[32,2,2,2,128]{4,0,1,2,3:T(8,128)S(1)} collective-permute-done((f32[32,2,2,2,128]{4,0,1,2,3:T(8,128)S(1)}, f32[32,2,2,2,128]{4,0,1,2,3:T(8,128)S(1)}, u32[]{:S(2)}, u32[]{:S(2)}) %collective-permute-start.12) | collective-permute-done | bytes 131104 | tf_op jit(solution)/shard_map/ppermute | solution.py:48
  82.0 4.9 %collective-permute-done.13 = f32[32,2,2,2,2,128]{5,0,1,2,3,4:T(8,128)S(1)} collective-permute-done((f32[32,2,2,2,2,128]{5,0,1,2,3,4:T(8,128)S(1)}, f32[32,2,2,2,2,128]{5,0,1,2,3,4:T(8,128)S(1)}, u32[]{:S(2)}, u32[]{:S(2)}) %collective-permute-start.13) | collective-permute-done | bytes 262176 | tf_op jit(solution)/shard_map/ppermute | solution.py:48
  90.7 6.5 %fusion.12 = (f32[32]{0:T(128)S(1)}, f32[32]{0:T(128)S(1)}, f32[32,128]{1,0:T(8,128)S(1)}) fusion(f32[32,2,4096]{2,0,1:T(8,128)S(1)} %select_n.250, f32[128,2,4096]{2,1,0:T(2,128)} %param.15), kind=kOutput, calls=%fused_computation.43 | convolution fusion | flops 201338816 | bytes 5259520 | tf_op jit(solution)/shard_map/qmk,nmk->qn/dot_general | solution.py:125
  99.9 2.1 %collective-permute-done.16 = f32[2,32]{1,0:T(2,128)S(1)} collective-permute-done((f32[2,32]{1,0:T(2,128)S(1)}, f32[2,32]{1,0:T(2,128)S(1)}, u32[]{:S(2)}, u32[]{:S(2)}) %collective-permute-start.16) | collective-permute-done | bytes 288 | tf_op jit(solution)/shard_map/ppermute | solution.py:59
  103.6 2.1 %collective-permute-done.17 = f32[2,32]{1,0:T(2,128)S(1)} collective-permute-done((f32[2,32]{1,0:T(2,128)S(1)}, f32[2,32]{1,0:T(2,128)S(1)}, u32[]{:S(2)}, u32[]{:S(2)}) %collective-permute-start.17) | collective-permute-done | bytes 288 | tf_op jit(solution)/shard_map/ppermute | solution.py:59
  109.3 2.8 %collective-permute-start.19 = (f32[2,32]{1,0:T(2,128)S(1)}, f32[2,32]{1,0:T(2,128)S(1)}, u32[]{:S(2)}, u32[]{:S(2)}) collective-permute-start(f32[2,32]{1,0:T(2,128)S(1)} %add.60), channel_id=1, source_target_pairs={{0,16},{1,17},{2,18},{3,19},{4,20},{5,21},{6,22},{7,23},{8,24},{9,... | collective-permute-start | bytes 776 | tf_op jit(solution)/shard_map/ppermute | solution.py:59
  (66 shorter events, 35.9 us)
Async XLA Ops:
  10.7 2.1 %collective-permute-start = (f32[32,2,2048]{2,1,0:T(2,128)S(1)}, f32[32,2,2048]{2,1,0:T(2,128)S(1)}, u32[]{:S(2)}, u32[]{:S(2)}) collective-permute-start(f32[32,2,2048]{2,1,0:T(2,128)S(1)} %broadcast_select_fusion), channel_id=1, source_target_pairs={{0,1},{1,0},{2,3},{3,2},{4,5},{5,4},{6,7},{7,6},{8,9},{9,8},{10,11... | collective-permute-start | bytes 1572872 | tf_op jit(solution)/shard_map/ppermute | solution.py:36
  14.6 9.5 %collective-permute-start.1 = (f32[32,2,1024]{2,1,0:T(2,128)S(1)}, f32[32,2,1024]{2,1,0:T(2,128)S(1)}, u32[]{:S(2)}, u32[]{:S(2)}) collective-permute-start(f32[32,2,1024]{2,1,0:T(2,128)S(1)} %broadcast_select_fusion.1), channel_id=1, source_target_pairs={{0,2},{1,3},{2,0},{3,1},{4,6},{5,7},{6,4},{7,5},{8,10},{9,11},{10,... | collective-permute-start | bytes 786440 | tf_op jit(solution)/shard_map/ppermute | solution.py:36
  24.4 5.0 %collective-permute-start.2 = (f32[32,2,512]{2,1,0:T(2,128)S(1)}, f32[32,2,512]{2,1,0:T(2,128)S(1)}, u32[]{:S(2)}, u32[]{:S(2)}) collective-permute-start(f32[32,2,512]{2,1,0:T(2,128)S(1)} %broadcast_select_fusion.2), channel_id=1, source_target_pairs={{0,4},{1,5},{2,6},{3,7},{4,0},{5,1},{6,2},{7,3},{8,12},{9,13},{10,... | collective-permute-start | bytes 393224 | tf_op jit(solution)/shard_map/ppermute | solution.py:36
  29.6 4.3 %collective-permute-start.3 = (f32[32,2,256]{2,1,0:T(2,128)S(1)}, f32[32,2,256]{2,1,0:T(2,128)S(1)}, u32[]{:S(2)}, u32[]{:S(2)}) collective-permute-start(f32[32,2,256]{2,1,0:T(2,128)S(1)} %broadcast_select_fusion.3), channel_id=1, source_target_pairs={{0,8},{1,9},{2,10},{3,11},{4,12},{5,13},{6,14},{7,15},{8,0},{9,1},... | collective-permute-start | bytes 196616 | tf_op jit(solution)/shard_map/ppermute | solution.py:36
  31.5 32.2 %copy-start = (f32[2,128,4096]{2,1,0:T(8,128)S(1)}, f32[2,128,4096]{2,1,0:T(8,128)}, u32[]{:S(2)}) copy-start(f32[2,128,4096]{2,1,0:T(8,128)} %param.14) | copy-start | bytes 12582916
  34.0 5.3 %collective-permute-start.4 = (f32[32,2,128]{2,1,0:T(2,128)S(1)}, f32[32,2,128]{2,1,0:T(2,128)S(1)}, u32[]{:S(2)}, u32[]{:S(2)}) collective-permute-start(f32[32,2,128]{2,1,0:T(2,128)S(1)} %broadcast_select_fusion.4), channel_id=1, source_target_pairs={{0,16},{1,17},{2,18},{3,19},{4,20},{5,21},{6,22},{7,23},{8,24},{9,... | collective-permute-start | bytes 98312 | tf_op jit(solution)/shard_map/ppermute | solution.py:36
  39.3 4.9 %collective-permute-start.5 = (f32[32,2,128]{2,1,0:T(2,128)S(1)}, f32[32,2,128]{2,1,0:T(2,128)S(1)}, u32[]{:S(2)}, u32[]{:S(2)}) collective-permute-start(f32[32,2,128]{2,1,0:T(2,128)S(1)} %select_add_fusion.4), channel_id=1, source_target_pairs={{0,16},{1,17},{2,18},{3,19},{4,20},{5,21},{6,22},{7,23},{8,24},{9,... | collective-permute-start | bytes 98312 | tf_op jit(solution)/shard_map/ppermute | solution.py:39
  44.2 4.3 %collective-permute-start.6 = (f32[32,2,256]{2,1,0:T(2,128)S(1)}, f32[32,2,256]{2,1,0:T(2,128)S(1)}, u32[]{:S(2)}, u32[]{:S(2)}) collective-permute-start(f32[32,2,256]{2,1,0:T(2,128)S(1)} %maximum_select_fusion.11), channel_id=1, source_target_pairs={{0,8},{1,9},{2,10},{3,11},{4,12},{5,13},{6,14},{7,15},{8,0},{9,1},... | collective-permute-start | bytes 196616 | tf_op jit(solution)/shard_map/ppermute | solution.py:39
  48.6 5.0 %collective-permute-start.7 = (f32[32,2,512]{2,1,0:T(2,128)S(1)}, f32[32,2,512]{2,1,0:T(2,128)S(1)}, u32[]{:S(2)}, u32[]{:S(2)}) collective-permute-start(f32[32,2,512]{2,1,0:T(2,128)S(1)} %maximum_select_fusion.8), channel_id=1, source_target_pairs={{0,4},{1,5},{2,6},{3,7},{4,0},{5,1},{6,2},{7,3},{8,12},{9,13},{10,... | collective-permute-start | bytes 393224 | tf_op jit(solution)/shard_map/ppermute | solution.py:39
  53.9 6.4 %collective-permute-start.8 = (f32[32,2,1024]{2,1,0:T(2,128)S(1)}, f32[32,2,1024]{2,1,0:T(2,128)S(1)}, u32[]{:S(2)}, u32[]{:S(2)}) collective-permute-start(f32[32,2,1024]{2,1,0:T(2,128)S(1)} %maximum_select_fusion.5), channel_id=1, source_target_pairs={{0,2},{1,3},{2,0},{3,1},{4,6},{5,7},{6,4},{7,5},{8,10},{9,11},{10,... | collective-permute-start | bytes 786440 | tf_op jit(solution)/shard_map/ppermute | solution.py:39
  60.7 2.0 %collective-permute-start.9 = (f32[32,2,2048]{2,1,0:T(2,128)S(1)}, f32[32,2,2048]{2,1,0:T(2,128)S(1)}, u32[]{:S(2)}, u32[]{:S(2)}) collective-permute-start(f32[32,2,2048]{2,1,0:T(2,128)S(1)} %maximum_select_fusion.2), channel_id=1, source_target_pairs={{0,1},{1,0},{2,3},{3,2},{4,5},{5,4},{6,7},{7,6},{8,9},{9,8},{10,11... | collective-permute-start | bytes 1572872 | tf_op jit(solution)/shard_map/ppermute | solution.py:39
  66.1 4.9 %collective-permute-start.10 = (f32[32,2,128]{2,0,1:T(8,128)S(1)}, f32[32,2,128]{2,0,1:T(8,128)S(1)}, u32[]{:S(2)}, u32[]{:S(2)}) collective-permute-start(f32[32,2,128]{2,0,1:T(8,128)S(1)} %bitcast.47), channel_id=1, source_target_pairs={{0,16},{1,17},{2,18},{3,19},{4,20},{5,21},{6,22},{7,23},{8,24},{9,... | collective-permute-start | bytes 98312 | tf_op jit(solution)/shard_map/ppermute | solution.py:48
  71.0 4.3 %collective-permute-start.11 = (f32[32,2,2,128]{3,0,1,2:T(8,128)S(1)}, f32[32,2,2,128]{3,0,1,2:T(8,128)S(1)}, u32[]{:S(2)}, u32[]{:S(2)}) collective-permute-start(f32[32,2,2,128]{3,0,1,2:T(8,128)S(1)} %maximum_select_fusion.13), channel_id=1, source_target_pairs={{0,8},{1,9},{2,10},{3,11},{4,12},{5,13},{6,14},{7,15},{8,0},{9,1},... | collective-permute-start | bytes 196616 | tf_op jit(solution)/shard_map/ppermute | solution.py:48
  75.4 5.0 %collective-permute-start.12 = (f32[32,2,2,2,128]{4,0,1,2,3:T(8,128)S(1)}, f32[32,2,2,2,128]{4,0,1,2,3:T(8,128)S(1)}, u32[]{:S(2)}, u32[]{:S(2)}) collective-permute-start(f32[32,2,2,2,128]{4,0,1,2,3:T(8,128)S(1)} %maximum_select_fusion.10), channel_id=1, source_target_pairs={{0,4},{1,5},{2,6},{3,7},{4,0},{5,1},{6,2},{7,3},{8,12},{9,13},{10,... | collective-permute-start | bytes 393224 | tf_op jit(solution)/shard_map/ppermute | solution.py:48
  80.4 6.4 %collective-permute-start.13 = (f32[32,2,2,2,2,128]{5,0,1,2,3,4:T(8,128)S(1)}, f32[32,2,2,2,2,128]{5,0,1,2,3,4:T(8,128)S(1)}, u32[]{:S(2)}, u32[]{:S(2)}) collective-permute-start(f32[32,2,2,2,2,128]{5,0,1,2,3,4:T(8,128)S(1)} %maximum_select_fusion.7), channel_id=1, source_target_pairs={{0,2},{1,3},{2,0},{3,1},{4,6},{5,7},{6,4},{7,5},{8,10},{9,11},{10,... | collective-permute-start | bytes 786440 | tf_op jit(solution)/shard_map/ppermute | solution.py:48
  86.9 2.0 %collective-permute-start.14 = (f32[32,2,2,2,2,2,128]{6,0,1,2,3,4,5:T(8,128)S(1)}, f32[32,2,2,2,2,2,128]{6,0,1,2,3,4,5:T(8,128)S(1)}, u32[]{:S(2)}, u32[]{:S(2)}) collective-permute-start(f32[32,2,2,2,2,2,128]{6,0,1,2,3,4,5:T(8,128)S(1)} %maximum_select_fusion.4), channel_id=1, source_target_pairs={{0,1},{1,0},{2,3},{3,2},{4,5},{5,4},{6,7},{7,6},{8,9},{9,8},{10,11... | collective-permute-start | bytes 1572872 | tf_op jit(solution)/shard_map/ppermute | solution.py:48
  97.2 1.2 %collective-permute-start.15 = (f32[2,32]{1,0:T(2,128)S(1)}, f32[2,32]{1,0:T(2,128)S(1)}, u32[]{:S(2)}, u32[]{:S(2)}) collective-permute-start(f32[2,32]{1,0:T(2,128)S(1)} %pad_maximum_fusion), channel_id=1, source_target_pairs={{0,1},{1,0},{2,3},{3,2},{4,5},{5,4},{6,7},{7,6},{8,9},{9,8},{10,11... | collective-permute-start | bytes 776 | tf_op jit(solution)/shard_map/ppermute | solution.py:59
  98.4 3.6 %collective-permute-start.16 = (f32[2,32]{1,0:T(2,128)S(1)}, f32[2,32]{1,0:T(2,128)S(1)}, u32[]{:S(2)}, u32[]{:S(2)}) collective-permute-start(f32[2,32]{1,0:T(2,128)S(1)} %fusion.11), channel_id=1, source_target_pairs={{0,2},{1,3},{2,0},{3,1},{4,6},{5,7},{6,4},{7,5},{8,10},{9,11},{10,... | collective-permute-start | bytes 776 | tf_op jit(solution)/shard_map/ppermute | solution.py:59
  102.1 3.6 %collective-permute-start.17 = (f32[2,32]{1,0:T(2,128)S(1)}, f32[2,32]{1,0:T(2,128)S(1)}, u32[]{:S(2)}, u32[]{:S(2)}) collective-permute-start(f32[2,32]{1,0:T(2,128)S(1)} %fusion.15), channel_id=1, source_target_pairs={{0,4},{1,5},{2,6},{3,7},{4,0},{5,1},{6,2},{7,3},{8,12},{9,13},{10,... | collective-permute-start | bytes 776 | tf_op jit(solution)/shard_map/ppermute | solution.py:59
  105.7 3.6 %collective-permute-start.18 = (f32[2,32]{1,0:T(2,128)S(1)}, f32[2,32]{1,0:T(2,128)S(1)}, u32[]{:S(2)}, u32[]{:S(2)}) collective-permute-start(f32[2,32]{1,0:T(2,128)S(1)} %add.59), channel_id=1, source_target_pairs={{0,8},{1,9},{2,10},{3,11},{4,12},{5,13},{6,14},{7,15},{8,0},{9,1},... | collective-permute-start | bytes 776 | tf_op jit(solution)/shard_map/ppermute | solution.py:59
  109.3 4.5 %collective-permute-start.19 = (f32[2,32]{1,0:T(2,128)S(1)}, f32[2,32]{1,0:T(2,128)S(1)}, u32[]{:S(2)}, u32[]{:S(2)}) collective-permute-start(f32[2,32]{1,0:T(2,128)S(1)} %add.60), channel_id=1, source_target_pairs={{0,16},{1,17},{2,18},{3,19},{4,20},{5,21},{6,22},{7,23},{8,24},{9,... | collective-permute-start | bytes 776 | tf_op jit(solution)/shard_map/ppermute | solution.py:59

commit v5 on v4

--- a/solution.py
+++ b/solution.py
@@ -52,6 +52,17 @@
 
 def _bf16_round(x):
     return lax.reduce_precision(x, exponent_bits=8, mantissa_bits=7)
+
+
+def _split(x):
+    high = _bf16_round(x)
+    return high.astype(jnp.bfloat16), (x - high).astype(jnp.bfloat16)
+
+
+def _dot3(spec, x, y_high, y_low):
+    x_high, x_low = _split(x)
+    f = lambda a, b: jnp.einsum(spec, a, b, preferred_element_type=jnp.float32)
+    return f(x_high, y_high) + (f(x_low, y_high) + f(x_high, y_low))
 
 
 def _butterfly_sum(x, size):
@@ -121,13 +132,8 @@
     ).astype(jnp.bfloat16)
     partial_value = _module_sums(acts, grads_out, proj_in, proj_out, selector_t)
     summed = _allreduce(partial_value, size, 2)
-    precond_cols = jnp.einsum("qmk,mck->qmc", summed, fisher_inv, precision=lax.Precision.HIGH)
-    scores = jnp.einsum(
-        "qmk,nmk->qn",
-        _allgather(precond_cols, size),
-        database,
-        precision=lax.Precision.HIGH,
-    )
+    precond_cols = _dot3("qmk,mck->qmc", summed, *_split(fisher_inv))
+    scores = _dot3("qmk,nmk->qn", _allgather(precond_cols, size), *_split(database))
     db_count = database.shape[0] * size
     moments = _butterfly_sum(
         jnp.stack([jnp.sum(scores, axis=1), jnp.sum(scores * scores, axis=1)]), size

time: 115 us -> 120 us (1.043)
  other arithmetic: 8.05 us -> 13.7 us
  local copies, waits for them, and re-layouts: 2.39 us -> 4.91 us
  waiting for transfers between devices: 53.4 us -> 51.4 us
  matrix products: 8.94 us -> 7.66 us
    convert_element_type x0 -> x3, other arithmetic: none -> 7.66 us  [_split(): return (high.astype(jnp.bfloat16), (x - high).astype(jnp.bfloat16))]
    select_n x2, local copies, waits for them, and re-layouts: 1.65 us -> 3.85 us  [_allgather(): jnp.where(low, jnp.stack([cur, other], -2), jnp.stack([other, cur], -2))]
    ppermute x5, waiting for transfers between devices: 14.5 us -> 12.6 us  [_allgather(): other = lax.ppermute(cur, 'rows', _xor_pairs(size, s))]
    dot_general x2 -> x6, matrix products: 8.94 us -> 7.66 us  [_dot3(): f = lambda a, b: jnp.einsum(spec, a, b, preferred_element_type=jnp.float32)]
    add x5, other arithmetic: 2.08 us -> 0.88 us  [_allreduce(): cur = keep + lax.ppermute(send, 'rows', _xor_pairs(size, s))]
  transfers between devices with their start and end apart: 20 -> 20, of which waited for: 20 -> 19; matrix products, arithmetic and copies ran while one was open for 0% -> 5% of each run, Pallas kernels for 0% -> 0%
where the time goes in v5:
time: 120 us
  waiting for transfers between devices  51.4 us (43%)
  starting transfers between devices  34.9 us (29%)
  other arithmetic  13.7 us (11%)
  matrix products  7.66 us (6%)
  Pallas kernels  6.9 us (6%)
  local copies, waits for them, and re-layouts  4.91 us (4%)
    ppermute x5, waiting for transfers between devices, _allreduce(): cur = keep + lax.ppermute(send, 'rows', _xor_pairs(size, s))  15.8 us
    ppermute x5, waiting for transfers between devices, _allreduce(): cur = _join(cur, lax.ppermute(cur, 'rows', _xor_pairs(size, s)), low, axis)  14.6 us
    ppermute x5, waiting for transfers between devices, _allgather(): other = lax.ppermute(cur, 'rows', _xor_pairs(size, s))  12.6 us
    ppermute x5, starting transfers between devices, _allreduce(): cur = keep + lax.ppermute(send, 'rows', _xor_pairs(size, s))  10.4 us
    ppermute x5, starting transfers between devices, _butterfly_sum(): x = x + lax.ppermute(x, 'rows', _xor_pairs(size, s))  8.38 us
    ppermute x5, waiting for transfers between devices, _butterfly_sum(): x = x + lax.ppermute(x, 'rows', _xor_pairs(size, s))  8.31 us
    ppermute x5, starting transfers between devices, _allreduce(): cur = _join(cur, lax.ppermute(cur, 'rows', _xor_pairs(size, s)), low, axis)  8.03 us
    ppermute x5, starting transfers between devices, _allgather(): other = lax.ppermute(cur, 'rows', _xor_pairs(size, s))  8.02 us
  transfers between devices with their start and end apart: 20, of which 19 were waited for; matrix products, arithmetic and copies ran while one was open for 5% of the time, Pallas kernels for 0%

profile of v5, /device:TPU:0, one launch (start us, length us, event | category | flops | bytes accessed | tf_op | source)
XLA Modules:
  0.0 119.6 jit_solution(7592108982290807650)
XLA Ops:
  2.3 6.9 %shard_map.82 = f32[32,2,4096]{2,1,0:T(2,128)} custom-call(bf16[128,2,4096]{2,1,0:T(2,128)(2,1)} %acts_ref.1, bf16[128,2,4096]{2,1,0:T(2,128)(2,1)} %gout_ref.1, bf16[4096,128]{1,0:T(8,128)(2,1)} %pin_ref.1, bf16[4096,128]{1,0:T(8,128)(2,1)} %pout_ref.1, bf16[32,128]{1,0:T(8,128)(2,1)} %fusion.41.sel_ref), custom_call_target="tpu_custom_call" | custom-call | tf_op jit(solution)/shard_map/pallas_call | solution.py:110
  13.5 2.9 %collective-permute-start.1 = (f32[32,2,1024]{2,1,0:T(2,128)S(1)}, f32[32,2,1024]{2,1,0:T(2,128)S(1)}, u32[]{:S(2)}, u32[]{:S(2)}) collective-permute-start(f32[32,2,1024]{2,1,0:T(2,128)S(1)} %broadcast_select_fusion.1), channel_id=1, source_target_pairs={{0,2},{1,3},{2,0},{3,1},{4,6},{5,7},{6,4},{7,5},{8,10},{9,11},{10,... | collective-permute-start | bytes 786440 | tf_op jit(solution)/shard_map/ppermute | solution.py:36
  16.4 6.6 %collective-permute-done.1 = f32[32,2,1024]{2,1,0:T(2,128)S(1)} collective-permute-done((f32[32,2,1024]{2,1,0:T(2,128)S(1)}, f32[32,2,1024]{2,1,0:T(2,128)S(1)}, u32[]{:S(2)}, u32[]{:S(2)}) %collective-permute-start.1) | collective-permute-done | bytes 262176 | tf_op jit(solution)/shard_map/ppermute | solution.py:36
  25.2 3.2 %collective-permute-done.2 = f32[32,2,512]{2,1,0:T(2,128)S(1)} collective-permute-done((f32[32,2,512]{2,1,0:T(2,128)S(1)}, f32[32,2,512]{2,1,0:T(2,128)S(1)}, u32[]{:S(2)}, u32[]{:S(2)}) %collective-permute-start.2) | collective-permute-done | bytes 131104 | tf_op jit(solution)/shard_map/ppermute | solution.py:36
  30.4 2.4 %collective-permute-done.3 = f32[32,2,256]{2,1,0:T(2,128)S(1)} collective-permute-done((f32[32,2,256]{2,1,0:T(2,128)S(1)}, f32[32,2,256]{2,1,0:T(2,128)S(1)}, u32[]{:S(2)}, u32[]{:S(2)}) %collective-permute-start.3) | collective-permute-done | bytes 65568 | tf_op jit(solution)/shard_map/ppermute | solution.py:36
  32.9 3.3 %collective-permute-start.4 = (f32[32,2,128]{2,1,0:T(2,128)S(1)}, f32[32,2,128]{2,1,0:T(2,128)S(1)}, u32[]{:S(2)}, u32[]{:S(2)}) collective-permute-start(f32[32,2,128]{2,1,0:T(2,128)S(1)} %broadcast_select_fusion.4), channel_id=1, source_target_pairs={{0,16},{1,17},{2,18},{3,19},{4,20},{5,21},{6,22},{7,23},{8,24},{9,... | collective-permute-start | bytes 98312 | tf_op jit(solution)/shard_map/ppermute | solution.py:36
  36.2 2.0 %collective-permute-done.4 = f32[32,2,128]{2,1,0:T(2,128)S(1)} collective-permute-done((f32[32,2,128]{2,1,0:T(2,128)S(1)}, f32[32,2,128]{2,1,0:T(2,128)S(1)}, u32[]{:S(2)}, u32[]{:S(2)}) %collective-permute-start.4) | collective-permute-done | bytes 32800 | tf_op jit(solution)/shard_map/ppermute | solution.py:36
  38.2 2.9 %collective-permute-start.5 = (f32[32,2,128]{2,1,0:T(2,128)S(1)}, f32[32,2,128]{2,1,0:T(2,128)S(1)}, u32[]{:S(2)}, u32[]{:S(2)}) collective-permute-start(f32[32,2,128]{2,1,0:T(2,128)S(1)} %select_add_fusion.4), channel_id=1, source_target_pairs={{0,16},{1,17},{2,18},{3,19},{4,20},{5,21},{6,22},{7,23},{8,24},{9,... | collective-permute-start | bytes 98312 | tf_op jit(solution)/shard_map/ppermute | solution.py:39
  41.1 2.0 %collective-permute-done.5 = f32[32,2,128]{2,1,0:T(2,128)S(1)} collective-permute-done((f32[32,2,128]{2,1,0:T(2,128)S(1)}, f32[32,2,128]{2,1,0:T(2,128)S(1)}, u32[]{:S(2)}, u32[]{:S(2)}) %collective-permute-start.5) | collective-permute-done | bytes 32800 | tf_op jit(solution)/shard_map/ppermute | solution.py:39
  43.1 2.0 %collective-permute-start.6 = (f32[32,2,256]{2,1,0:T(2,128)S(1)}, f32[32,2,256]{2,1,0:T(2,128)S(1)}, u32[]{:S(2)}, u32[]{:S(2)}) collective-permute-start(f32[32,2,256]{2,1,0:T(2,128)S(1)} %maximum_select_fusion.11), channel_id=1, source_target_pairs={{0,8},{1,9},{2,10},{3,11},{4,12},{5,13},{6,14},{7,15},{8,0},{9,1},... | collective-permute-start | bytes 196616 | tf_op jit(solution)/shard_map/ppermute | solution.py:39
  45.2 2.3 %collective-permute-done.6 = f32[32,2,256]{2,1,0:T(2,128)S(1)} collective-permute-done((f32[32,2,256]{2,1,0:T(2,128)S(1)}, f32[32,2,256]{2,1,0:T(2,128)S(1)}, u32[]{:S(2)}, u32[]{:S(2)}) %collective-permute-start.6) | collective-permute-done | bytes 65568 | tf_op jit(solution)/shard_map/ppermute | solution.py:39
  49.1 3.5 %collective-permute-done.7 = f32[32,2,512]{2,1,0:T(2,128)S(1)} collective-permute-done((f32[32,2,512]{2,1,0:T(2,128)S(1)}, f32[32,2,512]{2,1,0:T(2,128)S(1)}, u32[]{:S(2)}, u32[]{:S(2)}) %collective-permute-start.7) | collective-permute-done | bytes 131104 | tf_op jit(solution)/shard_map/ppermute | solution.py:39
  54.3 4.9 %collective-permute-done.8 = f32[32,2,1024]{2,1,0:T(2,128)S(1)} collective-permute-done((f32[32,2,1024]{2,1,0:T(2,128)S(1)}, f32[32,2,1024]{2,1,0:T(2,128)S(1)}, u32[]{:S(2)}, u32[]{:S(2)}) %collective-permute-start.8) | collective-permute-done | bytes 262176 | tf_op jit(solution)/shard_map/ppermute | solution.py:39
  65.9 2.9 %collective-permute-start.10 = (f32[32,2,128]{2,0,1:T(8,128)S(1)}, f32[32,2,128]{2,0,1:T(8,128)S(1)}, u32[]{:S(2)}, u32[]{:S(2)}) collective-permute-start(f32[32,2,128]{2,0,1:T(8,128)S(1)} %fusion.16), channel_id=1, source_target_pairs={{0,16},{1,17},{2,18},{3,19},{4,20},{5,21},{6,22},{7,23},{8,24},{9,... | collective-permute-start | bytes 98312 | tf_op jit(solution)/shard_map/ppermute | solution.py:48
  68.8 2.0 %collective-permute-done.10 = f32[32,2,128]{2,0,1:T(8,128)S(1)} collective-permute-done((f32[32,2,128]{2,0,1:T(8,128)S(1)}, f32[32,2,128]{2,0,1:T(8,128)S(1)}, u32[]{:S(2)}, u32[]{:S(2)}) %collective-permute-start.10) | collective-permute-done | bytes 32800 | tf_op jit(solution)/shard_map/ppermute | solution.py:48
  72.8 2.3 %collective-permute-done.11 = f32[32,2,2,128]{3,0,1,2:T(8,128)S(1)} collective-permute-done((f32[32,2,2,128]{3,0,1,2:T(8,128)S(1)}, f32[32,2,2,128]{3,0,1,2:T(8,128)S(1)}, u32[]{:S(2)}, u32[]{:S(2)}) %collective-permute-start.11) | collective-permute-done | bytes 65568 | tf_op jit(solution)/shard_map/ppermute | solution.py:48
  76.7 3.5 %collective-permute-done.12 = f32[32,2,2,2,128]{4,0,1,2,3:T(8,128)S(1)} collective-permute-done((f32[32,2,2,2,128]{4,0,1,2,3:T(8,128)S(1)}, f32[32,2,2,2,128]{4,0,1,2,3:T(8,128)S(1)}, u32[]{:S(2)}, u32[]{:S(2)}) %collective-permute-start.12) | collective-permute-done | bytes 131104 | tf_op jit(solution)/shard_map/ppermute | solution.py:48
  81.8 4.9 %collective-permute-done.13 = f32[32,2,2,2,2,128]{5,0,1,2,3,4:T(8,128)S(1)} collective-permute-done((f32[32,2,2,2,2,128]{5,0,1,2,3,4:T(8,128)S(1)}, f32[32,2,2,2,2,128]{5,0,1,2,3,4:T(8,128)S(1)}, u32[]{:S(2)}, u32[]{:S(2)}) %collective-permute-start.13) | collective-permute-done | bytes 262176 | tf_op jit(solution)/shard_map/ppermute | solution.py:48
  86.8 6.0 %fusion = (bf16[128,2,4096]{2,1,0:T(2,128)(2,1)}, bf16[128,2,4096]{2,1,0:T(2,128)(2,1)S(1)}) fusion(f32[128,2,4096]{2,1,0:T(2,128)S(1)} %copy-done.3), kind=kLoop, calls=%fused_computation.4 | loop fusion | flops 4194304 | bytes 8388608 | tf_op jit(solution)/shard_map/convert_element_type | solution.py:59
  94.7 2.1 %select_n.250 = f32[32,2,4096]{2,0,1:T(8,128)S(1)} reshape(f32[32,2,2,2,2,2,2,128]{7,6,5,4,3,2,0,1:T(2,128)} %copy.36) | data formatting | bytes 2097152 | tf_op jit(solution)/shard_map/jit(_where)/select_n | solution.py:49
  99.7 2.5 %fusion.45 = (f32[32]{0:T(128)S(1)}, f32[32]{0:T(128)S(1)}, f32[32,128]{1,0:T(8,128)S(1)}) fusion(f32[32,128]{1,0:T(8,128)S(1)} %fusion.19, f32[32,128]{1,0:T(8,128)S(1)} %fusion.22, bf16[128,2,4096]{2,1,0:T(2,128)(2,1)S(1)} %copy-done.2, f32[32,2,4096]{2,0,1:T(8,128)S(1)} %select_n.250), kind=kOutput, calls=%fused_computation.70 | convolution fusion | flops 67653568 | bytes 3195136 | tf_op jit(solution)/shard_map/qmk,nmk->qn/dot_general | solution.py:64
  105.1 2.1 %collective-permute-done.16 = f32[2,32]{1,0:T(2,128)S(1)} collective-permute-done((f32[2,32]{1,0:T(2,128)S(1)}, f32[2,32]{1,0:T(2,128)S(1)}, u32[]{:S(2)}, u32[]{:S(2)}) %collective-permute-start.16) | collective-permute-done | bytes 288 | tf_op jit(solution)/shard_map/ppermute | solution.py:70
  108.8 2.1 %collective-permute-done.17 = f32[2,32]{1,0:T(2,128)S(1)} collective-permute-done((f32[2,32]{1,0:T(2,128)S(1)}, f32[2,32]{1,0:T(2,128)S(1)}, u32[]{:S(2)}, u32[]{:S(2)}) %collective-permute-start.17) | collective-permute-done | bytes 288 | tf_op jit(solution)/shard_map/ppermute | solution.py:70
  114.5 2.8 %collective-permute-start.19 = (f32[2,32]{1,0:T(2,128)S(1)}, f32[2,32]{1,0:T(2,128)S(1)}, u32[]{:S(2)}, u32[]{:S(2)}) collective-permute-start(f32[2,32]{1,0:T(2,128)S(1)} %add.76), channel_id=1, source_target_pairs={{0,16},{1,17},{2,18},{3,19},{4,20},{5,21},{6,22},{7,23},{8,24},{9,... | collective-permute-start | bytes 776 | tf_op jit(solution)/shard_map/ppermute | solution.py:70
  (78 shorter events, 41.4 us)
Async XLA Ops:
  9.2 3.7 %copy-start.1 = (f32[32,2,4096]{2,1,0:T(2,128)S(1)}, f32[32,2,4096]{2,1,0:T(2,128)}, u32[]{:S(2)}) copy-start(f32[32,2,4096]{2,1,0:T(2,128)} %shard_map.82) | copy-start | bytes 3145732
  10.8 2.1 %collective-permute-start = (f32[32,2,2048]{2,1,0:T(2,128)S(1)}, f32[32,2,2048]{2,1,0:T(2,128)S(1)}, u32[]{:S(2)}, u32[]{:S(2)}) collective-permute-start(f32[32,2,2048]{2,1,0:T(2,128)S(1)} %broadcast_select_fusion), channel_id=1, source_target_pairs={{0,1},{1,0},{2,3},{3,2},{4,5},{5,4},{6,7},{7,6},{8,9},{9,8},{10,11... | collective-permute-start | bytes 1572872 | tf_op jit(solution)/shard_map/ppermute | solution.py:36
  13.5 9.5 %collective-permute-start.1 = (f32[32,2,1024]{2,1,0:T(2,128)S(1)}, f32[32,2,1024]{2,1,0:T(2,128)S(1)}, u32[]{:S(2)}, u32[]{:S(2)}) collective-permute-start(f32[32,2,1024]{2,1,0:T(2,128)S(1)} %broadcast_select_fusion.1), channel_id=1, source_target_pairs={{0,2},{1,3},{2,0},{3,1},{4,6},{5,7},{6,4},{7,5},{8,10},{9,11},{10,... | collective-permute-start | bytes 786440 | tf_op jit(solution)/shard_map/ppermute | solution.py:36
  23.3 5.0 %collective-permute-start.2 = (f32[32,2,512]{2,1,0:T(2,128)S(1)}, f32[32,2,512]{2,1,0:T(2,128)S(1)}, u32[]{:S(2)}, u32[]{:S(2)}) collective-permute-start(f32[32,2,512]{2,1,0:T(2,128)S(1)} %broadcast_select_fusion.2), channel_id=1, source_target_pairs={{0,4},{1,5},{2,6},{3,7},{4,0},{5,1},{6,2},{7,3},{8,12},{9,13},{10,... | collective-permute-start | bytes 393224 | tf_op jit(solution)/shard_map/ppermute | solution.py:36
  28.5 4.3 %collective-permute-start.3 = (f32[32,2,256]{2,1,0:T(2,128)S(1)}, f32[32,2,256]{2,1,0:T(2,128)S(1)}, u32[]{:S(2)}, u32[]{:S(2)}) collective-permute-start(f32[32,2,256]{2,1,0:T(2,128)S(1)} %broadcast_select_fusion.3), channel_id=1, source_target_pairs={{0,8},{1,9},{2,10},{3,11},{4,12},{5,13},{6,14},{7,15},{8,0},{9,1},... | collective-permute-start | bytes 196616 | tf_op jit(solution)/shard_map/ppermute | solution.py:36
  32.9 5.3 %collective-permute-start.4 = (f32[32,2,128]{2,1,0:T(2,128)S(1)}, f32[32,2,128]{2,1,0:T(2,128)S(1)}, u32[]{:S(2)}, u32[]{:S(2)}) collective-permute-start(f32[32,2,128]{2,1,0:T(2,128)S(1)} %broadcast_select_fusion.4), channel_id=1, source_target_pairs={{0,16},{1,17},{2,18},{3,19},{4,20},{5,21},{6,22},{7,23},{8,24},{9,... | collective-permute-start | bytes 98312 | tf_op jit(solution)/shard_map/ppermute | solution.py:36
  38.2 4.9 %collective-permute-start.5 = (f32[32,2,128]{2,1,0:T(2,128)S(1)}, f32[32,2,128]{2,1,0:T(2,128)S(1)}, u32[]{:S(2)}, u32[]{:S(2)}) collective-permute-start(f32[32,2,128]{2,1,0:T(2,128)S(1)} %select_add_fusion.4), channel_id=1, source_target_pairs={{0,16},{1,17},{2,18},{3,19},{4,20},{5,21},{6,22},{7,23},{8,24},{9,... | collective-permute-start | bytes 98312 | tf_op jit(solution)/shard_map/ppermute | solution.py:39
  43.1 4.3 %collective-permute-start.6 = (f32[32,2,256]{2,1,0:T(2,128)S(1)}, f32[32,2,256]{2,1,0:T(2,128)S(1)}, u32[]{:S(2)}, u32[]{:S(2)}) collective-permute-start(f32[32,2,256]{2,1,0:T(2,128)S(1)} %maximum_select_fusion.11), channel_id=1, source_target_pairs={{0,8},{1,9},{2,10},{3,11},{4,12},{5,13},{6,14},{7,15},{8,0},{9,1},... | collective-permute-start | bytes 196616 | tf_op jit(solution)/shard_map/ppermute | solution.py:39
  47.5 5.0 %collective-permute-start.7 = (f32[32,2,512]{2,1,0:T(2,128)S(1)}, f32[32,2,512]{2,1,0:T(2,128)S(1)}, u32[]{:S(2)}, u32[]{:S(2)}) collective-permute-start(f32[32,2,512]{2,1,0:T(2,128)S(1)} %maximum_select_fusion.8), channel_id=1, source_target_pairs={{0,4},{1,5},{2,6},{3,7},{4,0},{5,1},{6,2},{7,3},{8,12},{9,13},{10,... | collective-permute-start | bytes 393224 | tf_op jit(solution)/shard_map/ppermute | solution.py:39
  52.8 6.4 %collective-permute-start.8 = (f32[32,2,1024]{2,1,0:T(2,128)S(1)}, f32[32,2,1024]{2,1,0:T(2,128)S(1)}, u32[]{:S(2)}, u32[]{:S(2)}) collective-permute-start(f32[32,2,1024]{2,1,0:T(2,128)S(1)} %maximum_select_fusion.5), channel_id=1, source_target_pairs={{0,2},{1,3},{2,0},{3,1},{4,6},{5,7},{6,4},{7,5},{8,10},{9,11},{10,... | collective-permute-start | bytes 786440 | tf_op jit(solution)/shard_map/ppermute | solution.py:39
  59.6 3.7 %copy-start = (f32[2,128,4096]{2,1,0:T(8,128)S(1)}, f32[2,128,4096]{2,1,0:T(8,128)}, u32[]{:S(2)}) copy-start(f32[2,128,4096]{2,1,0:T(8,128)} %param.14) | copy-start | bytes 12582916
  59.6 2.0 %collective-permute-start.9 = (f32[32,2,2048]{2,1,0:T(2,128)S(1)}, f32[32,2,2048]{2,1,0:T(2,128)S(1)}, u32[]{:S(2)}, u32[]{:S(2)}) collective-permute-start(f32[32,2,2048]{2,1,0:T(2,128)S(1)} %maximum_select_fusion.2), channel_id=1, source_target_pairs={{0,1},{1,0},{2,3},{3,2},{4,5},{5,4},{6,7},{7,6},{8,9},{9,8},{10,11... | collective-permute-start | bytes 1572872 | tf_op jit(solution)/shard_map/ppermute | solution.py:39
  65.0 21.8 %copy-start.3 = (f32[128,2,4096]{2,1,0:T(2,128)S(1)}, f32[128,2,4096]{2,1,0:T(2,128)}, u32[]{:S(2)}) copy-start(f32[128,2,4096]{2,1,0:T(2,128)} %param.15) | copy-start | bytes 12582916
  65.9 4.9 %collective-permute-start.10 = (f32[32,2,128]{2,0,1:T(8,128)S(1)}, f32[32,2,128]{2,0,1:T(8,128)S(1)}, u32[]{:S(2)}, u32[]{:S(2)}) collective-permute-start(f32[32,2,128]{2,0,1:T(8,128)S(1)} %fusion.16), channel_id=1, source_target_pairs={{0,16},{1,17},{2,18},{3,19},{4,20},{5,21},{6,22},{7,23},{8,24},{9,... | collective-permute-start | bytes 98312 | tf_op jit(solution)/shard_map/ppermute | solution.py:48
  70.8 4.3 %collective-permute-start.11 = (f32[32,2,2,128]{3,0,1,2:T(8,128)S(1)}, f32[32,2,2,128]{3,0,1,2:T(8,128)S(1)}, u32[]{:S(2)}, u32[]{:S(2)}) collective-permute-start(f32[32,2,2,128]{3,0,1,2:T(8,128)S(1)} %maximum_select_fusion.13), channel_id=1, source_target_pairs={{0,8},{1,9},{2,10},{3,11},{4,12},{5,13},{6,14},{7,15},{8,0},{9,1},... | collective-permute-start | bytes 196616 | tf_op jit(solution)/shard_map/ppermute | solution.py:48
  75.1 5.0 %collective-permute-start.12 = (f32[32,2,2,2,128]{4,0,1,2,3:T(8,128)S(1)}, f32[32,2,2,2,128]{4,0,1,2,3:T(8,128)S(1)}, u32[]{:S(2)}, u32[]{:S(2)}) collective-permute-start(f32[32,2,2,2,128]{4,0,1,2,3:T(8,128)S(1)} %maximum_select_fusion.10), channel_id=1, source_target_pairs={{0,4},{1,5},{2,6},{3,7},{4,0},{5,1},{6,2},{7,3},{8,12},{9,13},{10,... | collective-permute-start | bytes 393224 | tf_op jit(solution)/shard_map/ppermute | solution.py:48
  80.2 6.4 %collective-permute-start.13 = (f32[32,2,2,2,2,128]{5,0,1,2,3,4:T(8,128)S(1)}, f32[32,2,2,2,2,128]{5,0,1,2,3,4:T(8,128)S(1)}, u32[]{:S(2)}, u32[]{:S(2)}) collective-permute-start(f32[32,2,2,2,2,128]{5,0,1,2,3,4:T(8,128)S(1)} %maximum_select_fusion.7), channel_id=1, source_target_pairs={{0,2},{1,3},{2,0},{3,1},{4,6},{5,7},{6,4},{7,5},{8,10},{9,11},{10,... | collective-permute-start | bytes 786440 | tf_op jit(solution)/shard_map/ppermute | solution.py:48
  86.7 6.2 %collective-permute-start.14 = (f32[32,2,2,2,2,2,128]{6,0,1,2,3,4,5:T(8,128)S(1)}, f32[32,2,2,2,2,2,128]{6,0,1,2,3,4,5:T(8,128)S(1)}, u32[]{:S(2)}, u32[]{:S(2)}) collective-permute-start(f32[32,2,2,2,2,2,128]{6,0,1,2,3,4,5:T(8,128)S(1)} %maximum_select_fusion.4), channel_id=1, source_target_pairs={{0,1},{1,0},{2,3},{3,2},{4,5},{5,4},{6,7},{7,6},{8,9},{9,8},{10,11... | collective-permute-start | bytes 1572872 | tf_op jit(solution)/shard_map/ppermute | solution.py:48
  98.1 1.6 %copy-start.2 = (bf16[128,2,4096]{2,1,0:T(2,128)(2,1)S(1)}, bf16[128,2,4096]{2,1,0:T(2,128)(2,1)}, u32[]{:S(2)}) copy-start(bf16[128,2,4096]{2,1,0:T(2,128)(2,1)} %get-tuple-element.9) | copy-start | bytes 6291460
  102.2 1.4 %collective-permute-start.15 = (f32[2,32]{1,0:T(2,128)S(1)}, f32[2,32]{1,0:T(2,128)S(1)}, u32[]{:S(2)}, u32[]{:S(2)}) collective-permute-start(f32[2,32]{1,0:T(2,128)S(1)} %pad_maximum_fusion), channel_id=1, source_target_pairs={{0,1},{1,0},{2,3},{3,2},{4,5},{5,4},{6,7},{7,6},{8,9},{9,8},{10,11... | collective-permute-start | bytes 776 | tf_op jit(solution)/shard_map/ppermute | solution.py:70
  103.6 3.6 %collective-permute-start.16 = (f32[2,32]{1,0:T(2,128)S(1)}, f32[2,32]{1,0:T(2,128)S(1)}, u32[]{:S(2)}, u32[]{:S(2)}) collective-permute-start(f32[2,32]{1,0:T(2,128)S(1)} %fusion.44), channel_id=1, source_target_pairs={{0,2},{1,3},{2,0},{3,1},{4,6},{5,7},{6,4},{7,5},{8,10},{9,11},{10,... | collective-permute-start | bytes 776 | tf_op jit(solution)/shard_map/ppermute | solution.py:70
  107.2 3.6 %collective-permute-start.17 = (f32[2,32]{1,0:T(2,128)S(1)}, f32[2,32]{1,0:T(2,128)S(1)}, u32[]{:S(2)}, u32[]{:S(2)}) collective-permute-start(f32[2,32]{1,0:T(2,128)S(1)} %fusion.46), channel_id=1, source_target_pairs={{0,4},{1,5},{2,6},{3,7},{4,0},{5,1},{6,2},{7,3},{8,12},{9,13},{10,... | collective-permute-start | bytes 776 | tf_op jit(solution)/shard_map/ppermute | solution.py:70
  110.9 3.6 %collective-permute-start.18 = (f32[2,32]{1,0:T(2,128)S(1)}, f32[2,32]{1,0:T(2,128)S(1)}, u32[]{:S(2)}, u32[]{:S(2)}) collective-permute-start(f32[2,32]{1,0:T(2,128)S(1)} %add.75), channel_id=1, source_target_pairs={{0,8},{1,9},{2,10},{3,11},{4,12},{5,13},{6,14},{7,15},{8,0},{9,1},... | collective-permute-start | bytes 776 | tf_op jit(solution)/shard_map/ppermute | solution.py:70
  114.5 4.5 %collective-permute-start.19 = (f32[2,32]{1,0:T(2,128)S(1)}, f32[2,32]{1,0:T(2,128)S(1)}, u32[]{:S(2)}, u32[]{:S(2)}) collective-permute-start(f32[2,32]{1,0:T(2,128)S(1)} %add.76), channel_id=1, source_target_pairs={{0,16},{1,17},{2,18},{3,19},{4,20},{5,21},{6,22},{7,23},{8,24},{9,... | collective-permute-start | bytes 776 | tf_op jit(solution)/shard_map/ppermute | solution.py:70

commit v6 on v4

--- a/solution.py
+++ b/solution.py
@@ -22,21 +22,36 @@
     )
 
 
+def _orders(size):
+    steps = _steps(size)
+    first = list(range(steps))
+    second = list(first)
+    if steps >= 3:
+        second[1], second[2] = second[2], second[1]
+    return first, second
+
+
+def _pairs(size, orders, t):
+    return [(i, i ^ (1 << orders[i & 1][t])) for i in range(size)]
+
+
 def _allreduce(x, size, axis):
     me = lax.axis_index("rows")
+    orders = _orders(size)
     steps = _steps(size)
+    bits = [jnp.where((me & 1) == 0, (me >> orders[0][t]) & 1, (me >> orders[1][t]) & 1) for t in range(steps)]
     cur = x
-    for s in range(steps):
+    for t in range(steps):
         half = cur.shape[axis] // 2
         lo = lax.slice_in_dim(cur, 0, half, axis=axis)
         hi = lax.slice_in_dim(cur, half, 2 * half, axis=axis)
-        low = ((me >> s) & 1) == 0
+        low = bits[t] == 0
         keep = jnp.where(low, lo, hi)
         send = jnp.where(low, hi, lo)
-        cur = keep + lax.ppermute(send, "rows", _xor_pairs(size, s))
-    for s in reversed(range(steps)):
-        low = ((me >> s) & 1) == 0
-        cur = _join(cur, lax.ppermute(cur, "rows", _xor_pairs(size, s)), low, axis)
+        cur = keep + lax.ppermute(send, "rows", _pairs(size, orders, t))
+    for t in reversed(range(steps)):
+        low = bits[t] == 0
+        cur = _join(cur, lax.ppermute(cur, "rows", _pairs(size, orders, t)), low, axis)
     return cur
 
 

time: 115 us -> 113 us (0.983)
  waiting for transfers between devices: 53.4 us -> 50.4 us
    ppermute x10, waiting for transfers between devices: 30.4 us -> 27.4 us  [the longest x5 14.4 us: _allreduce(): lax.ppermute(cur, 'rows', _pairs(size, orders, t))]
where the time goes in v6:
time: 113 us
  waiting for transfers between devices  50.4 us (45%)
  starting transfers between devices  35.7 us (32%)
  matrix products  8.94 us (8%)
  other arithmetic  8.06 us (7%)
  Pallas kernels  6.9 us (6%)
  local copies, waits for them, and re-layouts  2.39 us (2%)
    ppermute x5, waiting for transfers between devices, _allgather(): other = lax.ppermute(cur, 'rows', _xor_pairs(size, s))  14.5 us
    ppermute x5, waiting for transfers between devices, _allreduce(): lax.ppermute(cur, 'rows', _pairs(size, orders, t))  14.4 us
    ppermute x5, waiting for transfers between devices, _allreduce(): cur = keep + lax.ppermute(send, 'rows', _pairs(size, orders, t))  13 us
    ppermute x5, starting transfers between devices, _allreduce(): cur = keep + lax.ppermute(send, 'rows', _pairs(size, orders, t))  11.2 us
    ppermute x5, waiting for transfers between devices, _butterfly_sum(): x = x + lax.ppermute(x, 'rows', _xor_pairs(size, s))  8.53 us
    ppermute x5, starting transfers between devices, _allgather(): other = lax.ppermute(cur, 'rows', _xor_pairs(size, s))  8.27 us
    ppermute x5, starting transfers between devices, _allreduce(): lax.ppermute(cur, 'rows', _pairs(size, orders, t))  8.27 us
    ppermute x5, starting transfers between devices, _butterfly_sum(): x = x + lax.ppermute(x, 'rows', _xor_pairs(size, s))  8.03 us
  transfers between devices with their start and end apart: 20, of which 20 were waited for; matrix products, arithmetic and copies ran while one was open for 0% of the time, Pallas kernels for 0%

profile of v6, /device:TPU:0, one launch (start us, length us, event | category | flops | bytes accessed | tf_op | source)
XLA Modules:
  0.0 112.7 jit_solution(15917472547603009978)
XLA Ops:
  2.3 6.9 %shard_map.82 = f32[32,2,4096]{2,1,0:T(2,128)} custom-call(bf16[128,2,4096]{2,1,0:T(2,128)(2,1)} %acts_ref.1, bf16[128,2,4096]{2,1,0:T(2,128)(2,1)} %gout_ref.1, bf16[4096,128]{1,0:T(8,128)(2,1)} %pin_ref.1, bf16[4096,128]{1,0:T(8,128)(2,1)} %pout_ref.1, bf16[32,128]{1,0:T(8,128)(2,1)} %fusion.8.sel_ref), custom_call_target="tpu_custom_call" | custom-call | tf_op jit(solution)/shard_map/pallas_call | solution.py:114
  14.6 2.9 %collective-permute-start.1 = (f32[32,2,1024]{2,1,0:T(2,128)S(1)}, f32[32,2,1024]{2,1,0:T(2,128)S(1)}, u32[]{:S(2)}, u32[]{:S(2)}) collective-permute-start(f32[32,2,1024]{2,1,0:T(2,128)S(1)} %broadcast_select_fusion.1), channel_id=1, source_target_pairs={{0,2},{1,5},{2,0},{3,7},{4,6},{5,1},{6,4},{7,3},{8,10},{9,13},{10,... | collective-permute-start | bytes 786440 | tf_op jit(solution)/shard_map/ppermute | solution.py:51
  17.5 4.4 %collective-permute-done.1 = f32[32,2,1024]{2,1,0:T(2,128)S(1)} collective-permute-done((f32[32,2,1024]{2,1,0:T(2,128)S(1)}, f32[32,2,1024]{2,1,0:T(2,128)S(1)}, u32[]{:S(2)}, u32[]{:S(2)}) %collective-permute-start.1) | collective-permute-done | bytes 262176 | tf_op jit(solution)/shard_map/ppermute | solution.py:51
  22.2 2.1 %collective-permute-start.2 = (f32[32,2,512]{2,1,0:T(2,128)S(1)}, f32[32,2,512]{2,1,0:T(2,128)S(1)}, u32[]{:S(2)}, u32[]{:S(2)}) collective-permute-start(f32[32,2,512]{2,1,0:T(2,128)S(1)} %broadcast_select_fusion.2), channel_id=1, source_target_pairs={{0,4},{1,3},{2,6},{3,1},{4,0},{5,7},{6,2},{7,5},{8,12},{9,11},{10,... | collective-permute-start | bytes 393224 | tf_op jit(solution)/shard_map/ppermute | solution.py:51
  24.3 2.9 %collective-permute-done.2 = f32[32,2,512]{2,1,0:T(2,128)S(1)} collective-permute-done((f32[32,2,512]{2,1,0:T(2,128)S(1)}, f32[32,2,512]{2,1,0:T(2,128)S(1)}, u32[]{:S(2)}, u32[]{:S(2)}) %collective-permute-start.2) | collective-permute-done | bytes 131104 | tf_op jit(solution)/shard_map/ppermute | solution.py:51
  27.4 2.1 %collective-permute-start.3 = (f32[32,2,256]{2,1,0:T(2,128)S(1)}, f32[32,2,256]{2,1,0:T(2,128)S(1)}, u32[]{:S(2)}, u32[]{:S(2)}) collective-permute-start(f32[32,2,256]{2,1,0:T(2,128)S(1)} %broadcast_select_fusion.3), channel_id=1, source_target_pairs={{0,8},{1,9},{2,10},{3,11},{4,12},{5,13},{6,14},{7,15},{8,0},{9,1},... | collective-permute-start | bytes 196616 | tf_op jit(solution)/shard_map/ppermute | solution.py:51
  29.5 2.2 %collective-permute-done.3 = f32[32,2,256]{2,1,0:T(2,128)S(1)} collective-permute-done((f32[32,2,256]{2,1,0:T(2,128)S(1)}, f32[32,2,256]{2,1,0:T(2,128)S(1)}, u32[]{:S(2)}, u32[]{:S(2)}) %collective-permute-start.3) | collective-permute-done | bytes 65568 | tf_op jit(solution)/shard_map/ppermute | solution.py:51
  31.8 3.5 %collective-permute-start.4 = (f32[32,2,128]{2,1,0:T(2,128)S(1)}, f32[32,2,128]{2,1,0:T(2,128)S(1)}, u32[]{:S(2)}, u32[]{:S(2)}) collective-permute-start(f32[32,2,128]{2,1,0:T(2,128)S(1)} %broadcast_select_fusion.4), channel_id=1, source_target_pairs={{0,16},{1,17},{2,18},{3,19},{4,20},{5,21},{6,22},{7,23},{8,24},{9,... | collective-permute-start | bytes 98312 | tf_op jit(solution)/shard_map/ppermute | solution.py:51
  35.3 2.0 %collective-permute-done.4 = f32[32,2,128]{2,1,0:T(2,128)S(1)} collective-permute-done((f32[32,2,128]{2,1,0:T(2,128)S(1)}, f32[32,2,128]{2,1,0:T(2,128)S(1)}, u32[]{:S(2)}, u32[]{:S(2)}) %collective-permute-start.4) | collective-permute-done | bytes 32800 | tf_op jit(solution)/shard_map/ppermute | solution.py:51
  37.3 2.9 %collective-permute-start.5 = (f32[32,2,128]{2,1,0:T(2,128)S(1)}, f32[32,2,128]{2,1,0:T(2,128)S(1)}, u32[]{:S(2)}, u32[]{:S(2)}) collective-permute-start(f32[32,2,128]{2,1,0:T(2,128)S(1)} %select_add_fusion.4), channel_id=1, source_target_pairs={{0,16},{1,17},{2,18},{3,19},{4,20},{5,21},{6,22},{7,23},{8,24},{9,... | collective-permute-start | bytes 98312 | tf_op jit(solution)/shard_map/ppermute | solution.py:54
  40.2 2.0 %collective-permute-done.5 = f32[32,2,128]{2,1,0:T(2,128)S(1)} collective-permute-done((f32[32,2,128]{2,1,0:T(2,128)S(1)}, f32[32,2,128]{2,1,0:T(2,128)S(1)}, u32[]{:S(2)}, u32[]{:S(2)}) %collective-permute-start.5) | collective-permute-done | bytes 32800 | tf_op jit(solution)/shard_map/ppermute | solution.py:54
  42.2 2.1 %collective-permute-start.6 = (f32[32,2,256]{2,1,0:T(2,128)S(1)}, f32[32,2,256]{2,1,0:T(2,128)S(1)}, u32[]{:S(2)}, u32[]{:S(2)}) collective-permute-start(f32[32,2,256]{2,1,0:T(2,128)S(1)} %maximum_select_fusion.11), channel_id=1, source_target_pairs={{0,8},{1,9},{2,10},{3,11},{4,12},{5,13},{6,14},{7,15},{8,0},{9,1},... | collective-permute-start | bytes 196616 | tf_op jit(solution)/shard_map/ppermute | solution.py:54
  44.3 2.2 %collective-permute-done.6 = f32[32,2,256]{2,1,0:T(2,128)S(1)} collective-permute-done((f32[32,2,256]{2,1,0:T(2,128)S(1)}, f32[32,2,256]{2,1,0:T(2,128)S(1)}, u32[]{:S(2)}, u32[]{:S(2)}) %collective-permute-start.6) | collective-permute-done | bytes 65568 | tf_op jit(solution)/shard_map/ppermute | solution.py:54
  48.2 3.4 %collective-permute-done.7 = f32[32,2,512]{2,1,0:T(2,128)S(1)} collective-permute-done((f32[32,2,512]{2,1,0:T(2,128)S(1)}, f32[32,2,512]{2,1,0:T(2,128)S(1)}, u32[]{:S(2)}, u32[]{:S(2)}) %collective-permute-start.7) | collective-permute-done | bytes 131104 | tf_op jit(solution)/shard_map/ppermute | solution.py:54
  53.4 4.9 %collective-permute-done.8 = f32[32,2,1024]{2,1,0:T(2,128)S(1)} collective-permute-done((f32[32,2,1024]{2,1,0:T(2,128)S(1)}, f32[32,2,1024]{2,1,0:T(2,128)S(1)}, u32[]{:S(2)}, u32[]{:S(2)}) %collective-permute-start.8) | collective-permute-done | bytes 262176 | tf_op jit(solution)/shard_map/ppermute | solution.py:54
  61.6 2.5 %fusion.5 = f32[2,32,128]{2,1,0:T(8,128)S(1)} fusion(f32[2,128,4096]{2,1,0:T(8,128)S(1)} %copy-done, f32[32,2,4096]{2,1,0:T(2,128)S(1)} %maximum_select_fusion), kind=kOutput, calls=%fused_computation.5 | convolution fusion | flops 201326592 | bytes 5275648 | tf_op jit(solution)/shard_map/qmk,mck->qmc/dot_general | solution.py:139
  64.1 3.2 %collective-permute-start.10 = (f32[32,2,128]{2,0,1:T(8,128)S(1)}, f32[32,2,128]{2,0,1:T(8,128)S(1)}, u32[]{:S(2)}, u32[]{:S(2)}) collective-permute-start(f32[32,2,128]{2,0,1:T(8,128)S(1)} %bitcast.47), channel_id=1, source_target_pairs={{0,16},{1,17},{2,18},{3,19},{4,20},{5,21},{6,22},{7,23},{8,24},{9,... | collective-permute-start | bytes 98312 | tf_op jit(solution)/shard_map/ppermute | solution.py:63
  71.1 2.5 %collective-permute-done.11 = f32[32,2,2,128]{3,0,1,2:T(8,128)S(1)} collective-permute-done((f32[32,2,2,128]{3,0,1,2:T(8,128)S(1)}, f32[32,2,2,128]{3,0,1,2:T(8,128)S(1)}, u32[]{:S(2)}, u32[]{:S(2)}) %collective-permute-start.11) | collective-permute-done | bytes 65568 | tf_op jit(solution)/shard_map/ppermute | solution.py:63
  75.2 3.4 %collective-permute-done.12 = f32[32,2,2,2,128]{4,0,1,2,3:T(8,128)S(1)} collective-permute-done((f32[32,2,2,2,128]{4,0,1,2,3:T(8,128)S(1)}, f32[32,2,2,2,128]{4,0,1,2,3:T(8,128)S(1)}, u32[]{:S(2)}, u32[]{:S(2)}) %collective-permute-start.12) | collective-permute-done | bytes 131104 | tf_op jit(solution)/shard_map/ppermute | solution.py:63
  80.3 4.8 %collective-permute-done.13 = f32[32,2,2,2,2,128]{5,0,1,2,3,4:T(8,128)S(1)} collective-permute-done((f32[32,2,2,2,2,128]{5,0,1,2,3,4:T(8,128)S(1)}, f32[32,2,2,2,2,128]{5,0,1,2,3,4:T(8,128)S(1)}, u32[]{:S(2)}, u32[]{:S(2)}) %collective-permute-start.13) | collective-permute-done | bytes 262176 | tf_op jit(solution)/shard_map/ppermute | solution.py:63
  88.9 6.5 %fusion.12 = (f32[32]{0:T(128)S(1)}, f32[32]{0:T(128)S(1)}, f32[32,128]{1,0:T(8,128)S(1)}) fusion(f32[32,2,4096]{2,0,1:T(8,128)S(1)} %select_n.262, f32[128,2,4096]{2,1,0:T(2,128)} %param.15), kind=kOutput, calls=%fused_computation.43 | convolution fusion | flops 201338816 | bytes 5259520 | tf_op jit(solution)/shard_map/qmk,nmk->qn/dot_general | solution.py:140
  98.2 2.1 %collective-permute-done.16 = f32[2,32]{1,0:T(2,128)S(1)} collective-permute-done((f32[2,32]{1,0:T(2,128)S(1)}, f32[2,32]{1,0:T(2,128)S(1)}, u32[]{:S(2)}, u32[]{:S(2)}) %collective-permute-start.16) | collective-permute-done | bytes 288 | tf_op jit(solution)/shard_map/ppermute | solution.py:74
  101.9 2.1 %collective-permute-done.17 = f32[2,32]{1,0:T(2,128)S(1)} collective-permute-done((f32[2,32]{1,0:T(2,128)S(1)}, f32[2,32]{1,0:T(2,128)S(1)}, u32[]{:S(2)}, u32[]{:S(2)}) %collective-permute-start.17) | collective-permute-done | bytes 288 | tf_op jit(solution)/shard_map/ppermute | solution.py:74
  107.5 2.9 %collective-permute-start.19 = (f32[2,32]{1,0:T(2,128)S(1)}, f32[2,32]{1,0:T(2,128)S(1)}, u32[]{:S(2)}, u32[]{:S(2)}) collective-permute-start(f32[2,32]{1,0:T(2,128)S(1)} %add.60), channel_id=1, source_target_pairs={{0,16},{1,17},{2,18},{3,19},{4,20},{5,21},{6,22},{7,23},{8,24},{9,... | collective-permute-start | bytes 776 | tf_op jit(solution)/shard_map/ppermute | solution.py:74
  (66 shorter events, 35.9 us)
Async XLA Ops:
  10.7 2.1 %collective-permute-start = (f32[32,2,2048]{2,1,0:T(2,128)S(1)}, f32[32,2,2048]{2,1,0:T(2,128)S(1)}, u32[]{:S(2)}, u32[]{:S(2)}) collective-permute-start(f32[32,2,2048]{2,1,0:T(2,128)S(1)} %broadcast_select_fusion), channel_id=1, source_target_pairs={{0,1},{1,0},{2,3},{3,2},{4,5},{5,4},{6,7},{7,6},{8,9},{9,8},{10,11... | collective-permute-start | bytes 1572872 | tf_op jit(solution)/shard_map/ppermute | solution.py:51
  14.6 7.3 %collective-permute-start.1 = (f32[32,2,1024]{2,1,0:T(2,128)S(1)}, f32[32,2,1024]{2,1,0:T(2,128)S(1)}, u32[]{:S(2)}, u32[]{:S(2)}) collective-permute-start(f32[32,2,1024]{2,1,0:T(2,128)S(1)} %broadcast_select_fusion.1), channel_id=1, source_target_pairs={{0,2},{1,5},{2,0},{3,7},{4,6},{5,1},{6,4},{7,3},{8,10},{9,13},{10,... | collective-permute-start | bytes 786440 | tf_op jit(solution)/shard_map/ppermute | solution.py:51
  22.2 5.1 %collective-permute-start.2 = (f32[32,2,512]{2,1,0:T(2,128)S(1)}, f32[32,2,512]{2,1,0:T(2,128)S(1)}, u32[]{:S(2)}, u32[]{:S(2)}) collective-permute-start(f32[32,2,512]{2,1,0:T(2,128)S(1)} %broadcast_select_fusion.2), channel_id=1, source_target_pairs={{0,4},{1,3},{2,6},{3,1},{4,0},{5,7},{6,2},{7,5},{8,12},{9,11},{10,... | collective-permute-start | bytes 393224 | tf_op jit(solution)/shard_map/ppermute | solution.py:51
  27.4 4.4 %collective-permute-start.3 = (f32[32,2,256]{2,1,0:T(2,128)S(1)}, f32[32,2,256]{2,1,0:T(2,128)S(1)}, u32[]{:S(2)}, u32[]{:S(2)}) collective-permute-start(f32[32,2,256]{2,1,0:T(2,128)S(1)} %broadcast_select_fusion.3), channel_id=1, source_target_pairs={{0,8},{1,9},{2,10},{3,11},{4,12},{5,13},{6,14},{7,15},{8,0},{9,1},... | collective-permute-start | bytes 196616 | tf_op jit(solution)/shard_map/ppermute | solution.py:51
  29.5 32.1 %copy-start = (f32[2,128,4096]{2,1,0:T(8,128)S(1)}, f32[2,128,4096]{2,1,0:T(8,128)}, u32[]{:S(2)}) copy-start(f32[2,128,4096]{2,1,0:T(8,128)} %param.14) | copy-start | bytes 12582916
  31.8 5.4 %collective-permute-start.4 = (f32[32,2,128]{2,1,0:T(2,128)S(1)}, f32[32,2,128]{2,1,0:T(2,128)S(1)}, u32[]{:S(2)}, u32[]{:S(2)}) collective-permute-start(f32[32,2,128]{2,1,0:T(2,128)S(1)} %broadcast_select_fusion.4), channel_id=1, source_target_pairs={{0,16},{1,17},{2,18},{3,19},{4,20},{5,21},{6,22},{7,23},{8,24},{9,... | collective-permute-start | bytes 98312 | tf_op jit(solution)/shard_map/ppermute | solution.py:51
  37.3 4.9 %collective-permute-start.5 = (f32[32,2,128]{2,1,0:T(2,128)S(1)}, f32[32,2,128]{2,1,0:T(2,128)S(1)}, u32[]{:S(2)}, u32[]{:S(2)}) collective-permute-start(f32[32,2,128]{2,1,0:T(2,128)S(1)} %select_add_fusion.4), channel_id=1, source_target_pairs={{0,16},{1,17},{2,18},{3,19},{4,20},{5,21},{6,22},{7,23},{8,24},{9,... | collective-permute-start | bytes 98312 | tf_op jit(solution)/shard_map/ppermute | solution.py:54
  42.2 4.3 %collective-permute-start.6 = (f32[32,2,256]{2,1,0:T(2,128)S(1)}, f32[32,2,256]{2,1,0:T(2,128)S(1)}, u32[]{:S(2)}, u32[]{:S(2)}) collective-permute-start(f32[32,2,256]{2,1,0:T(2,128)S(1)} %maximum_select_fusion.11), channel_id=1, source_target_pairs={{0,8},{1,9},{2,10},{3,11},{4,12},{5,13},{6,14},{7,15},{8,0},{9,1},... | collective-permute-start | bytes 196616 | tf_op jit(solution)/shard_map/ppermute | solution.py:54
  46.6 5.0 %collective-permute-start.7 = (f32[32,2,512]{2,1,0:T(2,128)S(1)}, f32[32,2,512]{2,1,0:T(2,128)S(1)}, u32[]{:S(2)}, u32[]{:S(2)}) collective-permute-start(f32[32,2,512]{2,1,0:T(2,128)S(1)} %maximum_select_fusion.8), channel_id=1, source_target_pairs={{0,4},{1,3},{2,6},{3,1},{4,0},{5,7},{6,2},{7,5},{8,12},{9,11},{10,... | collective-permute-start | bytes 393224 | tf_op jit(solution)/shard_map/ppermute | solution.py:54
  51.9 6.4 %collective-permute-start.8 = (f32[32,2,1024]{2,1,0:T(2,128)S(1)}, f32[32,2,1024]{2,1,0:T(2,128)S(1)}, u32[]{:S(2)}, u32[]{:S(2)}) collective-permute-start(f32[32,2,1024]{2,1,0:T(2,128)S(1)} %maximum_select_fusion.5), channel_id=1, source_target_pairs={{0,2},{1,5},{2,0},{3,7},{4,6},{5,1},{6,4},{7,3},{8,10},{9,13},{10,... | collective-permute-start | bytes 786440 | tf_op jit(solution)/shard_map/ppermute | solution.py:54
  58.7 2.0 %collective-permute-start.9 = (f32[32,2,2048]{2,1,0:T(2,128)S(1)}, f32[32,2,2048]{2,1,0:T(2,128)S(1)}, u32[]{:S(2)}, u32[]{:S(2)}) collective-permute-start(f32[32,2,2048]{2,1,0:T(2,128)S(1)} %maximum_select_fusion.2), channel_id=1, source_target_pairs={{0,1},{1,0},{2,3},{3,2},{4,5},{5,4},{6,7},{7,6},{8,9},{9,8},{10,11... | collective-permute-start | bytes 1572872 | tf_op jit(solution)/shard_map/ppermute | solution.py:54
  64.1 5.1 %collective-permute-start.10 = (f32[32,2,128]{2,0,1:T(8,128)S(1)}, f32[32,2,128]{2,0,1:T(8,128)S(1)}, u32[]{:S(2)}, u32[]{:S(2)}) collective-permute-start(f32[32,2,128]{2,0,1:T(8,128)S(1)} %bitcast.47), channel_id=1, source_target_pairs={{0,16},{1,17},{2,18},{3,19},{4,20},{5,21},{6,22},{7,23},{8,24},{9,... | collective-permute-start | bytes 98312 | tf_op jit(solution)/shard_map/ppermute | solution.py:63
  69.3 4.3 %collective-permute-start.11 = (f32[32,2,2,128]{3,0,1,2:T(8,128)S(1)}, f32[32,2,2,128]{3,0,1,2:T(8,128)S(1)}, u32[]{:S(2)}, u32[]{:S(2)}) collective-permute-start(f32[32,2,2,128]{3,0,1,2:T(8,128)S(1)} %maximum_select_fusion.13), channel_id=1, source_target_pairs={{0,8},{1,9},{2,10},{3,11},{4,12},{5,13},{6,14},{7,15},{8,0},{9,1},... | collective-permute-start | bytes 196616 | tf_op jit(solution)/shard_map/ppermute | solution.py:63
  73.6 5.0 %collective-permute-start.12 = (f32[32,2,2,2,128]{4,0,1,2,3:T(8,128)S(1)}, f32[32,2,2,2,128]{4,0,1,2,3:T(8,128)S(1)}, u32[]{:S(2)}, u32[]{:S(2)}) collective-permute-start(f32[32,2,2,2,128]{4,0,1,2,3:T(8,128)S(1)} %maximum_select_fusion.10), channel_id=1, source_target_pairs={{0,4},{1,5},{2,6},{3,7},{4,0},{5,1},{6,2},{7,3},{8,12},{9,13},{10,... | collective-permute-start | bytes 393224 | tf_op jit(solution)/shard_map/ppermute | solution.py:63
  78.7 6.4 %collective-permute-start.13 = (f32[32,2,2,2,2,128]{5,0,1,2,3,4:T(8,128)S(1)}, f32[32,2,2,2,2,128]{5,0,1,2,3,4:T(8,128)S(1)}, u32[]{:S(2)}, u32[]{:S(2)}) collective-permute-start(f32[32,2,2,2,2,128]{5,0,1,2,3,4:T(8,128)S(1)} %maximum_select_fusion.7), channel_id=1, source_target_pairs={{0,2},{1,3},{2,0},{3,1},{4,6},{5,7},{6,4},{7,5},{8,10},{9,11},{10,... | collective-permute-start | bytes 786440 | tf_op jit(solution)/shard_map/ppermute | solution.py:63
  85.2 2.0 %collective-permute-start.14 = (f32[32,2,2,2,2,2,128]{6,0,1,2,3,4,5:T(8,128)S(1)}, f32[32,2,2,2,2,2,128]{6,0,1,2,3,4,5:T(8,128)S(1)}, u32[]{:S(2)}, u32[]{:S(2)}) collective-permute-start(f32[32,2,2,2,2,2,128]{6,0,1,2,3,4,5:T(8,128)S(1)} %maximum_select_fusion.4), channel_id=1, source_target_pairs={{0,1},{1,0},{2,3},{3,2},{4,5},{5,4},{6,7},{7,6},{8,9},{9,8},{10,11... | collective-permute-start | bytes 1572872 | tf_op jit(solution)/shard_map/ppermute | solution.py:63
  95.4 1.2 %collective-permute-start.15 = (f32[2,32]{1,0:T(2,128)S(1)}, f32[2,32]{1,0:T(2,128)S(1)}, u32[]{:S(2)}, u32[]{:S(2)}) collective-permute-start(f32[2,32]{1,0:T(2,128)S(1)} %pad_maximum_fusion), channel_id=1, source_target_pairs={{0,1},{1,0},{2,3},{3,2},{4,5},{5,4},{6,7},{7,6},{8,9},{9,8},{10,11... | collective-permute-start | bytes 776 | tf_op jit(solution)/shard_map/ppermute | solution.py:74
  96.6 3.6 %collective-permute-start.16 = (f32[2,32]{1,0:T(2,128)S(1)}, f32[2,32]{1,0:T(2,128)S(1)}, u32[]{:S(2)}, u32[]{:S(2)}) collective-permute-start(f32[2,32]{1,0:T(2,128)S(1)} %fusion.11), channel_id=1, source_target_pairs={{0,2},{1,3},{2,0},{3,1},{4,6},{5,7},{6,4},{7,5},{8,10},{9,11},{10,... | collective-permute-start | bytes 776 | tf_op jit(solution)/shard_map/ppermute | solution.py:74
  100.3 3.6 %collective-permute-start.17 = (f32[2,32]{1,0:T(2,128)S(1)}, f32[2,32]{1,0:T(2,128)S(1)}, u32[]{:S(2)}, u32[]{:S(2)}) collective-permute-start(f32[2,32]{1,0:T(2,128)S(1)} %fusion.15), channel_id=1, source_target_pairs={{0,4},{1,5},{2,6},{3,7},{4,0},{5,1},{6,2},{7,3},{8,12},{9,13},{10,... | collective-permute-start | bytes 776 | tf_op jit(solution)/shard_map/ppermute | solution.py:74
  103.9 3.6 %collective-permute-start.18 = (f32[2,32]{1,0:T(2,128)S(1)}, f32[2,32]{1,0:T(2,128)S(1)}, u32[]{:S(2)}, u32[]{:S(2)}) collective-permute-start(f32[2,32]{1,0:T(2,128)S(1)} %add.59), channel_id=1, source_target_pairs={{0,8},{1,9},{2,10},{3,11},{4,12},{5,13},{6,14},{7,15},{8,0},{9,1},... | collective-permute-start | bytes 776 | tf_op jit(solution)/shard_map/ppermute | solution.py:74
  107.5 4.5 %collective-permute-start.19 = (f32[2,32]{1,0:T(2,128)S(1)}, f32[2,32]{1,0:T(2,128)S(1)}, u32[]{:S(2)}, u32[]{:S(2)}) collective-permute-start(f32[2,32]{1,0:T(2,128)S(1)} %add.60), channel_id=1, source_target_pairs={{0,16},{1,17},{2,18},{3,19},{4,20},{5,21},{6,22},{7,23},{8,24},{9,... | collective-permute-start | bytes 776 | tf_op jit(solution)/shard_map/ppermute | solution.py:74

commit v7 on v6

--- a/solution.py
+++ b/solution.py
@@ -35,13 +35,13 @@
     return [(i, i ^ (1 << orders[i & 1][t])) for i in range(size)]
 
 
-def _allreduce(x, size, axis):
+def _allreduce(keep, send, size, axis):
     me = lax.axis_index("rows")
     orders = _orders(size)
     steps = _steps(size)
     bits = [jnp.where((me & 1) == 0, (me >> orders[0][t]) & 1, (me >> orders[1][t]) & 1) for t in range(steps)]
-    cur = x
-    for t in range(steps):
+    cur = keep + lax.ppermute(send, "rows", _pairs(size, orders, 0))
+    for t in range(1, steps):
         half = cur.shape[axis] // 2
         lo = lax.slice_in_dim(cur, 0, half, axis=axis)
         hi = lax.slice_in_dim(cur, half, 2 * half, axis=axis)
@@ -75,10 +75,13 @@
     return x
 
 
-def _sums_kernel(acts_ref, gout_ref, pin_ref, pout_ref, sel_ref, out_ref, act_scr, grad_scr):
+def _sums_kernel(len_ref, valid_ref, acts_ref, gout_ref, pin_ref, pout_ref, keep_ref, send_ref, act_scr, grad_scr):
     tokens, modules, width_in = acts_ref.shape
+    queries = len_ref.shape[1]
     rank = pin_ref.shape[1] // modules
     width = rank * rank
+    half = width // 2
+    me = lax.axis_index("rows")
     act_scr[...] = jnp.dot(
         acts_ref[...].reshape(tokens * modules, width_in), pin_ref[...],
         preferred_element_type=jnp.float32,
@@ -87,9 +90,17 @@
         gout_ref[...].reshape(tokens * modules, width_in), pout_ref[...],
         preferred_element_type=jnp.float32,
     )
+    qrow = lax.broadcasted_iota(jnp.int32, (queries, queries), 0)
+    qcol = lax.broadcasted_iota(jnp.int32, (queries, queries), 1)
+    lengths = jnp.broadcast_to(len_ref[...], (queries, queries))
+    ends = jnp.sum(jnp.where(qcol <= qrow, lengths, 0), axis=1, keepdims=True)
+    pos = lax.broadcasted_iota(jnp.int32, (queries, tokens), 1) + me * tokens
+    segment = jnp.sum((ends <= pos).astype(jnp.int32), axis=0, keepdims=True)
+    qid = lax.broadcasted_iota(jnp.int32, (queries, tokens), 0)
+    sel = ((segment == qid) & (valid_ref[...] == 1)).astype(jnp.bfloat16)
     col = lax.broadcasted_iota(jnp.int32, (modules * rank, width), 1)
     row = lax.broadcasted_iota(jnp.int32, (modules * rank, width), 0)
-    sel = sel_ref[...]
+    first = (me % 2) == 0
     for m in range(modules):
         repeat = (m * rank + col // rank == row).astype(jnp.bfloat16)
         tile = (m * rank + col % rank == row).astype(jnp.bfloat16)
@@ -101,21 +112,25 @@
         outer = grad_wide * act_wide
         high = outer.astype(jnp.bfloat16)
         low = (outer - high.astype(jnp.float32)).astype(jnp.bfloat16)
-        out_ref[:, m, :] = jnp.dot(sel, high, preferred_element_type=jnp.float32) + jnp.dot(
+        total = jnp.dot(sel, high, preferred_element_type=jnp.float32) + jnp.dot(
             sel, low, preferred_element_type=jnp.float32
         )
+        lo, hi = total[:, :half], total[:, half:]
+        keep_ref[:, m, :] = jnp.where(first, lo, hi)
+        send_ref[:, m, :] = jnp.where(first, hi, lo)
 
 
-def _module_sums(acts, grads_out, proj_in, proj_out, selector_t):
-    queries = selector_t.shape[0]
+def _module_sums(lengths, valid, acts, grads_out, proj_in, proj_out):
+    queries = lengths.shape[0]
     tokens, modules, _ = acts.shape
     rank = proj_in.shape[1] // modules
     scratch = pltpu.VMEM((tokens * modules, modules * rank), jnp.float32)
+    half = jax.ShapeDtypeStruct((queries, modules, rank * rank // 2), jnp.float32)
     return pl.pallas_call(
         _sums_kernel,
-        out_shape=jax.ShapeDtypeStruct((queries, modules, rank * rank), jnp.float32),
+        out_shape=(half, half),
         scratch_shapes=[scratch, scratch],
-    )(acts, grads_out, proj_in, proj_out, selector_t)
+    )(lengths.reshape(1, queries), valid.reshape(1, tokens), acts, grads_out, proj_in, proj_out)
 
 
 def shards(size, acts, grads_out, lengths, valid, proj_in, proj_out, fisher_inv, database):
@@ -124,18 +139,8 @@
     proj_rank = proj_in.shape[1] // modules
     queries = lengths.shape[0]
     flat_width = proj_rank * proj_rank
-    first_pos = lax.axis_index("rows") * tok_rows
-    positions = first_pos + jnp.arange(tok_rows, dtype=jnp.int32)
-    seg_ends = jnp.cumsum(lengths)
-    segment = jnp.sum((seg_ends[None, :] <= positions[:, None]).astype(jnp.int32), axis=1)
-    selector = (
-        (segment[:, None] == jnp.arange(queries, dtype=jnp.int32)[None, :]) & (valid[:, None] == 1)
-    ).astype(jnp.bfloat16)
-    selector_t = (
-        (jnp.arange(queries, dtype=jnp.int32)[:, None] == segment[None, :]) & (valid[None, :] == 1)
-    ).astype(jnp.bfloat16)
-    partial_value = _module_sums(acts, grads_out, proj_in, proj_out, selector_t)
-    summed = _allreduce(partial_value, size, 2)
+    keep, send = _module_sums(lengths, valid, acts, grads_out, proj_in, proj_out)
+    summed = _allreduce(keep, send, size, 2)
     precond_cols = jnp.einsum("qmk,mck->qmc", summed, fisher_inv, precision=lax.Precision.HIGH)
     scores = jnp.einsum(
         "qmk,nmk->qn",

time: 113 us -> 111 us (0.982)
  other arithmetic: 8.06 us -> 4.65 us
  matrix products: 8.94 us -> 11.1 us
    dot_general x1, matrix products: 2.47 us -> 4.63 us  [shards(): jnp.einsum('qmk,mck->qmc', summed, fisher_inv, precision=lax.Precision.HIGH)]
    ppermute x0 -> x1, waiting for transfers between devices: none -> 1.75 us  [_allreduce(): cur = keep + lax.ppermute(send, 'rows', _pairs(size, orders, 0))]
    add x5 -> x4, other arithmetic: 2.08 us -> 0.36 us  [_allreduce(): cur = keep + lax.ppermute(send, 'rows', _pairs(size, orders, t))]
    ppermute x5 -> x4, waiting for transfers between devices: 13 us -> 11.5 us  [_allreduce(): cur = keep + lax.ppermute(send, 'rows', _pairs(size, orders, t))]
    select_n x5 -> x4, other arithmetic: 1.75 us -> 0.27 us  [_allreduce(): send = jnp.where(low, hi, lo)]
    add x1, other arithmetic: 0.01 us -> 1.33 us  [_allreduce(): cur = keep + lax.ppermute(send, 'rows', _pairs(size, orders, 0))]
    ppermute x5 -> x4, starting transfers between devices: 11.2 us -> 10.6 us  [_allreduce(): cur = keep + lax.ppermute(send, 'rows', _pairs(size, orders, t))]
where the time goes in v7:
time: 111 us
  waiting for transfers between devices  50.6 us (46%)
  starting transfers between devices  35.7 us (32%)
  matrix products  11.1 us (10%)
  Pallas kernels  7.14 us (6%)
  other arithmetic  4.65 us (4%)
  local copies, waits for them, and re-layouts  1.65 us (1%)
    ppermute x5, waiting for transfers between devices, _allgather(): other = lax.ppermute(cur, 'rows', _xor_pairs(size, s))  14.5 us
    ppermute x5, waiting for transfers between devices, _allreduce(): lax.ppermute(cur, 'rows', _pairs(size, orders, t))  14.4 us
    ppermute x4, waiting for transfers between devices, _allreduce(): cur = keep + lax.ppermute(send, 'rows', _pairs(size, orders, t))  11.5 us
    ppermute x4, starting transfers between devices, _allreduce(): cur = keep + lax.ppermute(send, 'rows', _pairs(size, orders, t))  10.6 us
    ppermute x5, waiting for transfers between devices, _butterfly_sum(): x = x + lax.ppermute(x, 'rows', _xor_pairs(size, s))  8.52 us
    ppermute x5, starting transfers between devices, _allgather(): other = lax.ppermute(cur, 'rows', _xor_pairs(size, s))  8.29 us
    ppermute x5, starting transfers between devices, _allreduce(): lax.ppermute(cur, 'rows', _pairs(size, orders, t))  8.27 us
    ppermute x5, starting transfers between devices, _butterfly_sum(): x = x + lax.ppermute(x, 'rows', _xor_pairs(size, s))  8.05 us
  transfers between devices with their start and end apart: 20, of which 20 were waited for; matrix products, arithmetic and copies ran while one was open for 0% of the time, Pallas kernels for 0%

profile of v7, /device:TPU:0, one launch (start us, length us, event | category | flops | bytes accessed | tf_op | source)
XLA Modules:
  0.0 111.1 jit_solution(10630668852611494869)
XLA Ops:
  0.0 7.1 %shard_map.82 = (f32[32,2,2048]{2,1,0:T(2,128)}, f32[32,2,2048]{2,1,0:T(2,128)}) custom-call(s32[1,32]{1,0:T(1,128)} %bitcast.62, s32[1,128]{1,0:T(1,128)} %bitcast.63, bf16[128,2,4096]{2,1,0:T(2,128)(2,1)} %acts_ref.1, bf16[128,2,4096]{2,1,0:T(2,128)(2,1)} %gout_ref.1, bf16[4096,128]{1,0:T(8,128)(2,1)} %pin_ref.1, bf16[4096,128]{1,0:T(8,128)(2,1)} %pout_ref.1), custom_call_target="tpu_custom_call" | custom-call | tf_op jit(solution)/shard_map/pallas_call | solution.py:129
  10.9 2.9 %collective-permute-start.1 = (f32[32,2,1024]{2,1,0:T(2,128)S(1)}, f32[32,2,1024]{2,1,0:T(2,128)S(1)}, u32[]{:S(2)}, u32[]{:S(2)}) collective-permute-start(f32[32,2,1024]{2,1,0:T(2,128)S(1)} %broadcast_select_fusion), channel_id=1, source_target_pairs={{0,2},{1,5},{2,0},{3,7},{4,6},{5,1},{6,4},{7,3},{8,10},{9,13},{10,... | collective-permute-start | bytes 786440 | tf_op jit(solution)/shard_map/ppermute | solution.py:51
  13.8 4.4 %collective-permute-done.1 = f32[32,2,1024]{2,1,0:T(2,128)S(1)} collective-permute-done((f32[32,2,1024]{2,1,0:T(2,128)S(1)}, f32[32,2,1024]{2,1,0:T(2,128)S(1)}, u32[]{:S(2)}, u32[]{:S(2)}) %collective-permute-start.1) | collective-permute-done | bytes 262176 | tf_op jit(solution)/shard_map/ppermute | solution.py:51
  18.4 2.1 %collective-permute-start.2 = (f32[32,2,512]{2,1,0:T(2,128)S(1)}, f32[32,2,512]{2,1,0:T(2,128)S(1)}, u32[]{:S(2)}, u32[]{:S(2)}) collective-permute-start(f32[32,2,512]{2,1,0:T(2,128)S(1)} %broadcast_select_fusion.1), channel_id=1, source_target_pairs={{0,4},{1,3},{2,6},{3,1},{4,0},{5,7},{6,2},{7,5},{8,12},{9,11},{10,... | collective-permute-start | bytes 393224 | tf_op jit(solution)/shard_map/ppermute | solution.py:51
  20.5 2.9 %collective-permute-done.2 = f32[32,2,512]{2,1,0:T(2,128)S(1)} collective-permute-done((f32[32,2,512]{2,1,0:T(2,128)S(1)}, f32[32,2,512]{2,1,0:T(2,128)S(1)}, u32[]{:S(2)}, u32[]{:S(2)}) %collective-permute-start.2) | collective-permute-done | bytes 131104 | tf_op jit(solution)/shard_map/ppermute | solution.py:51
  23.6 2.1 %collective-permute-start.3 = (f32[32,2,256]{2,1,0:T(2,128)S(1)}, f32[32,2,256]{2,1,0:T(2,128)S(1)}, u32[]{:S(2)}, u32[]{:S(2)}) collective-permute-start(f32[32,2,256]{2,1,0:T(2,128)S(1)} %broadcast_select_fusion.2), channel_id=1, source_target_pairs={{0,8},{1,9},{2,10},{3,11},{4,12},{5,13},{6,14},{7,15},{8,0},{9,1},... | collective-permute-start | bytes 196616 | tf_op jit(solution)/shard_map/ppermute | solution.py:51
  25.8 2.2 %collective-permute-done.3 = f32[32,2,256]{2,1,0:T(2,128)S(1)} collective-permute-done((f32[32,2,256]{2,1,0:T(2,128)S(1)}, f32[32,2,256]{2,1,0:T(2,128)S(1)}, u32[]{:S(2)}, u32[]{:S(2)}) %collective-permute-start.3) | collective-permute-done | bytes 65568 | tf_op jit(solution)/shard_map/ppermute | solution.py:51
  28.1 3.4 %collective-permute-start.4 = (f32[32,2,128]{2,1,0:T(2,128)S(1)}, f32[32,2,128]{2,1,0:T(2,128)S(1)}, u32[]{:S(2)}, u32[]{:S(2)}) collective-permute-start(f32[32,2,128]{2,1,0:T(2,128)S(1)} %broadcast_select_fusion.3), channel_id=1, source_target_pairs={{0,16},{1,17},{2,18},{3,19},{4,20},{5,21},{6,22},{7,23},{8,24},{9,... | collective-permute-start | bytes 98312 | tf_op jit(solution)/shard_map/ppermute | solution.py:51
  31.5 2.0 %collective-permute-done.4 = f32[32,2,128]{2,1,0:T(2,128)S(1)} collective-permute-done((f32[32,2,128]{2,1,0:T(2,128)S(1)}, f32[32,2,128]{2,1,0:T(2,128)S(1)}, u32[]{:S(2)}, u32[]{:S(2)}) %collective-permute-start.4) | collective-permute-done | bytes 32800 | tf_op jit(solution)/shard_map/ppermute | solution.py:51
  33.5 2.9 %collective-permute-start.5 = (f32[32,2,128]{2,1,0:T(2,128)S(1)}, f32[32,2,128]{2,1,0:T(2,128)S(1)}, u32[]{:S(2)}, u32[]{:S(2)}) collective-permute-start(f32[32,2,128]{2,1,0:T(2,128)S(1)} %select_add_fusion.3), channel_id=1, source_target_pairs={{0,16},{1,17},{2,18},{3,19},{4,20},{5,21},{6,22},{7,23},{8,24},{9,... | collective-permute-start | bytes 98312 | tf_op jit(solution)/shard_map/ppermute | solution.py:54
  36.4 2.0 %collective-permute-done.5 = f32[32,2,128]{2,1,0:T(2,128)S(1)} collective-permute-done((f32[32,2,128]{2,1,0:T(2,128)S(1)}, f32[32,2,128]{2,1,0:T(2,128)S(1)}, u32[]{:S(2)}, u32[]{:S(2)}) %collective-permute-start.5) | collective-permute-done | bytes 32800 | tf_op jit(solution)/shard_map/ppermute | solution.py:54
  38.4 2.1 %collective-permute-start.6 = (f32[32,2,256]{2,1,0:T(2,128)S(1)}, f32[32,2,256]{2,1,0:T(2,128)S(1)}, u32[]{:S(2)}, u32[]{:S(2)}) collective-permute-start(f32[32,2,256]{2,1,0:T(2,128)S(1)} %maximum_select_fusion.11), channel_id=1, source_target_pairs={{0,8},{1,9},{2,10},{3,11},{4,12},{5,13},{6,14},{7,15},{8,0},{9,1},... | collective-permute-start | bytes 196616 | tf_op jit(solution)/shard_map/ppermute | solution.py:54
  40.5 2.2 %collective-permute-done.6 = f32[32,2,256]{2,1,0:T(2,128)S(1)} collective-permute-done((f32[32,2,256]{2,1,0:T(2,128)S(1)}, f32[32,2,256]{2,1,0:T(2,128)S(1)}, u32[]{:S(2)}, u32[]{:S(2)}) %collective-permute-start.6) | collective-permute-done | bytes 65568 | tf_op jit(solution)/shard_map/ppermute | solution.py:54
  44.5 3.4 %collective-permute-done.7 = f32[32,2,512]{2,1,0:T(2,128)S(1)} collective-permute-done((f32[32,2,512]{2,1,0:T(2,128)S(1)}, f32[32,2,512]{2,1,0:T(2,128)S(1)}, u32[]{:S(2)}, u32[]{:S(2)}) %collective-permute-start.7) | collective-permute-done | bytes 131104 | tf_op jit(solution)/shard_map/ppermute | solution.py:54
  49.7 4.8 %collective-permute-done.8 = f32[32,2,1024]{2,1,0:T(2,128)S(1)} collective-permute-done((f32[32,2,1024]{2,1,0:T(2,128)S(1)}, f32[32,2,1024]{2,1,0:T(2,128)S(1)}, u32[]{:S(2)}, u32[]{:S(2)}) %collective-permute-start.8) | collective-permute-done | bytes 262176 | tf_op jit(solution)/shard_map/ppermute | solution.py:54
  57.9 4.6 %fusion.5 = f32[2,32,128]{2,1,0:T(8,128)S(1)} fusion(f32[2,128,4096]{2,1,0:T(8,128)} %param.14, f32[32,2,4096]{2,1,0:T(2,128)S(1)} %maximum_select_fusion), kind=kOutput, calls=%fused_computation.5 | convolution fusion | flops 201326592 | bytes 5275648 | tf_op jit(solution)/shard_map/qmk,mck->qmc/dot_general | solution.py:144
  62.5 3.2 %collective-permute-start.10 = (f32[32,2,128]{2,0,1:T(8,128)S(1)}, f32[32,2,128]{2,0,1:T(8,128)S(1)}, u32[]{:S(2)}, u32[]{:S(2)}) collective-permute-start(f32[32,2,128]{2,0,1:T(8,128)S(1)} %bitcast.48), channel_id=1, source_target_pairs={{0,16},{1,17},{2,18},{3,19},{4,20},{5,21},{6,22},{7,23},{8,24},{9,... | collective-permute-start | bytes 98312 | tf_op jit(solution)/shard_map/ppermute | solution.py:63
  69.5 2.5 %collective-permute-done.11 = f32[32,2,2,128]{3,0,1,2:T(8,128)S(1)} collective-permute-done((f32[32,2,2,128]{3,0,1,2:T(8,128)S(1)}, f32[32,2,2,128]{3,0,1,2:T(8,128)S(1)}, u32[]{:S(2)}, u32[]{:S(2)}) %collective-permute-start.11) | collective-permute-done | bytes 65568 | tf_op jit(solution)/shard_map/ppermute | solution.py:63
  73.6 3.4 %collective-permute-done.12 = f32[32,2,2,2,128]{4,0,1,2,3:T(8,128)S(1)} collective-permute-done((f32[32,2,2,2,128]{4,0,1,2,3:T(8,128)S(1)}, f32[32,2,2,2,128]{4,0,1,2,3:T(8,128)S(1)}, u32[]{:S(2)}, u32[]{:S(2)}) %collective-permute-start.12) | collective-permute-done | bytes 131104 | tf_op jit(solution)/shard_map/ppermute | solution.py:63
  78.7 4.8 %collective-permute-done.13 = f32[32,2,2,2,2,128]{5,0,1,2,3,4:T(8,128)S(1)} collective-permute-done((f32[32,2,2,2,2,128]{5,0,1,2,3,4:T(8,128)S(1)}, f32[32,2,2,2,2,128]{5,0,1,2,3,4:T(8,128)S(1)}, u32[]{:S(2)}, u32[]{:S(2)}) %collective-permute-start.13) | collective-permute-done | bytes 262176 | tf_op jit(solution)/shard_map/ppermute | solution.py:63
  87.3 6.5 %fusion.10 = (f32[32]{0:T(128)S(1)}, f32[32]{0:T(128)S(1)}, f32[32,128]{1,0:T(8,128)S(1)}) fusion(f32[32,2,4096]{2,0,1:T(8,128)S(1)} %select_n.249, f32[128,2,4096]{2,1,0:T(2,128)} %param.15), kind=kOutput, calls=%fused_computation.35 | convolution fusion | flops 201338816 | bytes 5259520 | tf_op jit(solution)/shard_map/qmk,nmk->qn/dot_general | solution.py:145
  96.6 2.1 %collective-permute-done.16 = f32[2,32]{1,0:T(2,128)S(1)} collective-permute-done((f32[2,32]{1,0:T(2,128)S(1)}, f32[2,32]{1,0:T(2,128)S(1)}, u32[]{:S(2)}, u32[]{:S(2)}) %collective-permute-start.16) | collective-permute-done | bytes 288 | tf_op jit(solution)/shard_map/ppermute | solution.py:74
  100.3 2.0 %collective-permute-done.17 = f32[2,32]{1,0:T(2,128)S(1)} collective-permute-done((f32[2,32]{1,0:T(2,128)S(1)}, f32[2,32]{1,0:T(2,128)S(1)}, u32[]{:S(2)}, u32[]{:S(2)}) %collective-permute-start.17) | collective-permute-done | bytes 288 | tf_op jit(solution)/shard_map/ppermute | solution.py:74
  105.9 2.9 %collective-permute-start.19 = (f32[2,32]{1,0:T(2,128)S(1)}, f32[2,32]{1,0:T(2,128)S(1)}, u32[]{:S(2)}, u32[]{:S(2)}) collective-permute-start(f32[2,32]{1,0:T(2,128)S(1)} %add.48), channel_id=1, source_target_pairs={{0,16},{1,17},{2,18},{3,19},{4,20},{5,21},{6,22},{7,23},{8,24},{9,... | collective-permute-start | bytes 776 | tf_op jit(solution)/shard_map/ppermute | solution.py:74
  (56 shorter events, 32.0 us)
Async XLA Ops:
  7.1 2.2 %collective-permute-start = (f32[32,2,2048]{2,1,0:T(2,128)}, f32[32,2,2048]{2,1,0:T(2,128)S(1)}, u32[]{:S(2)}, u32[]{:S(2)}) collective-permute-start(f32[32,2,2048]{2,1,0:T(2,128)} %get-tuple-element.8), channel_id=1, source_target_pairs={{0,1},{1,0},{2,3},{3,2},{4,5},{5,4},{6,7},{7,6},{8,9},{9,8},{10,11... | collective-permute-start | bytes 1572872 | tf_op jit(solution)/shard_map/ppermute | solution.py:43
  10.9 7.3 %collective-permute-start.1 = (f32[32,2,1024]{2,1,0:T(2,128)S(1)}, f32[32,2,1024]{2,1,0:T(2,128)S(1)}, u32[]{:S(2)}, u32[]{:S(2)}) collective-permute-start(f32[32,2,1024]{2,1,0:T(2,128)S(1)} %broadcast_select_fusion), channel_id=1, source_target_pairs={{0,2},{1,5},{2,0},{3,7},{4,6},{5,1},{6,4},{7,3},{8,10},{9,13},{10,... | collective-permute-start | bytes 786440 | tf_op jit(solution)/shard_map/ppermute | solution.py:51
  18.4 5.1 %collective-permute-start.2 = (f32[32,2,512]{2,1,0:T(2,128)S(1)}, f32[32,2,512]{2,1,0:T(2,128)S(1)}, u32[]{:S(2)}, u32[]{:S(2)}) collective-permute-start(f32[32,2,512]{2,1,0:T(2,128)S(1)} %broadcast_select_fusion.1), channel_id=1, source_target_pairs={{0,4},{1,3},{2,6},{3,1},{4,0},{5,7},{6,2},{7,5},{8,12},{9,11},{10,... | collective-permute-start | bytes 393224 | tf_op jit(solution)/shard_map/ppermute | solution.py:51
  23.6 4.4 %collective-permute-start.3 = (f32[32,2,256]{2,1,0:T(2,128)S(1)}, f32[32,2,256]{2,1,0:T(2,128)S(1)}, u32[]{:S(2)}, u32[]{:S(2)}) collective-permute-start(f32[32,2,256]{2,1,0:T(2,128)S(1)} %broadcast_select_fusion.2), channel_id=1, source_target_pairs={{0,8},{1,9},{2,10},{3,11},{4,12},{5,13},{6,14},{7,15},{8,0},{9,1},... | collective-permute-start | bytes 196616 | tf_op jit(solution)/shard_map/ppermute | solution.py:51
  28.1 5.4 %collective-permute-start.4 = (f32[32,2,128]{2,1,0:T(2,128)S(1)}, f32[32,2,128]{2,1,0:T(2,128)S(1)}, u32[]{:S(2)}, u32[]{:S(2)}) collective-permute-start(f32[32,2,128]{2,1,0:T(2,128)S(1)} %broadcast_select_fusion.3), channel_id=1, source_target_pairs={{0,16},{1,17},{2,18},{3,19},{4,20},{5,21},{6,22},{7,23},{8,24},{9,... | collective-permute-start | bytes 98312 | tf_op jit(solution)/shard_map/ppermute | solution.py:51
  33.5 4.9 %collective-permute-start.5 = (f32[32,2,128]{2,1,0:T(2,128)S(1)}, f32[32,2,128]{2,1,0:T(2,128)S(1)}, u32[]{:S(2)}, u32[]{:S(2)}) collective-permute-start(f32[32,2,128]{2,1,0:T(2,128)S(1)} %select_add_fusion.3), channel_id=1, source_target_pairs={{0,16},{1,17},{2,18},{3,19},{4,20},{5,21},{6,22},{7,23},{8,24},{9,... | collective-permute-start | bytes 98312 | tf_op jit(solution)/shard_map/ppermute | solution.py:54
  38.4 4.3 %collective-permute-start.6 = (f32[32,2,256]{2,1,0:T(2,128)S(1)}, f32[32,2,256]{2,1,0:T(2,128)S(1)}, u32[]{:S(2)}, u32[]{:S(2)}) collective-permute-start(f32[32,2,256]{2,1,0:T(2,128)S(1)} %maximum_select_fusion.11), channel_id=1, source_target_pairs={{0,8},{1,9},{2,10},{3,11},{4,12},{5,13},{6,14},{7,15},{8,0},{9,1},... | collective-permute-start | bytes 196616 | tf_op jit(solution)/shard_map/ppermute | solution.py:54
  42.8 5.0 %collective-permute-start.7 = (f32[32,2,512]{2,1,0:T(2,128)S(1)}, f32[32,2,512]{2,1,0:T(2,128)S(1)}, u32[]{:S(2)}, u32[]{:S(2)}) collective-permute-start(f32[32,2,512]{2,1,0:T(2,128)S(1)} %maximum_select_fusion.8), channel_id=1, source_target_pairs={{0,4},{1,3},{2,6},{3,1},{4,0},{5,7},{6,2},{7,5},{8,12},{9,11},{10,... | collective-permute-start | bytes 393224 | tf_op jit(solution)/shard_map/ppermute | solution.py:54
  48.1 6.4 %collective-permute-start.8 = (f32[32,2,1024]{2,1,0:T(2,128)S(1)}, f32[32,2,1024]{2,1,0:T(2,128)S(1)}, u32[]{:S(2)}, u32[]{:S(2)}) collective-permute-start(f32[32,2,1024]{2,1,0:T(2,128)S(1)} %maximum_select_fusion.5), channel_id=1, source_target_pairs={{0,2},{1,5},{2,0},{3,7},{4,6},{5,1},{6,4},{7,3},{8,10},{9,13},{10,... | collective-permute-start | bytes 786440 | tf_op jit(solution)/shard_map/ppermute | solution.py:54
  54.9 2.0 %collective-permute-start.9 = (f32[32,2,2048]{2,1,0:T(2,128)S(1)}, f32[32,2,2048]{2,1,0:T(2,128)S(1)}, u32[]{:S(2)}, u32[]{:S(2)}) collective-permute-start(f32[32,2,2048]{2,1,0:T(2,128)S(1)} %maximum_select_fusion.2), channel_id=1, source_target_pairs={{0,1},{1,0},{2,3},{3,2},{4,5},{5,4},{6,7},{7,6},{8,9},{9,8},{10,11... | collective-permute-start | bytes 1572872 | tf_op jit(solution)/shard_map/ppermute | solution.py:54
  62.5 5.1 %collective-permute-start.10 = (f32[32,2,128]{2,0,1:T(8,128)S(1)}, f32[32,2,128]{2,0,1:T(8,128)S(1)}, u32[]{:S(2)}, u32[]{:S(2)}) collective-permute-start(f32[32,2,128]{2,0,1:T(8,128)S(1)} %bitcast.48), channel_id=1, source_target_pairs={{0,16},{1,17},{2,18},{3,19},{4,20},{5,21},{6,22},{7,23},{8,24},{9,... | collective-permute-start | bytes 98312 | tf_op jit(solution)/shard_map/ppermute | solution.py:63
  67.6 4.3 %collective-permute-start.11 = (f32[32,2,2,128]{3,0,1,2:T(8,128)S(1)}, f32[32,2,2,128]{3,0,1,2:T(8,128)S(1)}, u32[]{:S(2)}, u32[]{:S(2)}) collective-permute-start(f32[32,2,2,128]{3,0,1,2:T(8,128)S(1)} %maximum_select_fusion.13), channel_id=1, source_target_pairs={{0,8},{1,9},{2,10},{3,11},{4,12},{5,13},{6,14},{7,15},{8,0},{9,1},... | collective-permute-start | bytes 196616 | tf_op jit(solution)/shard_map/ppermute | solution.py:63
  72.0 5.0 %collective-permute-start.12 = (f32[32,2,2,2,128]{4,0,1,2,3:T(8,128)S(1)}, f32[32,2,2,2,128]{4,0,1,2,3:T(8,128)S(1)}, u32[]{:S(2)}, u32[]{:S(2)}) collective-permute-start(f32[32,2,2,2,128]{4,0,1,2,3:T(8,128)S(1)} %maximum_select_fusion.10), channel_id=1, source_target_pairs={{0,4},{1,5},{2,6},{3,7},{4,0},{5,1},{6,2},{7,3},{8,12},{9,13},{10,... | collective-permute-start | bytes 393224 | tf_op jit(solution)/shard_map/ppermute | solution.py:63
  77.0 6.4 %collective-permute-start.13 = (f32[32,2,2,2,2,128]{5,0,1,2,3,4:T(8,128)S(1)}, f32[32,2,2,2,2,128]{5,0,1,2,3,4:T(8,128)S(1)}, u32[]{:S(2)}, u32[]{:S(2)}) collective-permute-start(f32[32,2,2,2,2,128]{5,0,1,2,3,4:T(8,128)S(1)} %maximum_select_fusion.7), channel_id=1, source_target_pairs={{0,2},{1,3},{2,0},{3,1},{4,6},{5,7},{6,4},{7,5},{8,10},{9,11},{10,... | collective-permute-start | bytes 786440 | tf_op jit(solution)/shard_map/ppermute | solution.py:63
  83.5 2.0 %collective-permute-start.14 = (f32[32,2,2,2,2,2,128]{6,0,1,2,3,4,5:T(8,128)S(1)}, f32[32,2,2,2,2,2,128]{6,0,1,2,3,4,5:T(8,128)S(1)}, u32[]{:S(2)}, u32[]{:S(2)}) collective-permute-start(f32[32,2,2,2,2,2,128]{6,0,1,2,3,4,5:T(8,128)S(1)} %maximum_select_fusion.4), channel_id=1, source_target_pairs={{0,1},{1,0},{2,3},{3,2},{4,5},{5,4},{6,7},{7,6},{8,9},{9,8},{10,11... | collective-permute-start | bytes 1572872 | tf_op jit(solution)/shard_map/ppermute | solution.py:63
  93.8 1.2 %collective-permute-start.15 = (f32[2,32]{1,0:T(2,128)S(1)}, f32[2,32]{1,0:T(2,128)S(1)}, u32[]{:S(2)}, u32[]{:S(2)}) collective-permute-start(f32[2,32]{1,0:T(2,128)S(1)} %pad_maximum_fusion), channel_id=1, source_target_pairs={{0,1},{1,0},{2,3},{3,2},{4,5},{5,4},{6,7},{7,6},{8,9},{9,8},{10,11... | collective-permute-start | bytes 776 | tf_op jit(solution)/shard_map/ppermute | solution.py:74
  95.0 3.6 %collective-permute-start.16 = (f32[2,32]{1,0:T(2,128)S(1)}, f32[2,32]{1,0:T(2,128)S(1)}, u32[]{:S(2)}, u32[]{:S(2)}) collective-permute-start(f32[2,32]{1,0:T(2,128)S(1)} %fusion.9), channel_id=1, source_target_pairs={{0,2},{1,3},{2,0},{3,1},{4,6},{5,7},{6,4},{7,5},{8,10},{9,11},{10,... | collective-permute-start | bytes 776 | tf_op jit(solution)/shard_map/ppermute | solution.py:74
  98.7 3.6 %collective-permute-start.17 = (f32[2,32]{1,0:T(2,128)S(1)}, f32[2,32]{1,0:T(2,128)S(1)}, u32[]{:S(2)}, u32[]{:S(2)}) collective-permute-start(f32[2,32]{1,0:T(2,128)S(1)} %fusion.13), channel_id=1, source_target_pairs={{0,4},{1,5},{2,6},{3,7},{4,0},{5,1},{6,2},{7,3},{8,12},{9,13},{10,... | collective-permute-start | bytes 776 | tf_op jit(solution)/shard_map/ppermute | solution.py:74
  102.3 3.6 %collective-permute-start.18 = (f32[2,32]{1,0:T(2,128)S(1)}, f32[2,32]{1,0:T(2,128)S(1)}, u32[]{:S(2)}, u32[]{:S(2)}) collective-permute-start(f32[2,32]{1,0:T(2,128)S(1)} %add.47), channel_id=1, source_target_pairs={{0,8},{1,9},{2,10},{3,11},{4,12},{5,13},{6,14},{7,15},{8,0},{9,1},... | collective-permute-start | bytes 776 | tf_op jit(solution)/shard_map/ppermute | solution.py:74
  105.9 4.5 %collective-permute-start.19 = (f32[2,32]{1,0:T(2,128)S(1)}, f32[2,32]{1,0:T(2,128)S(1)}, u32[]{:S(2)}, u32[]{:S(2)}) collective-permute-start(f32[2,32]{1,0:T(2,128)S(1)} %add.48), channel_id=1, source_target_pairs={{0,16},{1,17},{2,18},{3,19},{4,20},{5,21},{6,22},{7,23},{8,24},{9,... | collective-permute-start | bytes 776 | tf_op jit(solution)/shard_map/ppermute | solution.py:74

commit v8 on v7

--- a/solution.py
+++ b/solution.py
@@ -35,24 +35,33 @@
     return [(i, i ^ (1 << orders[i & 1][t])) for i in range(size)]
 
 
-def _allreduce(keep, send, size, axis):
+def _allreduce_apply(keep, send, size, apply):
     me = lax.axis_index("rows")
     orders = _orders(size)
     steps = _steps(size)
     bits = [jnp.where((me & 1) == 0, (me >> orders[0][t]) & 1, (me >> orders[1][t]) & 1) for t in range(steps)]
+    width = 2 * keep.shape[-1]
+    base = bits[0] * (width // 2)
     cur = keep + lax.ppermute(send, "rows", _pairs(size, orders, 0))
     for t in range(1, steps):
-        half = cur.shape[axis] // 2
-        lo = lax.slice_in_dim(cur, 0, half, axis=axis)
-        hi = lax.slice_in_dim(cur, half, 2 * half, axis=axis)
+        half = cur.shape[-1] // 2
+        lo = cur[..., :half]
+        hi = cur[..., half:]
         low = bits[t] == 0
         keep = jnp.where(low, lo, hi)
         send = jnp.where(low, hi, lo)
+        base = base + bits[t] * half
         cur = keep + lax.ppermute(send, "rows", _pairs(size, orders, t))
+    total = apply(cur, base)
     for t in reversed(range(steps)):
         low = bits[t] == 0
-        cur = _join(cur, lax.ppermute(cur, "rows", _pairs(size, orders, t)), low, axis)
-    return cur
+        span = cur.shape[-1]
+        other = lax.ppermute(cur, "rows", _pairs(size, orders, t))
+        total = total + apply(other, jnp.where(low, base + span, base - span))
+        if t:
+            cur = _join(cur, other, low, cur.ndim - 1)
+            base = jnp.where(low, base, base - span)
+    return total
 
 
 def _allgather(x, size):
@@ -140,8 +149,12 @@
     queries = lengths.shape[0]
     flat_width = proj_rank * proj_rank
     keep, send = _module_sums(lengths, valid, acts, grads_out, proj_in, proj_out)
-    summed = _allreduce(keep, send, size, 2)
-    precond_cols = jnp.einsum("qmk,mck->qmc", summed, fisher_inv, precision=lax.Precision.HIGH)
+
+    def precond_part(piece, offset):
+        block = lax.dynamic_slice_in_dim(fisher_inv, offset, piece.shape[-1], axis=2)
+        return jnp.einsum("qmk,mck->qmc", piece, block, precision=lax.Precision.HIGH)
+
+    precond_cols = _allreduce_apply(keep, send, size, precond_part)
     scores = jnp.einsum(
         "qmk,nmk->qn",
         _allgather(precond_cols, size),

time: 111 us -> 113 us (1.018)
  matrix products: 11.1 us -> 16 us
  waiting for transfers between devices: 50.6 us -> 48.2 us
    dot_general x1 -> x6, matrix products: 4.63 us -> 9.53 us  [precond_part(): jnp.einsum('qmk,mck->qmc', piece, block, precision=lax.Precision.HIGH)]
    ppermute x10, waiting for transfers between devices: 27.6 us -> 24.6 us  [the longest x4 11.5 us: _allreduce_apply(): cur = keep + lax.ppermute(send, 'rows', _pairs(size, orders, t))]
  transfers between devices with their start and end apart: 20 -> 20, of which waited for: 20 -> 19; matrix products, arithmetic and copies ran while one was open for 0% -> 5% of each run, Pallas kernels for 0% -> 0%
where the time goes in v8:
time: 113 us; the launch traced here: 112 us
  waiting for transfers between devices  48.2 us (43%)
  starting transfers between devices  35.3 us (31%)
  matrix products  16 us (14%)
  Pallas kernels  7.14 us (6%)
  other arithmetic  3.71 us (3%)
  local copies, waits for them, and re-layouts  1.65 us (1%)
    ppermute x5, waiting for transfers between devices, _allgather(): other = lax.ppermute(cur, 'rows', _xor_pairs(size, s))  14.7 us
    ppermute x4, waiting for transfers between devices, _allreduce_apply(): cur = keep + lax.ppermute(send, 'rows', _pairs(size, orders, t))  11.5 us
    ppermute x5, waiting for transfers between devices, _allreduce_apply(): other = lax.ppermute(cur, 'rows', _pairs(size, orders, t))  11.4 us
    ppermute x4, starting transfers between devices, _allreduce_apply(): cur = keep + lax.ppermute(send, 'rows', _pairs(size, orders, t))  10.6 us
    dot_general x6, matrix products, precond_part(): jnp.einsum('qmk,mck->qmc', piece, block, precision=lax.Precision.HIGH)  9.53 us
    ppermute x5, waiting for transfers between devices, _butterfly_sum(): x = x + lax.ppermute(x, 'rows', _xor_pairs(size, s))  8.79 us
    ppermute x5, starting transfers between devices, _allreduce_apply(): other = lax.ppermute(cur, 'rows', _pairs(size, orders, t))  8.27 us
    ppermute x5, starting transfers between devices, _allgather(): other = lax.ppermute(cur, 'rows', _xor_pairs(size, s))  8.16 us
  transfers between devices with their start and end apart: 20, of which 19 were waited for; matrix products, arithmetic and copies ran while one was open for 5% of the time, Pallas kernels for 0%

profile of v8, /device:TPU:0, one launch (start us, length us, event | category | flops | bytes accessed | tf_op | source)
XLA Modules:
  0.0 112.2 jit_solution(3260304253710172705)
XLA Ops:
  0.0 7.1 %shard_map.82 = (f32[32,2,2048]{2,1,0:T(2,128)}, f32[32,2,2048]{2,1,0:T(2,128)}) custom-call(s32[1,32]{1,0:T(1,128)} %bitcast.61, s32[1,128]{1,0:T(1,128)} %bitcast.62, bf16[128,2,4096]{2,1,0:T(2,128)(2,1)} %acts_ref.1, bf16[128,2,4096]{2,1,0:T(2,128)(2,1)} %gout_ref.1, bf16[4096,128]{1,0:T(8,128)(2,1)} %pin_ref.1, bf16[4096,128]{1,0:T(8,128)(2,1)} %pout_ref.1), custom_call_target="tpu_custom_call" | custom-call | tf_op jit(solution)/shard_map/pallas_call | solution.py:138
  10.9 2.9 %collective-permute-start.1 = (f32[32,2,1024]{2,1,0:T(2,128)S(1)}, f32[32,2,1024]{2,1,0:T(2,128)S(1)}, u32[]{:S(2)}, u32[]{:S(2)}) collective-permute-start(f32[32,2,1024]{2,1,0:T(2,128)S(1)} %broadcast_select_fusion), channel_id=1, source_target_pairs={{0,2},{1,5},{2,0},{3,7},{4,6},{5,1},{6,4},{7,3},{8,10},{9,13},{10,... | collective-permute-start | bytes 786440 | tf_op jit(solution)/shard_map/ppermute | solution.py:54
  13.8 4.4 %collective-permute-done.1 = f32[32,2,1024]{2,1,0:T(2,128)S(1)} collective-permute-done((f32[32,2,1024]{2,1,0:T(2,128)S(1)}, f32[32,2,1024]{2,1,0:T(2,128)S(1)}, u32[]{:S(2)}, u32[]{:S(2)}) %collective-permute-start.1) | collective-permute-done | bytes 262176 | tf_op jit(solution)/shard_map/ppermute | solution.py:54
  18.4 2.1 %collective-permute-start.2 = (f32[32,2,512]{2,1,0:T(2,128)S(1)}, f32[32,2,512]{2,1,0:T(2,128)S(1)}, u32[]{:S(2)}, u32[]{:S(2)}) collective-permute-start(f32[32,2,512]{2,1,0:T(2,128)S(1)} %broadcast_select_fusion.1), channel_id=1, source_target_pairs={{0,4},{1,3},{2,6},{3,1},{4,0},{5,7},{6,2},{7,5},{8,12},{9,11},{10,... | collective-permute-start | bytes 393224 | tf_op jit(solution)/shard_map/ppermute | solution.py:54
  20.5 2.9 %collective-permute-done.2 = f32[32,2,512]{2,1,0:T(2,128)S(1)} collective-permute-done((f32[32,2,512]{2,1,0:T(2,128)S(1)}, f32[32,2,512]{2,1,0:T(2,128)S(1)}, u32[]{:S(2)}, u32[]{:S(2)}) %collective-permute-start.2) | collective-permute-done | bytes 131104 | tf_op jit(solution)/shard_map/ppermute | solution.py:54
  23.6 2.1 %collective-permute-start.3 = (f32[32,2,256]{2,1,0:T(2,128)S(1)}, f32[32,2,256]{2,1,0:T(2,128)S(1)}, u32[]{:S(2)}, u32[]{:S(2)}) collective-permute-start(f32[32,2,256]{2,1,0:T(2,128)S(1)} %broadcast_select_fusion.2), channel_id=1, source_target_pairs={{0,8},{1,9},{2,10},{3,11},{4,12},{5,13},{6,14},{7,15},{8,0},{9,1},... | collective-permute-start | bytes 196616 | tf_op jit(solution)/shard_map/ppermute | solution.py:54
  25.8 2.2 %collective-permute-done.3 = f32[32,2,256]{2,1,0:T(2,128)S(1)} collective-permute-done((f32[32,2,256]{2,1,0:T(2,128)S(1)}, f32[32,2,256]{2,1,0:T(2,128)S(1)}, u32[]{:S(2)}, u32[]{:S(2)}) %collective-permute-start.3) | collective-permute-done | bytes 65568 | tf_op jit(solution)/shard_map/ppermute | solution.py:54
  28.1 3.4 %collective-permute-start.4 = (f32[32,2,128]{2,1,0:T(2,128)S(1)}, f32[32,2,128]{2,1,0:T(2,128)S(1)}, u32[]{:S(2)}, u32[]{:S(2)}) collective-permute-start(f32[32,2,128]{2,1,0:T(2,128)S(1)} %broadcast_select_fusion.3), channel_id=1, source_target_pairs={{0,16},{1,17},{2,18},{3,19},{4,20},{5,21},{6,22},{7,23},{8,24},{9,... | collective-permute-start | bytes 98312 | tf_op jit(solution)/shard_map/ppermute | solution.py:54
  31.5 2.0 %collective-permute-done.4 = f32[32,2,128]{2,1,0:T(2,128)S(1)} collective-permute-done((f32[32,2,128]{2,1,0:T(2,128)S(1)}, f32[32,2,128]{2,1,0:T(2,128)S(1)}, u32[]{:S(2)}, u32[]{:S(2)}) %collective-permute-start.4) | collective-permute-done | bytes 32800 | tf_op jit(solution)/shard_map/ppermute | solution.py:54
  33.5 2.9 %collective-permute-start.5 = (f32[32,2,128]{2,1,0:T(2,128)S(1)}, f32[32,2,128]{2,1,0:T(2,128)S(1)}, u32[]{:S(2)}, u32[]{:S(2)}) collective-permute-start(f32[32,2,128]{2,1,0:T(2,128)S(1)} %select_add_fusion.3), channel_id=1, source_target_pairs={{0,16},{1,17},{2,18},{3,19},{4,20},{5,21},{6,22},{7,23},{8,24},{9,... | collective-permute-start | bytes 98312 | tf_op jit(solution)/shard_map/ppermute | solution.py:59
  38.4 2.1 %collective-permute-start.6 = (f32[32,2,256]{2,1,0:T(2,128)S(1)}, f32[32,2,256]{2,1,0:T(2,128)S(1)}, u32[]{:S(2)}, u32[]{:S(2)}) collective-permute-start(f32[32,2,256]{2,1,0:T(2,128)S(1)} %maximum_select_fusion.10), channel_id=1, source_target_pairs={{0,8},{1,9},{2,10},{3,11},{4,12},{5,13},{6,14},{7,15},{8,0},{9,1},... | collective-permute-start | bytes 196616 | tf_op jit(solution)/shard_map/ppermute | solution.py:59
  40.5 2.2 %collective-permute-done.6 = f32[32,2,256]{2,1,0:T(2,128)S(1)} collective-permute-done((f32[32,2,256]{2,1,0:T(2,128)S(1)}, f32[32,2,256]{2,1,0:T(2,128)S(1)}, u32[]{:S(2)}, u32[]{:S(2)}) %collective-permute-start.6) | collective-permute-done | bytes 65568 | tf_op jit(solution)/shard_map/ppermute | solution.py:59
  44.5 3.4 %collective-permute-done.7 = f32[32,2,512]{2,1,0:T(2,128)S(1)} collective-permute-done((f32[32,2,512]{2,1,0:T(2,128)S(1)}, f32[32,2,512]{2,1,0:T(2,128)S(1)}, u32[]{:S(2)}, u32[]{:S(2)}) %collective-permute-start.7) | collective-permute-done | bytes 131104 | tf_op jit(solution)/shard_map/ppermute | solution.py:59
  50.8 3.7 %collective-permute-done.8 = f32[32,2,1024]{2,1,0:T(2,128)S(1)} collective-permute-done((f32[32,2,1024]{2,1,0:T(2,128)S(1)}, f32[32,2,1024]{2,1,0:T(2,128)S(1)}, u32[]{:S(2)}, u32[]{:S(2)}) %collective-permute-start.8) | collective-permute-done | bytes 262176 | tf_op jit(solution)/shard_map/ppermute | solution.py:59
  59.5 2.8 %fusion.2 = f32[2,128,32]{1,2,0:T(8,128)S(1)} fusion(f32[2,128,4096]{2,1,0:T(8,128)} %param.14, s32[]{:T(128)S(6)} %select_n.283, f32[32,2,2048]{2,1,0:T(2,128)S(1)} %collective-permute-done.9), kind=kOutput, calls=%fused_computation.2 | convolution fusion | flops 100663296 | bytes 2654212 | tf_op jit(solution)/shard_map/qmk,mck->qmc/dot_general | solution.py:155
  63.5 3.2 %collective-permute-start.10 = (f32[32,2,128]{2,0,1:T(8,128)S(1)}, f32[32,2,128]{2,0,1:T(8,128)S(1)}, u32[]{:S(2)}, u32[]{:S(2)}) collective-permute-start(f32[32,2,128]{2,0,1:T(8,128)S(1)} %bitcast.48), channel_id=1, source_target_pairs={{0,16},{1,17},{2,18},{3,19},{4,20},{5,21},{6,22},{7,23},{8,24},{9,... | collective-permute-start | bytes 98312 | tf_op jit(solution)/shard_map/ppermute | solution.py:72
  66.7 2.0 %collective-permute-done.10 = f32[32,2,128]{2,0,1:T(8,128)S(1)} collective-permute-done((f32[32,2,128]{2,0,1:T(8,128)S(1)}, f32[32,2,128]{2,0,1:T(8,128)S(1)}, u32[]{:S(2)}, u32[]{:S(2)}) %collective-permute-start.10) | collective-permute-done | bytes 32800 | tf_op jit(solution)/shard_map/ppermute | solution.py:72
  70.5 2.6 %collective-permute-done.11 = f32[32,2,2,128]{3,0,1,2:T(8,128)S(1)} collective-permute-done((f32[32,2,2,128]{3,0,1,2:T(8,128)S(1)}, f32[32,2,2,128]{3,0,1,2:T(8,128)S(1)}, u32[]{:S(2)}, u32[]{:S(2)}) %collective-permute-start.11) | collective-permute-done | bytes 65568 | tf_op jit(solution)/shard_map/ppermute | solution.py:72
  74.7 3.4 %collective-permute-done.12 = f32[32,2,2,2,128]{4,0,1,2,3:T(8,128)S(1)} collective-permute-done((f32[32,2,2,2,128]{4,0,1,2,3:T(8,128)S(1)}, f32[32,2,2,2,128]{4,0,1,2,3:T(8,128)S(1)}, u32[]{:S(2)}, u32[]{:S(2)}) %collective-permute-start.12) | collective-permute-done | bytes 131104 | tf_op jit(solution)/shard_map/ppermute | solution.py:72
  79.8 4.8 %collective-permute-done.13 = f32[32,2,2,2,2,128]{5,0,1,2,3,4:T(8,128)S(1)} collective-permute-done((f32[32,2,2,2,2,128]{5,0,1,2,3,4:T(8,128)S(1)}, f32[32,2,2,2,2,128]{5,0,1,2,3,4:T(8,128)S(1)}, u32[]{:S(2)}, u32[]{:S(2)}) %collective-permute-start.13) | collective-permute-done | bytes 262176 | tf_op jit(solution)/shard_map/ppermute | solution.py:72
  88.4 6.5 %fusion.35 = (f32[32]{0:T(128)S(1)}, f32[32]{0:T(128)S(1)}, f32[32,128]{1,0:T(8,128)S(1)}) fusion(f32[32,2,4096]{2,0,1:T(8,128)S(1)} %select_n.299, f32[128,2,4096]{2,1,0:T(2,128)} %param.15), kind=kOutput, calls=%fused_computation.60 | convolution fusion | flops 201338816 | bytes 5259520 | tf_op jit(solution)/shard_map/qmk,nmk->qn/dot_general | solution.py:158
  97.7 2.1 %collective-permute-done.16 = f32[2,32]{1,0:T(2,128)S(1)} collective-permute-done((f32[2,32]{1,0:T(2,128)S(1)}, f32[2,32]{1,0:T(2,128)S(1)}, u32[]{:S(2)}, u32[]{:S(2)}) %collective-permute-start.16) | collective-permute-done | bytes 288 | tf_op jit(solution)/shard_map/ppermute | solution.py:83
  101.4 2.0 %collective-permute-done.17 = f32[2,32]{1,0:T(2,128)S(1)} collective-permute-done((f32[2,32]{1,0:T(2,128)S(1)}, f32[2,32]{1,0:T(2,128)S(1)}, u32[]{:S(2)}, u32[]{:S(2)}) %collective-permute-start.17) | collective-permute-done | bytes 288 | tf_op jit(solution)/shard_map/ppermute | solution.py:83
  107.0 2.8 %collective-permute-start.19 = (f32[2,32]{1,0:T(2,128)S(1)}, f32[2,32]{1,0:T(2,128)S(1)}, u32[]{:S(2)}, u32[]{:S(2)}) collective-permute-start(f32[2,32]{1,0:T(2,128)S(1)} %add.140), channel_id=1, source_target_pairs={{0,16},{1,17},{2,18},{3,19},{4,20},{5,21},{6,22},{7,23},{8,24},{9,... | collective-permute-start | bytes 776 | tf_op jit(solution)/shard_map/ppermute | solution.py:83
  (60 shorter events, 35.9 us)
Async XLA Ops:
  7.1 2.2 %collective-permute-start = (f32[32,2,2048]{2,1,0:T(2,128)}, f32[32,2,2048]{2,1,0:T(2,128)S(1)}, u32[]{:S(2)}, u32[]{:S(2)}) collective-permute-start(f32[32,2,2048]{2,1,0:T(2,128)} %get-tuple-element.8), channel_id=1, source_target_pairs={{0,1},{1,0},{2,3},{3,2},{4,5},{5,4},{6,7},{7,6},{8,9},{9,8},{10,11... | collective-permute-start | bytes 1572872 | tf_op jit(solution)/shard_map/ppermute | solution.py:45
  10.9 7.3 %collective-permute-start.1 = (f32[32,2,1024]{2,1,0:T(2,128)S(1)}, f32[32,2,1024]{2,1,0:T(2,128)S(1)}, u32[]{:S(2)}, u32[]{:S(2)}) collective-permute-start(f32[32,2,1024]{2,1,0:T(2,128)S(1)} %broadcast_select_fusion), channel_id=1, source_target_pairs={{0,2},{1,5},{2,0},{3,7},{4,6},{5,1},{6,4},{7,3},{8,10},{9,13},{10,... | collective-permute-start | bytes 786440 | tf_op jit(solution)/shard_map/ppermute | solution.py:54
  18.4 5.1 %collective-permute-start.2 = (f32[32,2,512]{2,1,0:T(2,128)S(1)}, f32[32,2,512]{2,1,0:T(2,128)S(1)}, u32[]{:S(2)}, u32[]{:S(2)}) collective-permute-start(f32[32,2,512]{2,1,0:T(2,128)S(1)} %broadcast_select_fusion.1), channel_id=1, source_target_pairs={{0,4},{1,3},{2,6},{3,1},{4,0},{5,7},{6,2},{7,5},{8,12},{9,11},{10,... | collective-permute-start | bytes 393224 | tf_op jit(solution)/shard_map/ppermute | solution.py:54
  23.6 4.4 %collective-permute-start.3 = (f32[32,2,256]{2,1,0:T(2,128)S(1)}, f32[32,2,256]{2,1,0:T(2,128)S(1)}, u32[]{:S(2)}, u32[]{:S(2)}) collective-permute-start(f32[32,2,256]{2,1,0:T(2,128)S(1)} %broadcast_select_fusion.2), channel_id=1, source_target_pairs={{0,8},{1,9},{2,10},{3,11},{4,12},{5,13},{6,14},{7,15},{8,0},{9,1},... | collective-permute-start | bytes 196616 | tf_op jit(solution)/shard_map/ppermute | solution.py:54
  28.1 5.4 %collective-permute-start.4 = (f32[32,2,128]{2,1,0:T(2,128)S(1)}, f32[32,2,128]{2,1,0:T(2,128)S(1)}, u32[]{:S(2)}, u32[]{:S(2)}) collective-permute-start(f32[32,2,128]{2,1,0:T(2,128)S(1)} %broadcast_select_fusion.3), channel_id=1, source_target_pairs={{0,16},{1,17},{2,18},{3,19},{4,20},{5,21},{6,22},{7,23},{8,24},{9,... | collective-permute-start | bytes 98312 | tf_op jit(solution)/shard_map/ppermute | solution.py:54
  33.5 4.9 %collective-permute-start.5 = (f32[32,2,128]{2,1,0:T(2,128)S(1)}, f32[32,2,128]{2,1,0:T(2,128)S(1)}, u32[]{:S(2)}, u32[]{:S(2)}) collective-permute-start(f32[32,2,128]{2,1,0:T(2,128)S(1)} %select_add_fusion.3), channel_id=1, source_target_pairs={{0,16},{1,17},{2,18},{3,19},{4,20},{5,21},{6,22},{7,23},{8,24},{9,... | collective-permute-start | bytes 98312 | tf_op jit(solution)/shard_map/ppermute | solution.py:59
  38.4 4.3 %collective-permute-start.6 = (f32[32,2,256]{2,1,0:T(2,128)S(1)}, f32[32,2,256]{2,1,0:T(2,128)S(1)}, u32[]{:S(2)}, u32[]{:S(2)}) collective-permute-start(f32[32,2,256]{2,1,0:T(2,128)S(1)} %maximum_select_fusion.10), channel_id=1, source_target_pairs={{0,8},{1,9},{2,10},{3,11},{4,12},{5,13},{6,14},{7,15},{8,0},{9,1},... | collective-permute-start | bytes 196616 | tf_op jit(solution)/shard_map/ppermute | solution.py:59
  42.8 5.0 %collective-permute-start.7 = (f32[32,2,512]{2,1,0:T(2,128)S(1)}, f32[32,2,512]{2,1,0:T(2,128)S(1)}, u32[]{:S(2)}, u32[]{:S(2)}) collective-permute-start(f32[32,2,512]{2,1,0:T(2,128)S(1)} %maximum_select_fusion.7), channel_id=1, source_target_pairs={{0,4},{1,3},{2,6},{3,1},{4,0},{5,7},{6,2},{7,5},{8,12},{9,11},{10,... | collective-permute-start | bytes 393224 | tf_op jit(solution)/shard_map/ppermute | solution.py:59
  48.1 6.4 %collective-permute-start.8 = (f32[32,2,1024]{2,1,0:T(2,128)S(1)}, f32[32,2,1024]{2,1,0:T(2,128)S(1)}, u32[]{:S(2)}, u32[]{:S(2)}) collective-permute-start(f32[32,2,1024]{2,1,0:T(2,128)S(1)} %maximum_select_fusion.4), channel_id=1, source_target_pairs={{0,2},{1,5},{2,0},{3,7},{4,6},{5,1},{6,4},{7,3},{8,10},{9,13},{10,... | collective-permute-start | bytes 786440 | tf_op jit(solution)/shard_map/ppermute | solution.py:59
  54.9 4.5 %collective-permute-start.9 = (f32[32,2,2048]{2,1,0:T(2,128)S(1)}, f32[32,2,2048]{2,1,0:T(2,128)S(1)}, u32[]{:S(2)}, u32[]{:S(2)}) collective-permute-start(f32[32,2,2048]{2,1,0:T(2,128)S(1)} %maximum_select_fusion.1), channel_id=1, source_target_pairs={{0,1},{1,0},{2,3},{3,2},{4,5},{5,4},{6,7},{7,6},{8,9},{9,8},{10,11... | collective-permute-start | bytes 1572872 | tf_op jit(solution)/shard_map/ppermute | solution.py:59
  63.5 5.3 %collective-permute-start.10 = (f32[32,2,128]{2,0,1:T(8,128)S(1)}, f32[32,2,128]{2,0,1:T(8,128)S(1)}, u32[]{:S(2)}, u32[]{:S(2)}) collective-permute-start(f32[32,2,128]{2,0,1:T(8,128)S(1)} %bitcast.48), channel_id=1, source_target_pairs={{0,16},{1,17},{2,18},{3,19},{4,20},{5,21},{6,22},{7,23},{8,24},{9,... | collective-permute-start | bytes 98312 | tf_op jit(solution)/shard_map/ppermute | solution.py:72
  68.8 4.3 %collective-permute-start.11 = (f32[32,2,2,128]{3,0,1,2:T(8,128)S(1)}, f32[32,2,2,128]{3,0,1,2:T(8,128)S(1)}, u32[]{:S(2)}, u32[]{:S(2)}) collective-permute-start(f32[32,2,2,128]{3,0,1,2:T(8,128)S(1)} %maximum_select_fusion.12), channel_id=1, source_target_pairs={{0,8},{1,9},{2,10},{3,11},{4,12},{5,13},{6,14},{7,15},{8,0},{9,1},... | collective-permute-start | bytes 196616 | tf_op jit(solution)/shard_map/ppermute | solution.py:72
  73.1 5.0 %collective-permute-start.12 = (f32[32,2,2,2,128]{4,0,1,2,3:T(8,128)S(1)}, f32[32,2,2,2,128]{4,0,1,2,3:T(8,128)S(1)}, u32[]{:S(2)}, u32[]{:S(2)}) collective-permute-start(f32[32,2,2,2,128]{4,0,1,2,3:T(8,128)S(1)} %maximum_select_fusion.9), channel_id=1, source_target_pairs={{0,4},{1,5},{2,6},{3,7},{4,0},{5,1},{6,2},{7,3},{8,12},{9,13},{10,... | collective-permute-start | bytes 393224 | tf_op jit(solution)/shard_map/ppermute | solution.py:72
  78.2 6.4 %collective-permute-start.13 = (f32[32,2,2,2,2,128]{5,0,1,2,3,4:T(8,128)S(1)}, f32[32,2,2,2,2,128]{5,0,1,2,3,4:T(8,128)S(1)}, u32[]{:S(2)}, u32[]{:S(2)}) collective-permute-start(f32[32,2,2,2,2,128]{5,0,1,2,3,4:T(8,128)S(1)} %maximum_select_fusion.6), channel_id=1, source_target_pairs={{0,2},{1,3},{2,0},{3,1},{4,6},{5,7},{6,4},{7,5},{8,10},{9,11},{10,... | collective-permute-start | bytes 786440 | tf_op jit(solution)/shard_map/ppermute | solution.py:72
  84.7 2.0 %collective-permute-start.14 = (f32[32,2,2,2,2,2,128]{6,0,1,2,3,4,5:T(8,128)S(1)}, f32[32,2,2,2,2,2,128]{6,0,1,2,3,4,5:T(8,128)S(1)}, u32[]{:S(2)}, u32[]{:S(2)}) collective-permute-start(f32[32,2,2,2,2,2,128]{6,0,1,2,3,4,5:T(8,128)S(1)} %maximum_select_fusion.3), channel_id=1, source_target_pairs={{0,1},{1,0},{2,3},{3,2},{4,5},{5,4},{6,7},{7,6},{8,9},{9,8},{10,11... | collective-permute-start | bytes 1572872 | tf_op jit(solution)/shard_map/ppermute | solution.py:72
  94.9 1.2 %collective-permute-start.15 = (f32[2,32]{1,0:T(2,128)S(1)}, f32[2,32]{1,0:T(2,128)S(1)}, u32[]{:S(2)}, u32[]{:S(2)}) collective-permute-start(f32[2,32]{1,0:T(2,128)S(1)} %pad_maximum_fusion), channel_id=1, source_target_pairs={{0,1},{1,0},{2,3},{3,2},{4,5},{5,4},{6,7},{7,6},{8,9},{9,8},{10,11... | collective-permute-start | bytes 776 | tf_op jit(solution)/shard_map/ppermute | solution.py:83
  96.2 3.6 %collective-permute-start.16 = (f32[2,32]{1,0:T(2,128)S(1)}, f32[2,32]{1,0:T(2,128)S(1)}, u32[]{:S(2)}, u32[]{:S(2)}) collective-permute-start(f32[2,32]{1,0:T(2,128)S(1)} %fusion.34), channel_id=1, source_target_pairs={{0,2},{1,3},{2,0},{3,1},{4,6},{5,7},{6,4},{7,5},{8,10},{9,11},{10,... | collective-permute-start | bytes 776 | tf_op jit(solution)/shard_map/ppermute | solution.py:83
  99.8 3.6 %collective-permute-start.17 = (f32[2,32]{1,0:T(2,128)S(1)}, f32[2,32]{1,0:T(2,128)S(1)}, u32[]{:S(2)}, u32[]{:S(2)}) collective-permute-start(f32[2,32]{1,0:T(2,128)S(1)} %fusion.37), channel_id=1, source_target_pairs={{0,4},{1,5},{2,6},{3,7},{4,0},{5,1},{6,2},{7,3},{8,12},{9,13},{10,... | collective-permute-start | bytes 776 | tf_op jit(solution)/shard_map/ppermute | solution.py:83
  103.4 3.6 %collective-permute-start.18 = (f32[2,32]{1,0:T(2,128)S(1)}, f32[2,32]{1,0:T(2,128)S(1)}, u32[]{:S(2)}, u32[]{:S(2)}) collective-permute-start(f32[2,32]{1,0:T(2,128)S(1)} %add.139), channel_id=1, source_target_pairs={{0,8},{1,9},{2,10},{3,11},{4,12},{5,13},{6,14},{7,15},{8,0},{9,1},... | collective-permute-start | bytes 776 | tf_op jit(solution)/shard_map/ppermute | solution.py:83
  107.0 4.5 %collective-permute-start.19 = (f32[2,32]{1,0:T(2,128)S(1)}, f32[2,32]{1,0:T(2,128)S(1)}, u32[]{:S(2)}, u32[]{:S(2)}) collective-permute-start(f32[2,32]{1,0:T(2,128)S(1)} %add.140), channel_id=1, source_target_pairs={{0,16},{1,17},{2,18},{3,19},{4,20},{5,21},{6,22},{7,23},{8,24},{9,... | collective-permute-start | bytes 776 | tf_op jit(solution)/shard_map/ppermute | solution.py:83

commit v9 on v7

--- a/solution.py
+++ b/solution.py
@@ -133,6 +133,33 @@
     )(lengths.reshape(1, queries), valid.reshape(1, tokens), acts, grads_out, proj_in, proj_out)
 
 
+def _split_bf16(x):
+    high = x.astype(jnp.bfloat16)
+    return high, (x - high.astype(jnp.float32)).astype(jnp.bfloat16)
+
+
+def _scores_kernel(p_ref, db_ref, out_ref):
+    modules, width = p_ref.shape[1], p_ref.shape[2]
+    chunk = 512
+    nt = (((1,), (1,)), ((), ()))
+    f = lambda a, b: lax.dot_general(a, b, nt, preferred_element_type=jnp.float32)
+    out_ref[...] = jnp.zeros(out_ref.shape, jnp.float32)
+    for m in range(modules):
+        for c in range(width // chunk):
+            cols = pl.ds(c * chunk, chunk)
+            p_high, p_low = _split_bf16(p_ref[:, m, cols])
+            d_high, d_low = _split_bf16(db_ref[:, m, cols])
+            out_ref[...] += f(p_high, d_high) + (f(p_low, d_high) + f(p_high, d_low))
+
+
+def _scores(precond, database):
+    return pl.pallas_call(
+        _scores_kernel,
+        out_shape=jax.ShapeDtypeStruct((precond.shape[0], database.shape[0]), jnp.float32),
+        compiler_params=pltpu.CompilerParams(vmem_limit_bytes=56 * 1024 * 1024),
+    )(precond, database)
+
+
 def shards(size, acts, grads_out, lengths, valid, proj_in, proj_out, fisher_inv, database):
     tok_rows = acts.shape[0]
     modules = acts.shape[1]
@@ -142,12 +169,7 @@
     keep, send = _module_sums(lengths, valid, acts, grads_out, proj_in, proj_out)
     summed = _allreduce(keep, send, size, 2)
     precond_cols = jnp.einsum("qmk,mck->qmc", summed, fisher_inv, precision=lax.Precision.HIGH)
-    scores = jnp.einsum(
-        "qmk,nmk->qn",
-        _allgather(precond_cols, size),
-        database,
-        precision=lax.Precision.HIGH,
-    )
+    scores = _scores(_allgather(precond_cols, size), database)
     db_count = database.shape[0] * size
     moments = _butterfly_sum(
         jnp.stack([jnp.sum(scores, axis=1), jnp.sum(scores * scores, axis=1)]), size

time: 111 us -> 131 us (1.18)
  Pallas kernels: 7.14 us -> 30.4 us
  matrix products: 11.1 us -> 4.63 us
  other arithmetic: 4.65 us -> 6.19 us
  local copies, waits for them, and re-layouts: 1.65 us -> 2.98 us
    pallas_call x0 -> x1, Pallas kernels: none -> 23.3 us  [_scores(): pl.pallas_call(_scores_kernel, out_shape=jax.ShapeDtypeStruct((precond.sh...]
    dot_general x1 -> x0, matrix products: 6.48 us -> none  [shards(): jnp.einsum('qmk,nmk->qn', _allgather(precond_cols, size), database, preci...]
    select_n x2, local copies, waits for them, and re-layouts: 1.65 us -> 2.98 us  [_allgather(): jnp.where(low, jnp.stack([cur, other], -2), jnp.stack([other, cur], -2))]
where the time goes in v9:
time: 131 us
  waiting for transfers between devices  50.6 us (39%)
  starting transfers between devices  35.7 us (27%)
  Pallas kernels  30.4 us (23%)
  other arithmetic  6.19 us (5%)
  matrix products  4.63 us (4%)
  local copies, waits for them, and re-layouts  2.98 us (2%)
    pallas_call x1, Pallas kernels, _scores(): pl.pallas_call(_scores_kernel, out_shape=jax.ShapeDtypeStruct((precond.sh...  23.3 us
    ppermute x5, waiting for transfers between devices, _allgather(): other = lax.ppermute(cur, 'rows', _xor_pairs(size, s))  14.5 us
    ppermute x5, waiting for transfers between devices, _allreduce(): lax.ppermute(cur, 'rows', _pairs(size, orders, t))  14.4 us
    ppermute x4, waiting for transfers between devices, _allreduce(): cur = keep + lax.ppermute(send, 'rows', _pairs(size, orders, t))  11.5 us
    ppermute x4, starting transfers between devices, _allreduce(): cur = keep + lax.ppermute(send, 'rows', _pairs(size, orders, t))  10.6 us
    ppermute x5, waiting for transfers between devices, _butterfly_sum(): x = x + lax.ppermute(x, 'rows', _xor_pairs(size, s))  8.51 us
    ppermute x5, starting transfers between devices, _allgather(): other = lax.ppermute(cur, 'rows', _xor_pairs(size, s))  8.29 us
    ppermute x5, starting transfers between devices, _allreduce(): lax.ppermute(cur, 'rows', _pairs(size, orders, t))  8.27 us
  transfers between devices with their start and end apart: 20, of which 20 were waited for; matrix products, arithmetic and copies ran while one was open for 0% of the time, Pallas kernels for 0%

profile of v9, /device:TPU:0, one launch (start us, length us, event | category | flops | bytes accessed | tf_op | source)
XLA Modules:
  0.0 130.7 jit_solution(5542556748222389586)
XLA Ops:
  0.0 7.1 %shard_map.82 = (f32[32,2,2048]{2,1,0:T(2,128)}, f32[32,2,2048]{2,1,0:T(2,128)}) custom-call(s32[1,32]{1,0:T(1,128)} %bitcast.57, s32[1,128]{1,0:T(1,128)} %bitcast.58, bf16[128,2,4096]{2,1,0:T(2,128)(2,1)} %acts_ref.1, bf16[128,2,4096]{2,1,0:T(2,128)(2,1)} %gout_ref.1, bf16[4096,128]{1,0:T(8,128)(2,1)} %pin_ref.1, bf16[4096,128]{1,0:T(8,128)(2,1)} %pout_ref.1), custom_call_target="tpu_custom_call" | custom-call | tf_op jit(solution)/shard_map/pallas_call | solution.py:129
  10.9 2.9 %collective-permute-start.1 = (f32[32,2,1024]{2,1,0:T(2,128)S(1)}, f32[32,2,1024]{2,1,0:T(2,128)S(1)}, u32[]{:S(2)}, u32[]{:S(2)}) collective-permute-start(f32[32,2,1024]{2,1,0:T(2,128)S(1)} %broadcast_select_fusion), channel_id=1, source_target_pairs={{0,2},{1,5},{2,0},{3,7},{4,6},{5,1},{6,4},{7,3},{8,10},{9,13},{10,... | collective-permute-start | bytes 786440 | tf_op jit(solution)/shard_map/ppermute | solution.py:51
  13.8 4.4 %collective-permute-done.1 = f32[32,2,1024]{2,1,0:T(2,128)S(1)} collective-permute-done((f32[32,2,1024]{2,1,0:T(2,128)S(1)}, f32[32,2,1024]{2,1,0:T(2,128)S(1)}, u32[]{:S(2)}, u32[]{:S(2)}) %collective-permute-start.1) | collective-permute-done | bytes 262176 | tf_op jit(solution)/shard_map/ppermute | solution.py:51
  18.4 2.1 %collective-permute-start.2 = (f32[32,2,512]{2,1,0:T(2,128)S(1)}, f32[32,2,512]{2,1,0:T(2,128)S(1)}, u32[]{:S(2)}, u32[]{:S(2)}) collective-permute-start(f32[32,2,512]{2,1,0:T(2,128)S(1)} %broadcast_select_fusion.1), channel_id=1, source_target_pairs={{0,4},{1,3},{2,6},{3,1},{4,0},{5,7},{6,2},{7,5},{8,12},{9,11},{10,... | collective-permute-start | bytes 393224 | tf_op jit(solution)/shard_map/ppermute | solution.py:51
  20.5 2.9 %collective-permute-done.2 = f32[32,2,512]{2,1,0:T(2,128)S(1)} collective-permute-done((f32[32,2,512]{2,1,0:T(2,128)S(1)}, f32[32,2,512]{2,1,0:T(2,128)S(1)}, u32[]{:S(2)}, u32[]{:S(2)}) %collective-permute-start.2) | collective-permute-done | bytes 131104 | tf_op jit(solution)/shard_map/ppermute | solution.py:51
  23.6 2.1 %collective-permute-start.3 = (f32[32,2,256]{2,1,0:T(2,128)S(1)}, f32[32,2,256]{2,1,0:T(2,128)S(1)}, u32[]{:S(2)}, u32[]{:S(2)}) collective-permute-start(f32[32,2,256]{2,1,0:T(2,128)S(1)} %broadcast_select_fusion.2), channel_id=1, source_target_pairs={{0,8},{1,9},{2,10},{3,11},{4,12},{5,13},{6,14},{7,15},{8,0},{9,1},... | collective-permute-start | bytes 196616 | tf_op jit(solution)/shard_map/ppermute | solution.py:51
  25.8 2.2 %collective-permute-done.3 = f32[32,2,256]{2,1,0:T(2,128)S(1)} collective-permute-done((f32[32,2,256]{2,1,0:T(2,128)S(1)}, f32[32,2,256]{2,1,0:T(2,128)S(1)}, u32[]{:S(2)}, u32[]{:S(2)}) %collective-permute-start.3) | collective-permute-done | bytes 65568 | tf_op jit(solution)/shard_map/ppermute | solution.py:51
  28.1 3.4 %collective-permute-start.4 = (f32[32,2,128]{2,1,0:T(2,128)S(1)}, f32[32,2,128]{2,1,0:T(2,128)S(1)}, u32[]{:S(2)}, u32[]{:S(2)}) collective-permute-start(f32[32,2,128]{2,1,0:T(2,128)S(1)} %broadcast_select_fusion.3), channel_id=1, source_target_pairs={{0,16},{1,17},{2,18},{3,19},{4,20},{5,21},{6,22},{7,23},{8,24},{9,... | collective-permute-start | bytes 98312 | tf_op jit(solution)/shard_map/ppermute | solution.py:51
  31.5 2.0 %collective-permute-done.4 = f32[32,2,128]{2,1,0:T(2,128)S(1)} collective-permute-done((f32[32,2,128]{2,1,0:T(2,128)S(1)}, f32[32,2,128]{2,1,0:T(2,128)S(1)}, u32[]{:S(2)}, u32[]{:S(2)}) %collective-permute-start.4) | collective-permute-done | bytes 32800 | tf_op jit(solution)/shard_map/ppermute | solution.py:51
  33.5 2.9 %collective-permute-start.5 = (f32[32,2,128]{2,1,0:T(2,128)S(1)}, f32[32,2,128]{2,1,0:T(2,128)S(1)}, u32[]{:S(2)}, u32[]{:S(2)}) collective-permute-start(f32[32,2,128]{2,1,0:T(2,128)S(1)} %select_add_fusion.3), channel_id=1, source_target_pairs={{0,16},{1,17},{2,18},{3,19},{4,20},{5,21},{6,22},{7,23},{8,24},{9,... | collective-permute-start | bytes 98312 | tf_op jit(solution)/shard_map/ppermute | solution.py:54
  38.4 2.1 %collective-permute-start.6 = (f32[32,2,256]{2,1,0:T(2,128)S(1)}, f32[32,2,256]{2,1,0:T(2,128)S(1)}, u32[]{:S(2)}, u32[]{:S(2)}) collective-permute-start(f32[32,2,256]{2,1,0:T(2,128)S(1)} %maximum_select_fusion.11), channel_id=1, source_target_pairs={{0,8},{1,9},{2,10},{3,11},{4,12},{5,13},{6,14},{7,15},{8,0},{9,1},... | collective-permute-start | bytes 196616 | tf_op jit(solution)/shard_map/ppermute | solution.py:54
  40.5 2.2 %collective-permute-done.6 = f32[32,2,256]{2,1,0:T(2,128)S(1)} collective-permute-done((f32[32,2,256]{2,1,0:T(2,128)S(1)}, f32[32,2,256]{2,1,0:T(2,128)S(1)}, u32[]{:S(2)}, u32[]{:S(2)}) %collective-permute-start.6) | collective-permute-done | bytes 65568 | tf_op jit(solution)/shard_map/ppermute | solution.py:54
  44.5 3.4 %collective-permute-done.7 = f32[32,2,512]{2,1,0:T(2,128)S(1)} collective-permute-done((f32[32,2,512]{2,1,0:T(2,128)S(1)}, f32[32,2,512]{2,1,0:T(2,128)S(1)}, u32[]{:S(2)}, u32[]{:S(2)}) %collective-permute-start.7) | collective-permute-done | bytes 131104 | tf_op jit(solution)/shard_map/ppermute | solution.py:54
  49.7 4.8 %collective-permute-done.8 = f32[32,2,1024]{2,1,0:T(2,128)S(1)} collective-permute-done((f32[32,2,1024]{2,1,0:T(2,128)S(1)}, f32[32,2,1024]{2,1,0:T(2,128)S(1)}, u32[]{:S(2)}, u32[]{:S(2)}) %collective-permute-start.8) | collective-permute-done | bytes 262176 | tf_op jit(solution)/shard_map/ppermute | solution.py:54
  57.9 4.6 %fusion = f32[2,32,128]{2,1,0:T(8,128)S(1)} fusion(f32[2,128,4096]{2,1,0:T(8,128)} %param.14, f32[32,2,4096]{2,1,0:T(2,128)S(1)} %maximum_select_fusion), kind=kOutput, calls=%fused_computation.2 | convolution fusion | flops 201326592 | bytes 5275648 | tf_op jit(solution)/shard_map/qmk,mck->qmc/dot_general | solution.py:171
  62.5 3.2 %collective-permute-start.10 = (f32[32,2,128]{2,0,1:T(8,128)S(1)}, f32[32,2,128]{2,0,1:T(8,128)S(1)}, u32[]{:S(2)}, u32[]{:S(2)}) collective-permute-start(f32[32,2,128]{2,0,1:T(8,128)S(1)} %bitcast.43), channel_id=1, source_target_pairs={{0,16},{1,17},{2,18},{3,19},{4,20},{5,21},{6,22},{7,23},{8,24},{9,... | collective-permute-start | bytes 98312 | tf_op jit(solution)/shard_map/ppermute | solution.py:63
  69.5 2.5 %collective-permute-done.11 = f32[32,2,2,128]{3,0,1,2:T(8,128)S(1)} collective-permute-done((f32[32,2,2,128]{3,0,1,2:T(8,128)S(1)}, f32[32,2,2,128]{3,0,1,2:T(8,128)S(1)}, u32[]{:S(2)}, u32[]{:S(2)}) %collective-permute-start.11) | collective-permute-done | bytes 65568 | tf_op jit(solution)/shard_map/ppermute | solution.py:63
  73.6 3.4 %collective-permute-done.12 = f32[32,2,2,2,128]{4,0,1,2,3:T(8,128)S(1)} collective-permute-done((f32[32,2,2,2,128]{4,0,1,2,3:T(8,128)S(1)}, f32[32,2,2,2,128]{4,0,1,2,3:T(8,128)S(1)}, u32[]{:S(2)}, u32[]{:S(2)}) %collective-permute-start.12) | collective-permute-done | bytes 131104 | tf_op jit(solution)/shard_map/ppermute | solution.py:63
  78.7 4.8 %collective-permute-done.13 = f32[32,2,2,2,2,128]{5,0,1,2,3,4:T(8,128)S(1)} collective-permute-done((f32[32,2,2,2,2,128]{5,0,1,2,3,4:T(8,128)S(1)}, f32[32,2,2,2,2,128]{5,0,1,2,3,4:T(8,128)S(1)}, u32[]{:S(2)}, u32[]{:S(2)}) %collective-permute-start.13) | collective-permute-done | bytes 262176 | tf_op jit(solution)/shard_map/ppermute | solution.py:63
  86.4 2.2 %select_n.249.p_ref = f32[32,2,4096]{2,1,0:T(2,128)} reshape(f32[32,2,2,2,2,2,2,128]{7,6,5,4,3,2,1,0:T(2,128)S(1)} %copy.10) | data formatting | bytes 2097152 | tf_op jit(solution)/shard_map/jit(_where)/select_n | solution.py:64
  88.6 23.3 %shard_map.83 = f32[32,128]{1,0:T(8,128)} custom-call(f32[32,2,4096]{2,1,0:T(2,128)} %select_n.249.p_ref, f32[128,2,4096]{2,1,0:T(2,128)} %db_ref.1), custom_call_target="tpu_custom_call" | custom-call | tf_op jit(solution)/shard_map/pallas_call | solution.py:156
  115.5 2.1 %collective-permute-done.16 = f32[2,32]{1,0:T(2,128)S(1)} collective-permute-done((f32[2,32]{1,0:T(2,128)S(1)}, f32[2,32]{1,0:T(2,128)S(1)}, u32[]{:S(2)}, u32[]{:S(2)}) %collective-permute-start.16) | collective-permute-done | bytes 288 | tf_op jit(solution)/shard_map/ppermute | solution.py:74
  119.2 2.0 %collective-permute-done.17 = f32[2,32]{1,0:T(2,128)S(1)} collective-permute-done((f32[2,32]{1,0:T(2,128)S(1)}, f32[2,32]{1,0:T(2,128)S(1)}, u32[]{:S(2)}, u32[]{:S(2)}) %collective-permute-start.17) | collective-permute-done | bytes 288 | tf_op jit(solution)/shard_map/ppermute | solution.py:74
  124.8 2.9 %collective-permute-start.19 = (f32[2,32]{1,0:T(2,128)S(1)}, f32[2,32]{1,0:T(2,128)S(1)}, u32[]{:S(2)}, u32[]{:S(2)}) collective-permute-start(f32[2,32]{1,0:T(2,128)S(1)} %add.48), channel_id=1, source_target_pairs={{0,16},{1,17},{2,18},{3,19},{4,20},{5,21},{6,22},{7,23},{8,24},{9,... | collective-permute-start | bytes 776 | tf_op jit(solution)/shard_map/ppermute | solution.py:74
  (57 shorter events, 34.6 us)
Async XLA Ops:
  7.1 2.2 %collective-permute-start = (f32[32,2,2048]{2,1,0:T(2,128)}, f32[32,2,2048]{2,1,0:T(2,128)S(1)}, u32[]{:S(2)}, u32[]{:S(2)}) collective-permute-start(f32[32,2,2048]{2,1,0:T(2,128)} %get-tuple-element.8), channel_id=1, source_target_pairs={{0,1},{1,0},{2,3},{3,2},{4,5},{5,4},{6,7},{7,6},{8,9},{9,8},{10,11... | collective-permute-start | bytes 1572872 | tf_op jit(solution)/shard_map/ppermute | solution.py:43
  10.9 7.3 %collective-permute-start.1 = (f32[32,2,1024]{2,1,0:T(2,128)S(1)}, f32[32,2,1024]{2,1,0:T(2,128)S(1)}, u32[]{:S(2)}, u32[]{:S(2)}) collective-permute-start(f32[32,2,1024]{2,1,0:T(2,128)S(1)} %broadcast_select_fusion), channel_id=1, source_target_pairs={{0,2},{1,5},{2,0},{3,7},{4,6},{5,1},{6,4},{7,3},{8,10},{9,13},{10,... | collective-permute-start | bytes 786440 | tf_op jit(solution)/shard_map/ppermute | solution.py:51
  18.4 5.1 %collective-permute-start.2 = (f32[32,2,512]{2,1,0:T(2,128)S(1)}, f32[32,2,512]{2,1,0:T(2,128)S(1)}, u32[]{:S(2)}, u32[]{:S(2)}) collective-permute-start(f32[32,2,512]{2,1,0:T(2,128)S(1)} %broadcast_select_fusion.1), channel_id=1, source_target_pairs={{0,4},{1,3},{2,6},{3,1},{4,0},{5,7},{6,2},{7,5},{8,12},{9,11},{10,... | collective-permute-start | bytes 393224 | tf_op jit(solution)/shard_map/ppermute | solution.py:51
  23.6 4.4 %collective-permute-start.3 = (f32[32,2,256]{2,1,0:T(2,128)S(1)}, f32[32,2,256]{2,1,0:T(2,128)S(1)}, u32[]{:S(2)}, u32[]{:S(2)}) collective-permute-start(f32[32,2,256]{2,1,0:T(2,128)S(1)} %broadcast_select_fusion.2), channel_id=1, source_target_pairs={{0,8},{1,9},{2,10},{3,11},{4,12},{5,13},{6,14},{7,15},{8,0},{9,1},... | collective-permute-start | bytes 196616 | tf_op jit(solution)/shard_map/ppermute | solution.py:51
  28.1 5.4 %collective-permute-start.4 = (f32[32,2,128]{2,1,0:T(2,128)S(1)}, f32[32,2,128]{2,1,0:T(2,128)S(1)}, u32[]{:S(2)}, u32[]{:S(2)}) collective-permute-start(f32[32,2,128]{2,1,0:T(2,128)S(1)} %broadcast_select_fusion.3), channel_id=1, source_target_pairs={{0,16},{1,17},{2,18},{3,19},{4,20},{5,21},{6,22},{7,23},{8,24},{9,... | collective-permute-start | bytes 98312 | tf_op jit(solution)/shard_map/ppermute | solution.py:51
  33.5 4.9 %collective-permute-start.5 = (f32[32,2,128]{2,1,0:T(2,128)S(1)}, f32[32,2,128]{2,1,0:T(2,128)S(1)}, u32[]{:S(2)}, u32[]{:S(2)}) collective-permute-start(f32[32,2,128]{2,1,0:T(2,128)S(1)} %select_add_fusion.3), channel_id=1, source_target_pairs={{0,16},{1,17},{2,18},{3,19},{4,20},{5,21},{6,22},{7,23},{8,24},{9,... | collective-permute-start | bytes 98312 | tf_op jit(solution)/shard_map/ppermute | solution.py:54
  38.4 4.3 %collective-permute-start.6 = (f32[32,2,256]{2,1,0:T(2,128)S(1)}, f32[32,2,256]{2,1,0:T(2,128)S(1)}, u32[]{:S(2)}, u32[]{:S(2)}) collective-permute-start(f32[32,2,256]{2,1,0:T(2,128)S(1)} %maximum_select_fusion.11), channel_id=1, source_target_pairs={{0,8},{1,9},{2,10},{3,11},{4,12},{5,13},{6,14},{7,15},{8,0},{9,1},... | collective-permute-start | bytes 196616 | tf_op jit(solution)/shard_map/ppermute | solution.py:54
  42.8 5.0 %collective-permute-start.7 = (f32[32,2,512]{2,1,0:T(2,128)S(1)}, f32[32,2,512]{2,1,0:T(2,128)S(1)}, u32[]{:S(2)}, u32[]{:S(2)}) collective-permute-start(f32[32,2,512]{2,1,0:T(2,128)S(1)} %maximum_select_fusion.8), channel_id=1, source_target_pairs={{0,4},{1,3},{2,6},{3,1},{4,0},{5,7},{6,2},{7,5},{8,12},{9,11},{10,... | collective-permute-start | bytes 393224 | tf_op jit(solution)/shard_map/ppermute | solution.py:54
  48.1 6.4 %collective-permute-start.8 = (f32[32,2,1024]{2,1,0:T(2,128)S(1)}, f32[32,2,1024]{2,1,0:T(2,128)S(1)}, u32[]{:S(2)}, u32[]{:S(2)}) collective-permute-start(f32[32,2,1024]{2,1,0:T(2,128)S(1)} %maximum_select_fusion.5), channel_id=1, source_target_pairs={{0,2},{1,5},{2,0},{3,7},{4,6},{5,1},{6,4},{7,3},{8,10},{9,13},{10,... | collective-permute-start | bytes 786440 | tf_op jit(solution)/shard_map/ppermute | solution.py:54
  54.9 2.0 %collective-permute-start.9 = (f32[32,2,2048]{2,1,0:T(2,128)S(1)}, f32[32,2,2048]{2,1,0:T(2,128)S(1)}, u32[]{:S(2)}, u32[]{:S(2)}) collective-permute-start(f32[32,2,2048]{2,1,0:T(2,128)S(1)} %maximum_select_fusion.2), channel_id=1, source_target_pairs={{0,1},{1,0},{2,3},{3,2},{4,5},{5,4},{6,7},{7,6},{8,9},{9,8},{10,11... | collective-permute-start | bytes 1572872 | tf_op jit(solution)/shard_map/ppermute | solution.py:54
  62.5 5.1 %collective-permute-start.10 = (f32[32,2,128]{2,0,1:T(8,128)S(1)}, f32[32,2,128]{2,0,1:T(8,128)S(1)}, u32[]{:S(2)}, u32[]{:S(2)}) collective-permute-start(f32[32,2,128]{2,0,1:T(8,128)S(1)} %bitcast.43), channel_id=1, source_target_pairs={{0,16},{1,17},{2,18},{3,19},{4,20},{5,21},{6,22},{7,23},{8,24},{9,... | collective-permute-start | bytes 98312 | tf_op jit(solution)/shard_map/ppermute | solution.py:63
  67.6 4.3 %collective-permute-start.11 = (f32[32,2,2,128]{3,0,1,2:T(8,128)S(1)}, f32[32,2,2,128]{3,0,1,2:T(8,128)S(1)}, u32[]{:S(2)}, u32[]{:S(2)}) collective-permute-start(f32[32,2,2,128]{3,0,1,2:T(8,128)S(1)} %maximum_select_fusion.13), channel_id=1, source_target_pairs={{0,8},{1,9},{2,10},{3,11},{4,12},{5,13},{6,14},{7,15},{8,0},{9,1},... | collective-permute-start | bytes 196616 | tf_op jit(solution)/shard_map/ppermute | solution.py:63
  72.0 5.0 %collective-permute-start.12 = (f32[32,2,2,2,128]{4,0,1,2,3:T(8,128)S(1)}, f32[32,2,2,2,128]{4,0,1,2,3:T(8,128)S(1)}, u32[]{:S(2)}, u32[]{:S(2)}) collective-permute-start(f32[32,2,2,2,128]{4,0,1,2,3:T(8,128)S(1)} %maximum_select_fusion.10), channel_id=1, source_target_pairs={{0,4},{1,5},{2,6},{3,7},{4,0},{5,1},{6,2},{7,3},{8,12},{9,13},{10,... | collective-permute-start | bytes 393224 | tf_op jit(solution)/shard_map/ppermute | solution.py:63
  77.0 6.4 %collective-permute-start.13 = (f32[32,2,2,2,2,128]{5,0,1,2,3,4:T(8,128)S(1)}, f32[32,2,2,2,2,128]{5,0,1,2,3,4:T(8,128)S(1)}, u32[]{:S(2)}, u32[]{:S(2)}) collective-permute-start(f32[32,2,2,2,2,128]{5,0,1,2,3,4:T(8,128)S(1)} %maximum_select_fusion.7), channel_id=1, source_target_pairs={{0,2},{1,3},{2,0},{3,1},{4,6},{5,7},{6,4},{7,5},{8,10},{9,11},{10,... | collective-permute-start | bytes 786440 | tf_op jit(solution)/shard_map/ppermute | solution.py:63
  83.5 2.0 %collective-permute-start.14 = (f32[32,2,2,2,2,2,128]{6,0,1,2,3,4,5:T(8,128)S(1)}, f32[32,2,2,2,2,2,128]{6,0,1,2,3,4,5:T(8,128)S(1)}, u32[]{:S(2)}, u32[]{:S(2)}) collective-permute-start(f32[32,2,2,2,2,2,128]{6,0,1,2,3,4,5:T(8,128)S(1)} %maximum_select_fusion.4), channel_id=1, source_target_pairs={{0,1},{1,0},{2,3},{3,2},{4,5},{5,4},{6,7},{7,6},{8,9},{9,8},{10,11... | collective-permute-start | bytes 1572872 | tf_op jit(solution)/shard_map/ppermute | solution.py:63
  112.7 1.2 collective-permute-start.15
  113.9 3.6 %collective-permute-start.16 = (f32[2,32]{1,0:T(2,128)S(1)}, f32[2,32]{1,0:T(2,128)S(1)}, u32[]{:S(2)}, u32[]{:S(2)}) collective-permute-start(f32[2,32]{1,0:T(2,128)S(1)} %fusion.4), channel_id=1, source_target_pairs={{0,2},{1,3},{2,0},{3,1},{4,6},{5,7},{6,4},{7,5},{8,10},{9,11},{10,... | collective-permute-start | bytes 776 | tf_op jit(solution)/shard_map/ppermute | solution.py:74
  117.6 3.6 %collective-permute-start.17 = (f32[2,32]{1,0:T(2,128)S(1)}, f32[2,32]{1,0:T(2,128)S(1)}, u32[]{:S(2)}, u32[]{:S(2)}) collective-permute-start(f32[2,32]{1,0:T(2,128)S(1)} %fusion.7), channel_id=1, source_target_pairs={{0,4},{1,5},{2,6},{3,7},{4,0},{5,1},{6,2},{7,3},{8,12},{9,13},{10,... | collective-permute-start | bytes 776 | tf_op jit(solution)/shard_map/ppermute | solution.py:74
  121.2 3.6 %collective-permute-start.18 = (f32[2,32]{1,0:T(2,128)S(1)}, f32[2,32]{1,0:T(2,128)S(1)}, u32[]{:S(2)}, u32[]{:S(2)}) collective-permute-start(f32[2,32]{1,0:T(2,128)S(1)} %add.47), channel_id=1, source_target_pairs={{0,8},{1,9},{2,10},{3,11},{4,12},{5,13},{6,14},{7,15},{8,0},{9,1},... | collective-permute-start | bytes 776 | tf_op jit(solution)/shard_map/ppermute | solution.py:74
  124.8 4.5 %collective-permute-start.19 = (f32[2,32]{1,0:T(2,128)S(1)}, f32[2,32]{1,0:T(2,128)S(1)}, u32[]{:S(2)}, u32[]{:S(2)}) collective-permute-start(f32[2,32]{1,0:T(2,128)S(1)} %add.48), channel_id=1, source_target_pairs={{0,16},{1,17},{2,18},{3,19},{4,20},{5,21},{6,22},{7,23},{8,24},{9,... | collective-permute-start | bytes 776 | tf_op jit(solution)/shard_map/ppermute | solution.py:74

commit v10 on v7

--- a/solution.py
+++ b/solution.py
@@ -116,8 +116,8 @@
             sel, low, preferred_element_type=jnp.float32
         )
         lo, hi = total[:, :half], total[:, half:]
-        keep_ref[:, m, :] = jnp.where(first, lo, hi)
-        send_ref[:, m, :] = jnp.where(first, hi, lo)
+        keep_ref[m] = jnp.where(first, lo, hi)
+        send_ref[m] = jnp.where(first, hi, lo)
 
 
 def _module_sums(lengths, valid, acts, grads_out, proj_in, proj_out):
@@ -125,12 +125,35 @@
     tokens, modules, _ = acts.shape
     rank = proj_in.shape[1] // modules
     scratch = pltpu.VMEM((tokens * modules, modules * rank), jnp.float32)
-    half = jax.ShapeDtypeStruct((queries, modules, rank * rank // 2), jnp.float32)
+    half = jax.ShapeDtypeStruct((modules, queries, rank * rank // 2), jnp.float32)
     return pl.pallas_call(
         _sums_kernel,
         out_shape=(half, half),
         scratch_shapes=[scratch, scratch],
     )(lengths.reshape(1, queries), valid.reshape(1, tokens), acts, grads_out, proj_in, proj_out)
+
+
+def _split_bf16(x):
+    high = x.astype(jnp.bfloat16)
+    return high, (x - high.astype(jnp.float32)).astype(jnp.bfloat16)
+
+
+def _precond_kernel(g_ref, f_ref, out_ref):
+    nt = (((1,), (1,)), ((), ()))
+    f = lambda a, b: lax.dot_general(a, b, nt, preferred_element_type=jnp.float32)
+    for m in range(g_ref.shape[0]):
+        g_high, g_low = _split_bf16(g_ref[m])
+        f_high, f_low = _split_bf16(f_ref[m])
+        out_ref[m] = f(g_high, f_high) + (f(g_low, f_high) + f(g_high, f_low))
+
+
+def _precond(grads, fisher_inv):
+    modules, queries, _ = grads.shape
+    return pl.pallas_call(
+        _precond_kernel,
+        out_shape=jax.ShapeDtypeStruct((modules, queries, fisher_inv.shape[1]), jnp.float32),
+        compiler_params=pltpu.CompilerParams(vmem_limit_bytes=48 * 1024 * 1024),
+    )(grads, fisher_inv)
 
 
 def shards(size, acts, grads_out, lengths, valid, proj_in, proj_out, fisher_inv, database):
@@ -141,9 +164,9 @@
     flat_width = proj_rank * proj_rank
     keep, send = _module_sums(lengths, valid, acts, grads_out, proj_in, proj_out)
     summed = _allreduce(keep, send, size, 2)
-    precond_cols = jnp.einsum("qmk,mck->qmc", summed, fisher_inv, precision=lax.Precision.HIGH)
+    precond_cols = _precond(summed, fisher_inv)
     scores = jnp.einsum(
-        "qmk,nmk->qn",
+        "mqk,nmk->qn",
         _allgather(precond_cols, size),
         database,
         precision=lax.Precision.HIGH,

time: 111 us -> 108 us (0.973)
  matrix products: 11.1 us -> 6.3 us
  local copies, waits for them, and re-layouts: 1.65 us -> 3.83 us
  other arithmetic: 4.65 us -> 2.51 us
  Pallas kernels: 7.14 us -> 9.12 us
    dot_general x2 -> x1, matrix products: 11.1 us -> 6.3 us  [shards(): jnp.einsum('mqk,nmk->qn', _allgather(precond_cols, size), database, preci...]
    unnamed x0 -> x2, local copies, waits for them, and re-layouts: none -> 2.18 us
    pallas_call x0 -> x1, Pallas kernels: none -> 2.15 us  [_precond(): pl.pallas_call(_precond_kernel, out_shape=jax.ShapeDtypeStruct((modules,...]
    select_n x5, other arithmetic: 1.65 us -> 0.22 us  [_join(): jnp.where(low, jnp.concatenate([mine, other], axis), jnp.concatenate([oth...]
where the time goes in v10:
time: 108 us
  waiting for transfers between devices  50.2 us (46%)
  starting transfers between devices  35.8 us (33%)
  Pallas kernels  9.12 us (8%)
  matrix products  6.3 us (6%)
  local copies, waits for them, and re-layouts  3.83 us (4%)
  other arithmetic  2.51 us (2%)
    ppermute x5, waiting for transfers between devices, _allreduce(): lax.ppermute(cur, 'rows', _pairs(size, orders, t))  14.4 us
    ppermute x5, waiting for transfers between devices, _allgather(): other = lax.ppermute(cur, 'rows', _xor_pairs(size, s))  14.3 us
    ppermute x4, waiting for transfers between devices, _allreduce(): cur = keep + lax.ppermute(send, 'rows', _pairs(size, orders, t))  11.5 us
    ppermute x4, starting transfers between devices, _allreduce(): cur = keep + lax.ppermute(send, 'rows', _pairs(size, orders, t))  10.6 us
    ppermute x5, waiting for transfers between devices, _butterfly_sum(): x = x + lax.ppermute(x, 'rows', _xor_pairs(size, s))  8.36 us
    ppermute x5, starting transfers between devices, _allreduce(): lax.ppermute(cur, 'rows', _pairs(size, orders, t))  8.29 us
    ppermute x5, starting transfers between devices, _allgather(): other = lax.ppermute(cur, 'rows', _xor_pairs(size, s))  8.24 us
    ppermute x5, starting transfers between devices, _butterfly_sum(): x = x + lax.ppermute(x, 'rows', _xor_pairs(size, s))  8.19 us
  transfers between devices with their start and end apart: 20, of which 20 were waited for; matrix products, arithmetic and copies ran while one was open for 0% of the time, Pallas kernels for 0%

profile of v10, /device:TPU:0, one launch (start us, length us, event | category | flops | bytes accessed | tf_op | source)
XLA Modules:
  0.0 108.0 jit_solution(3057391832506449507)
XLA Ops:
  0.0 7.0 %shard_map.82 = (f32[2,32,2048]{2,1,0:T(8,128)}, f32[2,32,2048]{2,1,0:T(8,128)}) custom-call(s32[1,32]{1,0:T(1,128)} %bitcast.55, s32[1,128]{1,0:T(1,128)} %bitcast.56, bf16[128,2,4096]{2,1,0:T(2,128)(2,1)} %acts_ref.1, bf16[128,2,4096]{2,1,0:T(2,128)(2,1)} %gout_ref.1, bf16[4096,128]{1,0:T(8,128)(2,1)} %pin_ref.1, bf16[4096,128]{1,0:T(8,128)(2,1)} %pout_ref.1), custom_call_target="tpu_custom_call" | custom-call | tf_op jit(solution)/shard_map/pallas_call | solution.py:129
  10.3 2.9 %collective-permute-start.1 = (f32[2,32,1024]{2,1,0:T(8,128)S(1)}, f32[2,32,1024]{2,1,0:T(8,128)S(1)}, u32[]{:S(2)}, u32[]{:S(2)}) collective-permute-start(f32[2,32,1024]{2,1,0:T(8,128)S(1)} %slice_select_fusion), channel_id=1, source_target_pairs={{0,2},{1,5},{2,0},{3,7},{4,6},{5,1},{6,4},{7,3},{8,10},{9,13},{10,... | collective-permute-start | bytes 786440 | tf_op jit(solution)/shard_map/ppermute | solution.py:51
  13.3 4.4 %collective-permute-done.1 = f32[2,32,1024]{2,1,0:T(8,128)S(1)} collective-permute-done((f32[2,32,1024]{2,1,0:T(8,128)S(1)}, f32[2,32,1024]{2,1,0:T(8,128)S(1)}, u32[]{:S(2)}, u32[]{:S(2)}) %collective-permute-start.1) | collective-permute-done | bytes 262176 | tf_op jit(solution)/shard_map/ppermute | solution.py:51
  17.7 2.1 %collective-permute-start.2 = (f32[2,32,512]{2,1,0:T(8,128)S(1)}, f32[2,32,512]{2,1,0:T(8,128)S(1)}, u32[]{:S(2)}, u32[]{:S(2)}) collective-permute-start(f32[2,32,512]{2,1,0:T(8,128)S(1)} %slice_select_fusion.1), channel_id=1, source_target_pairs={{0,4},{1,3},{2,6},{3,1},{4,0},{5,7},{6,2},{7,5},{8,12},{9,11},{10,... | collective-permute-start | bytes 393224 | tf_op jit(solution)/shard_map/ppermute | solution.py:51
  19.8 2.9 %collective-permute-done.2 = f32[2,32,512]{2,1,0:T(8,128)S(1)} collective-permute-done((f32[2,32,512]{2,1,0:T(8,128)S(1)}, f32[2,32,512]{2,1,0:T(8,128)S(1)}, u32[]{:S(2)}, u32[]{:S(2)}) %collective-permute-start.2) | collective-permute-done | bytes 131104 | tf_op jit(solution)/shard_map/ppermute | solution.py:51
  22.8 2.1 %collective-permute-start.3 = (f32[2,32,256]{2,1,0:T(8,128)S(1)}, f32[2,32,256]{2,1,0:T(8,128)S(1)}, u32[]{:S(2)}, u32[]{:S(2)}) collective-permute-start(f32[2,32,256]{2,1,0:T(8,128)S(1)} %slice_select_fusion.2), channel_id=1, source_target_pairs={{0,8},{1,9},{2,10},{3,11},{4,12},{5,13},{6,14},{7,15},{8,0},{9,1},... | collective-permute-start | bytes 196616 | tf_op jit(solution)/shard_map/ppermute | solution.py:51
  24.9 2.2 %collective-permute-done.3 = f32[2,32,256]{2,1,0:T(8,128)S(1)} collective-permute-done((f32[2,32,256]{2,1,0:T(8,128)S(1)}, f32[2,32,256]{2,1,0:T(8,128)S(1)}, u32[]{:S(2)}, u32[]{:S(2)}) %collective-permute-start.3) | collective-permute-done | bytes 65568 | tf_op jit(solution)/shard_map/ppermute | solution.py:51
  27.2 3.4 %collective-permute-start.4 = (f32[2,32,128]{2,1,0:T(8,128)S(1)}, f32[2,32,128]{2,1,0:T(8,128)S(1)}, u32[]{:S(2)}, u32[]{:S(2)}) collective-permute-start(f32[2,32,128]{2,1,0:T(8,128)S(1)} %slice_select_fusion.3), channel_id=1, source_target_pairs={{0,16},{1,17},{2,18},{3,19},{4,20},{5,21},{6,22},{7,23},{8,24},{9,... | collective-permute-start | bytes 98312 | tf_op jit(solution)/shard_map/ppermute | solution.py:51
  32.6 2.9 %collective-permute-start.5 = (f32[2,32,128]{2,1,0:T(8,128)S(1)}, f32[2,32,128]{2,1,0:T(8,128)S(1)}, u32[]{:S(2)}, u32[]{:S(2)}) collective-permute-start(f32[2,32,128]{2,1,0:T(8,128)S(1)} %select_add_fusion.3), channel_id=1, source_target_pairs={{0,16},{1,17},{2,18},{3,19},{4,20},{5,21},{6,22},{7,23},{8,24},{9,... | collective-permute-start | bytes 98312 | tf_op jit(solution)/shard_map/ppermute | solution.py:54
  37.5 2.1 %collective-permute-start.6 = (f32[2,32,256]{2,1,0:T(8,128)S(1)}, f32[2,32,256]{2,1,0:T(8,128)S(1)}, u32[]{:S(2)}, u32[]{:S(2)}) collective-permute-start(f32[2,32,256]{2,1,0:T(8,128)S(1)} %maximum_select_fusion.11), channel_id=1, source_target_pairs={{0,8},{1,9},{2,10},{3,11},{4,12},{5,13},{6,14},{7,15},{8,0},{9,1},... | collective-permute-start | bytes 196616 | tf_op jit(solution)/shard_map/ppermute | solution.py:54
  39.6 2.3 %collective-permute-done.6 = f32[2,32,256]{2,1,0:T(8,128)S(1)} collective-permute-done((f32[2,32,256]{2,1,0:T(8,128)S(1)}, f32[2,32,256]{2,1,0:T(8,128)S(1)}, u32[]{:S(2)}, u32[]{:S(2)}) %collective-permute-start.6) | collective-permute-done | bytes 65568 | tf_op jit(solution)/shard_map/ppermute | solution.py:54
  43.5 3.4 %collective-permute-done.7 = f32[2,32,512]{2,1,0:T(8,128)S(1)} collective-permute-done((f32[2,32,512]{2,1,0:T(8,128)S(1)}, f32[2,32,512]{2,1,0:T(8,128)S(1)}, u32[]{:S(2)}, u32[]{:S(2)}) %collective-permute-start.7) | collective-permute-done | bytes 131104 | tf_op jit(solution)/shard_map/ppermute | solution.py:54
  48.5 4.8 %collective-permute-done.8 = f32[2,32,1024]{2,1,0:T(8,128)S(1)} collective-permute-done((f32[2,32,1024]{2,1,0:T(8,128)S(1)}, f32[2,32,1024]{2,1,0:T(8,128)S(1)}, u32[]{:S(2)}, u32[]{:S(2)}) %collective-permute-start.8) | collective-permute-done | bytes 262176 | tf_op jit(solution)/shard_map/ppermute | solution.py:54
  55.5 2.2 %copy-done = f32[2,128,4096]{2,1,0:T(8,128)S(1)} copy-done((f32[2,128,4096]{2,1,0:T(8,128)S(1)}, f32[2,128,4096]{2,1,0:T(8,128)}, u32[]{:S(2)}) %copy-start) | copy-done | bytes 4194328
  57.7 2.2 %shard_map.83 = f32[2,32,128]{2,1,0:T(8,128)S(1)} custom-call(f32[2,32,4096]{2,1,0:T(8,128)S(1)} %maximum_select_fusion.g_ref, f32[2,128,4096]{2,1,0:T(8,128)S(1)} %copy-done), custom_call_target="tpu_custom_call" | custom-call | tf_op jit(solution)/shard_map/pallas_call | solution.py:152
  59.9 3.0 %collective-permute-start.10 = (f32[2,32,128]{2,1,0:T(8,128)S(1)}, f32[2,32,128]{2,1,0:T(8,128)S(1)}, u32[]{:S(2)}, u32[]{:S(2)}) collective-permute-start(f32[2,32,128]{2,1,0:T(8,128)S(1)} %shard_map.83), channel_id=1, source_target_pairs={{0,16},{1,17},{2,18},{3,19},{4,20},{5,21},{6,22},{7,23},{8,24},{9,... | collective-permute-start | bytes 98312 | tf_op jit(solution)/shard_map/ppermute | solution.py:63
  64.8 2.0 %collective-permute-start.11 = (f32[2,32,2,128]{3,1,0,2:T(8,128)S(1)}, f32[2,32,2,128]{3,1,0,2:T(8,128)S(1)}, u32[]{:S(2)}, u32[]{:S(2)}) collective-permute-start(f32[2,32,2,128]{3,1,0,2:T(8,128)S(1)} %maximum_select_fusion.13), channel_id=1, source_target_pairs={{0,8},{1,9},{2,10},{3,11},{4,12},{5,13},{6,14},{7,15},{8,0},{9,1},... | collective-permute-start | bytes 196616 | tf_op jit(solution)/shard_map/ppermute | solution.py:63
  66.8 2.3 %collective-permute-done.11 = f32[2,32,2,128]{3,1,0,2:T(8,128)S(1)} collective-permute-done((f32[2,32,2,128]{3,1,0,2:T(8,128)S(1)}, f32[2,32,2,128]{3,1,0,2:T(8,128)S(1)}, u32[]{:S(2)}, u32[]{:S(2)}) %collective-permute-start.11) | collective-permute-done | bytes 65568 | tf_op jit(solution)/shard_map/ppermute | solution.py:63
  70.8 3.4 %collective-permute-done.12 = f32[2,32,2,2,128]{4,1,0,2,3:T(8,128)S(1)} collective-permute-done((f32[2,32,2,2,128]{4,1,0,2,3:T(8,128)S(1)}, f32[2,32,2,2,128]{4,1,0,2,3:T(8,128)S(1)}, u32[]{:S(2)}, u32[]{:S(2)}) %collective-permute-start.12) | collective-permute-done | bytes 131104 | tf_op jit(solution)/shard_map/ppermute | solution.py:63
  75.8 4.8 %collective-permute-done.13 = f32[2,32,2,2,2,128]{5,1,0,2,3,4:T(8,128)S(1)} collective-permute-done((f32[2,32,2,2,2,128]{5,1,0,2,3,4:T(8,128)S(1)}, f32[2,32,2,2,2,128]{5,1,0,2,3,4:T(8,128)S(1)}, u32[]{:S(2)}, u32[]{:S(2)}) %collective-permute-start.13) | collective-permute-done | bytes 262176 | tf_op jit(solution)/shard_map/ppermute | solution.py:63
  84.4 6.3 %fusion.8 = (f32[32]{0:T(128)S(1)}, f32[32]{0:T(128)S(1)}, f32[32,128]{1,0:T(8,128)S(1)}) fusion(f32[2,32,4096]{2,1,0:T(8,128)S(1)} %select_n.249, f32[128,2,4096]{2,1,0:T(2,128)} %param.15), kind=kOutput, calls=%fused_computation.33 | convolution fusion | flops 201338816 | bytes 5259520 | tf_op jit(solution)/shard_map/mqk,nmk->qn/dot_general | solution.py:168
  93.5 2.1 %collective-permute-done.16 = f32[2,32]{1,0:T(2,128)S(1)} collective-permute-done((f32[2,32]{1,0:T(2,128)S(1)}, f32[2,32]{1,0:T(2,128)S(1)}, u32[]{:S(2)}, u32[]{:S(2)}) %collective-permute-start.16) | collective-permute-done | bytes 288 | tf_op jit(solution)/shard_map/ppermute | solution.py:74
  97.2 2.0 %collective-permute-done.17 = f32[2,32]{1,0:T(2,128)S(1)} collective-permute-done((f32[2,32]{1,0:T(2,128)S(1)}, f32[2,32]{1,0:T(2,128)S(1)}, u32[]{:S(2)}, u32[]{:S(2)}) %collective-permute-start.17) | collective-permute-done | bytes 288 | tf_op jit(solution)/shard_map/ppermute | solution.py:74
  102.9 2.9 %collective-permute-start.19 = (f32[2,32]{1,0:T(2,128)S(1)}, f32[2,32]{1,0:T(2,128)S(1)}, u32[]{:S(2)}, u32[]{:S(2)}) collective-permute-start(f32[2,32]{1,0:T(2,128)S(1)} %add.48), channel_id=1, source_target_pairs={{0,16},{1,17},{2,18},{3,19},{4,20},{5,21},{6,22},{7,23},{8,24},{9,... | collective-permute-start | bytes 776 | tf_op jit(solution)/shard_map/ppermute | solution.py:74
  (58 shorter events, 31.9 us)
Async XLA Ops:
  7.0 2.2 %collective-permute-start = (f32[2,32,2048]{2,1,0:T(8,128)}, f32[2,32,2048]{2,1,0:T(8,128)S(1)}, u32[]{:S(2)}, u32[]{:S(2)}) collective-permute-start(f32[2,32,2048]{2,1,0:T(8,128)} %get-tuple-element.8), channel_id=1, source_target_pairs={{0,1},{1,0},{2,3},{3,2},{4,5},{5,4},{6,7},{7,6},{8,9},{9,8},{10,11... | collective-permute-start | bytes 1572872 | tf_op jit(solution)/shard_map/ppermute | solution.py:43
  10.3 7.3 %collective-permute-start.1 = (f32[2,32,1024]{2,1,0:T(8,128)S(1)}, f32[2,32,1024]{2,1,0:T(8,128)S(1)}, u32[]{:S(2)}, u32[]{:S(2)}) collective-permute-start(f32[2,32,1024]{2,1,0:T(8,128)S(1)} %slice_select_fusion), channel_id=1, source_target_pairs={{0,2},{1,5},{2,0},{3,7},{4,6},{5,1},{6,4},{7,3},{8,10},{9,13},{10,... | collective-permute-start | bytes 786440 | tf_op jit(solution)/shard_map/ppermute | solution.py:51
  17.7 5.1 %collective-permute-start.2 = (f32[2,32,512]{2,1,0:T(8,128)S(1)}, f32[2,32,512]{2,1,0:T(8,128)S(1)}, u32[]{:S(2)}, u32[]{:S(2)}) collective-permute-start(f32[2,32,512]{2,1,0:T(8,128)S(1)} %slice_select_fusion.1), channel_id=1, source_target_pairs={{0,4},{1,3},{2,6},{3,1},{4,0},{5,7},{6,2},{7,5},{8,12},{9,11},{10,... | collective-permute-start | bytes 393224 | tf_op jit(solution)/shard_map/ppermute | solution.py:51
  22.8 4.4 %collective-permute-start.3 = (f32[2,32,256]{2,1,0:T(8,128)S(1)}, f32[2,32,256]{2,1,0:T(8,128)S(1)}, u32[]{:S(2)}, u32[]{:S(2)}) collective-permute-start(f32[2,32,256]{2,1,0:T(8,128)S(1)} %slice_select_fusion.2), channel_id=1, source_target_pairs={{0,8},{1,9},{2,10},{3,11},{4,12},{5,13},{6,14},{7,15},{8,0},{9,1},... | collective-permute-start | bytes 196616 | tf_op jit(solution)/shard_map/ppermute | solution.py:51
  27.2 5.4 %collective-permute-start.4 = (f32[2,32,128]{2,1,0:T(8,128)S(1)}, f32[2,32,128]{2,1,0:T(8,128)S(1)}, u32[]{:S(2)}, u32[]{:S(2)}) collective-permute-start(f32[2,32,128]{2,1,0:T(8,128)S(1)} %slice_select_fusion.3), channel_id=1, source_target_pairs={{0,16},{1,17},{2,18},{3,19},{4,20},{5,21},{6,22},{7,23},{8,24},{9,... | collective-permute-start | bytes 98312 | tf_op jit(solution)/shard_map/ppermute | solution.py:51
  32.6 4.9 %collective-permute-start.5 = (f32[2,32,128]{2,1,0:T(8,128)S(1)}, f32[2,32,128]{2,1,0:T(8,128)S(1)}, u32[]{:S(2)}, u32[]{:S(2)}) collective-permute-start(f32[2,32,128]{2,1,0:T(8,128)S(1)} %select_add_fusion.3), channel_id=1, source_target_pairs={{0,16},{1,17},{2,18},{3,19},{4,20},{5,21},{6,22},{7,23},{8,24},{9,... | collective-permute-start | bytes 98312 | tf_op jit(solution)/shard_map/ppermute | solution.py:54
  37.5 4.3 %collective-permute-start.6 = (f32[2,32,256]{2,1,0:T(8,128)S(1)}, f32[2,32,256]{2,1,0:T(8,128)S(1)}, u32[]{:S(2)}, u32[]{:S(2)}) collective-permute-start(f32[2,32,256]{2,1,0:T(8,128)S(1)} %maximum_select_fusion.11), channel_id=1, source_target_pairs={{0,8},{1,9},{2,10},{3,11},{4,12},{5,13},{6,14},{7,15},{8,0},{9,1},... | collective-permute-start | bytes 196616 | tf_op jit(solution)/shard_map/ppermute | solution.py:54
  41.8 5.0 %collective-permute-start.7 = (f32[2,32,512]{2,1,0:T(8,128)S(1)}, f32[2,32,512]{2,1,0:T(8,128)S(1)}, u32[]{:S(2)}, u32[]{:S(2)}) collective-permute-start(f32[2,32,512]{2,1,0:T(8,128)S(1)} %maximum_select_fusion.8), channel_id=1, source_target_pairs={{0,4},{1,3},{2,6},{3,1},{4,0},{5,7},{6,2},{7,5},{8,12},{9,11},{10,... | collective-permute-start | bytes 393224 | tf_op jit(solution)/shard_map/ppermute | solution.py:54
  46.9 6.4 %collective-permute-start.8 = (f32[2,32,1024]{2,1,0:T(8,128)S(1)}, f32[2,32,1024]{2,1,0:T(8,128)S(1)}, u32[]{:S(2)}, u32[]{:S(2)}) collective-permute-start(f32[2,32,1024]{2,1,0:T(8,128)S(1)} %maximum_select_fusion.5), channel_id=1, source_target_pairs={{0,2},{1,5},{2,0},{3,7},{4,6},{5,1},{6,4},{7,3},{8,10},{9,13},{10,... | collective-permute-start | bytes 786440 | tf_op jit(solution)/shard_map/ppermute | solution.py:54
  53.4 2.0 %collective-permute-start.9 = (f32[2,32,2048]{2,1,0:T(8,128)S(1)}, f32[2,32,2048]{2,1,0:T(8,128)S(1)}, u32[]{:S(2)}, u32[]{:S(2)}) collective-permute-start(f32[2,32,2048]{2,1,0:T(8,128)S(1)} %maximum_select_fusion.2), channel_id=1, source_target_pairs={{0,1},{1,0},{2,3},{3,2},{4,5},{5,4},{6,7},{7,6},{8,9},{9,8},{10,11... | collective-permute-start | bytes 1572872 | tf_op jit(solution)/shard_map/ppermute | solution.py:54
  55.5 2.2 %copy-start = (f32[2,128,4096]{2,1,0:T(8,128)S(1)}, f32[2,128,4096]{2,1,0:T(8,128)}, u32[]{:S(2)}) copy-start(f32[2,128,4096]{2,1,0:T(8,128)} %f_ref.1) | copy-start | bytes 12582916
  59.9 4.9 %collective-permute-start.10 = (f32[2,32,128]{2,1,0:T(8,128)S(1)}, f32[2,32,128]{2,1,0:T(8,128)S(1)}, u32[]{:S(2)}, u32[]{:S(2)}) collective-permute-start(f32[2,32,128]{2,1,0:T(8,128)S(1)} %shard_map.83), channel_id=1, source_target_pairs={{0,16},{1,17},{2,18},{3,19},{4,20},{5,21},{6,22},{7,23},{8,24},{9,... | collective-permute-start | bytes 98312 | tf_op jit(solution)/shard_map/ppermute | solution.py:63
  64.8 4.3 %collective-permute-start.11 = (f32[2,32,2,128]{3,1,0,2:T(8,128)S(1)}, f32[2,32,2,128]{3,1,0,2:T(8,128)S(1)}, u32[]{:S(2)}, u32[]{:S(2)}) collective-permute-start(f32[2,32,2,128]{3,1,0,2:T(8,128)S(1)} %maximum_select_fusion.13), channel_id=1, source_target_pairs={{0,8},{1,9},{2,10},{3,11},{4,12},{5,13},{6,14},{7,15},{8,0},{9,1},... | collective-permute-start | bytes 196616 | tf_op jit(solution)/shard_map/ppermute | solution.py:63
  69.1 5.0 %collective-permute-start.12 = (f32[2,32,2,2,128]{4,1,0,2,3:T(8,128)S(1)}, f32[2,32,2,2,128]{4,1,0,2,3:T(8,128)S(1)}, u32[]{:S(2)}, u32[]{:S(2)}) collective-permute-start(f32[2,32,2,2,128]{4,1,0,2,3:T(8,128)S(1)} %maximum_select_fusion.10), channel_id=1, source_target_pairs={{0,4},{1,5},{2,6},{3,7},{4,0},{5,1},{6,2},{7,3},{8,12},{9,13},{10,... | collective-permute-start | bytes 393224 | tf_op jit(solution)/shard_map/ppermute | solution.py:63
  74.2 6.4 %collective-permute-start.13 = (f32[2,32,2,2,2,128]{5,1,0,2,3,4:T(8,128)S(1)}, f32[2,32,2,2,2,128]{5,1,0,2,3,4:T(8,128)S(1)}, u32[]{:S(2)}, u32[]{:S(2)}) collective-permute-start(f32[2,32,2,2,2,128]{5,1,0,2,3,4:T(8,128)S(1)} %maximum_select_fusion.7), channel_id=1, source_target_pairs={{0,2},{1,3},{2,0},{3,1},{4,6},{5,7},{6,4},{7,5},{8,10},{9,11},{10,... | collective-permute-start | bytes 786440 | tf_op jit(solution)/shard_map/ppermute | solution.py:63
  80.7 2.0 %collective-permute-start.14 = (f32[2,32,2,2,2,2,128]{6,1,0,2,3,4,5:T(8,128)S(1)}, f32[2,32,2,2,2,2,128]{6,1,0,2,3,4,5:T(8,128)S(1)}, u32[]{:S(2)}, u32[]{:S(2)}) collective-permute-start(f32[2,32,2,2,2,2,128]{6,1,0,2,3,4,5:T(8,128)S(1)} %maximum_select_fusion.4), channel_id=1, source_target_pairs={{0,1},{1,0},{2,3},{3,2},{4,5},{5,4},{6,7},{7,6},{8,9},{9,8},{10,11... | collective-permute-start | bytes 1572872 | tf_op jit(solution)/shard_map/ppermute | solution.py:63
  90.7 1.2 %collective-permute-start.15 = (f32[2,32]{1,0:T(2,128)S(1)}, f32[2,32]{1,0:T(2,128)S(1)}, u32[]{:S(2)}, u32[]{:S(2)}) collective-permute-start(f32[2,32]{1,0:T(2,128)S(1)} %pad_maximum_fusion), channel_id=1, source_target_pairs={{0,1},{1,0},{2,3},{3,2},{4,5},{5,4},{6,7},{7,6},{8,9},{9,8},{10,11... | collective-permute-start | bytes 776 | tf_op jit(solution)/shard_map/ppermute | solution.py:74
  92.0 3.6 %collective-permute-start.16 = (f32[2,32]{1,0:T(2,128)S(1)}, f32[2,32]{1,0:T(2,128)S(1)}, u32[]{:S(2)}, u32[]{:S(2)}) collective-permute-start(f32[2,32]{1,0:T(2,128)S(1)} %fusion.7), channel_id=1, source_target_pairs={{0,2},{1,3},{2,0},{3,1},{4,6},{5,7},{6,4},{7,5},{8,10},{9,11},{10,... | collective-permute-start | bytes 776 | tf_op jit(solution)/shard_map/ppermute | solution.py:74
  95.6 3.6 %collective-permute-start.17 = (f32[2,32]{1,0:T(2,128)S(1)}, f32[2,32]{1,0:T(2,128)S(1)}, u32[]{:S(2)}, u32[]{:S(2)}) collective-permute-start(f32[2,32]{1,0:T(2,128)S(1)} %fusion.10), channel_id=1, source_target_pairs={{0,4},{1,5},{2,6},{3,7},{4,0},{5,1},{6,2},{7,3},{8,12},{9,13},{10,... | collective-permute-start | bytes 776 | tf_op jit(solution)/shard_map/ppermute | solution.py:74
  99.3 3.6 %collective-permute-start.18 = (f32[2,32]{1,0:T(2,128)S(1)}, f32[2,32]{1,0:T(2,128)S(1)}, u32[]{:S(2)}, u32[]{:S(2)}) collective-permute-start(f32[2,32]{1,0:T(2,128)S(1)} %add.47), channel_id=1, source_target_pairs={{0,8},{1,9},{2,10},{3,11},{4,12},{5,13},{6,14},{7,15},{8,0},{9,1},... | collective-permute-start | bytes 776 | tf_op jit(solution)/shard_map/ppermute | solution.py:74
  102.9 4.5 %collective-permute-start.19 = (f32[2,32]{1,0:T(2,128)S(1)}, f32[2,32]{1,0:T(2,128)S(1)}, u32[]{:S(2)}, u32[]{:S(2)}) collective-permute-start(f32[2,32]{1,0:T(2,128)S(1)} %add.48), channel_id=1, source_target_pairs={{0,16},{1,17},{2,18},{3,19},{4,20},{5,21},{6,22},{7,23},{8,24},{9,... | collective-permute-start | bytes 776 | tf_op jit(solution)/shard_map/ppermute | solution.py:74

commit v11 on v10

--- a/solution.py
+++ b/solution.py
@@ -139,20 +139,31 @@
 
 
 def _precond_kernel(g_ref, f_ref, out_ref):
+    @pl.when(pl.program_id(0) == 0)
+    def _():
+        out_ref[...] = jnp.zeros(out_ref.shape, jnp.float32)
+
     nt = (((1,), (1,)), ((), ()))
     f = lambda a, b: lax.dot_general(a, b, nt, preferred_element_type=jnp.float32)
     for m in range(g_ref.shape[0]):
         g_high, g_low = _split_bf16(g_ref[m])
         f_high, f_low = _split_bf16(f_ref[m])
-        out_ref[m] = f(g_high, f_high) + (f(g_low, f_high) + f(g_high, f_low))
+        out_ref[m] += f(g_high, f_high) + (f(g_low, f_high) + f(g_high, f_low))
 
 
 def _precond(grads, fisher_inv):
-    modules, queries, _ = grads.shape
+    modules, queries, width = grads.shape
+    cols = fisher_inv.shape[1]
+    block = min(width, 1024)
     return pl.pallas_call(
         _precond_kernel,
-        out_shape=jax.ShapeDtypeStruct((modules, queries, fisher_inv.shape[1]), jnp.float32),
-        compiler_params=pltpu.CompilerParams(vmem_limit_bytes=48 * 1024 * 1024),
+        out_shape=jax.ShapeDtypeStruct((modules, queries, cols), jnp.float32),
+        grid=(width // block,),
+        in_specs=[
+            pl.BlockSpec((modules, queries, block), lambda k: (0, 0, k)),
+            pl.BlockSpec((modules, cols, block), lambda k: (0, 0, k)),
+        ],
+        out_specs=pl.BlockSpec((modules, queries, cols), lambda k: (0, 0, 0)),
     )(grads, fisher_inv)
 
 

time: 108 us -> 111 us (1.028)
  other arithmetic: 2.51 us -> 5.99 us
  Pallas kernels: 9.12 us -> 12.2 us
  local copies, waits for them, and re-layouts: 3.83 us -> 1.65 us
  waiting for transfers between devices: 50.2 us -> 48.8 us
    pallas_call x1, Pallas kernels: 2.15 us -> 5.25 us  [_precond(): pl.pallas_call(_precond_kernel, out_shape=jax.ShapeDtypeStruct((modules,...]
    unnamed x2 -> x0, local copies, waits for them, and re-layouts: 2.18 us -> none
    select_n x9, other arithmetic: 0.26 us -> 1.93 us  [_allgather(): jnp.where(low, jnp.stack([cur, other], -2), jnp.stack([other, cur], -2))]
    ppermute x5, waiting for transfers between devices: 14.3 us -> 12.9 us  [_allgather(): other = lax.ppermute(cur, 'rows', _xor_pairs(size, s))]
  transfers between devices with their start and end apart: 20 -> 20, of which waited for: 20 -> 20; matrix products, arithmetic and copies ran while one was open for 0% -> 2% of each run, Pallas kernels for 0% -> 0%
where the time goes in v11:
time: 111 us
  waiting for transfers between devices  48.8 us (44%)
  starting transfers between devices  35.8 us (32%)
  Pallas kernels  12.2 us (11%)
  matrix products  6.3 us (6%)
  other arithmetic  5.99 us (5%)
  local copies, waits for them, and re-layouts  1.65 us (1%)
    ppermute x5, waiting for transfers between devices, _allreduce(): lax.ppermute(cur, 'rows', _pairs(size, orders, t))  14.3 us
    ppermute x5, waiting for transfers between devices, _allgather(): other = lax.ppermute(cur, 'rows', _xor_pairs(size, s))  12.9 us
    ppermute x4, waiting for transfers between devices, _allreduce(): cur = keep + lax.ppermute(send, 'rows', _pairs(size, orders, t))  11.5 us
    ppermute x4, starting transfers between devices, _allreduce(): cur = keep + lax.ppermute(send, 'rows', _pairs(size, orders, t))  10.6 us
    ppermute x5, waiting for transfers between devices, _butterfly_sum(): x = x + lax.ppermute(x, 'rows', _xor_pairs(size, s))  8.38 us
    ppermute x5, starting transfers between devices, _allreduce(): lax.ppermute(cur, 'rows', _pairs(size, orders, t))  8.29 us
    ppermute x5, starting transfers between devices, _allgather(): other = lax.ppermute(cur, 'rows', _xor_pairs(size, s))  8.19 us
    ppermute x5, starting transfers between devices, _butterfly_sum(): x = x + lax.ppermute(x, 'rows', _xor_pairs(size, s))  8.18 us
  transfers between devices with their start and end apart: 20, of which 20 were waited for; matrix products, arithmetic and copies ran while one was open for 2% of the time, Pallas kernels for 0%

profile of v11, /device:TPU:0, one launch (start us, length us, event | category | flops | bytes accessed | tf_op | source)
XLA Modules:
  0.0 110.9 jit_solution(6000744263820705599)
XLA Ops:
  0.0 7.0 %shard_map.82 = (f32[2,32,2048]{2,1,0:T(8,128)}, f32[2,32,2048]{2,1,0:T(8,128)}) custom-call(s32[1,32]{1,0:T(1,128)} %bitcast.55, s32[1,128]{1,0:T(1,128)} %bitcast.56, bf16[128,2,4096]{2,1,0:T(2,128)(2,1)} %acts_ref.1, bf16[128,2,4096]{2,1,0:T(2,128)(2,1)} %gout_ref.1, bf16[4096,128]{1,0:T(8,128)(2,1)} %pin_ref.1, bf16[4096,128]{1,0:T(8,128)(2,1)} %pout_ref.1), custom_call_target="tpu_custom_call" | custom-call | tf_op jit(solution)/shard_map/pallas_call | solution.py:129
  10.3 2.9 %collective-permute-start.1 = (f32[2,32,1024]{2,1,0:T(8,128)S(1)}, f32[2,32,1024]{2,1,0:T(8,128)S(1)}, u32[]{:S(2)}, u32[]{:S(2)}) collective-permute-start(f32[2,32,1024]{2,1,0:T(8,128)S(1)} %slice_select_fusion), channel_id=1, source_target_pairs={{0,2},{1,5},{2,0},{3,7},{4,6},{5,1},{6,4},{7,3},{8,10},{9,13},{10,... | collective-permute-start | bytes 786440 | tf_op jit(solution)/shard_map/ppermute | solution.py:51
  13.3 4.4 %collective-permute-done.1 = f32[2,32,1024]{2,1,0:T(8,128)S(1)} collective-permute-done((f32[2,32,1024]{2,1,0:T(8,128)S(1)}, f32[2,32,1024]{2,1,0:T(8,128)S(1)}, u32[]{:S(2)}, u32[]{:S(2)}) %collective-permute-start.1) | collective-permute-done | bytes 262176 | tf_op jit(solution)/shard_map/ppermute | solution.py:51
  17.7 2.1 %collective-permute-start.2 = (f32[2,32,512]{2,1,0:T(8,128)S(1)}, f32[2,32,512]{2,1,0:T(8,128)S(1)}, u32[]{:S(2)}, u32[]{:S(2)}) collective-permute-start(f32[2,32,512]{2,1,0:T(8,128)S(1)} %slice_select_fusion.1), channel_id=1, source_target_pairs={{0,4},{1,3},{2,6},{3,1},{4,0},{5,7},{6,2},{7,5},{8,12},{9,11},{10,... | collective-permute-start | bytes 393224 | tf_op jit(solution)/shard_map/ppermute | solution.py:51
  19.8 2.9 %collective-permute-done.2 = f32[2,32,512]{2,1,0:T(8,128)S(1)} collective-permute-done((f32[2,32,512]{2,1,0:T(8,128)S(1)}, f32[2,32,512]{2,1,0:T(8,128)S(1)}, u32[]{:S(2)}, u32[]{:S(2)}) %collective-permute-start.2) | collective-permute-done | bytes 131104 | tf_op jit(solution)/shard_map/ppermute | solution.py:51
  22.8 2.1 %collective-permute-start.3 = (f32[2,32,256]{2,1,0:T(8,128)S(1)}, f32[2,32,256]{2,1,0:T(8,128)S(1)}, u32[]{:S(2)}, u32[]{:S(2)}) collective-permute-start(f32[2,32,256]{2,1,0:T(8,128)S(1)} %slice_select_fusion.2), channel_id=1, source_target_pairs={{0,8},{1,9},{2,10},{3,11},{4,12},{5,13},{6,14},{7,15},{8,0},{9,1},... | collective-permute-start | bytes 196616 | tf_op jit(solution)/shard_map/ppermute | solution.py:51
  24.9 2.2 %collective-permute-done.3 = f32[2,32,256]{2,1,0:T(8,128)S(1)} collective-permute-done((f32[2,32,256]{2,1,0:T(8,128)S(1)}, f32[2,32,256]{2,1,0:T(8,128)S(1)}, u32[]{:S(2)}, u32[]{:S(2)}) %collective-permute-start.3) | collective-permute-done | bytes 65568 | tf_op jit(solution)/shard_map/ppermute | solution.py:51
  27.2 3.4 %collective-permute-start.4 = (f32[2,32,128]{2,1,0:T(8,128)S(1)}, f32[2,32,128]{2,1,0:T(8,128)S(1)}, u32[]{:S(2)}, u32[]{:S(2)}) collective-permute-start(f32[2,32,128]{2,1,0:T(8,128)S(1)} %slice_select_fusion.3), channel_id=1, source_target_pairs={{0,16},{1,17},{2,18},{3,19},{4,20},{5,21},{6,22},{7,23},{8,24},{9,... | collective-permute-start | bytes 98312 | tf_op jit(solution)/shard_map/ppermute | solution.py:51
  30.7 1.9 %collective-permute-done.4 = f32[2,32,128]{2,1,0:T(8,128)S(1)} collective-permute-done((f32[2,32,128]{2,1,0:T(8,128)S(1)}, f32[2,32,128]{2,1,0:T(8,128)S(1)}, u32[]{:S(2)}, u32[]{:S(2)}) %collective-permute-start.4) | collective-permute-done | bytes 32800 | tf_op jit(solution)/shard_map/ppermute | solution.py:51
  32.6 2.9 %collective-permute-start.5 = (f32[2,32,128]{2,1,0:T(8,128)S(1)}, f32[2,32,128]{2,1,0:T(8,128)S(1)}, u32[]{:S(2)}, u32[]{:S(2)}) collective-permute-start(f32[2,32,128]{2,1,0:T(8,128)S(1)} %select_add_fusion.3), channel_id=1, source_target_pairs={{0,16},{1,17},{2,18},{3,19},{4,20},{5,21},{6,22},{7,23},{8,24},{9,... | collective-permute-start | bytes 98312 | tf_op jit(solution)/shard_map/ppermute | solution.py:54
  37.5 2.1 %collective-permute-start.6 = (f32[2,32,256]{2,1,0:T(8,128)S(1)}, f32[2,32,256]{2,1,0:T(8,128)S(1)}, u32[]{:S(2)}, u32[]{:S(2)}) collective-permute-start(f32[2,32,256]{2,1,0:T(8,128)S(1)} %maximum_select_fusion.11), channel_id=1, source_target_pairs={{0,8},{1,9},{2,10},{3,11},{4,12},{5,13},{6,14},{7,15},{8,0},{9,1},... | collective-permute-start | bytes 196616 | tf_op jit(solution)/shard_map/ppermute | solution.py:54
  39.6 2.3 %collective-permute-done.6 = f32[2,32,256]{2,1,0:T(8,128)S(1)} collective-permute-done((f32[2,32,256]{2,1,0:T(8,128)S(1)}, f32[2,32,256]{2,1,0:T(8,128)S(1)}, u32[]{:S(2)}, u32[]{:S(2)}) %collective-permute-start.6) | collective-permute-done | bytes 65568 | tf_op jit(solution)/shard_map/ppermute | solution.py:54
  43.4 3.4 %collective-permute-done.7 = f32[2,32,512]{2,1,0:T(8,128)S(1)} collective-permute-done((f32[2,32,512]{2,1,0:T(8,128)S(1)}, f32[2,32,512]{2,1,0:T(8,128)S(1)}, u32[]{:S(2)}, u32[]{:S(2)}) %collective-permute-start.7) | collective-permute-done | bytes 131104 | tf_op jit(solution)/shard_map/ppermute | solution.py:54
  48.5 4.8 %collective-permute-done.8 = f32[2,32,1024]{2,1,0:T(8,128)S(1)} collective-permute-done((f32[2,32,1024]{2,1,0:T(8,128)S(1)}, f32[2,32,1024]{2,1,0:T(8,128)S(1)}, u32[]{:S(2)}, u32[]{:S(2)}) %collective-permute-start.8) | collective-permute-done | bytes 262176 | tf_op jit(solution)/shard_map/ppermute | solution.py:54
  56.5 5.2 %shard_map.83 = f32[2,32,128]{2,1,0:T(8,128)} custom-call(f32[2,32,4096]{2,1,0:T(8,128)} %maximum_select_fusion.g_ref, f32[2,128,4096]{2,1,0:T(8,128)} %f_ref.1), custom_call_target="tpu_custom_call" | custom-call | tf_op jit(solution)/shard_map/pallas_call | solution.py:158
  61.7 3.0 %collective-permute-start.10 = (f32[2,32,128]{2,1,0:T(8,128)}, f32[2,32,128]{2,1,0:T(8,128)S(1)}, u32[]{:S(2)}, u32[]{:S(2)}) collective-permute-start(f32[2,32,128]{2,1,0:T(8,128)} %shard_map.83), channel_id=1, source_target_pairs={{0,16},{1,17},{2,18},{3,19},{4,20},{5,21},{6,22},{7,23},{8,24},{9,... | collective-permute-start | bytes 98312 | tf_op jit(solution)/shard_map/ppermute | solution.py:63
  64.7 2.1 %collective-permute-done.10 = f32[2,32,128]{2,1,0:T(8,128)S(1)} collective-permute-done((f32[2,32,128]{2,1,0:T(8,128)}, f32[2,32,128]{2,1,0:T(8,128)S(1)}, u32[]{:S(2)}, u32[]{:S(2)}) %collective-permute-start.10) | collective-permute-done | bytes 32800 | tf_op jit(solution)/shard_map/ppermute | solution.py:63
  67.7 2.0 %collective-permute-start.11 = (f32[2,32,2,128]{3,1,0,2:T(8,128)S(1)}, f32[2,32,2,128]{3,1,0,2:T(8,128)S(1)}, u32[]{:S(2)}, u32[]{:S(2)}) collective-permute-start(f32[2,32,2,128]{3,1,0,2:T(8,128)S(1)} %maximum_select_fusion.13), channel_id=1, source_target_pairs={{0,8},{1,9},{2,10},{3,11},{4,12},{5,13},{6,14},{7,15},{8,0},{9,1},... | collective-permute-start | bytes 196616 | tf_op jit(solution)/shard_map/ppermute | solution.py:63
  74.4 2.6 %collective-permute-done.12 = f32[2,32,2,2,128]{4,1,0,2,3:T(8,128)S(1)} collective-permute-done((f32[2,32,2,2,128]{4,1,0,2,3:T(8,128)S(1)}, f32[2,32,2,2,128]{4,1,0,2,3:T(8,128)S(1)}, u32[]{:S(2)}, u32[]{:S(2)}) %collective-permute-start.12) | collective-permute-done | bytes 131104 | tf_op jit(solution)/shard_map/ppermute | solution.py:63
  78.7 4.8 %collective-permute-done.13 = f32[2,32,2,2,2,128]{5,1,0,2,3,4:T(8,128)S(1)} collective-permute-done((f32[2,32,2,2,2,128]{5,1,0,2,3,4:T(8,128)S(1)}, f32[2,32,2,2,2,128]{5,1,0,2,3,4:T(8,128)S(1)}, u32[]{:S(2)}, u32[]{:S(2)}) %collective-permute-start.13) | collective-permute-done | bytes 262176 | tf_op jit(solution)/shard_map/ppermute | solution.py:63
  87.3 6.3 %fusion.8 = (f32[32]{0:T(128)S(1)}, f32[32]{0:T(128)S(1)}, f32[32,128]{1,0:T(8,128)S(1)}) fusion(f32[2,32,4096]{2,1,0:T(8,128)S(1)} %select_n.249, f32[128,2,4096]{2,1,0:T(2,128)} %param.15), kind=kOutput, calls=%fused_computation.33 | convolution fusion | flops 201338816 | bytes 5259520 | tf_op jit(solution)/shard_map/mqk,nmk->qn/dot_general | solution.py:179
  96.4 2.1 %collective-permute-done.16 = f32[2,32]{1,0:T(2,128)S(1)} collective-permute-done((f32[2,32]{1,0:T(2,128)S(1)}, f32[2,32]{1,0:T(2,128)S(1)}, u32[]{:S(2)}, u32[]{:S(2)}) %collective-permute-start.16) | collective-permute-done | bytes 288 | tf_op jit(solution)/shard_map/ppermute | solution.py:74
  100.1 2.1 %collective-permute-done.17 = f32[2,32]{1,0:T(2,128)S(1)} collective-permute-done((f32[2,32]{1,0:T(2,128)S(1)}, f32[2,32]{1,0:T(2,128)S(1)}, u32[]{:S(2)}, u32[]{:S(2)}) %collective-permute-start.17) | collective-permute-done | bytes 288 | tf_op jit(solution)/shard_map/ppermute | solution.py:74
  105.7 2.9 %collective-permute-start.19 = (f32[2,32]{1,0:T(2,128)S(1)}, f32[2,32]{1,0:T(2,128)S(1)}, u32[]{:S(2)}, u32[]{:S(2)}) collective-permute-start(f32[2,32]{1,0:T(2,128)S(1)} %add.48), channel_id=1, source_target_pairs={{0,16},{1,17},{2,18},{3,19},{4,20},{5,21},{6,22},{7,23},{8,24},{9,... | collective-permute-start | bytes 776 | tf_op jit(solution)/shard_map/ppermute | solution.py:74
  (56 shorter events, 33.0 us)
Async XLA Ops:
  7.0 2.2 %collective-permute-start = (f32[2,32,2048]{2,1,0:T(8,128)}, f32[2,32,2048]{2,1,0:T(8,128)S(1)}, u32[]{:S(2)}, u32[]{:S(2)}) collective-permute-start(f32[2,32,2048]{2,1,0:T(8,128)} %get-tuple-element.8), channel_id=1, source_target_pairs={{0,1},{1,0},{2,3},{3,2},{4,5},{5,4},{6,7},{7,6},{8,9},{9,8},{10,11... | collective-permute-start | bytes 1572872 | tf_op jit(solution)/shard_map/ppermute | solution.py:43
  10.3 7.3 %collective-permute-start.1 = (f32[2,32,1024]{2,1,0:T(8,128)S(1)}, f32[2,32,1024]{2,1,0:T(8,128)S(1)}, u32[]{:S(2)}, u32[]{:S(2)}) collective-permute-start(f32[2,32,1024]{2,1,0:T(8,128)S(1)} %slice_select_fusion), channel_id=1, source_target_pairs={{0,2},{1,5},{2,0},{3,7},{4,6},{5,1},{6,4},{7,3},{8,10},{9,13},{10,... | collective-permute-start | bytes 786440 | tf_op jit(solution)/shard_map/ppermute | solution.py:51
  17.7 5.1 %collective-permute-start.2 = (f32[2,32,512]{2,1,0:T(8,128)S(1)}, f32[2,32,512]{2,1,0:T(8,128)S(1)}, u32[]{:S(2)}, u32[]{:S(2)}) collective-permute-start(f32[2,32,512]{2,1,0:T(8,128)S(1)} %slice_select_fusion.1), channel_id=1, source_target_pairs={{0,4},{1,3},{2,6},{3,1},{4,0},{5,7},{6,2},{7,5},{8,12},{9,11},{10,... | collective-permute-start | bytes 393224 | tf_op jit(solution)/shard_map/ppermute | solution.py:51
  22.8 4.4 %collective-permute-start.3 = (f32[2,32,256]{2,1,0:T(8,128)S(1)}, f32[2,32,256]{2,1,0:T(8,128)S(1)}, u32[]{:S(2)}, u32[]{:S(2)}) collective-permute-start(f32[2,32,256]{2,1,0:T(8,128)S(1)} %slice_select_fusion.2), channel_id=1, source_target_pairs={{0,8},{1,9},{2,10},{3,11},{4,12},{5,13},{6,14},{7,15},{8,0},{9,1},... | collective-permute-start | bytes 196616 | tf_op jit(solution)/shard_map/ppermute | solution.py:51
  27.2 5.4 %collective-permute-start.4 = (f32[2,32,128]{2,1,0:T(8,128)S(1)}, f32[2,32,128]{2,1,0:T(8,128)S(1)}, u32[]{:S(2)}, u32[]{:S(2)}) collective-permute-start(f32[2,32,128]{2,1,0:T(8,128)S(1)} %slice_select_fusion.3), channel_id=1, source_target_pairs={{0,16},{1,17},{2,18},{3,19},{4,20},{5,21},{6,22},{7,23},{8,24},{9,... | collective-permute-start | bytes 98312 | tf_op jit(solution)/shard_map/ppermute | solution.py:51
  32.6 4.9 %collective-permute-start.5 = (f32[2,32,128]{2,1,0:T(8,128)S(1)}, f32[2,32,128]{2,1,0:T(8,128)S(1)}, u32[]{:S(2)}, u32[]{:S(2)}) collective-permute-start(f32[2,32,128]{2,1,0:T(8,128)S(1)} %select_add_fusion.3), channel_id=1, source_target_pairs={{0,16},{1,17},{2,18},{3,19},{4,20},{5,21},{6,22},{7,23},{8,24},{9,... | collective-permute-start | bytes 98312 | tf_op jit(solution)/shard_map/ppermute | solution.py:54
  37.5 4.3 %collective-permute-start.6 = (f32[2,32,256]{2,1,0:T(8,128)S(1)}, f32[2,32,256]{2,1,0:T(8,128)S(1)}, u32[]{:S(2)}, u32[]{:S(2)}) collective-permute-start(f32[2,32,256]{2,1,0:T(8,128)S(1)} %maximum_select_fusion.11), channel_id=1, source_target_pairs={{0,8},{1,9},{2,10},{3,11},{4,12},{5,13},{6,14},{7,15},{8,0},{9,1},... | collective-permute-start | bytes 196616 | tf_op jit(solution)/shard_map/ppermute | solution.py:54
  41.8 5.0 %collective-permute-start.7 = (f32[2,32,512]{2,1,0:T(8,128)S(1)}, f32[2,32,512]{2,1,0:T(8,128)S(1)}, u32[]{:S(2)}, u32[]{:S(2)}) collective-permute-start(f32[2,32,512]{2,1,0:T(8,128)S(1)} %maximum_select_fusion.8), channel_id=1, source_target_pairs={{0,4},{1,3},{2,6},{3,1},{4,0},{5,7},{6,2},{7,5},{8,12},{9,11},{10,... | collective-permute-start | bytes 393224 | tf_op jit(solution)/shard_map/ppermute | solution.py:54
  46.9 6.4 %collective-permute-start.8 = (f32[2,32,1024]{2,1,0:T(8,128)S(1)}, f32[2,32,1024]{2,1,0:T(8,128)S(1)}, u32[]{:S(2)}, u32[]{:S(2)}) collective-permute-start(f32[2,32,1024]{2,1,0:T(8,128)S(1)} %maximum_select_fusion.5), channel_id=1, source_target_pairs={{0,2},{1,5},{2,0},{3,7},{4,6},{5,1},{6,4},{7,3},{8,10},{9,13},{10,... | collective-permute-start | bytes 786440 | tf_op jit(solution)/shard_map/ppermute | solution.py:54
  53.4 2.0 %collective-permute-start.9 = (f32[2,32,2048]{2,1,0:T(8,128)S(1)}, f32[2,32,2048]{2,1,0:T(8,128)S(1)}, u32[]{:S(2)}, u32[]{:S(2)}) collective-permute-start(f32[2,32,2048]{2,1,0:T(8,128)S(1)} %maximum_select_fusion.2), channel_id=1, source_target_pairs={{0,1},{1,0},{2,3},{3,2},{4,5},{5,4},{6,7},{7,6},{8,9},{9,8},{10,11... | collective-permute-start | bytes 1572872 | tf_op jit(solution)/shard_map/ppermute | solution.py:54
  61.7 5.1 %collective-permute-start.10 = (f32[2,32,128]{2,1,0:T(8,128)}, f32[2,32,128]{2,1,0:T(8,128)S(1)}, u32[]{:S(2)}, u32[]{:S(2)}) collective-permute-start(f32[2,32,128]{2,1,0:T(8,128)} %shard_map.83), channel_id=1, source_target_pairs={{0,16},{1,17},{2,18},{3,19},{4,20},{5,21},{6,22},{7,23},{8,24},{9,... | collective-permute-start | bytes 98312 | tf_op jit(solution)/shard_map/ppermute | solution.py:63
  67.7 4.3 %collective-permute-start.11 = (f32[2,32,2,128]{3,1,0,2:T(8,128)S(1)}, f32[2,32,2,128]{3,1,0,2:T(8,128)S(1)}, u32[]{:S(2)}, u32[]{:S(2)}) collective-permute-start(f32[2,32,2,128]{3,1,0,2:T(8,128)S(1)} %maximum_select_fusion.13), channel_id=1, source_target_pairs={{0,8},{1,9},{2,10},{3,11},{4,12},{5,13},{6,14},{7,15},{8,0},{9,1},... | collective-permute-start | bytes 196616 | tf_op jit(solution)/shard_map/ppermute | solution.py:63
  72.0 5.0 %collective-permute-start.12 = (f32[2,32,2,2,128]{4,1,0,2,3:T(8,128)S(1)}, f32[2,32,2,2,128]{4,1,0,2,3:T(8,128)S(1)}, u32[]{:S(2)}, u32[]{:S(2)}) collective-permute-start(f32[2,32,2,2,128]{4,1,0,2,3:T(8,128)S(1)} %maximum_select_fusion.10), channel_id=1, source_target_pairs={{0,4},{1,5},{2,6},{3,7},{4,0},{5,1},{6,2},{7,3},{8,12},{9,13},{10,... | collective-permute-start | bytes 393224 | tf_op jit(solution)/shard_map/ppermute | solution.py:63
  77.1 6.4 %collective-permute-start.13 = (f32[2,32,2,2,2,128]{5,1,0,2,3,4:T(8,128)S(1)}, f32[2,32,2,2,2,128]{5,1,0,2,3,4:T(8,128)S(1)}, u32[]{:S(2)}, u32[]{:S(2)}) collective-permute-start(f32[2,32,2,2,2,128]{5,1,0,2,3,4:T(8,128)S(1)} %maximum_select_fusion.7), channel_id=1, source_target_pairs={{0,2},{1,3},{2,0},{3,1},{4,6},{5,7},{6,4},{7,5},{8,10},{9,11},{10,... | collective-permute-start | bytes 786440 | tf_op jit(solution)/shard_map/ppermute | solution.py:63
  83.6 2.0 %collective-permute-start.14 = (f32[2,32,2,2,2,2,128]{6,1,0,2,3,4,5:T(8,128)S(1)}, f32[2,32,2,2,2,2,128]{6,1,0,2,3,4,5:T(8,128)S(1)}, u32[]{:S(2)}, u32[]{:S(2)}) collective-permute-start(f32[2,32,2,2,2,2,128]{6,1,0,2,3,4,5:T(8,128)S(1)} %maximum_select_fusion.4), channel_id=1, source_target_pairs={{0,1},{1,0},{2,3},{3,2},{4,5},{5,4},{6,7},{7,6},{8,9},{9,8},{10,11... | collective-permute-start | bytes 1572872 | tf_op jit(solution)/shard_map/ppermute | solution.py:63
  93.6 1.2 %collective-permute-start.15 = (f32[2,32]{1,0:T(2,128)S(1)}, f32[2,32]{1,0:T(2,128)S(1)}, u32[]{:S(2)}, u32[]{:S(2)}) collective-permute-start(f32[2,32]{1,0:T(2,128)S(1)} %pad_maximum_fusion), channel_id=1, source_target_pairs={{0,1},{1,0},{2,3},{3,2},{4,5},{5,4},{6,7},{7,6},{8,9},{9,8},{10,11... | collective-permute-start | bytes 776 | tf_op jit(solution)/shard_map/ppermute | solution.py:74
  94.9 3.6 %collective-permute-start.16 = (f32[2,32]{1,0:T(2,128)S(1)}, f32[2,32]{1,0:T(2,128)S(1)}, u32[]{:S(2)}, u32[]{:S(2)}) collective-permute-start(f32[2,32]{1,0:T(2,128)S(1)} %fusion.7), channel_id=1, source_target_pairs={{0,2},{1,3},{2,0},{3,1},{4,6},{5,7},{6,4},{7,5},{8,10},{9,11},{10,... | collective-permute-start | bytes 776 | tf_op jit(solution)/shard_map/ppermute | solution.py:74
  98.5 3.6 %collective-permute-start.17 = (f32[2,32]{1,0:T(2,128)S(1)}, f32[2,32]{1,0:T(2,128)S(1)}, u32[]{:S(2)}, u32[]{:S(2)}) collective-permute-start(f32[2,32]{1,0:T(2,128)S(1)} %fusion.10), channel_id=1, source_target_pairs={{0,4},{1,5},{2,6},{3,7},{4,0},{5,1},{6,2},{7,3},{8,12},{9,13},{10,... | collective-permute-start | bytes 776 | tf_op jit(solution)/shard_map/ppermute | solution.py:74
  102.2 3.6 %collective-permute-start.18 = (f32[2,32]{1,0:T(2,128)S(1)}, f32[2,32]{1,0:T(2,128)S(1)}, u32[]{:S(2)}, u32[]{:S(2)}) collective-permute-start(f32[2,32]{1,0:T(2,128)S(1)} %add.47), channel_id=1, source_target_pairs={{0,8},{1,9},{2,10},{3,11},{4,12},{5,13},{6,14},{7,15},{8,0},{9,1},... | collective-permute-start | bytes 776 | tf_op jit(solution)/shard_map/ppermute | solution.py:74
  105.7 4.5 %collective-permute-start.19 = (f32[2,32]{1,0:T(2,128)S(1)}, f32[2,32]{1,0:T(2,128)S(1)}, u32[]{:S(2)}, u32[]{:S(2)}) collective-permute-start(f32[2,32]{1,0:T(2,128)S(1)} %add.48), channel_id=1, source_target_pairs={{0,16},{1,17},{2,18},{3,19},{4,20},{5,21},{6,22},{7,23},{8,24},{9,... | collective-permute-start | bytes 776 | tf_op jit(solution)/shard_map/ppermute | solution.py:74

commit v12 on v10

--- a/solution.py
+++ b/solution.py
@@ -57,11 +57,19 @@
 
 def _allgather(x, size):
     me = lax.axis_index("rows")
+    steps = _steps(size)
+    orders = [list(reversed(o)) for o in _orders(size)]
+    lead = x.ndim - 1
     cur = x
-    for s in reversed(range(_steps(size))):
-        low = ((me >> s) & 1) == 0
-        other = lax.ppermute(cur, "rows", _xor_pairs(size, s))
-        cur = jnp.where(low, jnp.stack([cur, other], -2), jnp.stack([other, cur], -2))
+    for t in range(steps):
+        if t == steps - 1 and orders[0] != orders[1]:
+            perm = list(range(cur.ndim))
+            a, b = lead + steps - 3, lead + steps - 2
+            perm[a], perm[b] = perm[b], perm[a]
+            cur = jnp.where((me & 1) == 0, cur, jnp.transpose(cur, perm))
+        bit = jnp.where((me & 1) == 0, (me >> orders[0][t]) & 1, (me >> orders[1][t]) & 1)
+        other = lax.ppermute(cur, "rows", [(i, i ^ (1 << orders[i & 1][t])) for i in range(size)])
+        cur = jnp.where(bit == 0, jnp.stack([cur, other], -2), jnp.stack([other, cur], -2))
     return cur.reshape(*x.shape[:-1], size * x.shape[-1])
 
 

time: 108 us -> 109 us (level)
  no operation moved by 1% of the time
where the time goes in v12:
time: 109 us
  waiting for transfers between devices  50.5 us (46%)
  starting transfers between devices  36.2 us (33%)
  Pallas kernels  9.12 us (8%)
  matrix products  6.3 us (6%)
  local copies, waits for them, and re-layouts  3.83 us (4%)
  other arithmetic  2.52 us (2%)
    ppermute x5, waiting for transfers between devices, _allgather(): lax.ppermute(cur, 'rows', [(i, i ^ 1 << orders[i & 1][t]) for i in range(...  14.6 us
    ppermute x5, waiting for transfers between devices, _allreduce(): lax.ppermute(cur, 'rows', _pairs(size, orders, t))  14.3 us
    ppermute x4, waiting for transfers between devices, _allreduce(): cur = keep + lax.ppermute(send, 'rows', _pairs(size, orders, t))  11.5 us
    ppermute x4, starting transfers between devices, _allreduce(): cur = keep + lax.ppermute(send, 'rows', _pairs(size, orders, t))  10.6 us
    ppermute x5, starting transfers between devices, _butterfly_sum(): x = x + lax.ppermute(x, 'rows', _xor_pairs(size, s))  8.53 us
    ppermute x5, starting transfers between devices, _allreduce(): lax.ppermute(cur, 'rows', _pairs(size, orders, t))  8.29 us
    ppermute x5, waiting for transfers between devices, _butterfly_sum(): x = x + lax.ppermute(x, 'rows', _xor_pairs(size, s))  8.26 us
    ppermute x5, starting transfers between devices, _allgather(): lax.ppermute(cur, 'rows', [(i, i ^ 1 << orders[i & 1][t]) for i in range(...  8.24 us
  transfers between devices with their start and end apart: 20, of which 20 were waited for; matrix products, arithmetic and copies ran while one was open for 0% of the time, Pallas kernels for 0%

profile of v12, /device:TPU:0, one launch (start us, length us, event | category | flops | bytes accessed | tf_op | source)
XLA Modules:
  0.0 108.6 jit_solution(4871582584339975450)
XLA Ops:
  0.0 7.0 %shard_map.82 = (f32[2,32,2048]{2,1,0:T(8,128)}, f32[2,32,2048]{2,1,0:T(8,128)}) custom-call(s32[1,32]{1,0:T(1,128)} %bitcast.56, s32[1,128]{1,0:T(1,128)} %bitcast.57, bf16[128,2,4096]{2,1,0:T(2,128)(2,1)} %acts_ref.1, bf16[128,2,4096]{2,1,0:T(2,128)(2,1)} %gout_ref.1, bf16[4096,128]{1,0:T(8,128)(2,1)} %pin_ref.1, bf16[4096,128]{1,0:T(8,128)(2,1)} %pout_ref.1), custom_call_target="tpu_custom_call" | custom-call | tf_op jit(solution)/shard_map/pallas_call | solution.py:137
  10.3 2.9 %collective-permute-start.1 = (f32[2,32,1024]{2,1,0:T(8,128)S(1)}, f32[2,32,1024]{2,1,0:T(8,128)S(1)}, u32[]{:S(2)}, u32[]{:S(2)}) collective-permute-start(f32[2,32,1024]{2,1,0:T(8,128)S(1)} %slice_select_fusion), channel_id=1, source_target_pairs={{0,2},{1,5},{2,0},{3,7},{4,6},{5,1},{6,4},{7,3},{8,10},{9,13},{10,... | collective-permute-start | bytes 786440 | tf_op jit(solution)/shard_map/ppermute | solution.py:51
  13.3 4.4 %collective-permute-done.1 = f32[2,32,1024]{2,1,0:T(8,128)S(1)} collective-permute-done((f32[2,32,1024]{2,1,0:T(8,128)S(1)}, f32[2,32,1024]{2,1,0:T(8,128)S(1)}, u32[]{:S(2)}, u32[]{:S(2)}) %collective-permute-start.1) | collective-permute-done | bytes 262176 | tf_op jit(solution)/shard_map/ppermute | solution.py:51
  17.7 2.1 %collective-permute-start.2 = (f32[2,32,512]{2,1,0:T(8,128)S(1)}, f32[2,32,512]{2,1,0:T(8,128)S(1)}, u32[]{:S(2)}, u32[]{:S(2)}) collective-permute-start(f32[2,32,512]{2,1,0:T(8,128)S(1)} %slice_select_fusion.1), channel_id=1, source_target_pairs={{0,4},{1,3},{2,6},{3,1},{4,0},{5,7},{6,2},{7,5},{8,12},{9,11},{10,... | collective-permute-start | bytes 393224 | tf_op jit(solution)/shard_map/ppermute | solution.py:51
  19.8 2.9 %collective-permute-done.2 = f32[2,32,512]{2,1,0:T(8,128)S(1)} collective-permute-done((f32[2,32,512]{2,1,0:T(8,128)S(1)}, f32[2,32,512]{2,1,0:T(8,128)S(1)}, u32[]{:S(2)}, u32[]{:S(2)}) %collective-permute-start.2) | collective-permute-done | bytes 131104 | tf_op jit(solution)/shard_map/ppermute | solution.py:51
  22.8 2.1 %collective-permute-start.3 = (f32[2,32,256]{2,1,0:T(8,128)S(1)}, f32[2,32,256]{2,1,0:T(8,128)S(1)}, u32[]{:S(2)}, u32[]{:S(2)}) collective-permute-start(f32[2,32,256]{2,1,0:T(8,128)S(1)} %slice_select_fusion.2), channel_id=1, source_target_pairs={{0,8},{1,9},{2,10},{3,11},{4,12},{5,13},{6,14},{7,15},{8,0},{9,1},... | collective-permute-start | bytes 196616 | tf_op jit(solution)/shard_map/ppermute | solution.py:51
  24.9 2.2 %collective-permute-done.3 = f32[2,32,256]{2,1,0:T(8,128)S(1)} collective-permute-done((f32[2,32,256]{2,1,0:T(8,128)S(1)}, f32[2,32,256]{2,1,0:T(8,128)S(1)}, u32[]{:S(2)}, u32[]{:S(2)}) %collective-permute-start.3) | collective-permute-done | bytes 65568 | tf_op jit(solution)/shard_map/ppermute | solution.py:51
  27.2 3.4 %collective-permute-start.4 = (f32[2,32,128]{2,1,0:T(8,128)S(1)}, f32[2,32,128]{2,1,0:T(8,128)S(1)}, u32[]{:S(2)}, u32[]{:S(2)}) collective-permute-start(f32[2,32,128]{2,1,0:T(8,128)S(1)} %slice_select_fusion.3), channel_id=1, source_target_pairs={{0,16},{1,17},{2,18},{3,19},{4,20},{5,21},{6,22},{7,23},{8,24},{9,... | collective-permute-start | bytes 98312 | tf_op jit(solution)/shard_map/ppermute | solution.py:51
  32.6 2.9 %collective-permute-start.5 = (f32[2,32,128]{2,1,0:T(8,128)S(1)}, f32[2,32,128]{2,1,0:T(8,128)S(1)}, u32[]{:S(2)}, u32[]{:S(2)}) collective-permute-start(f32[2,32,128]{2,1,0:T(8,128)S(1)} %select_add_fusion.3), channel_id=1, source_target_pairs={{0,16},{1,17},{2,18},{3,19},{4,20},{5,21},{6,22},{7,23},{8,24},{9,... | collective-permute-start | bytes 98312 | tf_op jit(solution)/shard_map/ppermute | solution.py:54
  37.5 2.1 %collective-permute-start.6 = (f32[2,32,256]{2,1,0:T(8,128)S(1)}, f32[2,32,256]{2,1,0:T(8,128)S(1)}, u32[]{:S(2)}, u32[]{:S(2)}) collective-permute-start(f32[2,32,256]{2,1,0:T(8,128)S(1)} %maximum_select_fusion.10), channel_id=1, source_target_pairs={{0,8},{1,9},{2,10},{3,11},{4,12},{5,13},{6,14},{7,15},{8,0},{9,1},... | collective-permute-start | bytes 196616 | tf_op jit(solution)/shard_map/ppermute | solution.py:54
  39.6 2.3 %collective-permute-done.6 = f32[2,32,256]{2,1,0:T(8,128)S(1)} collective-permute-done((f32[2,32,256]{2,1,0:T(8,128)S(1)}, f32[2,32,256]{2,1,0:T(8,128)S(1)}, u32[]{:S(2)}, u32[]{:S(2)}) %collective-permute-start.6) | collective-permute-done | bytes 65568 | tf_op jit(solution)/shard_map/ppermute | solution.py:54
  43.5 3.4 %collective-permute-done.7 = f32[2,32,512]{2,1,0:T(8,128)S(1)} collective-permute-done((f32[2,32,512]{2,1,0:T(8,128)S(1)}, f32[2,32,512]{2,1,0:T(8,128)S(1)}, u32[]{:S(2)}, u32[]{:S(2)}) %collective-permute-start.7) | collective-permute-done | bytes 131104 | tf_op jit(solution)/shard_map/ppermute | solution.py:54
  48.5 4.8 %collective-permute-done.8 = f32[2,32,1024]{2,1,0:T(8,128)S(1)} collective-permute-done((f32[2,32,1024]{2,1,0:T(8,128)S(1)}, f32[2,32,1024]{2,1,0:T(8,128)S(1)}, u32[]{:S(2)}, u32[]{:S(2)}) %collective-permute-start.8) | collective-permute-done | bytes 262176 | tf_op jit(solution)/shard_map/ppermute | solution.py:54
  55.5 2.2 %copy-done = f32[2,128,4096]{2,1,0:T(8,128)S(1)} copy-done((f32[2,128,4096]{2,1,0:T(8,128)S(1)}, f32[2,128,4096]{2,1,0:T(8,128)}, u32[]{:S(2)}) %copy-start) | copy-done | bytes 4194328
  57.7 2.2 %shard_map.83 = f32[2,32,128]{2,1,0:T(8,128)S(1)} custom-call(f32[2,32,4096]{2,1,0:T(8,128)S(1)} %maximum_select_fusion.g_ref, f32[2,128,4096]{2,1,0:T(8,128)S(1)} %copy-done), custom_call_target="tpu_custom_call" | custom-call | tf_op jit(solution)/shard_map/pallas_call | solution.py:160
  59.9 3.0 %collective-permute-start.10 = (f32[2,32,128]{2,1,0:T(8,128)S(1)}, f32[2,32,128]{2,1,0:T(8,128)S(1)}, u32[]{:S(2)}, u32[]{:S(2)}) collective-permute-start(f32[2,32,128]{2,1,0:T(8,128)S(1)} %shard_map.83), channel_id=1, source_target_pairs={{0,16},{1,17},{2,18},{3,19},{4,20},{5,21},{6,22},{7,23},{8,24},{9,... | collective-permute-start | bytes 98312 | tf_op jit(solution)/shard_map/ppermute | solution.py:71
  66.8 2.3 %collective-permute-done.11 = f32[2,32,2,128]{3,1,0,2:T(8,128)S(1)} collective-permute-done((f32[2,32,2,128]{3,1,0,2:T(8,128)S(1)}, f32[2,32,2,128]{3,1,0,2:T(8,128)S(1)}, u32[]{:S(2)}, u32[]{:S(2)}) %collective-permute-start.11) | collective-permute-done | bytes 65568 | tf_op jit(solution)/shard_map/ppermute | solution.py:71
  70.8 3.7 %collective-permute-done.12 = f32[2,32,2,2,128]{4,1,0,2,3:T(8,128)S(1)} collective-permute-done((f32[2,32,2,2,128]{4,1,0,2,3:T(8,128)S(1)}, f32[2,32,2,2,128]{4,1,0,2,3:T(8,128)S(1)}, u32[]{:S(2)}, u32[]{:S(2)}) %collective-permute-start.12) | collective-permute-done | bytes 131104 | tf_op jit(solution)/shard_map/ppermute | solution.py:71
  76.1 4.8 %collective-permute-done.13 = f32[2,32,2,2,2,128]{5,1,0,2,3,4:T(8,128)S(1)} collective-permute-done((f32[2,32,2,2,2,128]{5,1,0,2,3,4:T(8,128)S(1)}, f32[2,32,2,2,2,128]{5,1,0,2,3,4:T(8,128)S(1)}, u32[]{:S(2)}, u32[]{:S(2)}) %collective-permute-start.13) | collective-permute-done | bytes 262176 | tf_op jit(solution)/shard_map/ppermute | solution.py:71
  84.8 6.3 %fusion.8 = (f32[32]{0:T(128)S(1)}, f32[32]{0:T(128)S(1)}, f32[32,128]{1,0:T(8,128)S(1)}) fusion(f32[2,32,4096]{2,1,0:T(8,128)S(1)} %select_n.240, f32[128,2,4096]{2,1,0:T(2,128)} %param.15), kind=kOutput, calls=%fused_computation.33 | convolution fusion | flops 201338816 | bytes 5259520 | tf_op jit(solution)/shard_map/mqk,nmk->qn/dot_general | solution.py:176
  93.9 2.1 %collective-permute-done.16 = f32[2,32]{1,0:T(2,128)S(1)} collective-permute-done((f32[2,32]{1,0:T(2,128)S(1)}, f32[2,32]{1,0:T(2,128)S(1)}, u32[]{:S(2)}, u32[]{:S(2)}) %collective-permute-start.16) | collective-permute-done | bytes 288 | tf_op jit(solution)/shard_map/ppermute | solution.py:82
  97.6 2.1 %collective-permute-done.17 = f32[2,32]{1,0:T(2,128)S(1)} collective-permute-done((f32[2,32]{1,0:T(2,128)S(1)}, f32[2,32]{1,0:T(2,128)S(1)}, u32[]{:S(2)}, u32[]{:S(2)}) %collective-permute-start.17) | collective-permute-done | bytes 288 | tf_op jit(solution)/shard_map/ppermute | solution.py:82
  99.6 2.1 %collective-permute-start.18 = (f32[2,32]{1,0:T(2,128)S(1)}, f32[2,32]{1,0:T(2,128)S(1)}, u32[]{:S(2)}, u32[]{:S(2)}) collective-permute-start(f32[2,32]{1,0:T(2,128)S(1)} %add.47), channel_id=1, source_target_pairs={{0,8},{1,9},{2,10},{3,11},{4,12},{5,13},{6,14},{7,15},{8,0},{9,1},... | collective-permute-start | bytes 776 | tf_op jit(solution)/shard_map/ppermute | solution.py:82
  103.3 3.1 %collective-permute-start.19 = (f32[2,32]{1,0:T(2,128)S(1)}, f32[2,32]{1,0:T(2,128)S(1)}, u32[]{:S(2)}, u32[]{:S(2)}) collective-permute-start(f32[2,32]{1,0:T(2,128)S(1)} %add.48), channel_id=1, source_target_pairs={{0,16},{1,17},{2,18},{3,19},{4,20},{5,21},{6,22},{7,23},{8,24},{9,... | collective-permute-start | bytes 776 | tf_op jit(solution)/shard_map/ppermute | solution.py:82
  (58 shorter events, 31.9 us)
Async XLA Ops:
  7.0 2.2 %collective-permute-start = (f32[2,32,2048]{2,1,0:T(8,128)}, f32[2,32,2048]{2,1,0:T(8,128)S(1)}, u32[]{:S(2)}, u32[]{:S(2)}) collective-permute-start(f32[2,32,2048]{2,1,0:T(8,128)} %get-tuple-element.8), channel_id=1, source_target_pairs={{0,1},{1,0},{2,3},{3,2},{4,5},{5,4},{6,7},{7,6},{8,9},{9,8},{10,11... | collective-permute-start | bytes 1572872 | tf_op jit(solution)/shard_map/ppermute | solution.py:43
  10.3 7.3 %collective-permute-start.1 = (f32[2,32,1024]{2,1,0:T(8,128)S(1)}, f32[2,32,1024]{2,1,0:T(8,128)S(1)}, u32[]{:S(2)}, u32[]{:S(2)}) collective-permute-start(f32[2,32,1024]{2,1,0:T(8,128)S(1)} %slice_select_fusion), channel_id=1, source_target_pairs={{0,2},{1,5},{2,0},{3,7},{4,6},{5,1},{6,4},{7,3},{8,10},{9,13},{10,... | collective-permute-start | bytes 786440 | tf_op jit(solution)/shard_map/ppermute | solution.py:51
  17.7 5.1 %collective-permute-start.2 = (f32[2,32,512]{2,1,0:T(8,128)S(1)}, f32[2,32,512]{2,1,0:T(8,128)S(1)}, u32[]{:S(2)}, u32[]{:S(2)}) collective-permute-start(f32[2,32,512]{2,1,0:T(8,128)S(1)} %slice_select_fusion.1), channel_id=1, source_target_pairs={{0,4},{1,3},{2,6},{3,1},{4,0},{5,7},{6,2},{7,5},{8,12},{9,11},{10,... | collective-permute-start | bytes 393224 | tf_op jit(solution)/shard_map/ppermute | solution.py:51
  22.8 4.4 %collective-permute-start.3 = (f32[2,32,256]{2,1,0:T(8,128)S(1)}, f32[2,32,256]{2,1,0:T(8,128)S(1)}, u32[]{:S(2)}, u32[]{:S(2)}) collective-permute-start(f32[2,32,256]{2,1,0:T(8,128)S(1)} %slice_select_fusion.2), channel_id=1, source_target_pairs={{0,8},{1,9},{2,10},{3,11},{4,12},{5,13},{6,14},{7,15},{8,0},{9,1},... | collective-permute-start | bytes 196616 | tf_op jit(solution)/shard_map/ppermute | solution.py:51
  27.2 5.4 %collective-permute-start.4 = (f32[2,32,128]{2,1,0:T(8,128)S(1)}, f32[2,32,128]{2,1,0:T(8,128)S(1)}, u32[]{:S(2)}, u32[]{:S(2)}) collective-permute-start(f32[2,32,128]{2,1,0:T(8,128)S(1)} %slice_select_fusion.3), channel_id=1, source_target_pairs={{0,16},{1,17},{2,18},{3,19},{4,20},{5,21},{6,22},{7,23},{8,24},{9,... | collective-permute-start | bytes 98312 | tf_op jit(solution)/shard_map/ppermute | solution.py:51
  32.6 4.9 %collective-permute-start.5 = (f32[2,32,128]{2,1,0:T(8,128)S(1)}, f32[2,32,128]{2,1,0:T(8,128)S(1)}, u32[]{:S(2)}, u32[]{:S(2)}) collective-permute-start(f32[2,32,128]{2,1,0:T(8,128)S(1)} %select_add_fusion.3), channel_id=1, source_target_pairs={{0,16},{1,17},{2,18},{3,19},{4,20},{5,21},{6,22},{7,23},{8,24},{9,... | collective-permute-start | bytes 98312 | tf_op jit(solution)/shard_map/ppermute | solution.py:54
  37.5 4.3 %collective-permute-start.6 = (f32[2,32,256]{2,1,0:T(8,128)S(1)}, f32[2,32,256]{2,1,0:T(8,128)S(1)}, u32[]{:S(2)}, u32[]{:S(2)}) collective-permute-start(f32[2,32,256]{2,1,0:T(8,128)S(1)} %maximum_select_fusion.10), channel_id=1, source_target_pairs={{0,8},{1,9},{2,10},{3,11},{4,12},{5,13},{6,14},{7,15},{8,0},{9,1},... | collective-permute-start | bytes 196616 | tf_op jit(solution)/shard_map/ppermute | solution.py:54
  41.8 5.0 %collective-permute-start.7 = (f32[2,32,512]{2,1,0:T(8,128)S(1)}, f32[2,32,512]{2,1,0:T(8,128)S(1)}, u32[]{:S(2)}, u32[]{:S(2)}) collective-permute-start(f32[2,32,512]{2,1,0:T(8,128)S(1)} %maximum_select_fusion.7), channel_id=1, source_target_pairs={{0,4},{1,3},{2,6},{3,1},{4,0},{5,7},{6,2},{7,5},{8,12},{9,11},{10,... | collective-permute-start | bytes 393224 | tf_op jit(solution)/shard_map/ppermute | solution.py:54
  46.9 6.4 %collective-permute-start.8 = (f32[2,32,1024]{2,1,0:T(8,128)S(1)}, f32[2,32,1024]{2,1,0:T(8,128)S(1)}, u32[]{:S(2)}, u32[]{:S(2)}) collective-permute-start(f32[2,32,1024]{2,1,0:T(8,128)S(1)} %maximum_select_fusion.4), channel_id=1, source_target_pairs={{0,2},{1,5},{2,0},{3,7},{4,6},{5,1},{6,4},{7,3},{8,10},{9,13},{10,... | collective-permute-start | bytes 786440 | tf_op jit(solution)/shard_map/ppermute | solution.py:54
  53.4 2.0 %collective-permute-start.9 = (f32[2,32,2048]{2,1,0:T(8,128)S(1)}, f32[2,32,2048]{2,1,0:T(8,128)S(1)}, u32[]{:S(2)}, u32[]{:S(2)}) collective-permute-start(f32[2,32,2048]{2,1,0:T(8,128)S(1)} %maximum_select_fusion.2), channel_id=1, source_target_pairs={{0,1},{1,0},{2,3},{3,2},{4,5},{5,4},{6,7},{7,6},{8,9},{9,8},{10,11... | collective-permute-start | bytes 1572872 | tf_op jit(solution)/shard_map/ppermute | solution.py:54
  55.5 2.2 %copy-start = (f32[2,128,4096]{2,1,0:T(8,128)S(1)}, f32[2,128,4096]{2,1,0:T(8,128)}, u32[]{:S(2)}) copy-start(f32[2,128,4096]{2,1,0:T(8,128)} %f_ref.1) | copy-start | bytes 12582916
  59.9 4.9 %collective-permute-start.10 = (f32[2,32,128]{2,1,0:T(8,128)S(1)}, f32[2,32,128]{2,1,0:T(8,128)S(1)}, u32[]{:S(2)}, u32[]{:S(2)}) collective-permute-start(f32[2,32,128]{2,1,0:T(8,128)S(1)} %shard_map.83), channel_id=1, source_target_pairs={{0,16},{1,17},{2,18},{3,19},{4,20},{5,21},{6,22},{7,23},{8,24},{9,... | collective-permute-start | bytes 98312 | tf_op jit(solution)/shard_map/ppermute | solution.py:71
  64.8 4.3 %collective-permute-start.11 = (f32[2,32,2,128]{3,1,0,2:T(8,128)S(1)}, f32[2,32,2,128]{3,1,0,2:T(8,128)S(1)}, u32[]{:S(2)}, u32[]{:S(2)}) collective-permute-start(f32[2,32,2,128]{3,1,0,2:T(8,128)S(1)} %maximum_select_fusion.12), channel_id=1, source_target_pairs={{0,8},{1,9},{2,10},{3,11},{4,12},{5,13},{6,14},{7,15},{8,0},{9,1},... | collective-permute-start | bytes 196616 | tf_op jit(solution)/shard_map/ppermute | solution.py:71
  69.1 5.3 %collective-permute-start.12 = (f32[2,32,2,2,128]{4,1,0,2,3:T(8,128)S(1)}, f32[2,32,2,2,128]{4,1,0,2,3:T(8,128)S(1)}, u32[]{:S(2)}, u32[]{:S(2)}) collective-permute-start(f32[2,32,2,2,128]{4,1,0,2,3:T(8,128)S(1)} %maximum_select_fusion.9), channel_id=1, source_target_pairs={{0,4},{1,3},{2,6},{3,1},{4,0},{5,7},{6,2},{7,5},{8,12},{9,11},{10,... | collective-permute-start | bytes 393224 | tf_op jit(solution)/shard_map/ppermute | solution.py:71
  74.5 6.4 %collective-permute-start.13 = (f32[2,32,2,2,2,128]{5,1,0,2,3,4:T(8,128)S(1)}, f32[2,32,2,2,2,128]{5,1,0,2,3,4:T(8,128)S(1)}, u32[]{:S(2)}, u32[]{:S(2)}) collective-permute-start(f32[2,32,2,2,2,128]{5,1,0,2,3,4:T(8,128)S(1)} %maximum_select_fusion.6), channel_id=1, source_target_pairs={{0,2},{1,5},{2,0},{3,7},{4,6},{5,1},{6,4},{7,3},{8,10},{9,13},{10,... | collective-permute-start | bytes 786440 | tf_op jit(solution)/shard_map/ppermute | solution.py:71
  81.0 2.0 %collective-permute-start.14 = (f32[2,32,2,2,2,2,128]{6,1,0,2,3,4,5:T(8,128)S(1)}, f32[2,32,2,2,2,2,128]{6,1,0,2,3,4,5:T(8,128)S(1)}, u32[]{:S(2)}, u32[]{:S(2)}) collective-permute-start(f32[2,32,2,2,2,2,128]{6,1,0,2,3,4,5:T(8,128)S(1)} %bitcast_select_fusion), channel_id=1, source_target_pairs={{0,1},{1,0},{2,3},{3,2},{4,5},{5,4},{6,7},{7,6},{8,9},{9,8},{10,11... | collective-permute-start | bytes 1572872 | tf_op jit(solution)/shard_map/ppermute | solution.py:71
  91.1 1.2 %collective-permute-start.15 = (f32[2,32]{1,0:T(2,128)S(1)}, f32[2,32]{1,0:T(2,128)S(1)}, u32[]{:S(2)}, u32[]{:S(2)}) collective-permute-start(f32[2,32]{1,0:T(2,128)S(1)} %pad_maximum_fusion), channel_id=1, source_target_pairs={{0,1},{1,0},{2,3},{3,2},{4,5},{5,4},{6,7},{7,6},{8,9},{9,8},{10,11... | collective-permute-start | bytes 776 | tf_op jit(solution)/shard_map/ppermute | solution.py:82
  92.3 3.6 %collective-permute-start.16 = (f32[2,32]{1,0:T(2,128)S(1)}, f32[2,32]{1,0:T(2,128)S(1)}, u32[]{:S(2)}, u32[]{:S(2)}) collective-permute-start(f32[2,32]{1,0:T(2,128)S(1)} %fusion.7), channel_id=1, source_target_pairs={{0,2},{1,3},{2,0},{3,1},{4,6},{5,7},{6,4},{7,5},{8,10},{9,11},{10,... | collective-permute-start | bytes 776 | tf_op jit(solution)/shard_map/ppermute | solution.py:82
  96.0 3.6 %collective-permute-start.17 = (f32[2,32]{1,0:T(2,128)S(1)}, f32[2,32]{1,0:T(2,128)S(1)}, u32[]{:S(2)}, u32[]{:S(2)}) collective-permute-start(f32[2,32]{1,0:T(2,128)S(1)} %fusion.10), channel_id=1, source_target_pairs={{0,4},{1,5},{2,6},{3,7},{4,0},{5,1},{6,2},{7,3},{8,12},{9,13},{10,... | collective-permute-start | bytes 776 | tf_op jit(solution)/shard_map/ppermute | solution.py:82
  99.6 3.6 %collective-permute-start.18 = (f32[2,32]{1,0:T(2,128)S(1)}, f32[2,32]{1,0:T(2,128)S(1)}, u32[]{:S(2)}, u32[]{:S(2)}) collective-permute-start(f32[2,32]{1,0:T(2,128)S(1)} %add.47), channel_id=1, source_target_pairs={{0,8},{1,9},{2,10},{3,11},{4,12},{5,13},{6,14},{7,15},{8,0},{9,1},... | collective-permute-start | bytes 776 | tf_op jit(solution)/shard_map/ppermute | solution.py:82
  103.3 4.6 %collective-permute-start.19 = (f32[2,32]{1,0:T(2,128)S(1)}, f32[2,32]{1,0:T(2,128)S(1)}, u32[]{:S(2)}, u32[]{:S(2)}) collective-permute-start(f32[2,32]{1,0:T(2,128)S(1)} %add.48), channel_id=1, source_target_pairs={{0,16},{1,17},{2,18},{3,19},{4,20},{5,21},{6,22},{7,23},{8,24},{9,... | collective-permute-start | bytes 776 | tf_op jit(solution)/shard_map/ppermute | solution.py:82

commit v13 on v10

--- a/solution.py
+++ b/solution.py
@@ -141,17 +141,23 @@
 def _precond_kernel(g_ref, f_ref, out_ref):
     nt = (((1,), (1,)), ((), ()))
     f = lambda a, b: lax.dot_general(a, b, nt, preferred_element_type=jnp.float32)
-    for m in range(g_ref.shape[0]):
-        g_high, g_low = _split_bf16(g_ref[m])
-        f_high, f_low = _split_bf16(f_ref[m])
-        out_ref[m] = f(g_high, f_high) + (f(g_low, f_high) + f(g_high, f_low))
+    g_high, g_low = _split_bf16(g_ref[0])
+    f_high, f_low = _split_bf16(f_ref[0])
+    out_ref[0] = f(g_high, f_high) + (f(g_low, f_high) + f(g_high, f_low))
 
 
 def _precond(grads, fisher_inv):
-    modules, queries, _ = grads.shape
+    modules, queries, width = grads.shape
+    cols = fisher_inv.shape[1]
     return pl.pallas_call(
         _precond_kernel,
-        out_shape=jax.ShapeDtypeStruct((modules, queries, fisher_inv.shape[1]), jnp.float32),
+        out_shape=jax.ShapeDtypeStruct((modules, queries, cols), jnp.float32),
+        grid=(modules,),
+        in_specs=[
+            pl.BlockSpec((1, queries, width), lambda m: (m, 0, 0)),
+            pl.BlockSpec((1, cols, width), lambda m: (m, 0, 0)),
+        ],
+        out_specs=pl.BlockSpec((1, queries, cols), lambda m: (m, 0, 0)),
         compiler_params=pltpu.CompilerParams(vmem_limit_bytes=48 * 1024 * 1024),
     )(grads, fisher_inv)
 

time: 108 us -> 108 us (level)
  no operation moved by 1% of the time
where the time goes in v13:
time: 108 us
  waiting for transfers between devices  50.3 us (47%)
  starting transfers between devices  35.8 us (33%)
  Pallas kernels  9.14 us (8%)
  matrix products  6.3 us (6%)
  local copies, waits for them, and re-layouts  3.83 us (4%)
  other arithmetic  2.51 us (2%)
    ppermute x5, waiting for transfers between devices, _allreduce(): lax.ppermute(cur, 'rows', _pairs(size, orders, t))  14.3 us
    ppermute x5, waiting for transfers between devices, _allgather(): other = lax.ppermute(cur, 'rows', _xor_pairs(size, s))  14.3 us
    ppermute x4, waiting for transfers between devices, _allreduce(): cur = keep + lax.ppermute(send, 'rows', _pairs(size, orders, t))  11.5 us
    ppermute x4, starting transfers between devices, _allreduce(): cur = keep + lax.ppermute(send, 'rows', _pairs(size, orders, t))  10.6 us
    ppermute x5, waiting for transfers between devices, _butterfly_sum(): x = x + lax.ppermute(x, 'rows', _xor_pairs(size, s))  8.37 us
    ppermute x5, starting transfers between devices, _allreduce(): lax.ppermute(cur, 'rows', _pairs(size, orders, t))  8.29 us
    ppermute x5, starting transfers between devices, _allgather(): other = lax.ppermute(cur, 'rows', _xor_pairs(size, s))  8.24 us
    ppermute x5, starting transfers between devices, _butterfly_sum(): x = x + lax.ppermute(x, 'rows', _xor_pairs(size, s))  8.19 us
  transfers between devices with their start and end apart: 20, of which 20 were waited for; matrix products, arithmetic and copies ran while one was open for 0% of the time, Pallas kernels for 0%

profile of v13, /device:TPU:0, one launch (start us, length us, event | category | flops | bytes accessed | tf_op | source)
XLA Modules:
  0.0 108.1 jit_solution(14511546687564239595)
XLA Ops:
  0.0 7.0 %shard_map.82 = (f32[2,32,2048]{2,1,0:T(8,128)}, f32[2,32,2048]{2,1,0:T(8,128)}) custom-call(s32[1,32]{1,0:T(1,128)} %bitcast.55, s32[1,128]{1,0:T(1,128)} %bitcast.56, bf16[128,2,4096]{2,1,0:T(2,128)(2,1)} %acts_ref.1, bf16[128,2,4096]{2,1,0:T(2,128)(2,1)} %gout_ref.1, bf16[4096,128]{1,0:T(8,128)(2,1)} %pin_ref.1, bf16[4096,128]{1,0:T(8,128)(2,1)} %pout_ref.1), custom_call_target="tpu_custom_call" | custom-call | tf_op jit(solution)/shard_map/pallas_call | solution.py:129
  10.3 2.9 %collective-permute-start.1 = (f32[2,32,1024]{2,1,0:T(8,128)S(1)}, f32[2,32,1024]{2,1,0:T(8,128)S(1)}, u32[]{:S(2)}, u32[]{:S(2)}) collective-permute-start(f32[2,32,1024]{2,1,0:T(8,128)S(1)} %slice_select_fusion), channel_id=1, source_target_pairs={{0,2},{1,5},{2,0},{3,7},{4,6},{5,1},{6,4},{7,3},{8,10},{9,13},{10,... | collective-permute-start | bytes 786440 | tf_op jit(solution)/shard_map/ppermute | solution.py:51
  13.3 4.4 %collective-permute-done.1 = f32[2,32,1024]{2,1,0:T(8,128)S(1)} collective-permute-done((f32[2,32,1024]{2,1,0:T(8,128)S(1)}, f32[2,32,1024]{2,1,0:T(8,128)S(1)}, u32[]{:S(2)}, u32[]{:S(2)}) %collective-permute-start.1) | collective-permute-done | bytes 262176 | tf_op jit(solution)/shard_map/ppermute | solution.py:51
  17.7 2.1 %collective-permute-start.2 = (f32[2,32,512]{2,1,0:T(8,128)S(1)}, f32[2,32,512]{2,1,0:T(8,128)S(1)}, u32[]{:S(2)}, u32[]{:S(2)}) collective-permute-start(f32[2,32,512]{2,1,0:T(8,128)S(1)} %slice_select_fusion.1), channel_id=1, source_target_pairs={{0,4},{1,3},{2,6},{3,1},{4,0},{5,7},{6,2},{7,5},{8,12},{9,11},{10,... | collective-permute-start | bytes 393224 | tf_op jit(solution)/shard_map/ppermute | solution.py:51
  19.8 2.9 %collective-permute-done.2 = f32[2,32,512]{2,1,0:T(8,128)S(1)} collective-permute-done((f32[2,32,512]{2,1,0:T(8,128)S(1)}, f32[2,32,512]{2,1,0:T(8,128)S(1)}, u32[]{:S(2)}, u32[]{:S(2)}) %collective-permute-start.2) | collective-permute-done | bytes 131104 | tf_op jit(solution)/shard_map/ppermute | solution.py:51
  22.8 2.1 %collective-permute-start.3 = (f32[2,32,256]{2,1,0:T(8,128)S(1)}, f32[2,32,256]{2,1,0:T(8,128)S(1)}, u32[]{:S(2)}, u32[]{:S(2)}) collective-permute-start(f32[2,32,256]{2,1,0:T(8,128)S(1)} %slice_select_fusion.2), channel_id=1, source_target_pairs={{0,8},{1,9},{2,10},{3,11},{4,12},{5,13},{6,14},{7,15},{8,0},{9,1},... | collective-permute-start | bytes 196616 | tf_op jit(solution)/shard_map/ppermute | solution.py:51
  24.9 2.2 %collective-permute-done.3 = f32[2,32,256]{2,1,0:T(8,128)S(1)} collective-permute-done((f32[2,32,256]{2,1,0:T(8,128)S(1)}, f32[2,32,256]{2,1,0:T(8,128)S(1)}, u32[]{:S(2)}, u32[]{:S(2)}) %collective-permute-start.3) | collective-permute-done | bytes 65568 | tf_op jit(solution)/shard_map/ppermute | solution.py:51
  27.2 3.4 %collective-permute-start.4 = (f32[2,32,128]{2,1,0:T(8,128)S(1)}, f32[2,32,128]{2,1,0:T(8,128)S(1)}, u32[]{:S(2)}, u32[]{:S(2)}) collective-permute-start(f32[2,32,128]{2,1,0:T(8,128)S(1)} %slice_select_fusion.3), channel_id=1, source_target_pairs={{0,16},{1,17},{2,18},{3,19},{4,20},{5,21},{6,22},{7,23},{8,24},{9,... | collective-permute-start | bytes 98312 | tf_op jit(solution)/shard_map/ppermute | solution.py:51
  32.6 2.9 %collective-permute-start.5 = (f32[2,32,128]{2,1,0:T(8,128)S(1)}, f32[2,32,128]{2,1,0:T(8,128)S(1)}, u32[]{:S(2)}, u32[]{:S(2)}) collective-permute-start(f32[2,32,128]{2,1,0:T(8,128)S(1)} %select_add_fusion.3), channel_id=1, source_target_pairs={{0,16},{1,17},{2,18},{3,19},{4,20},{5,21},{6,22},{7,23},{8,24},{9,... | collective-permute-start | bytes 98312 | tf_op jit(solution)/shard_map/ppermute | solution.py:54
  37.5 2.1 %collective-permute-start.6 = (f32[2,32,256]{2,1,0:T(8,128)S(1)}, f32[2,32,256]{2,1,0:T(8,128)S(1)}, u32[]{:S(2)}, u32[]{:S(2)}) collective-permute-start(f32[2,32,256]{2,1,0:T(8,128)S(1)} %maximum_select_fusion.11), channel_id=1, source_target_pairs={{0,8},{1,9},{2,10},{3,11},{4,12},{5,13},{6,14},{7,15},{8,0},{9,1},... | collective-permute-start | bytes 196616 | tf_op jit(solution)/shard_map/ppermute | solution.py:54
  39.6 2.3 %collective-permute-done.6 = f32[2,32,256]{2,1,0:T(8,128)S(1)} collective-permute-done((f32[2,32,256]{2,1,0:T(8,128)S(1)}, f32[2,32,256]{2,1,0:T(8,128)S(1)}, u32[]{:S(2)}, u32[]{:S(2)}) %collective-permute-start.6) | collective-permute-done | bytes 65568 | tf_op jit(solution)/shard_map/ppermute | solution.py:54
  43.5 3.4 %collective-permute-done.7 = f32[2,32,512]{2,1,0:T(8,128)S(1)} collective-permute-done((f32[2,32,512]{2,1,0:T(8,128)S(1)}, f32[2,32,512]{2,1,0:T(8,128)S(1)}, u32[]{:S(2)}, u32[]{:S(2)}) %collective-permute-start.7) | collective-permute-done | bytes 131104 | tf_op jit(solution)/shard_map/ppermute | solution.py:54
  48.5 4.8 %collective-permute-done.8 = f32[2,32,1024]{2,1,0:T(8,128)S(1)} collective-permute-done((f32[2,32,1024]{2,1,0:T(8,128)S(1)}, f32[2,32,1024]{2,1,0:T(8,128)S(1)}, u32[]{:S(2)}, u32[]{:S(2)}) %collective-permute-start.8) | collective-permute-done | bytes 262176 | tf_op jit(solution)/shard_map/ppermute | solution.py:54
  55.5 2.2 %copy-done = f32[2,128,4096]{2,1,0:T(8,128)S(1)} copy-done((f32[2,128,4096]{2,1,0:T(8,128)S(1)}, f32[2,128,4096]{2,1,0:T(8,128)}, u32[]{:S(2)}) %copy-start) | copy-done | bytes 4194328
  57.7 2.2 %shard_map.83 = f32[2,32,128]{2,1,0:T(8,128)S(1)} custom-call(f32[2,32,4096]{2,1,0:T(8,128)S(1)} %maximum_select_fusion.g_ref, f32[2,128,4096]{2,1,0:T(8,128)S(1)} %copy-done), custom_call_target="tpu_custom_call" | custom-call | tf_op jit(solution)/shard_map/pallas_call | solution.py:152
  59.9 3.0 %collective-permute-start.10 = (f32[2,32,128]{2,1,0:T(8,128)S(1)}, f32[2,32,128]{2,1,0:T(8,128)S(1)}, u32[]{:S(2)}, u32[]{:S(2)}) collective-permute-start(f32[2,32,128]{2,1,0:T(8,128)S(1)} %shard_map.83), channel_id=1, source_target_pairs={{0,16},{1,17},{2,18},{3,19},{4,20},{5,21},{6,22},{7,23},{8,24},{9,... | collective-permute-start | bytes 98312 | tf_op jit(solution)/shard_map/ppermute | solution.py:63
  64.8 2.0 %collective-permute-start.11 = (f32[2,32,2,128]{3,1,0,2:T(8,128)S(1)}, f32[2,32,2,128]{3,1,0,2:T(8,128)S(1)}, u32[]{:S(2)}, u32[]{:S(2)}) collective-permute-start(f32[2,32,2,128]{3,1,0,2:T(8,128)S(1)} %maximum_select_fusion.13), channel_id=1, source_target_pairs={{0,8},{1,9},{2,10},{3,11},{4,12},{5,13},{6,14},{7,15},{8,0},{9,1},... | collective-permute-start | bytes 196616 | tf_op jit(solution)/shard_map/ppermute | solution.py:63
  66.8 2.3 %collective-permute-done.11 = f32[2,32,2,128]{3,1,0,2:T(8,128)S(1)} collective-permute-done((f32[2,32,2,128]{3,1,0,2:T(8,128)S(1)}, f32[2,32,2,128]{3,1,0,2:T(8,128)S(1)}, u32[]{:S(2)}, u32[]{:S(2)}) %collective-permute-start.11) | collective-permute-done | bytes 65568 | tf_op jit(solution)/shard_map/ppermute | solution.py:63
  70.8 3.4 %collective-permute-done.12 = f32[2,32,2,2,128]{4,1,0,2,3:T(8,128)S(1)} collective-permute-done((f32[2,32,2,2,128]{4,1,0,2,3:T(8,128)S(1)}, f32[2,32,2,2,128]{4,1,0,2,3:T(8,128)S(1)}, u32[]{:S(2)}, u32[]{:S(2)}) %collective-permute-start.12) | collective-permute-done | bytes 131104 | tf_op jit(solution)/shard_map/ppermute | solution.py:63
  75.8 4.8 %collective-permute-done.13 = f32[2,32,2,2,2,128]{5,1,0,2,3,4:T(8,128)S(1)} collective-permute-done((f32[2,32,2,2,2,128]{5,1,0,2,3,4:T(8,128)S(1)}, f32[2,32,2,2,2,128]{5,1,0,2,3,4:T(8,128)S(1)}, u32[]{:S(2)}, u32[]{:S(2)}) %collective-permute-start.13) | collective-permute-done | bytes 262176 | tf_op jit(solution)/shard_map/ppermute | solution.py:63
  84.5 6.3 %fusion.8 = (f32[32]{0:T(128)S(1)}, f32[32]{0:T(128)S(1)}, f32[32,128]{1,0:T(8,128)S(1)}) fusion(f32[2,32,4096]{2,1,0:T(8,128)S(1)} %select_n.249, f32[128,2,4096]{2,1,0:T(2,128)} %param.15), kind=kOutput, calls=%fused_computation.33 | convolution fusion | flops 201338816 | bytes 5259520 | tf_op jit(solution)/shard_map/mqk,nmk->qn/dot_general | solution.py:174
  93.6 2.1 %collective-permute-done.16 = f32[2,32]{1,0:T(2,128)S(1)} collective-permute-done((f32[2,32]{1,0:T(2,128)S(1)}, f32[2,32]{1,0:T(2,128)S(1)}, u32[]{:S(2)}, u32[]{:S(2)}) %collective-permute-start.16) | collective-permute-done | bytes 288 | tf_op jit(solution)/shard_map/ppermute | solution.py:74
  97.3 2.1 %collective-permute-done.17 = f32[2,32]{1,0:T(2,128)S(1)} collective-permute-done((f32[2,32]{1,0:T(2,128)S(1)}, f32[2,32]{1,0:T(2,128)S(1)}, u32[]{:S(2)}, u32[]{:S(2)}) %collective-permute-start.17) | collective-permute-done | bytes 288 | tf_op jit(solution)/shard_map/ppermute | solution.py:74
  102.9 2.9 %collective-permute-start.19 = (f32[2,32]{1,0:T(2,128)S(1)}, f32[2,32]{1,0:T(2,128)S(1)}, u32[]{:S(2)}, u32[]{:S(2)}) collective-permute-start(f32[2,32]{1,0:T(2,128)S(1)} %add.48), channel_id=1, source_target_pairs={{0,16},{1,17},{2,18},{3,19},{4,20},{5,21},{6,22},{7,23},{8,24},{9,... | collective-permute-start | bytes 776 | tf_op jit(solution)/shard_map/ppermute | solution.py:74
  (58 shorter events, 31.9 us)
Async XLA Ops:
  7.0 2.2 %collective-permute-start = (f32[2,32,2048]{2,1,0:T(8,128)}, f32[2,32,2048]{2,1,0:T(8,128)S(1)}, u32[]{:S(2)}, u32[]{:S(2)}) collective-permute-start(f32[2,32,2048]{2,1,0:T(8,128)} %get-tuple-element.8), channel_id=1, source_target_pairs={{0,1},{1,0},{2,3},{3,2},{4,5},{5,4},{6,7},{7,6},{8,9},{9,8},{10,11... | collective-permute-start | bytes 1572872 | tf_op jit(solution)/shard_map/ppermute | solution.py:43
  10.3 7.3 %collective-permute-start.1 = (f32[2,32,1024]{2,1,0:T(8,128)S(1)}, f32[2,32,1024]{2,1,0:T(8,128)S(1)}, u32[]{:S(2)}, u32[]{:S(2)}) collective-permute-start(f32[2,32,1024]{2,1,0:T(8,128)S(1)} %slice_select_fusion), channel_id=1, source_target_pairs={{0,2},{1,5},{2,0},{3,7},{4,6},{5,1},{6,4},{7,3},{8,10},{9,13},{10,... | collective-permute-start | bytes 786440 | tf_op jit(solution)/shard_map/ppermute | solution.py:51
  17.7 5.1 %collective-permute-start.2 = (f32[2,32,512]{2,1,0:T(8,128)S(1)}, f32[2,32,512]{2,1,0:T(8,128)S(1)}, u32[]{:S(2)}, u32[]{:S(2)}) collective-permute-start(f32[2,32,512]{2,1,0:T(8,128)S(1)} %slice_select_fusion.1), channel_id=1, source_target_pairs={{0,4},{1,3},{2,6},{3,1},{4,0},{5,7},{6,2},{7,5},{8,12},{9,11},{10,... | collective-permute-start | bytes 393224 | tf_op jit(solution)/shard_map/ppermute | solution.py:51
  22.8 4.4 %collective-permute-start.3 = (f32[2,32,256]{2,1,0:T(8,128)S(1)}, f32[2,32,256]{2,1,0:T(8,128)S(1)}, u32[]{:S(2)}, u32[]{:S(2)}) collective-permute-start(f32[2,32,256]{2,1,0:T(8,128)S(1)} %slice_select_fusion.2), channel_id=1, source_target_pairs={{0,8},{1,9},{2,10},{3,11},{4,12},{5,13},{6,14},{7,15},{8,0},{9,1},... | collective-permute-start | bytes 196616 | tf_op jit(solution)/shard_map/ppermute | solution.py:51
  27.2 5.4 %collective-permute-start.4 = (f32[2,32,128]{2,1,0:T(8,128)S(1)}, f32[2,32,128]{2,1,0:T(8,128)S(1)}, u32[]{:S(2)}, u32[]{:S(2)}) collective-permute-start(f32[2,32,128]{2,1,0:T(8,128)S(1)} %slice_select_fusion.3), channel_id=1, source_target_pairs={{0,16},{1,17},{2,18},{3,19},{4,20},{5,21},{6,22},{7,23},{8,24},{9,... | collective-permute-start | bytes 98312 | tf_op jit(solution)/shard_map/ppermute | solution.py:51
  32.6 4.9 %collective-permute-start.5 = (f32[2,32,128]{2,1,0:T(8,128)S(1)}, f32[2,32,128]{2,1,0:T(8,128)S(1)}, u32[]{:S(2)}, u32[]{:S(2)}) collective-permute-start(f32[2,32,128]{2,1,0:T(8,128)S(1)} %select_add_fusion.3), channel_id=1, source_target_pairs={{0,16},{1,17},{2,18},{3,19},{4,20},{5,21},{6,22},{7,23},{8,24},{9,... | collective-permute-start | bytes 98312 | tf_op jit(solution)/shard_map/ppermute | solution.py:54
  37.5 4.3 %collective-permute-start.6 = (f32[2,32,256]{2,1,0:T(8,128)S(1)}, f32[2,32,256]{2,1,0:T(8,128)S(1)}, u32[]{:S(2)}, u32[]{:S(2)}) collective-permute-start(f32[2,32,256]{2,1,0:T(8,128)S(1)} %maximum_select_fusion.11), channel_id=1, source_target_pairs={{0,8},{1,9},{2,10},{3,11},{4,12},{5,13},{6,14},{7,15},{8,0},{9,1},... | collective-permute-start | bytes 196616 | tf_op jit(solution)/shard_map/ppermute | solution.py:54
  41.8 5.0 %collective-permute-start.7 = (f32[2,32,512]{2,1,0:T(8,128)S(1)}, f32[2,32,512]{2,1,0:T(8,128)S(1)}, u32[]{:S(2)}, u32[]{:S(2)}) collective-permute-start(f32[2,32,512]{2,1,0:T(8,128)S(1)} %maximum_select_fusion.8), channel_id=1, source_target_pairs={{0,4},{1,3},{2,6},{3,1},{4,0},{5,7},{6,2},{7,5},{8,12},{9,11},{10,... | collective-permute-start | bytes 393224 | tf_op jit(solution)/shard_map/ppermute | solution.py:54
  46.9 6.4 %collective-permute-start.8 = (f32[2,32,1024]{2,1,0:T(8,128)S(1)}, f32[2,32,1024]{2,1,0:T(8,128)S(1)}, u32[]{:S(2)}, u32[]{:S(2)}) collective-permute-start(f32[2,32,1024]{2,1,0:T(8,128)S(1)} %maximum_select_fusion.5), channel_id=1, source_target_pairs={{0,2},{1,5},{2,0},{3,7},{4,6},{5,1},{6,4},{7,3},{8,10},{9,13},{10,... | collective-permute-start | bytes 786440 | tf_op jit(solution)/shard_map/ppermute | solution.py:54
  53.4 2.0 %collective-permute-start.9 = (f32[2,32,2048]{2,1,0:T(8,128)S(1)}, f32[2,32,2048]{2,1,0:T(8,128)S(1)}, u32[]{:S(2)}, u32[]{:S(2)}) collective-permute-start(f32[2,32,2048]{2,1,0:T(8,128)S(1)} %maximum_select_fusion.2), channel_id=1, source_target_pairs={{0,1},{1,0},{2,3},{3,2},{4,5},{5,4},{6,7},{7,6},{8,9},{9,8},{10,11... | collective-permute-start | bytes 1572872 | tf_op jit(solution)/shard_map/ppermute | solution.py:54
  55.5 2.2 %copy-start = (f32[2,128,4096]{2,1,0:T(8,128)S(1)}, f32[2,128,4096]{2,1,0:T(8,128)}, u32[]{:S(2)}) copy-start(f32[2,128,4096]{2,1,0:T(8,128)} %f_ref.1) | copy-start | bytes 12582916
  59.9 4.9 %collective-permute-start.10 = (f32[2,32,128]{2,1,0:T(8,128)S(1)}, f32[2,32,128]{2,1,0:T(8,128)S(1)}, u32[]{:S(2)}, u32[]{:S(2)}) collective-permute-start(f32[2,32,128]{2,1,0:T(8,128)S(1)} %shard_map.83), channel_id=1, source_target_pairs={{0,16},{1,17},{2,18},{3,19},{4,20},{5,21},{6,22},{7,23},{8,24},{9,... | collective-permute-start | bytes 98312 | tf_op jit(solution)/shard_map/ppermute | solution.py:63
  64.8 4.3 %collective-permute-start.11 = (f32[2,32,2,128]{3,1,0,2:T(8,128)S(1)}, f32[2,32,2,128]{3,1,0,2:T(8,128)S(1)}, u32[]{:S(2)}, u32[]{:S(2)}) collective-permute-start(f32[2,32,2,128]{3,1,0,2:T(8,128)S(1)} %maximum_select_fusion.13), channel_id=1, source_target_pairs={{0,8},{1,9},{2,10},{3,11},{4,12},{5,13},{6,14},{7,15},{8,0},{9,1},... | collective-permute-start | bytes 196616 | tf_op jit(solution)/shard_map/ppermute | solution.py:63
  69.2 5.0 %collective-permute-start.12 = (f32[2,32,2,2,128]{4,1,0,2,3:T(8,128)S(1)}, f32[2,32,2,2,128]{4,1,0,2,3:T(8,128)S(1)}, u32[]{:S(2)}, u32[]{:S(2)}) collective-permute-start(f32[2,32,2,2,128]{4,1,0,2,3:T(8,128)S(1)} %maximum_select_fusion.10), channel_id=1, source_target_pairs={{0,4},{1,5},{2,6},{3,7},{4,0},{5,1},{6,2},{7,3},{8,12},{9,13},{10,... | collective-permute-start | bytes 393224 | tf_op jit(solution)/shard_map/ppermute | solution.py:63
  74.2 6.4 %collective-permute-start.13 = (f32[2,32,2,2,2,128]{5,1,0,2,3,4:T(8,128)S(1)}, f32[2,32,2,2,2,128]{5,1,0,2,3,4:T(8,128)S(1)}, u32[]{:S(2)}, u32[]{:S(2)}) collective-permute-start(f32[2,32,2,2,2,128]{5,1,0,2,3,4:T(8,128)S(1)} %maximum_select_fusion.7), channel_id=1, source_target_pairs={{0,2},{1,3},{2,0},{3,1},{4,6},{5,7},{6,4},{7,5},{8,10},{9,11},{10,... | collective-permute-start | bytes 786440 | tf_op jit(solution)/shard_map/ppermute | solution.py:63
  80.7 2.0 %collective-permute-start.14 = (f32[2,32,2,2,2,2,128]{6,1,0,2,3,4,5:T(8,128)S(1)}, f32[2,32,2,2,2,2,128]{6,1,0,2,3,4,5:T(8,128)S(1)}, u32[]{:S(2)}, u32[]{:S(2)}) collective-permute-start(f32[2,32,2,2,2,2,128]{6,1,0,2,3,4,5:T(8,128)S(1)} %maximum_select_fusion.4), channel_id=1, source_target_pairs={{0,1},{1,0},{2,3},{3,2},{4,5},{5,4},{6,7},{7,6},{8,9},{9,8},{10,11... | collective-permute-start | bytes 1572872 | tf_op jit(solution)/shard_map/ppermute | solution.py:63
  90.8 1.2 %collective-permute-start.15 = (f32[2,32]{1,0:T(2,128)S(1)}, f32[2,32]{1,0:T(2,128)S(1)}, u32[]{:S(2)}, u32[]{:S(2)}) collective-permute-start(f32[2,32]{1,0:T(2,128)S(1)} %pad_maximum_fusion), channel_id=1, source_target_pairs={{0,1},{1,0},{2,3},{3,2},{4,5},{5,4},{6,7},{7,6},{8,9},{9,8},{10,11... | collective-permute-start | bytes 776 | tf_op jit(solution)/shard_map/ppermute | solution.py:74
  92.0 3.6 %collective-permute-start.16 = (f32[2,32]{1,0:T(2,128)S(1)}, f32[2,32]{1,0:T(2,128)S(1)}, u32[]{:S(2)}, u32[]{:S(2)}) collective-permute-start(f32[2,32]{1,0:T(2,128)S(1)} %fusion.7), channel_id=1, source_target_pairs={{0,2},{1,3},{2,0},{3,1},{4,6},{5,7},{6,4},{7,5},{8,10},{9,11},{10,... | collective-permute-start | bytes 776 | tf_op jit(solution)/shard_map/ppermute | solution.py:74
  95.7 3.6 %collective-permute-start.17 = (f32[2,32]{1,0:T(2,128)S(1)}, f32[2,32]{1,0:T(2,128)S(1)}, u32[]{:S(2)}, u32[]{:S(2)}) collective-permute-start(f32[2,32]{1,0:T(2,128)S(1)} %fusion.10), channel_id=1, source_target_pairs={{0,4},{1,5},{2,6},{3,7},{4,0},{5,1},{6,2},{7,3},{8,12},{9,13},{10,... | collective-permute-start | bytes 776 | tf_op jit(solution)/shard_map/ppermute | solution.py:74
  99.3 3.6 %collective-permute-start.18 = (f32[2,32]{1,0:T(2,128)S(1)}, f32[2,32]{1,0:T(2,128)S(1)}, u32[]{:S(2)}, u32[]{:S(2)}) collective-permute-start(f32[2,32]{1,0:T(2,128)S(1)} %add.47), channel_id=1, source_target_pairs={{0,8},{1,9},{2,10},{3,11},{4,12},{5,13},{6,14},{7,15},{8,0},{9,1},... | collective-permute-start | bytes 776 | tf_op jit(solution)/shard_map/ppermute | solution.py:74
  102.9 4.5 %collective-permute-start.19 = (f32[2,32]{1,0:T(2,128)S(1)}, f32[2,32]{1,0:T(2,128)S(1)}, u32[]{:S(2)}, u32[]{:S(2)}) collective-permute-start(f32[2,32]{1,0:T(2,128)S(1)} %add.48), channel_id=1, source_target_pairs={{0,16},{1,17},{2,18},{3,19},{4,20},{5,21},{6,22},{7,23},{8,24},{9,... | collective-permute-start | bytes 776 | tf_op jit(solution)/shard_map/ppermute | solution.py:74

commit v14 on v10

--- a/solution.py
+++ b/solution.py
@@ -40,15 +40,16 @@
     orders = _orders(size)
     steps = _steps(size)
     bits = [jnp.where((me & 1) == 0, (me >> orders[0][t]) & 1, (me >> orders[1][t]) & 1) for t in range(steps)]
-    cur = keep + lax.ppermute(send, "rows", _pairs(size, orders, 0))
+    recv = lax.ppermute(send, "rows", _pairs(size, orders, 0))
     for t in range(1, steps):
-        half = cur.shape[axis] // 2
-        lo = lax.slice_in_dim(cur, 0, half, axis=axis)
-        hi = lax.slice_in_dim(cur, half, 2 * half, axis=axis)
+        half = keep.shape[axis] // 2
+        part = lambda a, lo_half: lax.slice_in_dim(a, 0 if lo_half else half, half if lo_half else 2 * half, axis=axis)
+        lo = part(keep, True) + part(recv, True)
+        hi = part(keep, False) + part(recv, False)
         low = bits[t] == 0
-        keep = jnp.where(low, lo, hi)
-        send = jnp.where(low, hi, lo)
-        cur = keep + lax.ppermute(send, "rows", _pairs(size, orders, t))
+        keep, send = jnp.where(low, lo, hi), jnp.where(low, hi, lo)
+        recv = lax.ppermute(send, "rows", _pairs(size, orders, t))
+    cur = keep + recv
     for t in reversed(range(steps)):
         low = bits[t] == 0
         cur = _join(cur, lax.ppermute(cur, "rows", _pairs(size, orders, t)), low, axis)

time: 108 us -> 108 us (level)
    add x5 -> x1, other arithmetic: 1.18 us -> 0.01 us  [_allreduce(): cur = keep + recv]
    select_n x4, other arithmetic: 0.07 us -> 1.16 us  [_allreduce(): keep, send = (jnp.where(low, lo, hi), jnp.where(low, hi, lo))]
where the time goes in v14:
time: 108 us
  waiting for transfers between devices  50.3 us (47%)
  starting transfers between devices  35.8 us (33%)
  Pallas kernels  9.13 us (8%)
  matrix products  6.3 us (6%)
  local copies, waits for them, and re-layouts  3.83 us (4%)
  other arithmetic  2.42 us (2%)
    ppermute x5, waiting for transfers between devices, _allreduce(): lax.ppermute(cur, 'rows', _pairs(size, orders, t))  14.4 us
    ppermute x5, waiting for transfers between devices, _allgather(): other = lax.ppermute(cur, 'rows', _xor_pairs(size, s))  14.3 us
    ppermute x4, waiting for transfers between devices, _allreduce(): recv = lax.ppermute(send, 'rows', _pairs(size, orders, t))  11.5 us
    ppermute x4, starting transfers between devices, _allreduce(): recv = lax.ppermute(send, 'rows', _pairs(size, orders, t))  10.6 us
    ppermute x5, waiting for transfers between devices, _butterfly_sum(): x = x + lax.ppermute(x, 'rows', _xor_pairs(size, s))  8.35 us
    ppermute x5, starting transfers between devices, _allreduce(): lax.ppermute(cur, 'rows', _pairs(size, orders, t))  8.27 us
    ppermute x5, starting transfers between devices, _allgather(): other = lax.ppermute(cur, 'rows', _xor_pairs(size, s))  8.22 us
    ppermute x5, starting transfers between devices, _butterfly_sum(): x = x + lax.ppermute(x, 'rows', _xor_pairs(size, s))  8.2 us
  transfers between devices with their start and end apart: 20, of which 20 were waited for; matrix products, arithmetic and copies ran while one was open for 0% of the time, Pallas kernels for 0%

profile of v14, /device:TPU:0, one launch (start us, length us, event | category | flops | bytes accessed | tf_op | source)
XLA Modules:
  0.0 107.9 jit_solution(11759402384555125607)
XLA Ops:
  0.0 7.0 %shard_map.82 = (f32[2,32,2048]{2,1,0:T(8,128)}, f32[2,32,2048]{2,1,0:T(8,128)}) custom-call(s32[1,32]{1,0:T(1,128)} %bitcast.55, s32[1,128]{1,0:T(1,128)} %bitcast.56, bf16[128,2,4096]{2,1,0:T(2,128)(2,1)} %acts_ref.1, bf16[128,2,4096]{2,1,0:T(2,128)(2,1)} %gout_ref.1, bf16[4096,128]{1,0:T(8,128)(2,1)} %pin_ref.1, bf16[4096,128]{1,0:T(8,128)(2,1)} %pout_ref.1), custom_call_target="tpu_custom_call" | custom-call | tf_op jit(solution)/shard_map/pallas_call | solution.py:130
  10.3 2.9 %collective-permute-start.1 = (f32[2,32,1024]{2,1,0:T(8,128)S(1)}, f32[2,32,1024]{2,1,0:T(8,128)S(1)}, u32[]{:S(2)}, u32[]{:S(2)}) collective-permute-start(f32[2,32,1024]{2,1,0:T(8,128)S(1)} %get-tuple-element.12), channel_id=1, source_target_pairs={{0,2},{1,5},{2,0},{3,7},{4,6},{5,1},{6,4},{7,3},{8,10},{9,13},{10,... | collective-permute-start | bytes 786440 | tf_op jit(solution)/shard_map/ppermute | solution.py:51
  13.2 4.4 %collective-permute-done.1 = f32[2,32,1024]{2,1,0:T(8,128)S(1)} collective-permute-done((f32[2,32,1024]{2,1,0:T(8,128)S(1)}, f32[2,32,1024]{2,1,0:T(8,128)S(1)}, u32[]{:S(2)}, u32[]{:S(2)}) %collective-permute-start.1) | collective-permute-done | bytes 262176 | tf_op jit(solution)/shard_map/ppermute | solution.py:51
  17.6 2.1 %collective-permute-start.2 = (f32[2,32,512]{2,1,0:T(8,128)S(1)}, f32[2,32,512]{2,1,0:T(8,128)S(1)}, u32[]{:S(2)}, u32[]{:S(2)}) collective-permute-start(f32[2,32,512]{2,1,0:T(8,128)S(1)} %get-tuple-element.14), channel_id=1, source_target_pairs={{0,4},{1,3},{2,6},{3,1},{4,0},{5,7},{6,2},{7,5},{8,12},{9,11},{10,... | collective-permute-start | bytes 393224 | tf_op jit(solution)/shard_map/ppermute | solution.py:51
  19.7 2.9 %collective-permute-done.2 = f32[2,32,512]{2,1,0:T(8,128)S(1)} collective-permute-done((f32[2,32,512]{2,1,0:T(8,128)S(1)}, f32[2,32,512]{2,1,0:T(8,128)S(1)}, u32[]{:S(2)}, u32[]{:S(2)}) %collective-permute-start.2) | collective-permute-done | bytes 131104 | tf_op jit(solution)/shard_map/ppermute | solution.py:51
  22.7 2.1 %collective-permute-start.3 = (f32[2,32,256]{2,1,0:T(8,128)S(1)}, f32[2,32,256]{2,1,0:T(8,128)S(1)}, u32[]{:S(2)}, u32[]{:S(2)}) collective-permute-start(f32[2,32,256]{2,1,0:T(8,128)S(1)} %get-tuple-element.16), channel_id=1, source_target_pairs={{0,8},{1,9},{2,10},{3,11},{4,12},{5,13},{6,14},{7,15},{8,0},{9,1},... | collective-permute-start | bytes 196616 | tf_op jit(solution)/shard_map/ppermute | solution.py:51
  24.8 2.2 %collective-permute-done.3 = f32[2,32,256]{2,1,0:T(8,128)S(1)} collective-permute-done((f32[2,32,256]{2,1,0:T(8,128)S(1)}, f32[2,32,256]{2,1,0:T(8,128)S(1)}, u32[]{:S(2)}, u32[]{:S(2)}) %collective-permute-start.3) | collective-permute-done | bytes 65568 | tf_op jit(solution)/shard_map/ppermute | solution.py:51
  27.1 3.4 %collective-permute-start.4 = (f32[2,32,128]{2,1,0:T(8,128)S(1)}, f32[2,32,128]{2,1,0:T(8,128)S(1)}, u32[]{:S(2)}, u32[]{:S(2)}) collective-permute-start(f32[2,32,128]{2,1,0:T(8,128)S(1)} %broadcast_select_fusion.6), channel_id=1, source_target_pairs={{0,16},{1,17},{2,18},{3,19},{4,20},{5,21},{6,22},{7,23},{8,24},{9,... | collective-permute-start | bytes 98312 | tf_op jit(solution)/shard_map/ppermute | solution.py:51
  32.5 2.9 %collective-permute-start.5 = (f32[2,32,128]{2,1,0:T(8,128)S(1)}, f32[2,32,128]{2,1,0:T(8,128)S(1)}, u32[]{:S(2)}, u32[]{:S(2)}) collective-permute-start(f32[2,32,128]{2,1,0:T(8,128)S(1)} %select_add_fusion), channel_id=1, source_target_pairs={{0,16},{1,17},{2,18},{3,19},{4,20},{5,21},{6,22},{7,23},{8,24},{9,... | collective-permute-start | bytes 98312 | tf_op jit(solution)/shard_map/ppermute | solution.py:55
  37.4 2.1 %collective-permute-start.6 = (f32[2,32,256]{2,1,0:T(8,128)S(1)}, f32[2,32,256]{2,1,0:T(8,128)S(1)}, u32[]{:S(2)}, u32[]{:S(2)}) collective-permute-start(f32[2,32,256]{2,1,0:T(8,128)S(1)} %maximum_select_fusion.11), channel_id=1, source_target_pairs={{0,8},{1,9},{2,10},{3,11},{4,12},{5,13},{6,14},{7,15},{8,0},{9,1},... | collective-permute-start | bytes 196616 | tf_op jit(solution)/shard_map/ppermute | solution.py:55
  39.5 2.3 %collective-permute-done.6 = f32[2,32,256]{2,1,0:T(8,128)S(1)} collective-permute-done((f32[2,32,256]{2,1,0:T(8,128)S(1)}, f32[2,32,256]{2,1,0:T(8,128)S(1)}, u32[]{:S(2)}, u32[]{:S(2)}) %collective-permute-start.6) | collective-permute-done | bytes 65568 | tf_op jit(solution)/shard_map/ppermute | solution.py:55
  43.4 3.4 %collective-permute-done.7 = f32[2,32,512]{2,1,0:T(8,128)S(1)} collective-permute-done((f32[2,32,512]{2,1,0:T(8,128)S(1)}, f32[2,32,512]{2,1,0:T(8,128)S(1)}, u32[]{:S(2)}, u32[]{:S(2)}) %collective-permute-start.7) | collective-permute-done | bytes 131104 | tf_op jit(solution)/shard_map/ppermute | solution.py:55
  48.4 4.8 %collective-permute-done.8 = f32[2,32,1024]{2,1,0:T(8,128)S(1)} collective-permute-done((f32[2,32,1024]{2,1,0:T(8,128)S(1)}, f32[2,32,1024]{2,1,0:T(8,128)S(1)}, u32[]{:S(2)}, u32[]{:S(2)}) %collective-permute-start.8) | collective-permute-done | bytes 262176 | tf_op jit(solution)/shard_map/ppermute | solution.py:55
  55.4 2.2 %copy-done = f32[2,128,4096]{2,1,0:T(8,128)S(1)} copy-done((f32[2,128,4096]{2,1,0:T(8,128)S(1)}, f32[2,128,4096]{2,1,0:T(8,128)}, u32[]{:S(2)}) %copy-start) | copy-done | bytes 4194328
  57.6 2.2 %shard_map.83 = f32[2,32,128]{2,1,0:T(8,128)S(1)} custom-call(f32[2,32,4096]{2,1,0:T(8,128)S(1)} %maximum_select_fusion.g_ref, f32[2,128,4096]{2,1,0:T(8,128)S(1)} %copy-done), custom_call_target="tpu_custom_call" | custom-call | tf_op jit(solution)/shard_map/pallas_call | solution.py:153
  59.8 3.0 %collective-permute-start.10 = (f32[2,32,128]{2,1,0:T(8,128)S(1)}, f32[2,32,128]{2,1,0:T(8,128)S(1)}, u32[]{:S(2)}, u32[]{:S(2)}) collective-permute-start(f32[2,32,128]{2,1,0:T(8,128)S(1)} %shard_map.83), channel_id=1, source_target_pairs={{0,16},{1,17},{2,18},{3,19},{4,20},{5,21},{6,22},{7,23},{8,24},{9,... | collective-permute-start | bytes 98312 | tf_op jit(solution)/shard_map/ppermute | solution.py:64
  64.7 2.0 %collective-permute-start.11 = (f32[2,32,2,128]{3,1,0,2:T(8,128)S(1)}, f32[2,32,2,128]{3,1,0,2:T(8,128)S(1)}, u32[]{:S(2)}, u32[]{:S(2)}) collective-permute-start(f32[2,32,2,128]{3,1,0,2:T(8,128)S(1)} %maximum_select_fusion.13), channel_id=1, source_target_pairs={{0,8},{1,9},{2,10},{3,11},{4,12},{5,13},{6,14},{7,15},{8,0},{9,1},... | collective-permute-start | bytes 196616 | tf_op jit(solution)/shard_map/ppermute | solution.py:64
  66.7 2.3 %collective-permute-done.11 = f32[2,32,2,128]{3,1,0,2:T(8,128)S(1)} collective-permute-done((f32[2,32,2,128]{3,1,0,2:T(8,128)S(1)}, f32[2,32,2,128]{3,1,0,2:T(8,128)S(1)}, u32[]{:S(2)}, u32[]{:S(2)}) %collective-permute-start.11) | collective-permute-done | bytes 65568 | tf_op jit(solution)/shard_map/ppermute | solution.py:64
  70.6 3.4 %collective-permute-done.12 = f32[2,32,2,2,128]{4,1,0,2,3:T(8,128)S(1)} collective-permute-done((f32[2,32,2,2,128]{4,1,0,2,3:T(8,128)S(1)}, f32[2,32,2,2,128]{4,1,0,2,3:T(8,128)S(1)}, u32[]{:S(2)}, u32[]{:S(2)}) %collective-permute-start.12) | collective-permute-done | bytes 131104 | tf_op jit(solution)/shard_map/ppermute | solution.py:64
  75.7 4.8 %collective-permute-done.13 = f32[2,32,2,2,2,128]{5,1,0,2,3,4:T(8,128)S(1)} collective-permute-done((f32[2,32,2,2,2,128]{5,1,0,2,3,4:T(8,128)S(1)}, f32[2,32,2,2,2,128]{5,1,0,2,3,4:T(8,128)S(1)}, u32[]{:S(2)}, u32[]{:S(2)}) %collective-permute-start.13) | collective-permute-done | bytes 262176 | tf_op jit(solution)/shard_map/ppermute | solution.py:64
  84.3 6.3 %fusion.8 = (f32[32]{0:T(128)S(1)}, f32[32]{0:T(128)S(1)}, f32[32,128]{1,0:T(8,128)S(1)}) fusion(f32[2,32,4096]{2,1,0:T(8,128)S(1)} %select_n.249, f32[128,2,4096]{2,1,0:T(2,128)} %param.15), kind=kOutput, calls=%fused_computation.41 | convolution fusion | flops 201338816 | bytes 5259520 | tf_op jit(solution)/shard_map/mqk,nmk->qn/dot_general | solution.py:169
  93.4 2.1 %collective-permute-done.16 = f32[2,32]{1,0:T(2,128)S(1)} collective-permute-done((f32[2,32]{1,0:T(2,128)S(1)}, f32[2,32]{1,0:T(2,128)S(1)}, u32[]{:S(2)}, u32[]{:S(2)}) %collective-permute-start.16) | collective-permute-done | bytes 288 | tf_op jit(solution)/shard_map/ppermute | solution.py:75
  97.1 2.1 %collective-permute-done.17 = f32[2,32]{1,0:T(2,128)S(1)} collective-permute-done((f32[2,32]{1,0:T(2,128)S(1)}, f32[2,32]{1,0:T(2,128)S(1)}, u32[]{:S(2)}, u32[]{:S(2)}) %collective-permute-start.17) | collective-permute-done | bytes 288 | tf_op jit(solution)/shard_map/ppermute | solution.py:75
  102.8 2.9 %collective-permute-start.19 = (f32[2,32]{1,0:T(2,128)S(1)}, f32[2,32]{1,0:T(2,128)S(1)}, u32[]{:S(2)}, u32[]{:S(2)}) collective-permute-start(f32[2,32]{1,0:T(2,128)S(1)} %add.64), channel_id=1, source_target_pairs={{0,16},{1,17},{2,18},{3,19},{4,20},{5,21},{6,22},{7,23},{8,24},{9,... | collective-permute-start | bytes 776 | tf_op jit(solution)/shard_map/ppermute | solution.py:75
  (54 shorter events, 31.8 us)
Async XLA Ops:
  7.0 2.2 %collective-permute-start = (f32[2,32,2048]{2,1,0:T(8,128)}, f32[2,32,2048]{2,1,0:T(8,128)S(1)}, u32[]{:S(2)}, u32[]{:S(2)}) collective-permute-start(f32[2,32,2048]{2,1,0:T(8,128)} %get-tuple-element.8), channel_id=1, source_target_pairs={{0,1},{1,0},{2,3},{3,2},{4,5},{5,4},{6,7},{7,6},{8,9},{9,8},{10,11... | collective-permute-start | bytes 1572872 | tf_op jit(solution)/shard_map/ppermute | solution.py:43
  10.3 7.3 %collective-permute-start.1 = (f32[2,32,1024]{2,1,0:T(8,128)S(1)}, f32[2,32,1024]{2,1,0:T(8,128)S(1)}, u32[]{:S(2)}, u32[]{:S(2)}) collective-permute-start(f32[2,32,1024]{2,1,0:T(8,128)S(1)} %get-tuple-element.12), channel_id=1, source_target_pairs={{0,2},{1,5},{2,0},{3,7},{4,6},{5,1},{6,4},{7,3},{8,10},{9,13},{10,... | collective-permute-start | bytes 786440 | tf_op jit(solution)/shard_map/ppermute | solution.py:51
  17.6 5.1 %collective-permute-start.2 = (f32[2,32,512]{2,1,0:T(8,128)S(1)}, f32[2,32,512]{2,1,0:T(8,128)S(1)}, u32[]{:S(2)}, u32[]{:S(2)}) collective-permute-start(f32[2,32,512]{2,1,0:T(8,128)S(1)} %get-tuple-element.14), channel_id=1, source_target_pairs={{0,4},{1,3},{2,6},{3,1},{4,0},{5,7},{6,2},{7,5},{8,12},{9,11},{10,... | collective-permute-start | bytes 393224 | tf_op jit(solution)/shard_map/ppermute | solution.py:51
  22.7 4.4 %collective-permute-start.3 = (f32[2,32,256]{2,1,0:T(8,128)S(1)}, f32[2,32,256]{2,1,0:T(8,128)S(1)}, u32[]{:S(2)}, u32[]{:S(2)}) collective-permute-start(f32[2,32,256]{2,1,0:T(8,128)S(1)} %get-tuple-element.16), channel_id=1, source_target_pairs={{0,8},{1,9},{2,10},{3,11},{4,12},{5,13},{6,14},{7,15},{8,0},{9,1},... | collective-permute-start | bytes 196616 | tf_op jit(solution)/shard_map/ppermute | solution.py:51
  27.1 5.4 %collective-permute-start.4 = (f32[2,32,128]{2,1,0:T(8,128)S(1)}, f32[2,32,128]{2,1,0:T(8,128)S(1)}, u32[]{:S(2)}, u32[]{:S(2)}) collective-permute-start(f32[2,32,128]{2,1,0:T(8,128)S(1)} %broadcast_select_fusion.6), channel_id=1, source_target_pairs={{0,16},{1,17},{2,18},{3,19},{4,20},{5,21},{6,22},{7,23},{8,24},{9,... | collective-permute-start | bytes 98312 | tf_op jit(solution)/shard_map/ppermute | solution.py:51
  32.5 4.9 %collective-permute-start.5 = (f32[2,32,128]{2,1,0:T(8,128)S(1)}, f32[2,32,128]{2,1,0:T(8,128)S(1)}, u32[]{:S(2)}, u32[]{:S(2)}) collective-permute-start(f32[2,32,128]{2,1,0:T(8,128)S(1)} %select_add_fusion), channel_id=1, source_target_pairs={{0,16},{1,17},{2,18},{3,19},{4,20},{5,21},{6,22},{7,23},{8,24},{9,... | collective-permute-start | bytes 98312 | tf_op jit(solution)/shard_map/ppermute | solution.py:55
  37.4 4.3 %collective-permute-start.6 = (f32[2,32,256]{2,1,0:T(8,128)S(1)}, f32[2,32,256]{2,1,0:T(8,128)S(1)}, u32[]{:S(2)}, u32[]{:S(2)}) collective-permute-start(f32[2,32,256]{2,1,0:T(8,128)S(1)} %maximum_select_fusion.11), channel_id=1, source_target_pairs={{0,8},{1,9},{2,10},{3,11},{4,12},{5,13},{6,14},{7,15},{8,0},{9,1},... | collective-permute-start | bytes 196616 | tf_op jit(solution)/shard_map/ppermute | solution.py:55
  41.8 5.0 %collective-permute-start.7 = (f32[2,32,512]{2,1,0:T(8,128)S(1)}, f32[2,32,512]{2,1,0:T(8,128)S(1)}, u32[]{:S(2)}, u32[]{:S(2)}) collective-permute-start(f32[2,32,512]{2,1,0:T(8,128)S(1)} %maximum_select_fusion.8), channel_id=1, source_target_pairs={{0,4},{1,3},{2,6},{3,1},{4,0},{5,7},{6,2},{7,5},{8,12},{9,11},{10,... | collective-permute-start | bytes 393224 | tf_op jit(solution)/shard_map/ppermute | solution.py:55
  46.8 6.4 %collective-permute-start.8 = (f32[2,32,1024]{2,1,0:T(8,128)S(1)}, f32[2,32,1024]{2,1,0:T(8,128)S(1)}, u32[]{:S(2)}, u32[]{:S(2)}) collective-permute-start(f32[2,32,1024]{2,1,0:T(8,128)S(1)} %maximum_select_fusion.5), channel_id=1, source_target_pairs={{0,2},{1,5},{2,0},{3,7},{4,6},{5,1},{6,4},{7,3},{8,10},{9,13},{10,... | collective-permute-start | bytes 786440 | tf_op jit(solution)/shard_map/ppermute | solution.py:55
  53.3 2.0 %collective-permute-start.9 = (f32[2,32,2048]{2,1,0:T(8,128)S(1)}, f32[2,32,2048]{2,1,0:T(8,128)S(1)}, u32[]{:S(2)}, u32[]{:S(2)}) collective-permute-start(f32[2,32,2048]{2,1,0:T(8,128)S(1)} %maximum_select_fusion.2), channel_id=1, source_target_pairs={{0,1},{1,0},{2,3},{3,2},{4,5},{5,4},{6,7},{7,6},{8,9},{9,8},{10,11... | collective-permute-start | bytes 1572872 | tf_op jit(solution)/shard_map/ppermute | solution.py:55
  55.4 2.2 %copy-start = (f32[2,128,4096]{2,1,0:T(8,128)S(1)}, f32[2,128,4096]{2,1,0:T(8,128)}, u32[]{:S(2)}) copy-start(f32[2,128,4096]{2,1,0:T(8,128)} %f_ref.1) | copy-start | bytes 12582916
  59.8 4.9 %collective-permute-start.10 = (f32[2,32,128]{2,1,0:T(8,128)S(1)}, f32[2,32,128]{2,1,0:T(8,128)S(1)}, u32[]{:S(2)}, u32[]{:S(2)}) collective-permute-start(f32[2,32,128]{2,1,0:T(8,128)S(1)} %shard_map.83), channel_id=1, source_target_pairs={{0,16},{1,17},{2,18},{3,19},{4,20},{5,21},{6,22},{7,23},{8,24},{9,... | collective-permute-start | bytes 98312 | tf_op jit(solution)/shard_map/ppermute | solution.py:64
  64.7 4.3 %collective-permute-start.11 = (f32[2,32,2,128]{3,1,0,2:T(8,128)S(1)}, f32[2,32,2,128]{3,1,0,2:T(8,128)S(1)}, u32[]{:S(2)}, u32[]{:S(2)}) collective-permute-start(f32[2,32,2,128]{3,1,0,2:T(8,128)S(1)} %maximum_select_fusion.13), channel_id=1, source_target_pairs={{0,8},{1,9},{2,10},{3,11},{4,12},{5,13},{6,14},{7,15},{8,0},{9,1},... | collective-permute-start | bytes 196616 | tf_op jit(solution)/shard_map/ppermute | solution.py:64
  69.0 5.0 %collective-permute-start.12 = (f32[2,32,2,2,128]{4,1,0,2,3:T(8,128)S(1)}, f32[2,32,2,2,128]{4,1,0,2,3:T(8,128)S(1)}, u32[]{:S(2)}, u32[]{:S(2)}) collective-permute-start(f32[2,32,2,2,128]{4,1,0,2,3:T(8,128)S(1)} %maximum_select_fusion.10), channel_id=1, source_target_pairs={{0,4},{1,5},{2,6},{3,7},{4,0},{5,1},{6,2},{7,3},{8,12},{9,13},{10,... | collective-permute-start | bytes 393224 | tf_op jit(solution)/shard_map/ppermute | solution.py:64
  74.1 6.4 %collective-permute-start.13 = (f32[2,32,2,2,2,128]{5,1,0,2,3,4:T(8,128)S(1)}, f32[2,32,2,2,2,128]{5,1,0,2,3,4:T(8,128)S(1)}, u32[]{:S(2)}, u32[]{:S(2)}) collective-permute-start(f32[2,32,2,2,2,128]{5,1,0,2,3,4:T(8,128)S(1)} %maximum_select_fusion.7), channel_id=1, source_target_pairs={{0,2},{1,3},{2,0},{3,1},{4,6},{5,7},{6,4},{7,5},{8,10},{9,11},{10,... | collective-permute-start | bytes 786440 | tf_op jit(solution)/shard_map/ppermute | solution.py:64
  80.6 2.0 %collective-permute-start.14 = (f32[2,32,2,2,2,2,128]{6,1,0,2,3,4,5:T(8,128)S(1)}, f32[2,32,2,2,2,2,128]{6,1,0,2,3,4,5:T(8,128)S(1)}, u32[]{:S(2)}, u32[]{:S(2)}) collective-permute-start(f32[2,32,2,2,2,2,128]{6,1,0,2,3,4,5:T(8,128)S(1)} %maximum_select_fusion.4), channel_id=1, source_target_pairs={{0,1},{1,0},{2,3},{3,2},{4,5},{5,4},{6,7},{7,6},{8,9},{9,8},{10,11... | collective-permute-start | bytes 1572872 | tf_op jit(solution)/shard_map/ppermute | solution.py:64
  90.6 1.2 %collective-permute-start.15 = (f32[2,32]{1,0:T(2,128)S(1)}, f32[2,32]{1,0:T(2,128)S(1)}, u32[]{:S(2)}, u32[]{:S(2)}) collective-permute-start(f32[2,32]{1,0:T(2,128)S(1)} %pad_maximum_fusion), channel_id=1, source_target_pairs={{0,1},{1,0},{2,3},{3,2},{4,5},{5,4},{6,7},{7,6},{8,9},{9,8},{10,11... | collective-permute-start | bytes 776 | tf_op jit(solution)/shard_map/ppermute | solution.py:75
  91.9 3.6 %collective-permute-start.16 = (f32[2,32]{1,0:T(2,128)S(1)}, f32[2,32]{1,0:T(2,128)S(1)}, u32[]{:S(2)}, u32[]{:S(2)}) collective-permute-start(f32[2,32]{1,0:T(2,128)S(1)} %fusion.7), channel_id=1, source_target_pairs={{0,2},{1,3},{2,0},{3,1},{4,6},{5,7},{6,4},{7,5},{8,10},{9,11},{10,... | collective-permute-start | bytes 776 | tf_op jit(solution)/shard_map/ppermute | solution.py:75
  95.5 3.6 %collective-permute-start.17 = (f32[2,32]{1,0:T(2,128)S(1)}, f32[2,32]{1,0:T(2,128)S(1)}, u32[]{:S(2)}, u32[]{:S(2)}) collective-permute-start(f32[2,32]{1,0:T(2,128)S(1)} %fusion.10), channel_id=1, source_target_pairs={{0,4},{1,5},{2,6},{3,7},{4,0},{5,1},{6,2},{7,3},{8,12},{9,13},{10,... | collective-permute-start | bytes 776 | tf_op jit(solution)/shard_map/ppermute | solution.py:75
  99.2 3.6 %collective-permute-start.18 = (f32[2,32]{1,0:T(2,128)S(1)}, f32[2,32]{1,0:T(2,128)S(1)}, u32[]{:S(2)}, u32[]{:S(2)}) collective-permute-start(f32[2,32]{1,0:T(2,128)S(1)} %add.63), channel_id=1, source_target_pairs={{0,8},{1,9},{2,10},{3,11},{4,12},{5,13},{6,14},{7,15},{8,0},{9,1},... | collective-permute-start | bytes 776 | tf_op jit(solution)/shard_map/ppermute | solution.py:75
  102.8 4.5 %collective-permute-start.19 = (f32[2,32]{1,0:T(2,128)S(1)}, f32[2,32]{1,0:T(2,128)S(1)}, u32[]{:S(2)}, u32[]{:S(2)}) collective-permute-start(f32[2,32]{1,0:T(2,128)S(1)} %add.64), channel_id=1, source_target_pairs={{0,16},{1,17},{2,18},{3,19},{4,20},{5,21},{6,22},{7,23},{8,24},{9,... | collective-permute-start | bytes 776 | tf_op jit(solution)/shard_map/ppermute | solution.py:75
